TPU v7x, 32 devices: a whole 2x2x4 slice. The times are simulated.
32 devices in a mesh: groups: 2 (over y), lat: 4 (over x, core), lon: 4 (over z).
Axes of the slice: x: 2, y: 2, z: 4, core: 2. Of those that a mesh axis runs over, the one named last changes fastest.
Arguments:
- fields: bfloat16 [512, 4, 512], P('groups', 'lat', 'lon'), parts along dimension 0, may hold values from -6 to 6
- upstream: bfloat16 [512, 4, 512], P('groups', 'lat', 'lon'), parts along dimension 0, may hold values from -6 to 6
- weights: bfloat16 [9, 256, 256], replicated, may hold values from -0.125 to 0.125
- filter_taps: bfloat16 [4, 9, 3, 2, 64], P('lat'), may hold values from -0.3125 to 0.3125
- cycle_counts: int32 [4], P('lat'), may hold values from 1 to 2, as said below
- cycle_blocks: int32 [4, 2], P('lat'), may hold values from -2 to 1, as said below
Outputs:
- outputs: bfloat16 [512, 4, 512], P('groups', 'lat', 'lon'), parts along dimension 0
- input_grad: bfloat16 [512, 4, 512], P('groups', 'lat', 'lon'), parts along dimension 0
- weight_grad: float32 [18, 256, 256], P('groups', 'lon'), parts along dimension 0
There are 2 independent parts, one for each index of `groups`. A program takes and returns all parts, laid end to end along the dimension named above; an argument that names none is the same for every part. Nothing has to cross between parts.
Inputs may be any that keep to these rules, and one draw needn't show every extreme that they name: Cycle i uses its first cycle_counts[i] slots; the first quarter of the cycles (at least one) uses all 2, the last cycle one. `cycle_blocks`: the 2 block numbers of a cycle are distinct; the first cycle holds the lowest and the highest.
All inputs are finite; a program needn't handle non-finite values.
Results may differ from a plain program's by a relative error of at most 0.0049.
Values may be sent and summed in bfloat16 or wider, within the bound.
No kernel may reach another device: no remote copies, remote signals or barrier semaphores. Data moves between devices by JAX's collectives and lax.ppermute only.
A program may use at most 64 MiB of HBM per device.

v0:
```python
import jax
import jax.numpy as jnp
from jax import lax
from jax.sharding import PartitionSpec as P

HALO = 128


def padded_2(cells, sides, width, closed):
    for axis, dim in sides:
        count = lax.axis_size(axis)
        ends = count if closed else count - 1
        head = lax.slice_in_dim(cells, 0, width, axis=dim)
        tail = lax.slice_in_dim(cells, cells.shape[dim] - width, cells.shape[dim], axis=dim)
        cells = jnp.concatenate(
            [
                lax.ppermute(tail, axis, [(i, (i + 1) % count) for i in range(ends)]),
                cells,
                lax.ppermute(head, axis, [((i + 1) % count, i) for i in range(ends)]),
            ],
            axis=dim,
        )
    return cells


def build_taps(filter_taps, cycle_counts, cycle_blocks):
    slot_total = cycle_blocks.shape[1]
    width_block = filter_taps.shape[4]
    offsets = jnp.arange(width_block, dtype=jnp.int32)
    places = HALO + width_block * cycle_blocks[:, :, None] + offsets[None, None, :]
    live_slots = jnp.arange(slot_total, dtype=jnp.int32)[None, :] < cycle_counts[:, None]
    positions = jnp.arange(2 * HALO, dtype=jnp.int32)
    onehot = jnp.where(
        (places[:, :, :, None] == positions) & live_slots[:, :, None, None], 1.0, 0.0
    ).astype(jnp.float32)
    return jnp.einsum("ikrst,istu->ikru", filter_taps.astype(jnp.float32), onehot)


def banded_matrix(tap_row, out_width, tap_reach):
    kernels = tap_row.shape[0]
    stencil_rows = tap_row.shape[1]
    window_len = out_width + tap_reach
    padded = jnp.concatenate(
        [tap_row, jnp.zeros((kernels, stencil_rows, window_len + 1 - tap_reach), tap_row.dtype)],
        axis=2,
    )
    repeated = jnp.tile(padded, (1, 1, out_width))[:, :, : out_width * window_len]
    repeated = repeated.reshape(kernels, stencil_rows, out_width, window_len)
    return jnp.transpose(repeated, (1, 3, 0, 2))


def body(fields, upstream, weights, filter_taps, cycle_counts, cycle_blocks):
    channels, lat_rows, lon_cols = fields.shape
    kernels = weights.shape[0]
    window_len = lon_cols + 2 * HALO
    tap_table = build_taps(filter_taps, cycle_counts, cycle_blocks).astype(jnp.bfloat16)
    banded = padded_2(fields, (("lat", 1),), 1, False)
    widened = padded_2(banded, (("lon", 2),), HALO, True)
    matrices = [
        banded_matrix(tap_table[0], lon_cols, 2 * HALO).reshape(3 * window_len, kernels * lon_cols)
    ]
    cycle_row = 0
    responses = [
        jnp.dot(
            widened.reshape(channels, 3 * window_len),
            matrices[cycle_row],
            preferred_element_type=jnp.float32,
        )
    ]
    response = (
        jnp.stack(responses, axis=1)
        .reshape(channels, lat_rows, kernels, lon_cols)
        .astype(jnp.bfloat16)
    )
    outputs = jnp.einsum(
        "koc,cikj->oij", weights, response, preferred_element_type=jnp.float32
    ).astype(jnp.bfloat16)
    response_grad = jnp.einsum(
        "koc,oij->cikj", weights, upstream, preferred_element_type=jnp.float32
    ).astype(jnp.bfloat16)
    grad_terms = jnp.einsum("oij,cikj->koc", upstream, response, preferred_element_type=jnp.float32)
    grad_share = lax.psum_scatter(grad_terms, "lon", scatter_dimension=1, tiled=True)
    weight_grad = lax.psum(grad_share, "lat")
    accumulated = jnp.zeros((channels, lat_rows + 2, window_len), jnp.float32)
    cycle_row = 0
    grad_piece = response_grad[:, cycle_row].reshape(channels, kernels * lon_cols)
    contrib = jnp.einsum(
        "cn,mn->cm", grad_piece, matrices[cycle_row], preferred_element_type=jnp.float32
    )
    accumulated = accumulated.at[:, cycle_row : cycle_row + 3].add(
        contrib.reshape(channels, 3, window_len)
    )
    rim_columns = jnp.concatenate(
        [accumulated[:, :, :HALO], accumulated[:, :, HALO + lon_cols :]], axis=2
    )
    arrived = padded_2(rim_columns, (("lon", 2),), HALO, True)
    interior = accumulated[:, :, HALO : HALO + lon_cols]
    interior = interior.at[:, :, :HALO].add(arrived[:, :, :HALO])
    interior = interior.at[:, :, lon_cols - HALO :].add(arrived[:, :, 3 * HALO :])
    edge_rows = jnp.stack([interior[:, 0], interior[:, lat_rows + 1]], axis=1)
    arrived = padded_2(edge_rows, (("lat", 1),), 1, False)
    result = interior[:, 1 : lat_rows + 1]
    result = result.at[:, 0].add(arrived[:, 0])
    result = result.at[:, lat_rows - 1].add(arrived[:, 3])
    return (outputs, result.astype(jnp.bfloat16), weight_grad)


def solution(mesh):
    return jax.shard_map(
        body,
        mesh=mesh,
        in_specs=(
            P("groups", "lat", "lon"),
            P("groups", "lat", "lon"),
            P(),
            P("lat", None, None, None, None),
            P("lat"),
            P("lat", None),
        ),
        out_specs=(P("groups", "lat", "lon"), P("groups", "lat", "lon"), P("groups", "lon", None)),
        check_vma=False,
    )
```

profile of v0, /device:TPU:1, one launch (start us, length us, event | category | flops | bytes accessed | tf_op | source)
XLA Modules:
  0.0 197.0 jit_solution(18379826614206599920)
XLA Ops:
  7.2 1.0 copy.32
  8.3 2.0 collective-permute-start.1
  10.2 4.5 %collective-permute-start = (bf16[256,1,128]{0,2,1:T(8,128)(2,1)S(1)}, bf16[256,1,128]{0,2,1:T(8,128)(2,1)S(1)}, u32[]{:S(2)}, u32[]{:S(2)}) collective-permute-start(bf16[256,1,128]{0,2,1:T(8,128)(2,1)S(1)} %copy.32), channel_id=1, source_target_pairs={{0,4},{4,8},{8,12},{1,5},{5,9},{9,13},{2,6},{6,10},{10,14},{3,7},{... | collective-permute-start | bytes 196616 | tf_op jit(solution)/shard_map/ppermute | solution.py:17
  15.3 0.7 add_bitcast_fusion
  16.0 0.1 iota_add_fusion
  16.1 3.4 %collective-permute-start.3 = (bf16[256,3,128]{0,2,1:T(8,128)(2,1)S(1)}, bf16[256,3,128]{0,2,1:T(8,128)(2,1)S(1)}, u32[]{:S(2)}, u32[]{:S(2)}) collective-permute-start(bf16[256,3,128]{0,2,1:T(8,128)(2,1)S(1)} %pad_maximum_fusion.1), channel_id=1, source_target_pairs={{1,0},{2,1},{3,2},{0,3},{5,4},{6,5},{7,6},{4,7},{9,8},{10,9},{11,1... | collective-permute-start | bytes 589832 | tf_op jit(solution)/shard_map/ppermute | solution.py:19
  19.5 0.9 fusion.3
  20.5 2.1 %tile.4 = bf16[9,3,128,385]{3,2,1,0:T(8,128)(2,1)} broadcast(bf16[9,3,385]{2,1,0:T(4,128)(2,1)S(1)} %concatenate.21.clone), dimensions={0,1,3} | broadcast | bytes 2681910 | tf_op jit(solution)/shard_map/tile | solution.py:47
  22.5 11.0 %tile.10 = bf16[9,3,49280]{2,1,0:T(4,128)(2,1)} reshape(bf16[9,3,128,385]{3,2,1,0:T(8,128)(2,1)} %tile.4) | data formatting | bytes 5322240 | tf_op jit(solution)/shard_map/tile | solution.py:47
  33.6 5.1 %slice.123 = bf16[9,3,49152]{2,1,0:T(4,128)(2,1)} slice(bf16[9,3,49280]{2,1,0:T(4,128)(2,1)} %tile.10), slice={[0:9], [0:3], [0:49152]} | slice | bytes 5308416 | tf_op jit(solution)/shard_map/slice | solution.py:47
  38.7 8.2 %reshape.267 = bf16[9,3,128,384]{3,2,1,0:T(8,128)(2,1)} reshape(bf16[9,3,49152]{2,1,0:T(4,128)(2,1)} %slice.123) | data formatting | bytes 5308416 | tf_op jit(solution)/shard_map/reshape | solution.py:48
  46.9 4.0 %copy.37 = bf16[3,384,9,128]{1,0,3,2:T(4,128)(2,1)S(1)} copy(bf16[3,384,9,128]{1,3,0,2:T(8,128)(2,1)} %bitcast.68) | data formatting | bytes 5308416 | tf_op jit(solution)/shard_map/transpose | solution.py:49
  51.0 0.5 copy.57
  51.5 1.1 convolution_convert_fusion.1
  52.7 0.8 copy-done.1
  53.5 0.5 convolution_bitcast_fusion
  53.9 3.4 %copy.44 = f32[9,256,256]{2,0,1:T(8,128)} copy(f32[9,256,256]{1,2,0:T(8,128)S(1)} %convolution_bitcast_fusion) | data formatting | bytes 4718592 | tf_op jit(solution)/shard_map/oij,cikj->koc/transpose | solution.py:81
  57.4 2.0 %copy.41 = bf16[3,384,9,128]{1,3,2,0:T(8,128)(2,1)S(1)} copy(bf16[3,384,9,128]{1,3,0,2:T(8,128)(2,1)} %bitcast.69) | data formatting | bytes 5308416 | tf_op jit(solution)/shard_map/transpose | solution.py:49
  59.5 0.3 convolution_convert_fusion
  59.9 1.0 fusion.22
  61.0 3.3 %collective-permute-start.5 = (f32[256,3,128]{2,0,1:T(8,128)S(1)}, f32[256,3,128]{2,0,1:T(8,128)S(1)}, u32[]{:S(2)}, u32[]{:S(2)}) collective-permute-start(f32[256,3,128]{2,0,1:T(8,128)S(1)} %get-tuple-element.97), channel_id=1, source_target_pairs={{1,0},{2,1},{3,2},{0,3},{5,4},{6,5},{7,6},{4,7},{9,8},{10,9},{11,1... | collective-permute-start | bytes 1179656 | tf_op jit(solution)/shard_map/ppermute | solution.py:19
  64.3 13.4 %collective-permute-done.4 = f32[256,3,128]{2,0,1:T(8,128)S(1)} collective-permute-done((f32[256,3,128]{2,0,1:T(8,128)S(1)}, f32[256,3,128]{2,0,1:T(8,128)S(1)}, u32[]{:S(2)}, u32[]{:S(2)}) %collective-permute-start.4) | collective-permute-done | bytes 393248 | tf_op jit(solution)/shard_map/ppermute | solution.py:17
  77.7 14.8 %collective-permute-done.5 = f32[256,3,128]{2,0,1:T(8,128)S(1)} collective-permute-done((f32[256,3,128]{2,0,1:T(8,128)S(1)}, f32[256,3,128]{2,0,1:T(8,128)S(1)}, u32[]{:S(2)}, u32[]{:S(2)}) %collective-permute-start.5) | collective-permute-done | bytes 393248 | tf_op jit(solution)/shard_map/ppermute | solution.py:19
  92.5 0.1 fusion.4
  92.6 7.2 %collective-permute-start.6 = (f32[256,1,128]{2,0,1:T(8,128)S(1)}, f32[256,1,128]{2,0,1:T(8,128)S(1)}, u32[]{:S(2)}, u32[]{:S(2)}) collective-permute-start(f32[256,1,128]{2,0,1:T(8,128)S(1)} %get-tuple-element.98), channel_id=1, source_target_pairs={{0,4},{4,8},{8,12},{1,5},{5,9},{9,13},{2,6},{6,10},{10,14},{3,7},{... | collective-permute-start | bytes 393224 | tf_op jit(solution)/shard_map/ppermute | solution.py:17
  99.8 1.9 collective-permute-start.7
  101.8 47.6 %reduce-scatter.2.cloned.1.call-done = f32[9,64,256]{2,0,1:T(8,128)} async-done(((f32[9,256,256]{2,0,1:T(8,128)}), f32[9,64,256]{2,0,1:T(8,128)}) %reduce-scatter.2.cloned.1.call-update) | async-done | bytes 589840 | tf_op jit(solution)/shard_map/reduce_scatter | solution.py:82
  149.4 0.5 fusion.1
  150.0 0.7 copy.45
  150.7 0.7 fusion.6
  151.4 36.4 %all-reduce.3.cloned.1.call-done = f32[9,64,256]{2,0,1:T(8,128)} async-done(((f32[9,64,256]{2,0,1:T(8,128)}), f32[9,64,256]{2,0,1:T(8,128)}) %all-reduce.3.cloned.1.call-update) | async-done | bytes 589840 | tf_op jit(solution)/shard_map/psum | solution.py:83
  187.8 2.4 %copy.46 = f32[9,64,256]{2,1,0:T(8,128)} copy(f32[9,64,256]{2,0,1:T(8,128)} %all-reduce.3.cloned.1.call-done) | data formatting | bytes 1179648
  (28 shorter events, 0.4 us)
Async XLA Ops:
  7.2 52.3 %copy-start = (bf16[9,256,256]{2,1,0:T(8,128)(2,1)S(1)}, bf16[9,256,256]{2,1,0:T(8,128)(2,1)}, u32[]{:S(2)}) copy-start(bf16[9,256,256]{2,1,0:T(8,128)(2,1)} %param.24) | copy-start | bytes 3538948
  7.2 142.2 %reduce-scatter.2.cloned.1.call-start = ((), (), s32[]{:S(2)}) async-start(), calls=%async_computation.1 | async-start | bytes 5242880 | tf_op jit(solution)/shard_map/reduce_scatter | solution.py:82
  8.3 7.8 %collective-permute-start.1 = (bf16[256,1,128]{0,2,1:T(8,128)(2,1)S(1)}, bf16[256,1,128]{0,2,1:T(8,128)(2,1)S(1)}, u32[]{:S(2)}, u32[]{:S(2)}) collective-permute-start(bf16[256,1,128]{0,2,1:T(8,128)(2,1)S(1)} %copy.32), channel_id=1, source_target_pairs={{4,0},{8,4},{12,8},{5,1},{9,5},{13,9},{6,2},{10,6},{14,10},{7,3},{... | collective-permute-start | bytes 196616 | tf_op jit(solution)/shard_map/ppermute | solution.py:19
  10.2 5.9 %collective-permute-start = (bf16[256,1,128]{0,2,1:T(8,128)(2,1)S(1)}, bf16[256,1,128]{0,2,1:T(8,128)(2,1)S(1)}, u32[]{:S(2)}, u32[]{:S(2)}) collective-permute-start(bf16[256,1,128]{0,2,1:T(8,128)(2,1)S(1)} %copy.32), channel_id=1, source_target_pairs={{0,4},{4,8},{8,12},{1,5},{5,9},{9,13},{2,6},{6,10},{10,14},{3,7},{... | collective-permute-start | bytes 196616 | tf_op jit(solution)/shard_map/ppermute | solution.py:17
  16.1 35.3 %collective-permute-start.3 = (bf16[256,3,128]{0,2,1:T(8,128)(2,1)S(1)}, bf16[256,3,128]{0,2,1:T(8,128)(2,1)S(1)}, u32[]{:S(2)}, u32[]{:S(2)}) collective-permute-start(bf16[256,3,128]{0,2,1:T(8,128)(2,1)S(1)} %pad_maximum_fusion.1), channel_id=1, source_target_pairs={{1,0},{2,1},{3,2},{0,3},{5,4},{6,5},{7,6},{4,7},{9,8},{10,9},{11,1... | collective-permute-start | bytes 589832 | tf_op jit(solution)/shard_map/ppermute | solution.py:19
  19.5 32.0 %collective-permute-start.2 = (bf16[256,3,128]{0,2,1:T(8,128)(2,1)S(1)}, bf16[256,3,128]{0,2,1:T(8,128)(2,1)S(1)}, u32[]{:S(2)}, u32[]{:S(2)}) collective-permute-start(bf16[256,3,128]{0,2,1:T(8,128)(2,1)S(1)} %pad_maximum_fusion.1), channel_id=1, source_target_pairs={{0,1},{1,2},{2,3},{3,0},{4,5},{5,6},{6,7},{7,4},{8,9},{9,10},{10,1... | collective-permute-start | bytes 589832 | tf_op jit(solution)/shard_map/ppermute | solution.py:17
  51.5 1.9 copy-start.3
  52.6 0.8 copy-start.1
  57.4 2.1 %copy-start.4 = (bf16[256,1,128]{2,0,1:T(8,128)(2,1)S(1)}, bf16[256,1,128]{2,0,1:T(8,128)(2,1)}, u32[]{:S(2)}) copy-start(bf16[256,1,128]{2,0,1:T(8,128)(2,1)} %param.23) | copy-start | bytes 196612
  57.4 130.4 %all-reduce.3.cloned.1.call-start = ((), (), s32[]{:S(2)}) async-start(), calls=%async_computation.2 | async-start | bytes 2097152 | tf_op jit(solution)/shard_map/psum | solution.py:83
  61.0 16.7 %collective-permute-start.4 = (f32[256,3,128]{2,0,1:T(8,128)S(1)}, f32[256,3,128]{2,0,1:T(8,128)S(1)}, u32[]{:S(2)}, u32[]{:S(2)}) collective-permute-start(f32[256,3,128]{2,0,1:T(8,128)S(1)} %get-tuple-element.96), channel_id=1, source_target_pairs={{0,1},{1,2},{2,3},{3,0},{4,5},{5,6},{6,7},{7,4},{8,9},{9,10},{10,1... | collective-permute-start | bytes 1179656 | tf_op jit(solution)/shard_map/ppermute | solution.py:17
  61.0 31.5 %collective-permute-start.5 = (f32[256,3,128]{2,0,1:T(8,128)S(1)}, f32[256,3,128]{2,0,1:T(8,128)S(1)}, u32[]{:S(2)}, u32[]{:S(2)}) collective-permute-start(f32[256,3,128]{2,0,1:T(8,128)S(1)} %get-tuple-element.97), channel_id=1, source_target_pairs={{1,0},{2,1},{3,2},{0,3},{5,4},{6,5},{7,6},{4,7},{9,8},{10,9},{11,1... | collective-permute-start | bytes 1179656 | tf_op jit(solution)/shard_map/ppermute | solution.py:19
  92.6 56.9 %copy-start.2 = (bf16[256,9,128]{2,0,1:T(8,128)(2,1)S(1)}, bf16[256,9,128]{2,0,1:T(8,128)(2,1)}, u32[]{:S(2)}) copy-start(bf16[256,9,128]{2,0,1:T(8,128)(2,1)} %copy-done.1) | copy-start | bytes 1769476
  92.6 58.1 %collective-permute-start.6 = (f32[256,1,128]{2,0,1:T(8,128)S(1)}, f32[256,1,128]{2,0,1:T(8,128)S(1)}, u32[]{:S(2)}, u32[]{:S(2)}) collective-permute-start(f32[256,1,128]{2,0,1:T(8,128)S(1)} %get-tuple-element.98), channel_id=1, source_target_pairs={{0,4},{4,8},{8,12},{1,5},{5,9},{9,13},{2,6},{6,10},{10,14},{3,7},{... | collective-permute-start | bytes 393224 | tf_op jit(solution)/shard_map/ppermute | solution.py:17
  99.8 50.9 %collective-permute-start.7 = (f32[256,1,128]{2,0,1:T(8,128)S(1)}, f32[256,1,128]{2,0,1:T(8,128)S(1)}, u32[]{:S(2)}, u32[]{:S(2)}) collective-permute-start(f32[256,1,128]{2,0,1:T(8,128)S(1)} %get-tuple-element.99), channel_id=1, source_target_pairs={{4,0},{8,4},{12,8},{5,1},{9,5},{13,9},{6,2},{10,6},{14,10},{7,3},{... | collective-permute-start | bytes 393224 | tf_op jit(solution)/shard_map/ppermute | solution.py:19
Sparse Core Ops, SparseCore 0:
  57.5 91.8 reduce-scatter.1
  151.9 35.8 all-reduce.2
where the time goes:
time: 199 us; the launch traced here: 197 us
  waiting for transfers between devices  112 us (56%)
  local copies, waits for them, and re-layouts  41.5 us (21%)
  starting transfers between devices  22.4 us (11%)
  between operations  14.9 us (7%)
  matrix products  4.4 us (2%)
    reduce_scatter x1, waiting for transfers between devices, body(): lax.psum_scatter(grad_terms, 'lon', scatter_dimension=1, tiled=True)  47.6 us
    psum x1, waiting for transfers between devices, body(): weight_grad = lax.psum(grad_share, 'lat')  36.4 us
    ppermute x4, waiting for transfers between devices, padded_2(): lax.ppermute(head, axis, [((i + 1) % count, i) for i in range(ends)])  14.8 us
    ppermute x4, waiting for transfers between devices, padded_2(): lax.ppermute(tail, axis, [(i, (i + 1) % count) for i in range(ends)])  13.4 us
    another operation x2, local copies, waits for them, and re-layouts, banded_matrix(): jnp.tile(padded, (1, 1, out_width))[:, :, :out_width * window_len]  13.1 us
    ppermute x4, starting transfers between devices, padded_2(): lax.ppermute(tail, axis, [(i, (i + 1) % count) for i in range(ends)])  11.8 us
    ppermute x4, starting transfers between devices, padded_2(): lax.ppermute(head, axis, [((i + 1) % count, i) for i in range(ends)])  10.6 us
    reshape x1, local copies, waits for them, and re-layouts, banded_matrix(): repeated = repeated.reshape(kernels, stencil_rows, out_width, window_len)  8.24 us
  transfers between devices with their start and end apart: 10, of which 4 were waited for; matrix products, arithmetic and copies ran while one was open for 19% of the time, Pallas kernels for 0%

commit v1 on v0

--- a/solution.py
+++ b/solution.py
@@ -1,6 +1,8 @@
 import jax
 import jax.numpy as jnp
 from jax import lax
+from jax.experimental import pallas as pl
+from jax.experimental.pallas import tpu as pltpu
 from jax.sharding import PartitionSpec as P
 
 HALO = 128
@@ -36,17 +38,28 @@
     return jnp.einsum("ikrst,istu->ikru", filter_taps.astype(jnp.float32), onehot)
 
 
-def banded_matrix(tap_row, out_width, tap_reach):
-    kernels = tap_row.shape[0]
-    stencil_rows = tap_row.shape[1]
-    window_len = out_width + tap_reach
-    padded = jnp.concatenate(
-        [tap_row, jnp.zeros((kernels, stencil_rows, window_len + 1 - tap_reach), tap_row.dtype)],
-        axis=2,
-    )
-    repeated = jnp.tile(padded, (1, 1, out_width))[:, :, : out_width * window_len]
-    repeated = repeated.reshape(kernels, stencil_rows, out_width, window_len)
-    return jnp.transpose(repeated, (1, 3, 0, 2))
+def toeplitz_kernel(tap_ref, out_ref):
+    kernels, lon_cols, width = out_ref.shape
+    window_len = tap_ref.shape[1]
+    stencil_rows = width // window_len
+    for k in range(kernels):
+        for r in range(stencil_rows):
+            row = tap_ref[pl.ds(k * stencil_rows + r, 1), :]
+            tiled = jnp.broadcast_to(row, (lon_cols, window_len))
+            rolled = pltpu.roll(tiled, 0, 1, stride=1, stride_axis=0)
+            out_ref[k, :, pl.ds(r * window_len, window_len)] = rolled.astype(out_ref.dtype)
+
+
+def toeplitz(tap_row, out_width):
+    kernels, stencil_rows, reach = tap_row.shape
+    window_len = out_width + reach
+    padded = jnp.pad(tap_row.astype(jnp.float32), ((0, 0), (0, 0), (0, window_len - reach)))
+    padded = padded.reshape(kernels * stencil_rows, window_len)
+    out = pl.pallas_call(
+        toeplitz_kernel,
+        out_shape=jax.ShapeDtypeStruct((kernels, out_width, stencil_rows * window_len), jnp.bfloat16),
+    )(padded)
+    return out.reshape(kernels * out_width, stencil_rows * window_len)
 
 
 def body(fields, upstream, weights, filter_taps, cycle_counts, cycle_blocks):
@@ -56,14 +69,13 @@
     tap_table = build_taps(filter_taps, cycle_counts, cycle_blocks).astype(jnp.bfloat16)
     banded = padded_2(fields, (("lat", 1),), 1, False)
     widened = padded_2(banded, (("lon", 2),), HALO, True)
-    matrices = [
-        banded_matrix(tap_table[0], lon_cols, 2 * HALO).reshape(3 * window_len, kernels * lon_cols)
-    ]
+    matrices = [toeplitz(tap_table[0], lon_cols)]
     cycle_row = 0
     responses = [
-        jnp.dot(
+        lax.dot_general(
             widened.reshape(channels, 3 * window_len),
             matrices[cycle_row],
+            (((1,), (1,)), ((), ())),
             preferred_element_type=jnp.float32,
         )
     ]
@@ -84,9 +96,7 @@
     accumulated = jnp.zeros((channels, lat_rows + 2, window_len), jnp.float32)
     cycle_row = 0
     grad_piece = response_grad[:, cycle_row].reshape(channels, kernels * lon_cols)
-    contrib = jnp.einsum(
-        "cn,mn->cm", grad_piece, matrices[cycle_row], preferred_element_type=jnp.float32
-    )
+    contrib = jnp.dot(grad_piece, matrices[cycle_row], preferred_element_type=jnp.float32)
     accumulated = accumulated.at[:, cycle_row : cycle_row + 3].add(
         contrib.reshape(channels, 3, window_len)
     )

time: 199 us -> 178 us (0.89)
  local copies, waits for them, and re-layouts: 41.5 us -> 14.4 us
  waiting for transfers between devices: 112 us -> 117 us
  starting transfers between devices: 22.4 us -> 18.3 us
  matrix products: 4.4 us -> 8.04 us
  Pallas kernels: 0 us -> 3.08 us
    another operation x2 -> x0, local copies, waits for them, and re-layouts: 13.1 us -> none  [banded_matrix(): jnp.tile(padded, (1, 1, out_width))[:, :, :out_width * window_len]]
    ppermute x4, waiting for transfers between devices: 13.4 us -> 22.7 us  [padded_2(): lax.ppermute(tail, axis, [(i, (i + 1) % count) for i in range(ends)])]
    reshape x1 -> x2, local copies, waits for them, and re-layouts: 8.24 us -> 0.67 us  [toeplitz(): padded = padded.reshape(kernels * stencil_rows, window_len)]
    reduce_scatter x1, waiting for transfers between devices: 47.6 us -> 40.8 us  [body(): lax.psum_scatter(grad_terms, 'lon', scatter_dimension=1, tiled=True)]
    transpose x2 -> x0, local copies, waits for them, and re-layouts: 6.08 us -> none  [banded_matrix(): return jnp.transpose(repeated, (1, 3, 0, 2))]
    dot_general x0 -> x1, local copies, waits for them, and re-layouts: none -> 5.25 us  [body(): jnp.dot(grad_piece, matrices[cycle_row], preferred_element_type=jnp.float32)]
    slice x1 -> x0, local copies, waits for them, and re-layouts: 5.13 us -> none  [banded_matrix(): jnp.tile(padded, (1, 1, out_width))[:, :, :out_width * window_len]]
    dot_general x2, matrix products: 2.13 us -> 5.78 us  [the longest x1 2.9 us: body(): jnp.dot(grad_piece, matrices[cycle_row], preferred_element_type=jnp.float32)]
  transfers between devices with their start and end apart: 10 -> 10, of which waited for: 4 -> 6; matrix products, arithmetic and copies ran while one was open for 19% -> 7% of each run, Pallas kernels for 0% -> 2%
where the time goes in v1:
time: 178 us; the launch traced here: 177 us
  waiting for transfers between devices  117 us (66%)
  starting transfers between devices  18.3 us (10%)
  between operations  14.9 us (8%)
  local copies, waits for them, and re-layouts  14.4 us (8%)
  matrix products  8.04 us (5%)
  Pallas kernels  3.08 us (2%)
    reduce_scatter x1, waiting for transfers between devices, body(): lax.psum_scatter(grad_terms, 'lon', scatter_dimension=1, tiled=True)  40.8 us
    psum x1, waiting for transfers between devices, body(): weight_grad = lax.psum(grad_share, 'lat')  36.8 us
    ppermute x4, waiting for transfers between devices, padded_2(): lax.ppermute(tail, axis, [(i, (i + 1) % count) for i in range(ends)])  22.7 us
    ppermute x4, waiting for transfers between devices, padded_2(): lax.ppermute(head, axis, [((i + 1) % count, i) for i in range(ends)])  16.5 us
    ppermute x4, starting transfers between devices, padded_2(): lax.ppermute(head, axis, [((i + 1) % count, i) for i in range(ends)])  9.16 us
    ppermute x4, starting transfers between devices, padded_2(): lax.ppermute(tail, axis, [(i, (i + 1) % count) for i in range(ends)])  9.09 us
    dot_general x1, local copies, waits for them, and re-layouts, body(): jnp.dot(grad_piece, matrices[cycle_row], preferred_element_type=jnp.float32)  5.25 us
    unnamed x13, local copies, waits for them, and re-layouts  4.98 us
  transfers between devices with their start and end apart: 10, of which 6 were waited for; matrix products, arithmetic and copies ran while one was open for 7% of the time, Pallas kernels for 2%

profile of v1, /device:TPU:1, one launch (start us, length us, event | category | flops | bytes accessed | tf_op | source)
XLA Modules:
  0.0 177.0 jit_solution(2246181637383484701)
XLA Ops:
  7.2 1.0 copy.30
  8.3 2.0 %collective-permute-start.1 = (bf16[256,1,128]{0,2,1:T(8,128)(2,1)S(1)}, bf16[256,1,128]{0,2,1:T(8,128)(2,1)S(1)}, u32[]{:S(2)}, u32[]{:S(2)}) collective-permute-start(bf16[256,1,128]{0,2,1:T(8,128)(2,1)S(1)} %copy.30), channel_id=1, source_target_pairs={{4,0},{8,4},{12,8},{5,1},{9,5},{13,9},{6,2},{10,6},{14,10},{7,3},{... | collective-permute-start | bytes 196616 | tf_op jit(solution)/shard_map/ppermute | solution.py:21
  10.2 4.5 %collective-permute-start = (bf16[256,1,128]{0,2,1:T(8,128)(2,1)S(1)}, bf16[256,1,128]{0,2,1:T(8,128)(2,1)S(1)}, u32[]{:S(2)}, u32[]{:S(2)}) collective-permute-start(bf16[256,1,128]{0,2,1:T(8,128)(2,1)S(1)} %copy.30), channel_id=1, source_target_pairs={{0,4},{4,8},{8,12},{1,5},{5,9},{9,13},{2,6},{6,10},{10,14},{3,7},{... | collective-permute-start | bytes 196616 | tf_op jit(solution)/shard_map/ppermute | solution.py:19
  15.3 0.7 add_bitcast_fusion
  16.0 0.1 iota_add_fusion
  16.1 3.4 %collective-permute-start.3 = (bf16[256,3,128]{0,2,1:T(8,128)(2,1)S(1)}, bf16[256,3,128]{0,2,1:T(8,128)(2,1)S(1)}, u32[]{:S(2)}, u32[]{:S(2)}) collective-permute-start(bf16[256,3,128]{0,2,1:T(8,128)(2,1)S(1)} %pad_maximum_fusion.1), channel_id=1, source_target_pairs={{1,0},{2,1},{3,2},{0,3},{5,4},{6,5},{7,6},{4,7},{9,8},{10,9},{11,1... | collective-permute-start | bytes 589832 | tf_op jit(solution)/shard_map/ppermute | solution.py:21
  19.5 0.9 fusion.3
  20.5 0.6 reshape.271.tap_ref
  21.1 3.1 %shard_map.100 = bf16[9,128,1152]{2,1,0:T(8,128)(2,1)} custom-call(f32[27,384]{1,0:T(8,128)} %reshape.271.tap_ref), custom_call_target="tpu_custom_call" | custom-call | tf_op jit(solution)/shard_map/pallas_call | solution.py:58
  24.2 0.1 collective-permute-done.3
  24.3 4.8 %collective-permute-done.2 = bf16[256,3,128]{0,2,1:T(8,128)(2,1)S(1)} collective-permute-done((bf16[256,3,128]{0,2,1:T(8,128)(2,1)S(1)}, bf16[256,3,128]{0,2,1:T(8,128)(2,1)S(1)}, u32[]{:S(2)}, u32[]{:S(2)}) %collective-permute-start.2) | collective-permute-done | bytes 196640 | tf_op jit(solution)/shard_map/ppermute | solution.py:19
  29.1 2.9 %convolution_convert_fusion.1 = bf16[256,9,128]{2,0,1:T(8,128)(2,1)S(1)} fusion(bf16[256,1152,1]{0,1,2:T(8,128)(2,1)S(1)} %bitcast.62, bf16[9,128,1152]{2,1,0:T(8,128)(2,1)} %shard_map.100), kind=kOutput, calls=%fused_computation.2 | convolution fusion | flops 679772160 | bytes 3833856 | tf_op jit(solution)/shard_map/dot_general | solution.py:75
  32.0 0.8 copy-done.1
  32.8 0.5 convolution_bitcast_fusion
  33.3 3.4 %copy.40 = f32[9,256,256]{2,0,1:T(8,128)} copy(f32[9,256,256]{1,2,0:T(8,128)S(1)} %convolution_bitcast_fusion) | data formatting | bytes 4718592 | tf_op jit(solution)/shard_map/oij,cikj->koc/transpose | solution.py:93
  36.8 5.3 %copy.38 = bf16[1152,1152]{1,0:T(8,128)(2,1)} copy(bf16[1152,1152]{0,1:T(8,128)(2,1)} %bitcast.59) | data formatting | bytes 5308416 | tf_op jit(solution)/shard_map/dot_general | solution.py:99
  42.0 0.3 convolution_convert_fusion
  42.4 2.9 %fusion.22 = f32[256,3,384]{2,0,1:T(8,128)S(1)} fusion(bf16[256,1152,1]{0,1,2:T(8,128)(2,1)S(1)} %bitcast.61, bf16[3,384,1152]{2,1,0:T(8,128)(2,1)} %bitcast.60), kind=kOutput, calls=%fused_computation.35 | convolution fusion | flops 679477248 | bytes 4423680 | tf_op jit(solution)/shard_map/dot_general | solution.py:99
  45.3 0.1 fusion.20
  45.3 1.4 collective-permute-start.4
  46.8 1.9 %collective-permute-start.5 = (f32[256,3,128]{2,0,1:T(8,128)S(1)}, f32[256,3,128]{2,0,1:T(8,128)S(1)}, u32[]{:S(2)}, u32[]{:S(2)}) collective-permute-start(f32[256,3,128]{2,0,1:T(8,128)S(1)} %get-tuple-element.97), channel_id=1, source_target_pairs={{1,0},{2,1},{3,2},{0,3},{5,4},{6,5},{7,6},{4,7},{9,8},{10,9},{11,1... | collective-permute-start | bytes 1179656 | tf_op jit(solution)/shard_map/ppermute | solution.py:21
  48.7 17.9 %collective-permute-done.4 = f32[256,3,128]{2,0,1:T(8,128)S(1)} collective-permute-done((f32[256,3,128]{2,0,1:T(8,128)S(1)}, f32[256,3,128]{2,0,1:T(8,128)S(1)}, u32[]{:S(2)}, u32[]{:S(2)}) %collective-permute-start.4) | collective-permute-done | bytes 393248 | tf_op jit(solution)/shard_map/ppermute | solution.py:19
  66.6 16.4 %collective-permute-done.5 = f32[256,3,128]{2,0,1:T(8,128)S(1)} collective-permute-done((f32[256,3,128]{2,0,1:T(8,128)S(1)}, f32[256,3,128]{2,0,1:T(8,128)S(1)}, u32[]{:S(2)}, u32[]{:S(2)}) %collective-permute-start.5) | collective-permute-done | bytes 393248 | tf_op jit(solution)/shard_map/ppermute | solution.py:21
  83.0 0.1 fusion.4
  83.1 3.2 %collective-permute-start.6 = (f32[256,1,128]{2,0,1:T(8,128)S(1)}, f32[256,1,128]{2,0,1:T(8,128)S(1)}, u32[]{:S(2)}, u32[]{:S(2)}) collective-permute-start(f32[256,1,128]{2,0,1:T(8,128)S(1)} %get-tuple-element.98), channel_id=1, source_target_pairs={{0,4},{4,8},{8,12},{1,5},{5,9},{9,13},{2,6},{6,10},{10,14},{3,7},{... | collective-permute-start | bytes 393224 | tf_op jit(solution)/shard_map/ppermute | solution.py:19
  86.3 1.9 %collective-permute-start.7 = (f32[256,1,128]{2,0,1:T(8,128)S(1)}, f32[256,1,128]{2,0,1:T(8,128)S(1)}, u32[]{:S(2)}, u32[]{:S(2)}) collective-permute-start(f32[256,1,128]{2,0,1:T(8,128)S(1)} %get-tuple-element.99), channel_id=1, source_target_pairs={{4,0},{8,4},{12,8},{5,1},{9,5},{13,9},{6,2},{10,6},{14,10},{7,3},{... | collective-permute-start | bytes 393224 | tf_op jit(solution)/shard_map/ppermute | solution.py:21
  88.2 40.8 %reduce-scatter.2.cloned.1.call-done = f32[9,64,256]{2,0,1:T(8,128)} async-done(((f32[9,256,256]{2,0,1:T(8,128)}), f32[9,64,256]{2,0,1:T(8,128)}) %reduce-scatter.2.cloned.1.call-update) | async-done | bytes 589840 | tf_op jit(solution)/shard_map/reduce_scatter | solution.py:94
  129.0 0.5 fusion.1
  129.6 0.7 copy.41
  130.3 0.7 fusion.6
  131.0 36.8 %all-reduce.3.cloned.1.call-done = f32[9,64,256]{2,0,1:T(8,128)} async-done(((f32[9,64,256]{2,0,1:T(8,128)}), f32[9,64,256]{2,0,1:T(8,128)}) %all-reduce.3.cloned.1.call-update) | async-done | bytes 589840 | tf_op jit(solution)/shard_map/psum | solution.py:95
  167.7 2.4 %copy.42 = f32[9,64,256]{2,1,0:T(8,128)} copy(f32[9,64,256]{2,0,1:T(8,128)} %all-reduce.3.cloned.1.call-done) | data formatting | bytes 1179648
  (24 shorter events, 0.3 us)
Async XLA Ops:
  7.2 34.9 %copy-start = (bf16[9,256,256]{2,1,0:T(8,128)(2,1)S(1)}, bf16[9,256,256]{2,1,0:T(8,128)(2,1)}, u32[]{:S(2)}) copy-start(bf16[9,256,256]{2,1,0:T(8,128)(2,1)} %param.24) | copy-start | bytes 3538948
  7.2 121.8 %reduce-scatter.2.cloned.1.call-start = ((), (), s32[]{:S(2)}) async-start(), calls=%async_computation.1 | async-start | bytes 5242880 | tf_op jit(solution)/shard_map/reduce_scatter | solution.py:94
  8.3 7.8 %collective-permute-start.1 = (bf16[256,1,128]{0,2,1:T(8,128)(2,1)S(1)}, bf16[256,1,128]{0,2,1:T(8,128)(2,1)S(1)}, u32[]{:S(2)}, u32[]{:S(2)}) collective-permute-start(bf16[256,1,128]{0,2,1:T(8,128)(2,1)S(1)} %copy.30), channel_id=1, source_target_pairs={{4,0},{8,4},{12,8},{5,1},{9,5},{13,9},{6,2},{10,6},{14,10},{7,3},{... | collective-permute-start | bytes 196616 | tf_op jit(solution)/shard_map/ppermute | solution.py:21
  10.2 5.9 %collective-permute-start = (bf16[256,1,128]{0,2,1:T(8,128)(2,1)S(1)}, bf16[256,1,128]{0,2,1:T(8,128)(2,1)S(1)}, u32[]{:S(2)}, u32[]{:S(2)}) collective-permute-start(bf16[256,1,128]{0,2,1:T(8,128)(2,1)S(1)} %copy.30), channel_id=1, source_target_pairs={{0,4},{4,8},{8,12},{1,5},{5,9},{9,13},{2,6},{6,10},{10,14},{3,7},{... | collective-permute-start | bytes 196616 | tf_op jit(solution)/shard_map/ppermute | solution.py:19
  16.1 8.1 %collective-permute-start.3 = (bf16[256,3,128]{0,2,1:T(8,128)(2,1)S(1)}, bf16[256,3,128]{0,2,1:T(8,128)(2,1)S(1)}, u32[]{:S(2)}, u32[]{:S(2)}) collective-permute-start(bf16[256,3,128]{0,2,1:T(8,128)(2,1)S(1)} %pad_maximum_fusion.1), channel_id=1, source_target_pairs={{1,0},{2,1},{3,2},{0,3},{5,4},{6,5},{7,6},{4,7},{9,8},{10,9},{11,1... | collective-permute-start | bytes 589832 | tf_op jit(solution)/shard_map/ppermute | solution.py:21
  19.5 9.6 %collective-permute-start.2 = (bf16[256,3,128]{0,2,1:T(8,128)(2,1)S(1)}, bf16[256,3,128]{0,2,1:T(8,128)(2,1)S(1)}, u32[]{:S(2)}, u32[]{:S(2)}) collective-permute-start(bf16[256,3,128]{0,2,1:T(8,128)(2,1)S(1)} %pad_maximum_fusion.1), channel_id=1, source_target_pairs={{0,1},{1,2},{2,3},{3,0},{4,5},{5,6},{6,7},{7,4},{8,9},{9,10},{10,1... | collective-permute-start | bytes 589832 | tf_op jit(solution)/shard_map/ppermute | solution.py:19
  29.1 3.7 %copy-start.3 = (bf16[256,1,128]{2,0,1:T(8,128)(2,1)S(1)}, bf16[256,1,128]{2,0,1:T(8,128)(2,1)}, u32[]{:S(2)}) copy-start(bf16[256,1,128]{2,0,1:T(8,128)(2,1)} %param.23) | copy-start | bytes 196612
  32.0 0.8 copy-start.1
  36.7 131.0 %all-reduce.3.cloned.1.call-start = ((), (), s32[]{:S(2)}) async-start(), calls=%async_computation.2 | async-start | bytes 2097152 | tf_op jit(solution)/shard_map/psum | solution.py:95
  36.8 5.3 %copy-start.4 = (bf16[256,1,128]{2,0,1:T(8,128)(2,1)S(1)}, bf16[256,1,128]{2,0,1:T(8,128)(2,1)}, u32[]{:S(2)}) copy-start(bf16[256,1,128]{2,0,1:T(8,128)(2,1)} %param.23) | copy-start | bytes 196612
  45.3 21.2 %collective-permute-start.4 = (f32[256,3,128]{2,0,1:T(8,128)S(1)}, f32[256,3,128]{2,0,1:T(8,128)S(1)}, u32[]{:S(2)}, u32[]{:S(2)}) collective-permute-start(f32[256,3,128]{2,0,1:T(8,128)S(1)} %get-tuple-element.96), channel_id=1, source_target_pairs={{0,1},{1,2},{2,3},{3,0},{4,5},{5,6},{6,7},{7,4},{8,9},{9,10},{10,1... | collective-permute-start | bytes 1179656 | tf_op jit(solution)/shard_map/ppermute | solution.py:19
  46.8 36.2 %collective-permute-start.5 = (f32[256,3,128]{2,0,1:T(8,128)S(1)}, f32[256,3,128]{2,0,1:T(8,128)S(1)}, u32[]{:S(2)}, u32[]{:S(2)}) collective-permute-start(f32[256,3,128]{2,0,1:T(8,128)S(1)} %get-tuple-element.97), channel_id=1, source_target_pairs={{1,0},{2,1},{3,2},{0,3},{5,4},{6,5},{7,6},{4,7},{9,8},{10,9},{11,1... | collective-permute-start | bytes 1179656 | tf_op jit(solution)/shard_map/ppermute | solution.py:21
  83.1 46.0 %copy-start.2 = (bf16[256,9,128]{2,0,1:T(8,128)(2,1)S(1)}, bf16[256,9,128]{2,0,1:T(8,128)(2,1)}, u32[]{:S(2)}) copy-start(bf16[256,9,128]{2,0,1:T(8,128)(2,1)} %copy-done.1) | copy-start | bytes 1769476
  83.1 47.2 %collective-permute-start.6 = (f32[256,1,128]{2,0,1:T(8,128)S(1)}, f32[256,1,128]{2,0,1:T(8,128)S(1)}, u32[]{:S(2)}, u32[]{:S(2)}) collective-permute-start(f32[256,1,128]{2,0,1:T(8,128)S(1)} %get-tuple-element.98), channel_id=1, source_target_pairs={{0,4},{4,8},{8,12},{1,5},{5,9},{9,13},{2,6},{6,10},{10,14},{3,7},{... | collective-permute-start | bytes 393224 | tf_op jit(solution)/shard_map/ppermute | solution.py:19
  86.3 44.0 %collective-permute-start.7 = (f32[256,1,128]{2,0,1:T(8,128)S(1)}, f32[256,1,128]{2,0,1:T(8,128)S(1)}, u32[]{:S(2)}, u32[]{:S(2)}) collective-permute-start(f32[256,1,128]{2,0,1:T(8,128)S(1)} %get-tuple-element.99), channel_id=1, source_target_pairs={{4,0},{8,4},{12,8},{5,1},{9,5},{13,9},{6,2},{10,6},{14,10},{7,3},{... | collective-permute-start | bytes 393224 | tf_op jit(solution)/shard_map/ppermute | solution.py:21
Sparse Core Ops, SparseCore 0:
  36.8 92.1 reduce-scatter.1
  131.5 36.2 all-reduce.2

commit v2 on v1

--- a/solution.py
+++ b/solution.py
@@ -62,41 +62,78 @@
     return out.reshape(kernels * out_width, stencil_rows * window_len)
 
 
+def lat_allreduce(x, axis, dim):
+    count = lax.axis_size(axis)
+    steps = count.bit_length() - 1
+    if (1 << steps) != count or x.shape[dim] % count:
+        return lax.psum(x, axis)
+    index = lax.axis_index(axis)
+    buf = x
+    for s in range(steps):
+        half = buf.shape[dim] // 2
+        bit = (index >> s) & 1
+        keep = lax.dynamic_slice_in_dim(buf, bit * half, half, axis=dim)
+        send = lax.dynamic_slice_in_dim(buf, (1 - bit) * half, half, axis=dim)
+        recv = lax.ppermute(send, axis, [(i, i ^ (1 << s)) for i in range(count)])
+        buf = keep + recv
+    for s in reversed(range(steps)):
+        size = buf.shape[dim]
+        bit = (index >> s) & 1
+        recv = lax.ppermute(buf, axis, [(i, i ^ (1 << s)) for i in range(count)])
+        shape = list(buf.shape)
+        shape[dim] = 2 * size
+        out = jnp.zeros(shape, buf.dtype)
+        out = lax.dynamic_update_slice_in_dim(out, buf, bit * size, axis=dim)
+        buf = lax.dynamic_update_slice_in_dim(out, recv, (1 - bit) * size, axis=dim)
+    return buf
+
+
 def body(fields, upstream, weights, filter_taps, cycle_counts, cycle_blocks):
     channels, lat_rows, lon_cols = fields.shape
     kernels = weights.shape[0]
     window_len = lon_cols + 2 * HALO
+    n_lon = lax.axis_size("lon")
+    lon_at = lax.axis_index("lon")
     tap_table = build_taps(filter_taps, cycle_counts, cycle_blocks).astype(jnp.bfloat16)
+    matrix = toeplitz(tap_table[0], lon_cols)
     banded = padded_2(fields, (("lat", 1),), 1, False)
-    widened = padded_2(banded, (("lon", 2),), HALO, True)
-    matrices = [toeplitz(tap_table[0], lon_cols)]
-    cycle_row = 0
-    responses = [
-        lax.dot_general(
-            widened.reshape(channels, 3 * window_len),
-            matrices[cycle_row],
-            (((1,), (1,)), ((), ())),
-            preferred_element_type=jnp.float32,
-        )
+    blocks = [banded] + [
+        lax.ppermute(banded, "lon", [(p, (p - d) % n_lon) for p in range(n_lon)])
+        for d in range(1, n_lon)
     ]
-    response = (
-        jnp.stack(responses, axis=1)
-        .reshape(channels, lat_rows, kernels, lon_cols)
-        .astype(jnp.bfloat16)
+    row = jnp.concatenate(blocks, axis=2)
+    ext = jnp.concatenate([row[:, :, row.shape[2] - HALO :], row, row[:, :, :HALO]], axis=2)
+    windows = jnp.stack(
+        [ext[:, :, d * lon_cols : d * lon_cols + window_len] for d in range(n_lon)], axis=0
     )
+    response_all = lax.dot_general(
+        windows.reshape(n_lon * channels, 3 * window_len),
+        matrix,
+        (((1,), (1,)), ((), ())),
+        preferred_element_type=jnp.float32,
+    ).astype(jnp.bfloat16).reshape(n_lon, channels, kernels, lon_cols)
+    response = response_all[0].reshape(channels, lat_rows, kernels, lon_cols)
     outputs = jnp.einsum(
         "koc,cikj->oij", weights, response, preferred_element_type=jnp.float32
     ).astype(jnp.bfloat16)
     response_grad = jnp.einsum(
         "koc,oij->cikj", weights, upstream, preferred_element_type=jnp.float32
     ).astype(jnp.bfloat16)
-    grad_terms = jnp.einsum("oij,cikj->koc", upstream, response, preferred_element_type=jnp.float32)
-    grad_share = lax.psum_scatter(grad_terms, "lon", scatter_dimension=1, tiled=True)
-    weight_grad = lax.psum(grad_share, "lat")
+    o_block = upstream.shape[0] // n_lon
+    up_row = upstream[:, 0]
+    up_parts = [lax.dynamic_slice_in_dim(up_row, lon_at * o_block, o_block, axis=0)]
+    for d in range(1, n_lon):
+        part = lax.dynamic_slice_in_dim(up_row, ((lon_at - d) % n_lon) * o_block, o_block, axis=0)
+        up_parts.append(lax.ppermute(part, "lon", [(p, (p - d) % n_lon) for p in range(n_lon)]))
+    up_rel = jnp.stack(up_parts, axis=0)
+    grad_terms = jnp.einsum(
+        "doj,dckj->koc", up_rel, response_all, preferred_element_type=jnp.float32
+    )
+    weight_grad = lat_allreduce(grad_terms, "lat", 1)
     accumulated = jnp.zeros((channels, lat_rows + 2, window_len), jnp.float32)
     cycle_row = 0
     grad_piece = response_grad[:, cycle_row].reshape(channels, kernels * lon_cols)
-    contrib = jnp.dot(grad_piece, matrices[cycle_row], preferred_element_type=jnp.float32)
+    contrib = jnp.dot(grad_piece, matrix, preferred_element_type=jnp.float32)
     accumulated = accumulated.at[:, cycle_row : cycle_row + 3].add(
         contrib.reshape(channels, 3, window_len)
     )

time: 178 us -> 93.2 us (0.52)
  waiting for transfers between devices: 117 us -> 11.8 us
  starting transfers between devices: 18.3 us -> 38 us
  between operations: 14.9 us -> 1.6 us
  local copies, waits for them, and re-layouts: 14.4 us -> 21.9 us
  matrix products: 8.04 us -> 11.6 us
  other arithmetic: 1.56 us -> 4.34 us
    reduce_scatter x1 -> x0, waiting for transfers between devices: 40.8 us -> none  [body(): lax.psum_scatter(grad_terms, 'lon', scatter_dimension=1, tiled=True)]
    psum x1 -> x0, waiting for transfers between devices: 36.8 us -> none  [body(): weight_grad = lax.psum(grad_share, 'lat')]
    ppermute x0 -> x10, starting transfers between devices: none -> 22.7 us  [the longest x3 15.4 us: body(): lax.ppermute(part, 'lon', [(p, (p - d) % n_lon) for p in range(n_lon)])]
    ppermute x4 -> x3, waiting for transfers between devices: 22.7 us -> 0.01 us  [padded_2(): lax.ppermute(tail, axis, [(i, (i + 1) % count) for i in range(ends)])]
    ppermute x4 -> x3, waiting for transfers between devices: 16.5 us -> 0.01 us  [padded_2(): lax.ppermute(head, axis, [((i + 1) % count, i) for i in range(ends)])]
    ppermute x0 -> x10, waiting for transfers between devices: none -> 11.7 us  [the longest x3 7.3 us: body(): lax.ppermute(banded, 'lon', [(p, (p - d) % n_lon) for p in range(n_lon)])]
    another operation x0 -> x2, local copies, waits for them, and re-layouts: none -> 4.01 us  [the longest x1 3.39 us: body(): jnp.stack([ext[:, :, d * lon_cols:d * lon_cols + window_len] for d in ran...]
    dot_general x3, matrix products: 6.24 us -> 9.84 us  [the longest x1 3.8 us: body(): lax.dot_general(windows.reshape(n_lon * channels, 3 * window_len), matrix...]
  transfers between devices with their start and end apart: 10 -> 16, of which waited for: 6 -> 4; matrix products, arithmetic and copies ran while one was open for 7% -> 38% of each run, Pallas kernels for 2% -> 3%
where the time goes in v2:
time: 93.2 us; the launch traced here: 92.3 us
  starting transfers between devices  38 us (41%)
  local copies, waits for them, and re-layouts  21.9 us (23%)
  waiting for transfers between devices  11.8 us (13%)
  matrix products  11.6 us (12%)
  other arithmetic  4.34 us (5%)
  Pallas kernels  3.08 us (3%)
  between operations  1.6 us (2%)
    ppermute x3, starting transfers between devices, body(): lax.ppermute(part, 'lon', [(p, (p - d) % n_lon) for p in range(n_lon)])  15.4 us
    ppermute x3, starting transfers between devices, padded_2(): lax.ppermute(tail, axis, [(i, (i + 1) % count) for i in range(ends)])  8.3 us
    ppermute x3, waiting for transfers between devices, body(): lax.ppermute(banded, 'lon', [(p, (p - d) % n_lon) for p in range(n_lon)])  7.3 us
    ppermute x3, starting transfers between devices, padded_2(): lax.ppermute(head, axis, [((i + 1) % count, i) for i in range(ends)])  6.93 us
    dot_general x1, local copies, waits for them, and re-layouts, body(): contrib = jnp.dot(grad_piece, matrix, preferred_element_type=jnp.float32)  5.27 us
    unnamed x20, local copies, waits for them, and re-layouts  4.89 us
    ppermute x2, waiting for transfers between devices, lat_allreduce(): recv = lax.ppermute(buf, axis, [(i, i ^ 1 << s) for i in range(count)])  4.42 us
    ppermute x3, starting transfers between devices, body(): lax.ppermute(banded, 'lon', [(p, (p - d) % n_lon) for p in range(n_lon)])  3.83 us
  transfers between devices with their start and end apart: 16, of which 4 were waited for; matrix products, arithmetic and copies ran while one was open for 38% of the time, Pallas kernels for 3%

profile of v2, /device:TPU:1, one launch (start us, length us, event | category | flops | bytes accessed | tf_op | source)
XLA Modules:
  0.0 92.3 jit_solution(12290074417325420671)
XLA Ops:
  0.6 4.6 %collective-permute-start = (bf16[256,1,128]{2,0,1:T(8,128)(2,1)}, bf16[256,1,128]{2,0,1:T(8,128)(2,1)S(1)}, u32[]{:S(2)}, u32[]{:S(2)}) collective-permute-start(bf16[256,1,128]{2,0,1:T(8,128)(2,1)} %param.22), channel_id=1, source_target_pairs={{0,4},{4,8},{8,12},{1,5},{5,9},{9,13},{2,6},{6,10},{10,14},{3,7},{... | collective-permute-start | bytes 196616 | tf_op jit(solution)/shard_map/ppermute | solution.py:19
  5.3 1.9 %collective-permute-start.1 = (bf16[256,1,128]{2,0,1:T(8,128)(2,1)}, bf16[256,1,128]{2,0,1:T(8,128)(2,1)S(1)}, u32[]{:S(2)}, u32[]{:S(2)}) collective-permute-start(bf16[256,1,128]{2,0,1:T(8,128)(2,1)} %param.22), channel_id=1, source_target_pairs={{4,0},{8,4},{12,8},{5,1},{9,5},{13,9},{6,2},{10,6},{14,10},{7,3},{... | collective-permute-start | bytes 196616 | tf_op jit(solution)/shard_map/ppermute | solution.py:21
  7.2 0.7 add_bitcast_fusion
  8.6 0.9 fusion.8
  10.2 3.1 %shard_map.100 = bf16[9,128,1152]{2,1,0:T(8,128)(2,1)} custom-call(f32[27,384]{1,0:T(8,128)} %reshape.278.tap_ref), custom_call_target="tpu_custom_call" | custom-call | tf_op jit(solution)/shard_map/pallas_call | solution.py:58
  13.3 5.3 %copy.22 = bf16[1152,1152]{1,0:T(8,128)(2,1)} copy(bf16[1152,1152]{0,1:T(8,128)(2,1)} %bitcast.85) | data formatting | bytes 5308416 | tf_op jit(solution)/shard_map/dot_general | solution.py:136
  19.0 2.9 %fusion.33 = f32[256,3,384]{2,0,1:T(8,128)S(1)} fusion(bf16[256,1152,1]{0,1,2:T(8,128)(2,1)S(1)} %bitcast.91, bf16[3,384,1152]{2,1,0:T(8,128)(2,1)} %bitcast.88), kind=kOutput, calls=%fused_computation.62 | convolution fusion | flops 679477248 | bytes 4423680 | tf_op jit(solution)/shard_map/dot_general | solution.py:136
  21.9 3.4 %collective-permute-start.3 = (bf16[256,3,128]{2,0,1:T(8,128)(2,1)S(1)}, bf16[256,3,128]{2,0,1:T(8,128)(2,1)S(1)}, u32[]{:S(2)}, u32[]{:S(2)}) collective-permute-start(bf16[256,3,128]{2,0,1:T(8,128)(2,1)S(1)} %constant_dynamic-update-slice_fusion), channel_id=1, source_target_pairs={{0,3},{1,0},{2,1},{3,2},{4,7},{5,4},{6,5},{7,6},{8,11},{9,8},{10,9... | collective-permute-start | bytes 589832 | tf_op jit(solution)/shard_map/ppermute | solution.py:101
  25.8 0.9 %fusion.31 = (f32[256,3,128]{2,0,1:T(8,128)}, f32[256,3,128]{2,0,1:T(8,128)}) fusion(f32[256,3,384]{2,0,1:T(8,128)S(1)} %fusion.33), kind=kLoop, calls=%fused_computation.60 | loop fusion | bytes 1572864 | tf_op jit(solution)/shard_map/slice | solution.py:141
  26.7 2.8 %collective-permute-start.6 = (f32[256,3,128]{2,0,1:T(8,128)}, f32[256,3,128]{2,0,1:T(8,128)}, u32[]{:S(2)}, u32[]{:S(2)}) collective-permute-start(f32[256,3,128]{2,0,1:T(8,128)} %get-tuple-element.96), channel_id=1, source_target_pairs={{1,0},{2,1},{3,2},{0,3},{5,4},{6,5},{7,6},{4,7},{9,8},{10,9},{11,1... | collective-permute-start | bytes 1179656 | tf_op jit(solution)/shard_map/ppermute | solution.py:21
  30.4 1.5 %collective-permute-start.11 = (bf16[64,128]{1,0:T(8,128)(2,1)}, bf16[64,128]{1,0:T(8,128)(2,1)}, u32[]{:S(2)}, u32[]{:S(2)}) collective-permute-start(bf16[64,128]{1,0:T(8,128)(2,1)} %get-tuple-element.105), channel_id=1, source_target_pairs={{0,1},{1,2},{2,3},{3,0},{4,5},{5,6},{6,7},{7,4},{8,9},{9,10},{10,1... | collective-permute-start | bytes 49160 | tf_op jit(solution)/shard_map/ppermute | solution.py:127
  31.9 2.4 %collective-permute-done.2 = bf16[256,3,128]{2,0,1:T(8,128)(2,1)S(1)} collective-permute-done((bf16[256,3,128]{2,0,1:T(8,128)(2,1)S(1)}, bf16[256,3,128]{2,0,1:T(8,128)(2,1)S(1)}, u32[]{:S(2)}, u32[]{:S(2)}) %collective-permute-start.2) | collective-permute-done | bytes 196640 | tf_op jit(solution)/shard_map/ppermute | solution.py:101
  34.3 2.4 %collective-permute-start.10 = (bf16[64,128]{1,0:T(8,128)(2,1)}, bf16[64,128]{1,0:T(8,128)(2,1)}, u32[]{:S(2)}, u32[]{:S(2)}) collective-permute-start(bf16[64,128]{1,0:T(8,128)(2,1)} %get-tuple-element.106), channel_id=1, source_target_pairs={{0,2},{1,3},{2,0},{3,1},{4,6},{5,7},{6,4},{7,5},{8,10},{9,11},{10,... | collective-permute-start | bytes 49160 | tf_op jit(solution)/shard_map/ppermute | solution.py:127
  36.7 4.9 %collective-permute-done.4 = bf16[256,3,128]{2,0,1:T(8,128)(2,1)S(1)} collective-permute-done((bf16[256,3,128]{2,0,1:T(8,128)(2,1)S(1)}, bf16[256,3,128]{2,0,1:T(8,128)(2,1)S(1)}, u32[]{:S(2)}, u32[]{:S(2)}) %collective-permute-start.4) | collective-permute-done | bytes 196640 | tf_op jit(solution)/shard_map/ppermute | solution.py:101
  41.6 11.5 %collective-permute-start.9 = (bf16[64,128]{1,0:T(8,128)(2,1)}, bf16[64,128]{1,0:T(8,128)(2,1)}, u32[]{:S(2)}, u32[]{:S(2)}) collective-permute-start(bf16[64,128]{1,0:T(8,128)(2,1)} %get-tuple-element.104), channel_id=1, source_target_pairs={{0,3},{1,0},{2,1},{3,2},{4,7},{5,4},{6,5},{7,6},{8,11},{9,8},{10,9... | collective-permute-start | bytes 49160 | tf_op jit(solution)/shard_map/ppermute | solution.py:127
  53.7 3.4 %copy.17 = bf16[4,256,3,384]{1,0,3,2:T(4,128)(2,1)} copy(bf16[4,256,3,384]{3,1,2,0:T(8,128)(2,1)S(1)} %pad_maximum_fusion) | data formatting | bytes 4718592 | tf_op jit(solution)/shard_map/stack | solution.py:106
  57.1 2.4 %copy.35 = bf16[144,8,4,256]{3,1,2,0:T(8,128)(2,1)S(1)} copy(bf16[144,8,4,256]{3,2,1,0:T(4,128)(2,1)} %bitcast.87) | data formatting | bytes 4718592
  59.6 3.8 %convolution_convert_fusion = bf16[1024,1152]{1,0:T(8,128)(2,1)S(1)} fusion(bf16[1024,1152]{0,1:T(8,128)(2,1)S(1)} %bitcast.90, bf16[1152,1152]{1,0:T(8,128)(2,1)S(1)} %bitcast.86), kind=kOutput, calls=%fused_computation | convolution fusion | flops 2719088640 | bytes 7372800 | tf_op jit(solution)/shard_map/dot_general | solution.py:109
  63.4 3.0 %reshape.286 = bf16[4,256,9,128]{3,2,1,0:T(8,128)(2,1)} reshape(bf16[1024,1152]{1,0:T(8,128)(2,1)S(1)} %convolution_convert_fusion) | data formatting | bytes 4718592 | tf_op jit(solution)/shard_map/reshape | solution.py:114
  66.4 3.2 %fusion.2 = f32[256,9,64]{0,2,1:T(8,128)S(1)} fusion(bf16[4,256,9,128]{3,2,1,0:T(8,128)(2,1)} %reshape.286, bf16[1,64,128]{2,1,0:T(8,128)(2,1)} %bitcast.30, bf16[1,64,128]{2,1,0:T(8,128)(2,1)} %bitcast.28, bf16[1,64,128]{2,1,0:T(8,128)(2,1)} %bitcast.26, bf16[1,64,128]{2,1,0:T(8,128)(2,1)S(1)} %get-tuple-element.103), kind=kOutput, calls=%fused_computation.5 | convolution fusion | flops 151093248 | bytes 3014656 | tf_op jit(solution)/shard_map/doj,dckj->koc/dot_general | solution.py:129
  69.6 0.8 copy-done.3
  70.4 0.7 dynamic-slice_bitcast_fusion
  71.2 0.9 slice.132
  72.0 1.4 %copy.20 = bf16[256,1152]{0,1:T(8,128)(2,1)S(1)} copy(bf16[256,1152]{1,0:T(8,128)(2,1)} %slice.132) | data formatting | bytes 1179648 | tf_op jit(solution)/shard_map/slice | solution.py:115
  73.4 1.3 %fusion.9 = f32[256,3,128]{2,0,1:T(8,128)S(1)} fusion(f32[256,3,128]{2,0,1:T(8,128)} %collective-permute-done.6, f32[256,3,128]{2,0,1:T(8,128)} %collective-permute-done.5, f32[256,3,384]{2,0,1:T(8,128)} %copy-done.2), kind=kLoop, calls=%fused_computation.17 | loop fusion | flops 196608 | bytes 1572864 | tf_op jit(solution)/shard_map/add | solution.py:146
  74.7 1.0 %bitcast_add_fusion = f32[9,32,256]{2,1,0:T(8,128)S(1)} fusion(f32[9,32,256]{2,1,0:T(8,128)} %collective-permute-done.12, f32[256,9,64]{0,2,1:T(8,128)S(1)} %copy-done.4, s32[]{:T(128)S(6)} %select_n.58), kind=kLoop, calls=%fused_computation.18 | loop fusion | flops 73728 | bytes 884740 | tf_op jit(solution)/shard_map/add | solution.py:78
  75.8 3.0 %collective-permute-start.13 = (f32[9,16,256]{2,1,0:T(8,128)S(1)}, f32[9,16,256]{2,1,0:T(8,128)S(1)}, u32[]{:S(2)}, u32[]{:S(2)}) collective-permute-start(f32[9,16,256]{2,1,0:T(8,128)S(1)} %constant_dynamic-slice_fusion), channel_id=1, source_target_pairs={{0,8},{4,12},{8,0},{12,4},{1,9},{5,13},{9,1},{13,5},{2,10},{6,14},... | collective-permute-start | bytes 442376 | tf_op jit(solution)/shard_map/ppermute | solution.py:77
  78.8 2.2 %collective-permute-start.8 = (f32[256,1,128]{2,0,1:T(8,128)S(1)}, f32[256,1,128]{2,0,1:T(8,128)S(1)}, u32[]{:S(2)}, u32[]{:S(2)}) collective-permute-start(f32[256,1,128]{2,0,1:T(8,128)S(1)} %get-tuple-element.98), channel_id=1, source_target_pairs={{4,0},{8,4},{12,8},{5,1},{9,5},{13,9},{6,2},{10,6},{14,10},{7,3},{... | collective-permute-start | bytes 393224 | tf_op jit(solution)/shard_map/ppermute | solution.py:21
  81.0 3.4 %collective-permute-start.7 = (f32[256,1,128]{2,0,1:T(8,128)S(1)}, f32[256,1,128]{2,0,1:T(8,128)S(1)}, u32[]{:S(2)}, u32[]{:S(2)}) collective-permute-start(f32[256,1,128]{2,0,1:T(8,128)S(1)} %get-tuple-element.97), channel_id=1, source_target_pairs={{0,4},{4,8},{8,12},{1,5},{5,9},{9,13},{2,6},{6,10},{10,14},{3,7},{... | collective-permute-start | bytes 393224 | tf_op jit(solution)/shard_map/ppermute | solution.py:19
  85.1 0.7 copy.26
  85.8 4.0 %collective-permute-done.14 = f32[9,16,256]{2,1,0:T(8,128)S(1)} collective-permute-done((f32[9,16,256]{2,1,0:T(8,128)S(1)}, f32[9,16,256]{2,1,0:T(8,128)S(1)}, u32[]{:S(2)}, u32[]{:S(2)}) %collective-permute-start.14) | collective-permute-done | bytes 147488 | tf_op jit(solution)/shard_map/ppermute | solution.py:82
  91.5 0.8 copy-done.5
  (55 shorter events, 5.6 us)
Async XLA Ops:
  0.6 18.0 %copy-start = (bf16[9,256,256]{2,1,0:T(8,128)(2,1)S(1)}, bf16[9,256,256]{2,1,0:T(8,128)(2,1)}, u32[]{:S(2)}) copy-start(bf16[9,256,256]{2,1,0:T(8,128)(2,1)} %param.24) | copy-start | bytes 3538948
  0.6 21.2 %collective-permute-start = (bf16[256,1,128]{2,0,1:T(8,128)(2,1)}, bf16[256,1,128]{2,0,1:T(8,128)(2,1)S(1)}, u32[]{:S(2)}, u32[]{:S(2)}) collective-permute-start(bf16[256,1,128]{2,0,1:T(8,128)(2,1)} %param.22), channel_id=1, source_target_pairs={{0,4},{4,8},{8,12},{1,5},{5,9},{9,13},{2,6},{6,10},{10,14},{3,7},{... | collective-permute-start | bytes 196616 | tf_op jit(solution)/shard_map/ppermute | solution.py:19
  5.3 16.6 %collective-permute-start.1 = (bf16[256,1,128]{2,0,1:T(8,128)(2,1)}, bf16[256,1,128]{2,0,1:T(8,128)(2,1)S(1)}, u32[]{:S(2)}, u32[]{:S(2)}) collective-permute-start(bf16[256,1,128]{2,0,1:T(8,128)(2,1)} %param.22), channel_id=1, source_target_pairs={{4,0},{8,4},{12,8},{5,1},{9,5},{13,9},{6,2},{10,6},{14,10},{7,3},{... | collective-permute-start | bytes 196616 | tf_op jit(solution)/shard_map/ppermute | solution.py:21
  13.3 5.3 %copy-start.6 = (bf16[256,1,128]{2,0,1:T(8,128)(2,1)S(1)}, bf16[256,1,128]{2,0,1:T(8,128)(2,1)}, u32[]{:S(2)}) copy-start(bf16[256,1,128]{2,0,1:T(8,128)(2,1)} %param.23) | copy-start | bytes 196612
  18.9 2.9 %copy-start.7 = (bf16[256,1,128]{2,0,1:T(8,128)(2,1)S(1)}, bf16[256,1,128]{2,0,1:T(8,128)(2,1)}, u32[]{:S(2)}) copy-start(bf16[256,1,128]{2,0,1:T(8,128)(2,1)} %param.22) | copy-start | bytes 196612
  21.8 3.9 %copy-start.2 = (f32[256,3,384]{2,0,1:T(8,128)}, f32[256,3,384]{2,0,1:T(8,128)S(1)}, u32[]{:S(2)}) copy-start(f32[256,3,384]{2,0,1:T(8,128)S(1)} %fusion.33) | copy-start | bytes 3538948
  21.9 8.5 %collective-permute-start.3 = (bf16[256,3,128]{2,0,1:T(8,128)(2,1)S(1)}, bf16[256,3,128]{2,0,1:T(8,128)(2,1)S(1)}, u32[]{:S(2)}, u32[]{:S(2)}) collective-permute-start(bf16[256,3,128]{2,0,1:T(8,128)(2,1)S(1)} %constant_dynamic-update-slice_fusion), channel_id=1, source_target_pairs={{0,3},{1,0},{2,1},{3,2},{4,7},{5,4},{6,5},{7,6},{8,11},{9,8},{10,9... | collective-permute-start | bytes 589832 | tf_op jit(solution)/shard_map/ppermute | solution.py:101
  25.3 9.0 %collective-permute-start.2 = (bf16[256,3,128]{2,0,1:T(8,128)(2,1)S(1)}, bf16[256,3,128]{2,0,1:T(8,128)(2,1)S(1)}, u32[]{:S(2)}, u32[]{:S(2)}) collective-permute-start(bf16[256,3,128]{2,0,1:T(8,128)(2,1)S(1)} %constant_dynamic-update-slice_fusion), channel_id=1, source_target_pairs={{0,1},{1,2},{2,3},{3,0},{4,5},{5,6},{6,7},{7,4},{8,9},{9,10},{10,1... | collective-permute-start | bytes 589832 | tf_op jit(solution)/shard_map/ppermute | solution.py:101
  25.3 16.3 %collective-permute-start.4 = (bf16[256,3,128]{2,0,1:T(8,128)(2,1)S(1)}, bf16[256,3,128]{2,0,1:T(8,128)(2,1)S(1)}, u32[]{:S(2)}, u32[]{:S(2)}) collective-permute-start(bf16[256,3,128]{2,0,1:T(8,128)(2,1)S(1)} %constant_dynamic-update-slice_fusion), channel_id=1, source_target_pairs={{0,2},{1,3},{2,0},{3,1},{4,6},{5,7},{6,4},{7,5},{8,10},{9,11},{10,... | collective-permute-start | bytes 589832 | tf_op jit(solution)/shard_map/ppermute | solution.py:101
  26.7 46.7 %collective-permute-start.6 = (f32[256,3,128]{2,0,1:T(8,128)}, f32[256,3,128]{2,0,1:T(8,128)}, u32[]{:S(2)}, u32[]{:S(2)}) collective-permute-start(f32[256,3,128]{2,0,1:T(8,128)} %get-tuple-element.96), channel_id=1, source_target_pairs={{1,0},{2,1},{3,2},{0,3},{5,4},{6,5},{7,6},{4,7},{9,8},{10,9},{11,1... | collective-permute-start | bytes 1179656 | tf_op jit(solution)/shard_map/ppermute | solution.py:21
  29.5 43.9 %collective-permute-start.5 = (f32[256,3,128]{2,0,1:T(8,128)}, f32[256,3,128]{2,0,1:T(8,128)}, u32[]{:S(2)}, u32[]{:S(2)}) collective-permute-start(f32[256,3,128]{2,0,1:T(8,128)} %get-tuple-element.95), channel_id=1, source_target_pairs={{0,1},{1,2},{2,3},{3,0},{4,5},{5,6},{6,7},{7,4},{8,9},{9,10},{10,1... | collective-permute-start | bytes 1179656 | tf_op jit(solution)/shard_map/ppermute | solution.py:19
  30.4 36.0 %collective-permute-start.11 = (bf16[64,128]{1,0:T(8,128)(2,1)}, bf16[64,128]{1,0:T(8,128)(2,1)}, u32[]{:S(2)}, u32[]{:S(2)}) collective-permute-start(bf16[64,128]{1,0:T(8,128)(2,1)} %get-tuple-element.105), channel_id=1, source_target_pairs={{0,1},{1,2},{2,3},{3,0},{4,5},{5,6},{6,7},{7,4},{8,9},{9,10},{10,1... | collective-permute-start | bytes 49160 | tf_op jit(solution)/shard_map/ppermute | solution.py:127
  34.3 32.1 %collective-permute-start.10 = (bf16[64,128]{1,0:T(8,128)(2,1)}, bf16[64,128]{1,0:T(8,128)(2,1)}, u32[]{:S(2)}, u32[]{:S(2)}) collective-permute-start(bf16[64,128]{1,0:T(8,128)(2,1)} %get-tuple-element.106), channel_id=1, source_target_pairs={{0,2},{1,3},{2,0},{3,1},{4,6},{5,7},{6,4},{7,5},{8,10},{9,11},{10,... | collective-permute-start | bytes 49160 | tf_op jit(solution)/shard_map/ppermute | solution.py:127
  41.6 24.8 %collective-permute-start.9 = (bf16[64,128]{1,0:T(8,128)(2,1)}, bf16[64,128]{1,0:T(8,128)(2,1)}, u32[]{:S(2)}, u32[]{:S(2)}) collective-permute-start(bf16[64,128]{1,0:T(8,128)(2,1)} %get-tuple-element.104), channel_id=1, source_target_pairs={{0,3},{1,0},{2,1},{3,2},{4,7},{5,4},{6,5},{7,6},{8,11},{9,8},{10,9... | collective-permute-start | bytes 49160 | tf_op jit(solution)/shard_map/ppermute | solution.py:127
  57.1 2.5 %copy-start.1 = (bf16[9,128,1152]{2,1,0:T(8,128)(2,1)S(1)}, bf16[9,128,1152]{2,1,0:T(8,128)(2,1)}, u32[]{:S(2)}) copy-start(bf16[9,128,1152]{2,1,0:T(8,128)(2,1)} %shard_map.100) | copy-start | bytes 7962628
  69.6 0.9 copy-start.3
  71.2 3.5 %collective-permute-start.12 = (f32[9,32,256]{2,1,0:T(8,128)}, f32[9,32,256]{2,1,0:T(8,128)}, u32[]{:S(2)}, u32[]{:S(2)}) collective-permute-start(f32[9,32,256]{2,1,0:T(8,128)} %dynamic-slice_bitcast_fusion), channel_id=1, source_target_pairs={{0,4},{4,0},{8,12},{12,8},{1,5},{5,1},{9,13},{13,9},{2,6},{6,2},{1... | collective-permute-start | bytes 884744 | tf_op jit(solution)/shard_map/ppermute | solution.py:77
  72.0 2.7 %copy-start.4 = (f32[256,9,64]{0,2,1:T(8,128)S(1)}, f32[256,9,64]{0,2,1:T(8,128)}, u32[]{:S(2)}) copy-start(f32[256,9,64]{0,2,1:T(8,128)} %copy-done.3) | copy-start | bytes 1769476
  75.8 8.6 %collective-permute-start.13 = (f32[9,16,256]{2,1,0:T(8,128)S(1)}, f32[9,16,256]{2,1,0:T(8,128)S(1)}, u32[]{:S(2)}, u32[]{:S(2)}) collective-permute-start(f32[9,16,256]{2,1,0:T(8,128)S(1)} %constant_dynamic-slice_fusion), channel_id=1, source_target_pairs={{0,8},{4,12},{8,0},{12,4},{1,9},{5,13},{9,1},{13,5},{2,10},{6,14},... | collective-permute-start | bytes 442376 | tf_op jit(solution)/shard_map/ppermute | solution.py:77
  78.8 11.5 %collective-permute-start.8 = (f32[256,1,128]{2,0,1:T(8,128)S(1)}, f32[256,1,128]{2,0,1:T(8,128)S(1)}, u32[]{:S(2)}, u32[]{:S(2)}) collective-permute-start(f32[256,1,128]{2,0,1:T(8,128)S(1)} %get-tuple-element.98), channel_id=1, source_target_pairs={{4,0},{8,4},{12,8},{5,1},{9,5},{13,9},{6,2},{10,6},{14,10},{7,3},{... | collective-permute-start | bytes 393224 | tf_op jit(solution)/shard_map/ppermute | solution.py:21
  81.0 9.3 %collective-permute-start.7 = (f32[256,1,128]{2,0,1:T(8,128)S(1)}, f32[256,1,128]{2,0,1:T(8,128)S(1)}, u32[]{:S(2)}, u32[]{:S(2)}) collective-permute-start(f32[256,1,128]{2,0,1:T(8,128)S(1)} %get-tuple-element.97), channel_id=1, source_target_pairs={{0,4},{4,8},{8,12},{1,5},{5,9},{9,13},{2,6},{6,10},{10,14},{3,7},{... | collective-permute-start | bytes 393224 | tf_op jit(solution)/shard_map/ppermute | solution.py:19
  84.4 5.3 %collective-permute-start.14 = (f32[9,16,256]{2,1,0:T(8,128)S(1)}, f32[9,16,256]{2,1,0:T(8,128)S(1)}, u32[]{:S(2)}, u32[]{:S(2)}) collective-permute-start(f32[9,16,256]{2,1,0:T(8,128)S(1)} %get-tuple-element.94), channel_id=1, source_target_pairs={{0,8},{4,12},{8,0},{12,4},{1,9},{5,13},{9,1},{13,5},{2,10},{6,14},... | collective-permute-start | bytes 442376 | tf_op jit(solution)/shard_map/ppermute | solution.py:82
  89.8 1.7 %collective-permute-start.15 = (f32[9,32,256]{2,1,0:T(8,128)S(1)}, f32[9,32,256]{2,1,0:T(8,128)S(1)}, u32[]{:S(2)}, u32[]{:S(2)}) collective-permute-start(f32[9,32,256]{2,1,0:T(8,128)S(1)} %constant_dynamic-update-slice_fusion.5), channel_id=1, source_target_pairs={{0,4},{4,0},{8,12},{12,8},{1,5},{5,1},{9,13},{13,9},{2,6},{6,2},{1... | collective-permute-start | bytes 884744 | tf_op jit(solution)/shard_map/ppermute | solution.py:82
  91.5 0.8 copy-start.5

commit v3 on v2

--- a/solution.py
+++ b/solution.py
@@ -68,24 +68,20 @@
     if (1 << steps) != count or x.shape[dim] % count:
         return lax.psum(x, axis)
     index = lax.axis_index(axis)
-    buf = x
+    size = x.shape[dim] // count
+    parts = [lax.dynamic_slice_in_dim(x, index * size, size, axis=dim)]
+    for d in range(1, count):
+        send = lax.dynamic_slice_in_dim(x, (index ^ d) * size, size, axis=dim)
+        parts.append(lax.ppermute(send, axis, [(i, i ^ d) for i in range(count)]))
     for s in range(steps):
-        half = buf.shape[dim] // 2
-        bit = (index >> s) & 1
-        keep = lax.dynamic_slice_in_dim(buf, bit * half, half, axis=dim)
-        send = lax.dynamic_slice_in_dim(buf, (1 - bit) * half, half, axis=dim)
-        recv = lax.ppermute(send, axis, [(i, i ^ (1 << s)) for i in range(count)])
-        buf = keep + recv
-    for s in reversed(range(steps)):
-        size = buf.shape[dim]
-        bit = (index >> s) & 1
-        recv = lax.ppermute(buf, axis, [(i, i ^ (1 << s)) for i in range(count)])
-        shape = list(buf.shape)
-        shape[dim] = 2 * size
-        out = jnp.zeros(shape, buf.dtype)
-        out = lax.dynamic_update_slice_in_dim(out, buf, bit * size, axis=dim)
-        buf = lax.dynamic_update_slice_in_dim(out, recv, (1 - bit) * size, axis=dim)
-    return buf
+        parts = [parts[2 * e] + parts[2 * e + 1] for e in range(len(parts) // 2)]
+    mine = parts[0]
+    out = jnp.zeros(x.shape, x.dtype)
+    out = lax.dynamic_update_slice_in_dim(out, mine, index * size, axis=dim)
+    for d in range(1, count):
+        recv = lax.ppermute(mine, axis, [(i, i ^ d) for i in range(count)])
+        out = lax.dynamic_update_slice_in_dim(out, recv, (index ^ d) * size, axis=dim)
+    return out
 
 
 def body(fields, upstream, weights, filter_taps, cycle_counts, cycle_blocks):
@@ -96,12 +92,11 @@
     lon_at = lax.axis_index("lon")
     tap_table = build_taps(filter_taps, cycle_counts, cycle_blocks).astype(jnp.bfloat16)
     matrix = toeplitz(tap_table[0], lon_cols)
-    banded = padded_2(fields, (("lat", 1),), 1, False)
-    blocks = [banded] + [
-        lax.ppermute(banded, "lon", [(p, (p - d) % n_lon) for p in range(n_lon)])
+    blocks = [fields] + [
+        lax.ppermute(fields, "lon", [(p, (p - d) % n_lon) for p in range(n_lon)])
         for d in range(1, n_lon)
     ]
-    row = jnp.concatenate(blocks, axis=2)
+    row = padded_2(jnp.concatenate(blocks, axis=2), (("lat", 1),), 1, False)
     ext = jnp.concatenate([row[:, :, row.shape[2] - HALO :], row, row[:, :, :HALO]], axis=2)
     windows = jnp.stack(
         [ext[:, :, d * lon_cols : d * lon_cols + window_len] for d in range(n_lon)], axis=0

time: 93.2 us -> 77.3 us (0.83)
  starting transfers between devices: 38 us -> 27.2 us
  waiting for transfers between devices: 11.8 us -> 6.01 us
  matrix products: 11.6 us -> 13.3 us
    ppermute x3, starting transfers between devices: 15.4 us -> 3.55 us  [body(): lax.ppermute(part, 'lon', [(p, (p - d) % n_lon) for p in range(n_lon)])]
    ppermute x7 -> x9, waiting for transfers between devices: 11.7 us -> 5.99 us  [the longest x3 5.97 us: lat_allreduce(): recv = lax.ppermute(mine, axis, [(i, i ^ d) for i in range(count)])]
    ppermute x3, starting transfers between devices: 8.3 us -> 6.17 us  [padded_2(): lax.ppermute(tail, axis, [(i, (i + 1) % count) for i in range(ends)])]
    ppermute x7 -> x9, starting transfers between devices: 7.35 us -> 9.08 us  [the longest x3 4.66 us: body(): lax.ppermute(fields, 'lon', [(p, (p - d) % n_lon) for p in range(n_lon)])]
    dot_general x1, matrix products: 0.55 us -> 2.24 us  [body(): jnp.einsum('koc,cikj->oij', weights, response, preferred_element_type=jnp...]
    ppermute x3, starting transfers between devices: 6.93 us -> 8.37 us  [padded_2(): lax.ppermute(head, axis, [((i + 1) % count, i) for i in range(ends)])]
    add x1 -> x0, other arithmetic: 1.01 us -> none  [lat_allreduce(): buf = keep + recv]
    unnamed x20 -> x17, local copies, waits for them, and re-layouts: 4.89 us -> 4.91 us
  transfers between devices with their start and end apart: 16 -> 18, of which waited for: 4 -> 2; matrix products, arithmetic and copies ran while one was open for 38% -> 49% of each run, Pallas kernels for 3% -> 4%
where the time goes in v3:
time: 77.3 us; the launch traced here: 76.7 us
  starting transfers between devices  27.2 us (35%)
  local copies, waits for them, and re-layouts  22 us (28%)
  matrix products  13.3 us (17%)
  waiting for transfers between devices  6.01 us (8%)
  other arithmetic  3.51 us (5%)
  Pallas kernels  3.07 us (4%)
  between operations  1.6 us (2%)
    ppermute x3, starting transfers between devices, padded_2(): lax.ppermute(head, axis, [((i + 1) % count, i) for i in range(ends)])  8.37 us
    ppermute x3, starting transfers between devices, padded_2(): lax.ppermute(tail, axis, [(i, (i + 1) % count) for i in range(ends)])  6.17 us
    ppermute x3, waiting for transfers between devices, lat_allreduce(): recv = lax.ppermute(mine, axis, [(i, i ^ d) for i in range(count)])  5.97 us
    dot_general x1, local copies, waits for them, and re-layouts, body(): contrib = jnp.dot(grad_piece, matrix, preferred_element_type=jnp.float32)  5.29 us
    unnamed x17, local copies, waits for them, and re-layouts  4.91 us
    ppermute x3, starting transfers between devices, body(): lax.ppermute(fields, 'lon', [(p, (p - d) % n_lon) for p in range(n_lon)])  4.66 us
    dot_general x1, matrix products, body(): lax.dot_general(windows.reshape(n_lon * channels, 3 * window_len), matrix...  3.8 us
    ppermute x3, starting transfers between devices, body(): lax.ppermute(part, 'lon', [(p, (p - d) % n_lon) for p in range(n_lon)])  3.55 us
  transfers between devices with their start and end apart: 18, of which 2 were waited for; matrix products, arithmetic and copies ran while one was open for 49% of the time, Pallas kernels for 4%

profile of v3, /device:TPU:1, one launch (start us, length us, event | category | flops | bytes accessed | tf_op | source)
XLA Modules:
  0.0 76.7 jit_solution(15197279930962448397)
XLA Ops:
  0.6 4.2 %collective-permute-start = (bf16[256,1,128]{2,0,1:T(8,128)(2,1)}, bf16[256,1,128]{2,0,1:T(8,128)(2,1)S(1)}, u32[]{:S(2)}, u32[]{:S(2)}) collective-permute-start(bf16[256,1,128]{2,0,1:T(8,128)(2,1)} %param.22), channel_id=1, source_target_pairs={{0,3},{1,0},{2,1},{3,2},{4,7},{5,4},{6,5},{7,6},{8,11},{9,8},{10,9... | collective-permute-start | bytes 196616 | tf_op jit(solution)/shard_map/ppermute | solution.py:96
  5.3 0.7 add_bitcast_fusion
  6.7 0.9 %fusion.8 = bf16[9,3,256]{2,0,1:T(8,128)(2,1)S(1)} fusion(s32[2,64]{1,0:T(2,128)S(1)} %iota_add_fusion, pred[2]{0:T(512)(128)(4,1)S(1)} %iota_compare_fusion.1, bf16[9,3,2,64]{3,2,1,0:T(2,128)(2,1)} %bitcast.99), kind=kOutput, calls=%fused_computation.11 | convolution fusion | flops 1874688 | bytes 21250 | tf_op jit(solution)/shard_map/ikrst,istu->ikru/dot_general | solution.py:38
  7.7 0.6 reshape.278.tap_ref
  8.3 3.1 %shard_map.100 = bf16[9,128,1152]{2,1,0:T(8,128)(2,1)} custom-call(f32[27,384]{1,0:T(8,128)} %reshape.278.tap_ref), custom_call_target="tpu_custom_call" | custom-call | tf_op jit(solution)/shard_map/pallas_call | solution.py:58
  11.4 5.3 %copy.22 = bf16[1152,1152]{1,0:T(8,128)(2,1)} copy(bf16[1152,1152]{0,1:T(8,128)(2,1)} %bitcast.92) | data formatting | bytes 5308416 | tf_op jit(solution)/shard_map/dot_general | solution.py:131
  17.0 2.9 %fusion.38 = f32[256,3,384]{2,0,1:T(8,128)S(1)} fusion(bf16[256,1152,1]{0,1,2:T(8,128)(2,1)S(1)} %bitcast.98, bf16[3,384,1152]{2,1,0:T(8,128)(2,1)} %bitcast.95), kind=kOutput, calls=%fused_computation.72 | convolution fusion | flops 679477248 | bytes 4423680 | tf_op jit(solution)/shard_map/dot_general | solution.py:131
  20.1 3.4 %collective-permute-start.4 = (bf16[256,1,512]{2,0,1:T(8,128)(2,1)S(1)}, bf16[256,1,512]{2,0,1:T(8,128)(2,1)S(1)}, u32[]{:S(2)}, u32[]{:S(2)}) collective-permute-start(bf16[256,1,512]{2,0,1:T(8,128)(2,1)S(1)} %constant_dynamic-update-slice_fusion), channel_id=1, source_target_pairs={{4,0},{8,4},{12,8},{5,1},{9,5},{13,9},{6,2},{10,6},{14,10},{7,3},{... | collective-permute-start | bytes 786440 | tf_op jit(solution)/shard_map/ppermute | solution.py:21
  23.5 3.0 %collective-permute-start.3 = (bf16[256,1,512]{2,0,1:T(8,128)(2,1)S(1)}, bf16[256,1,512]{2,0,1:T(8,128)(2,1)S(1)}, u32[]{:S(2)}, u32[]{:S(2)}) collective-permute-start(bf16[256,1,512]{2,0,1:T(8,128)(2,1)S(1)} %constant_dynamic-update-slice_fusion), channel_id=1, source_target_pairs={{0,4},{4,8},{8,12},{1,5},{5,9},{9,13},{2,6},{6,10},{10,14},{3,7},{... | collective-permute-start | bytes 786440 | tf_op jit(solution)/shard_map/ppermute | solution.py:19
  26.5 0.9 %fusion.35 = (f32[256,3,128]{2,0,1:T(8,128)}, f32[256,3,128]{2,0,1:T(8,128)}) fusion(f32[256,3,384]{2,0,1:T(8,128)S(1)} %fusion.38), kind=kLoop, calls=%fused_computation.69 | loop fusion | bytes 1572864 | tf_op jit(solution)/shard_map/slice | solution.py:136
  27.5 2.5 %collective-permute-start.6 = (f32[256,3,128]{2,0,1:T(8,128)}, f32[256,3,128]{2,0,1:T(8,128)}, u32[]{:S(2)}, u32[]{:S(2)}) collective-permute-start(f32[256,3,128]{2,0,1:T(8,128)} %get-tuple-element.96), channel_id=1, source_target_pairs={{1,0},{2,1},{3,2},{0,3},{5,4},{6,5},{7,6},{4,7},{9,8},{10,9},{11,1... | collective-permute-start | bytes 1179656 | tf_op jit(solution)/shard_map/ppermute | solution.py:21
  30.0 0.6 dynamic-slice_bitcast_fusion.6
  30.7 1.1 %collective-permute-start.11 = (bf16[64,128]{1,0:T(8,128)(2,1)}, bf16[64,128]{1,0:T(8,128)(2,1)}, u32[]{:S(2)}, u32[]{:S(2)}) collective-permute-start(bf16[64,128]{1,0:T(8,128)(2,1)} %get-tuple-element.110), channel_id=1, source_target_pairs={{0,1},{1,2},{2,3},{3,0},{4,5},{5,6},{6,7},{7,4},{8,9},{9,10},{10,1... | collective-permute-start | bytes 49160 | tf_op jit(solution)/shard_map/ppermute | solution.py:122
  31.8 2.4 %collective-permute-start.10 = (bf16[64,128]{1,0:T(8,128)(2,1)}, bf16[64,128]{1,0:T(8,128)(2,1)}, u32[]{:S(2)}, u32[]{:S(2)}) collective-permute-start(bf16[64,128]{1,0:T(8,128)(2,1)} %get-tuple-element.111), channel_id=1, source_target_pairs={{0,2},{1,3},{2,0},{3,1},{4,6},{5,7},{6,4},{7,5},{8,10},{9,11},{10,... | collective-permute-start | bytes 49160 | tf_op jit(solution)/shard_map/ppermute | solution.py:122
  35.1 3.4 %copy.17 = bf16[4,256,3,384]{1,0,3,2:T(4,128)(2,1)} copy(bf16[4,256,3,384]{3,1,2,0:T(8,128)(2,1)S(1)} %pad_maximum_fusion) | data formatting | bytes 4718592 | tf_op jit(solution)/shard_map/stack | solution.py:101
  38.5 2.4 %copy.35 = bf16[144,8,4,256]{3,1,2,0:T(8,128)(2,1)S(1)} copy(bf16[144,8,4,256]{3,2,1,0:T(4,128)(2,1)} %bitcast.94) | data formatting | bytes 4718592
  40.9 3.8 %convolution_convert_fusion = bf16[1024,1152]{1,0:T(8,128)(2,1)S(1)} fusion(bf16[1024,1152]{0,1:T(8,128)(2,1)S(1)} %bitcast.97, bf16[1152,1152]{1,0:T(8,128)(2,1)S(1)} %bitcast.93), kind=kOutput, calls=%fused_computation | convolution fusion | flops 2719088640 | bytes 7372800 | tf_op jit(solution)/shard_map/dot_general | solution.py:104
  44.7 0.9 %slice.154 = bf16[256,1152]{1,0:T(8,128)(2,1)} slice(bf16[1024,1152]{1,0:T(8,128)(2,1)S(1)} %convolution_convert_fusion), slice={[0:256], [0:1152]} | slice | bytes 1179648 | tf_op jit(solution)/shard_map/slice | solution.py:110
  45.6 2.1 %copy.20 = bf16[256,1152]{0,1:T(8,128)(2,1)} copy(bf16[256,1152]{1,0:T(8,128)(2,1)} %slice.154) | data formatting | bytes 1179648 | tf_op jit(solution)/shard_map/slice | solution.py:110
  47.7 2.2 %fusion.6 = bf16[256,1,128]{0,2,1:T(8,128)(2,1)} fusion(bf16[256,9,128]{0,2,1:T(8,128)(2,1)} %bitcast.96, bf16[9,256,256]{2,1,0:T(8,128)(2,1)S(1)} %copy-done), kind=kOutput, calls=%fused_computation.8 | convolution fusion | flops 151027712 | bytes 1835008 | tf_op jit(solution)/shard_map/koc,cikj->oij/dot_general | solution.py:111
  49.9 3.0 %reshape.286 = bf16[4,256,9,128]{3,2,1,0:T(8,128)(2,1)} reshape(bf16[1024,1152]{1,0:T(8,128)(2,1)S(1)} %convolution_convert_fusion) | data formatting | bytes 4718592 | tf_op jit(solution)/shard_map/reshape | solution.py:109
  52.9 1.6 %copy.26 = bf16[256,1,128]{2,0,1:T(8,128)(2,1)} copy(bf16[256,1,128]{0,2,1:T(8,128)(2,1)} %fusion.6) | data formatting | bytes 131072
  54.5 3.2 %fusion.2 = f32[256,9,64]{0,2,1:T(8,128)S(1)} fusion(bf16[4,256,9,128]{3,2,1,0:T(8,128)(2,1)} %reshape.286, bf16[1,64,128]{2,1,0:T(8,128)(2,1)} %bitcast.30, bf16[1,64,128]{2,1,0:T(8,128)(2,1)} %bitcast.28, bf16[1,64,128]{2,1,0:T(8,128)(2,1)} %bitcast.26, bf16[1,64,128]{2,1,0:T(8,128)(2,1)S(1)} %get-tuple-element.108), kind=kOutput, calls=%fused_computation.5 | convolution fusion | flops 151093248 | bytes 3014656 | tf_op jit(solution)/shard_map/doj,dckj->koc/dot_general | solution.py:124
  57.8 2.1 %collective-permute-start.14 = (f32[9,16,256]{2,1,0:T(8,128)S(1)}, f32[9,16,256]{2,1,0:T(8,128)S(1)}, u32[]{:S(2)}, u32[]{:S(2)}) collective-permute-start(f32[9,16,256]{2,1,0:T(8,128)S(1)} %get-tuple-element.104), channel_id=1, source_target_pairs={{0,12},{4,8},{8,4},{12,0},{1,13},{5,9},{9,5},{13,1},{2,14},{6,10},... | collective-permute-start | bytes 442376 | tf_op jit(solution)/shard_map/ppermute | solution.py:75
  59.9 1.3 %fusion.11 = f32[256,3,128]{2,0,1:T(8,128)S(1)} fusion(f32[256,3,128]{2,0,1:T(8,128)} %collective-permute-done.6, f32[256,3,128]{2,0,1:T(8,128)} %collective-permute-done.5, f32[256,3,384]{2,0,1:T(8,128)} %copy-done.2), kind=kLoop, calls=%fused_computation.24 | loop fusion | flops 196608 | bytes 1572864 | tf_op jit(solution)/shard_map/add | solution.py:141
  61.3 2.4 %collective-permute-start.8 = (f32[256,1,128]{2,0,1:T(8,128)S(1)}, f32[256,1,128]{2,0,1:T(8,128)S(1)}, u32[]{:S(2)}, u32[]{:S(2)}) collective-permute-start(f32[256,1,128]{2,0,1:T(8,128)S(1)} %get-tuple-element.107), channel_id=1, source_target_pairs={{4,0},{8,4},{12,8},{5,1},{9,5},{13,9},{6,2},{10,6},{14,10},{7,3},{... | collective-permute-start | bytes 393224 | tf_op jit(solution)/shard_map/ppermute | solution.py:21
  63.7 3.1 %collective-permute-start.7 = (f32[256,1,128]{2,0,1:T(8,128)S(1)}, f32[256,1,128]{2,0,1:T(8,128)S(1)}, u32[]{:S(2)}, u32[]{:S(2)}) collective-permute-start(f32[256,1,128]{2,0,1:T(8,128)S(1)} %get-tuple-element.106), channel_id=1, source_target_pairs={{0,4},{4,8},{8,12},{1,5},{5,9},{9,13},{2,6},{6,10},{10,14},{3,7},{... | collective-permute-start | bytes 393224 | tf_op jit(solution)/shard_map/ppermute | solution.py:19
  67.5 1.7 %collective-permute-start.17 = (f32[9,16,256]{2,1,0:T(8,128)S(1)}, f32[9,16,256]{2,1,0:T(8,128)S(1)}, u32[]{:S(2)}, u32[]{:S(2)}) collective-permute-start(f32[9,16,256]{2,1,0:T(8,128)S(1)} %get-tuple-element.94), channel_id=1, source_target_pairs={{0,12},{4,8},{8,4},{12,0},{1,13},{5,9},{9,5},{13,1},{2,14},{6,10},... | collective-permute-start | bytes 442376 | tf_op jit(solution)/shard_map/ppermute | solution.py:82
  69.2 0.7 fusion.14
  69.9 2.2 %collective-permute-done.16 = f32[9,16,256]{2,1,0:T(8,128)S(1)} collective-permute-done((f32[9,16,256]{2,1,0:T(8,128)S(1)}, f32[9,16,256]{2,1,0:T(8,128)S(1)}, u32[]{:S(2)}, u32[]{:S(2)}) %collective-permute-start.16) | collective-permute-done | bytes 147488 | tf_op jit(solution)/shard_map/ppermute | solution.py:82
  72.1 3.7 %collective-permute-done.17 = f32[9,16,256]{2,1,0:T(8,128)S(1)} collective-permute-done((f32[9,16,256]{2,1,0:T(8,128)S(1)}, f32[9,16,256]{2,1,0:T(8,128)S(1)}, u32[]{:S(2)}, u32[]{:S(2)}) %collective-permute-start.17) | collective-permute-done | bytes 147488 | tf_op jit(solution)/shard_map/ppermute | solution.py:82
  75.9 0.8 %copy-done.3 = f32[9,64,256]{2,1,0:T(8,128)} copy-done((f32[9,64,256]{2,1,0:T(8,128)}, f32[9,64,256]{2,1,0:T(8,128)S(1)}, u32[]{:S(2)}) %copy-start.3) | copy-done | bytes 589848
  (55 shorter events, 2.8 us)
Async XLA Ops:
  0.6 16.0 %copy-start = (bf16[9,256,256]{2,1,0:T(8,128)(2,1)S(1)}, bf16[9,256,256]{2,1,0:T(8,128)(2,1)}, u32[]{:S(2)}) copy-start(bf16[9,256,256]{2,1,0:T(8,128)(2,1)} %param.24) | copy-start | bytes 3538948
  0.6 19.3 %collective-permute-start = (bf16[256,1,128]{2,0,1:T(8,128)(2,1)}, bf16[256,1,128]{2,0,1:T(8,128)(2,1)S(1)}, u32[]{:S(2)}, u32[]{:S(2)}) collective-permute-start(bf16[256,1,128]{2,0,1:T(8,128)(2,1)} %param.22), channel_id=1, source_target_pairs={{0,3},{1,0},{2,1},{3,2},{4,7},{5,4},{6,5},{7,6},{8,11},{9,8},{10,9... | collective-permute-start | bytes 196616 | tf_op jit(solution)/shard_map/ppermute | solution.py:96
  4.8 15.2 %collective-permute-start.1 = (bf16[256,1,128]{2,0,1:T(8,128)(2,1)}, bf16[256,1,128]{2,0,1:T(8,128)(2,1)S(1)}, u32[]{:S(2)}, u32[]{:S(2)}) collective-permute-start(bf16[256,1,128]{2,0,1:T(8,128)(2,1)} %param.22), channel_id=1, source_target_pairs={{0,2},{1,3},{2,0},{3,1},{4,6},{5,7},{6,4},{7,5},{8,10},{9,11},{10,... | collective-permute-start | bytes 196616 | tf_op jit(solution)/shard_map/ppermute | solution.py:96
  4.9 15.2 %collective-permute-start.2 = (bf16[256,1,128]{2,0,1:T(8,128)(2,1)}, bf16[256,1,128]{2,0,1:T(8,128)(2,1)S(1)}, u32[]{:S(2)}, u32[]{:S(2)}) collective-permute-start(bf16[256,1,128]{2,0,1:T(8,128)(2,1)} %param.22), channel_id=1, source_target_pairs={{0,1},{1,2},{2,3},{3,0},{4,5},{5,6},{6,7},{7,4},{8,9},{9,10},{10,1... | collective-permute-start | bytes 196616 | tf_op jit(solution)/shard_map/ppermute | solution.py:96
  11.4 5.3 %copy-start.4 = (bf16[256,1,128]{2,0,1:T(8,128)(2,1)S(1)}, bf16[256,1,128]{2,0,1:T(8,128)(2,1)}, u32[]{:S(2)}) copy-start(bf16[256,1,128]{2,0,1:T(8,128)(2,1)} %param.23) | copy-start | bytes 196612
  17.0 2.9 %copy-start.5 = (bf16[256,1,128]{2,0,1:T(8,128)(2,1)S(1)}, bf16[256,1,128]{2,0,1:T(8,128)(2,1)}, u32[]{:S(2)}) copy-start(bf16[256,1,128]{2,0,1:T(8,128)(2,1)} %param.22) | copy-start | bytes 196612
  19.9 6.6 %copy-start.2 = (f32[256,3,384]{2,0,1:T(8,128)}, f32[256,3,384]{2,0,1:T(8,128)S(1)}, u32[]{:S(2)}) copy-start(f32[256,3,384]{2,0,1:T(8,128)S(1)} %fusion.38) | copy-start | bytes 3538948
  20.1 11.7 %collective-permute-start.4 = (bf16[256,1,512]{2,0,1:T(8,128)(2,1)S(1)}, bf16[256,1,512]{2,0,1:T(8,128)(2,1)S(1)}, u32[]{:S(2)}, u32[]{:S(2)}) collective-permute-start(bf16[256,1,512]{2,0,1:T(8,128)(2,1)S(1)} %constant_dynamic-update-slice_fusion), channel_id=1, source_target_pairs={{4,0},{8,4},{12,8},{5,1},{9,5},{13,9},{6,2},{10,6},{14,10},{7,3},{... | collective-permute-start | bytes 786440 | tf_op jit(solution)/shard_map/ppermute | solution.py:21
  23.5 10.7 %collective-permute-start.3 = (bf16[256,1,512]{2,0,1:T(8,128)(2,1)S(1)}, bf16[256,1,512]{2,0,1:T(8,128)(2,1)S(1)}, u32[]{:S(2)}, u32[]{:S(2)}) collective-permute-start(bf16[256,1,512]{2,0,1:T(8,128)(2,1)S(1)} %constant_dynamic-update-slice_fusion), channel_id=1, source_target_pairs={{0,4},{4,8},{8,12},{1,5},{5,9},{9,13},{2,6},{6,10},{10,14},{3,7},{... | collective-permute-start | bytes 786440 | tf_op jit(solution)/shard_map/ppermute | solution.py:19
  27.5 32.4 %collective-permute-start.6 = (f32[256,3,128]{2,0,1:T(8,128)}, f32[256,3,128]{2,0,1:T(8,128)}, u32[]{:S(2)}, u32[]{:S(2)}) collective-permute-start(f32[256,3,128]{2,0,1:T(8,128)} %get-tuple-element.96), channel_id=1, source_target_pairs={{1,0},{2,1},{3,2},{0,3},{5,4},{6,5},{7,6},{4,7},{9,8},{10,9},{11,1... | collective-permute-start | bytes 1179656 | tf_op jit(solution)/shard_map/ppermute | solution.py:21
  30.0 29.9 %collective-permute-start.5 = (f32[256,3,128]{2,0,1:T(8,128)}, f32[256,3,128]{2,0,1:T(8,128)}, u32[]{:S(2)}, u32[]{:S(2)}) collective-permute-start(f32[256,3,128]{2,0,1:T(8,128)} %get-tuple-element.95), channel_id=1, source_target_pairs={{0,1},{1,2},{2,3},{3,0},{4,5},{5,6},{6,7},{7,4},{8,9},{9,10},{10,1... | collective-permute-start | bytes 1179656 | tf_op jit(solution)/shard_map/ppermute | solution.py:19
  30.7 23.8 %collective-permute-start.11 = (bf16[64,128]{1,0:T(8,128)(2,1)}, bf16[64,128]{1,0:T(8,128)(2,1)}, u32[]{:S(2)}, u32[]{:S(2)}) collective-permute-start(bf16[64,128]{1,0:T(8,128)(2,1)} %get-tuple-element.110), channel_id=1, source_target_pairs={{0,1},{1,2},{2,3},{3,0},{4,5},{5,6},{6,7},{7,4},{8,9},{9,10},{10,1... | collective-permute-start | bytes 49160 | tf_op jit(solution)/shard_map/ppermute | solution.py:122
  31.8 22.7 %collective-permute-start.10 = (bf16[64,128]{1,0:T(8,128)(2,1)}, bf16[64,128]{1,0:T(8,128)(2,1)}, u32[]{:S(2)}, u32[]{:S(2)}) collective-permute-start(bf16[64,128]{1,0:T(8,128)(2,1)} %get-tuple-element.111), channel_id=1, source_target_pairs={{0,2},{1,3},{2,0},{3,1},{4,6},{5,7},{6,4},{7,5},{8,10},{9,11},{10,... | collective-permute-start | bytes 49160 | tf_op jit(solution)/shard_map/ppermute | solution.py:122
  34.2 20.3 %collective-permute-start.9 = (bf16[64,128]{1,0:T(8,128)(2,1)}, bf16[64,128]{1,0:T(8,128)(2,1)}, u32[]{:S(2)}, u32[]{:S(2)}) collective-permute-start(bf16[64,128]{1,0:T(8,128)(2,1)} %get-tuple-element.109), channel_id=1, source_target_pairs={{0,3},{1,0},{2,1},{3,2},{4,7},{5,4},{6,5},{7,6},{8,11},{9,8},{10,9... | collective-permute-start | bytes 49160 | tf_op jit(solution)/shard_map/ppermute | solution.py:122
  38.5 2.5 %copy-start.1 = (bf16[9,128,1152]{2,1,0:T(8,128)(2,1)S(1)}, bf16[9,128,1152]{2,1,0:T(8,128)(2,1)}, u32[]{:S(2)}) copy-start(bf16[9,128,1152]{2,1,0:T(8,128)(2,1)} %shard_map.100) | copy-start | bytes 7962628
  57.7 9.1 %collective-permute-start.13 = (f32[9,16,256]{2,1,0:T(8,128)S(1)}, f32[9,16,256]{2,1,0:T(8,128)S(1)}, u32[]{:S(2)}, u32[]{:S(2)}) collective-permute-start(f32[9,16,256]{2,1,0:T(8,128)S(1)} %get-tuple-element.105), channel_id=1, source_target_pairs={{0,8},{4,12},{8,0},{12,4},{1,9},{5,13},{9,1},{13,5},{2,10},{6,14},... | collective-permute-start | bytes 442376 | tf_op jit(solution)/shard_map/ppermute | solution.py:75
  57.8 9.1 %collective-permute-start.14 = (f32[9,16,256]{2,1,0:T(8,128)S(1)}, f32[9,16,256]{2,1,0:T(8,128)S(1)}, u32[]{:S(2)}, u32[]{:S(2)}) collective-permute-start(f32[9,16,256]{2,1,0:T(8,128)S(1)} %get-tuple-element.104), channel_id=1, source_target_pairs={{0,12},{4,8},{8,4},{12,0},{1,13},{5,9},{9,5},{13,1},{2,14},{6,10},... | collective-permute-start | bytes 442376 | tf_op jit(solution)/shard_map/ppermute | solution.py:75
  59.9 6.9 %collective-permute-start.12 = (f32[9,16,256]{2,1,0:T(8,128)S(1)}, f32[9,16,256]{2,1,0:T(8,128)S(1)}, u32[]{:S(2)}, u32[]{:S(2)}) collective-permute-start(f32[9,16,256]{2,1,0:T(8,128)S(1)} %get-tuple-element.103), channel_id=1, source_target_pairs={{0,4},{4,0},{8,12},{12,8},{1,5},{5,1},{9,13},{13,9},{2,6},{6,2},{1... | collective-permute-start | bytes 442376 | tf_op jit(solution)/shard_map/ppermute | solution.py:75
  61.3 7.9 %collective-permute-start.8 = (f32[256,1,128]{2,0,1:T(8,128)S(1)}, f32[256,1,128]{2,0,1:T(8,128)S(1)}, u32[]{:S(2)}, u32[]{:S(2)}) collective-permute-start(f32[256,1,128]{2,0,1:T(8,128)S(1)} %get-tuple-element.107), channel_id=1, source_target_pairs={{4,0},{8,4},{12,8},{5,1},{9,5},{13,9},{6,2},{10,6},{14,10},{7,3},{... | collective-permute-start | bytes 393224 | tf_op jit(solution)/shard_map/ppermute | solution.py:21
  63.7 5.5 %collective-permute-start.7 = (f32[256,1,128]{2,0,1:T(8,128)S(1)}, f32[256,1,128]{2,0,1:T(8,128)S(1)}, u32[]{:S(2)}, u32[]{:S(2)}) collective-permute-start(f32[256,1,128]{2,0,1:T(8,128)S(1)} %get-tuple-element.106), channel_id=1, source_target_pairs={{0,4},{4,8},{8,12},{1,5},{5,9},{9,13},{2,6},{6,10},{10,14},{3,7},{... | collective-permute-start | bytes 393224 | tf_op jit(solution)/shard_map/ppermute | solution.py:19
  67.0 2.9 %collective-permute-start.15 = (f32[9,16,256]{2,1,0:T(8,128)S(1)}, f32[9,16,256]{2,1,0:T(8,128)S(1)}, u32[]{:S(2)}, u32[]{:S(2)}) collective-permute-start(f32[9,16,256]{2,1,0:T(8,128)S(1)} %get-tuple-element.94), channel_id=1, source_target_pairs={{0,4},{4,0},{8,12},{12,8},{1,5},{5,1},{9,13},{13,9},{2,6},{6,2},{1... | collective-permute-start | bytes 442376 | tf_op jit(solution)/shard_map/ppermute | solution.py:82
  67.1 5.1 %collective-permute-start.16 = (f32[9,16,256]{2,1,0:T(8,128)S(1)}, f32[9,16,256]{2,1,0:T(8,128)S(1)}, u32[]{:S(2)}, u32[]{:S(2)}) collective-permute-start(f32[9,16,256]{2,1,0:T(8,128)S(1)} %get-tuple-element.94), channel_id=1, source_target_pairs={{0,8},{4,12},{8,0},{12,4},{1,9},{5,13},{9,1},{13,5},{2,10},{6,14},... | collective-permute-start | bytes 442376 | tf_op jit(solution)/shard_map/ppermute | solution.py:82
  67.5 8.3 %collective-permute-start.17 = (f32[9,16,256]{2,1,0:T(8,128)S(1)}, f32[9,16,256]{2,1,0:T(8,128)S(1)}, u32[]{:S(2)}, u32[]{:S(2)}) collective-permute-start(f32[9,16,256]{2,1,0:T(8,128)S(1)} %get-tuple-element.94), channel_id=1, source_target_pairs={{0,12},{4,8},{8,4},{12,0},{1,13},{5,9},{9,5},{13,1},{2,14},{6,10},... | collective-permute-start | bytes 442376 | tf_op jit(solution)/shard_map/ppermute | solution.py:82
  75.9 0.8 %copy-start.3 = (f32[9,64,256]{2,1,0:T(8,128)}, f32[9,64,256]{2,1,0:T(8,128)S(1)}, u32[]{:S(2)}) copy-start(f32[9,64,256]{2,1,0:T(8,128)S(1)} %constant_dynamic-update-slice_fusion.4) | copy-start | bytes 1769476

commit v4 on v3

--- a/solution.py
+++ b/solution.py
@@ -84,6 +84,62 @@
     return out
 
 
+def row_kernel(ext_ref, mt_ref, w_ref, up_ref, out_ref, gt_ref):
+    stencil_rows, channels, _ = ext_ref.shape
+    n_blocks, o_block, lon_cols = up_ref.shape
+    kernels = w_ref.shape[0]
+    window_len = mt_ref.shape[1] // stencil_rows
+    contract_last = (((1,), (1,)), ((), ()))
+    gt_ref[...] = jnp.zeros(gt_ref.shape, gt_ref.dtype)
+    for d in range(n_blocks):
+        acc = None
+        for r in range(stencil_rows):
+            win = ext_ref[r, :, pl.ds(d * lon_cols, window_len)]
+            part = lax.dot_general(
+                win,
+                mt_ref[:, pl.ds(r * window_len, window_len)],
+                contract_last,
+                preferred_element_type=jnp.float32,
+            )
+            acc = part if acc is None else acc + part
+        resp = acc.astype(jnp.bfloat16)
+        up_d = up_ref[d]
+        for k in range(kernels):
+            resp_k = resp[:, k * lon_cols : (k + 1) * lon_cols]
+            gt_ref[k] += lax.dot_general(
+                up_d, resp_k, contract_last, preferred_element_type=jnp.float32
+            )
+        if d == 0:
+            total = None
+            for k in range(kernels):
+                term = jnp.dot(
+                    w_ref[k],
+                    resp[:, k * lon_cols : (k + 1) * lon_cols],
+                    preferred_element_type=jnp.float32,
+                )
+                total = term if total is None else total + term
+            out_ref[...] = total.astype(out_ref.dtype)
+
+
+def row_products(ext, matrix, weights, up_rel):
+    stencil_rows, channels, _ = ext.shape
+    n_blocks, o_block, lon_cols = up_rel.shape
+    kernels = weights.shape[0]
+    flops = 2 * n_blocks * channels * matrix.shape[0] * matrix.shape[1]
+    flops += 2 * n_blocks * kernels * o_block * lon_cols * channels
+    flops += 2 * kernels * weights.shape[1] * channels * lon_cols
+    nbytes = 2 * (ext.size + matrix.size + weights.size + up_rel.size)
+    nbytes += 2 * weights.shape[1] * lon_cols + 4 * kernels * o_block * channels
+    return pl.pallas_call(
+        row_kernel,
+        out_shape=(
+            jax.ShapeDtypeStruct((weights.shape[1], lon_cols), jnp.bfloat16),
+            jax.ShapeDtypeStruct((kernels, o_block, channels), jnp.float32),
+        ),
+        cost_estimate=pl.CostEstimate(flops=flops, transcendentals=0, bytes_accessed=nbytes),
+    )(ext, matrix, weights, up_rel)
+
+
 def body(fields, upstream, weights, filter_taps, cycle_counts, cycle_blocks):
     channels, lat_rows, lon_cols = fields.shape
     kernels = weights.shape[0]
@@ -96,21 +152,12 @@
         lax.ppermute(fields, "lon", [(p, (p - d) % n_lon) for p in range(n_lon)])
         for d in range(1, n_lon)
     ]
-    row = padded_2(jnp.concatenate(blocks, axis=2), (("lat", 1),), 1, False)
-    ext = jnp.concatenate([row[:, :, row.shape[2] - HALO :], row, row[:, :, :HALO]], axis=2)
-    windows = jnp.stack(
-        [ext[:, :, d * lon_cols : d * lon_cols + window_len] for d in range(n_lon)], axis=0
-    )
-    response_all = lax.dot_general(
-        windows.reshape(n_lon * channels, 3 * window_len),
-        matrix,
-        (((1,), (1,)), ((), ())),
-        preferred_element_type=jnp.float32,
-    ).astype(jnp.bfloat16).reshape(n_lon, channels, kernels, lon_cols)
-    response = response_all[0].reshape(channels, lat_rows, kernels, lon_cols)
-    outputs = jnp.einsum(
-        "koc,cikj->oij", weights, response, preferred_element_type=jnp.float32
-    ).astype(jnp.bfloat16)
+    row = jnp.concatenate(blocks, axis=2)[:, 0]
+    count = lax.axis_size("lat")
+    below = lax.ppermute(row, "lat", [(i, i + 1) for i in range(count - 1)])
+    above = lax.ppermute(row, "lat", [(i + 1, i) for i in range(count - 1)])
+    rows = jnp.stack([below, row, above], axis=0)
+    ext = jnp.concatenate([rows[:, :, rows.shape[2] - HALO :], rows, rows[:, :, :HALO]], axis=2)
     response_grad = jnp.einsum(
         "koc,oij->cikj", weights, upstream, preferred_element_type=jnp.float32
     ).astype(jnp.bfloat16)
@@ -121,9 +168,8 @@
         part = lax.dynamic_slice_in_dim(up_row, ((lon_at - d) % n_lon) * o_block, o_block, axis=0)
         up_parts.append(lax.ppermute(part, "lon", [(p, (p - d) % n_lon) for p in range(n_lon)]))
     up_rel = jnp.stack(up_parts, axis=0)
-    grad_terms = jnp.einsum(
-        "doj,dckj->koc", up_rel, response_all, preferred_element_type=jnp.float32
-    )
+    out_row, grad_terms = row_products(ext, matrix, weights, up_rel)
+    outputs = out_row[:, None, :]
     weight_grad = lat_allreduce(grad_terms, "lat", 1)
     accumulated = jnp.zeros((channels, lat_rows + 2, window_len), jnp.float32)
     cycle_row = 0

time: 77.3 us -> 68.3 us (0.88)
  local copies, waits for them, and re-layouts: 22 us -> 7.72 us
  matrix products: 13.3 us -> 2.93 us
  Pallas kernels: 3.07 us -> 11.6 us
  waiting for transfers between devices: 6.01 us -> 8.9 us
  starting transfers between devices: 27.2 us -> 29.7 us
  other arithmetic: 3.51 us -> 5.15 us
    dot_general x3 -> x0, matrix products: 9.18 us -> none  [the longest x1 3.8 us: body(): lax.dot_general(windows.reshape(n_lon * channels, 3 * window_len), matrix...]
    pallas_call x0 -> x1, Pallas kernels: none -> 8.55 us  [row_products(): pl.pallas_call(row_kernel, out_shape=(jax.ShapeDtypeStruct((weights.shape...]
    ppermute x0 -> x2, starting transfers between devices: none -> 7 us  [the longest x1 5.08 us: body(): below = lax.ppermute(row, 'lat', [(i, i + 1) for i in range(count - 1)])]
    ppermute x3 -> x2, starting transfers between devices: 8.37 us -> 3.45 us  [padded_2(): lax.ppermute(head, axis, [((i + 1) % count, i) for i in range(ends)])]
    unnamed x17 -> x13, local copies, waits for them, and re-layouts: 4.91 us -> 0.89 us
    another operation x1 -> x0, local copies, waits for them, and re-layouts: 3.39 us -> none  [body(): jnp.stack([ext[:, :, d * lon_cols:d * lon_cols + window_len] for d in ran...]
    slice x3 -> x0, local copies, waits for them, and re-layouts: 3.06 us -> none  [the longest x2 2.99 us: body(): response = response_all[0].reshape(channels, lat_rows, kernels, lon_cols)]
    reshape x1 -> x0, local copies, waits for them, and re-layouts: 2.97 us -> none  [body(): response_all = lax.dot_general(windows.reshape(n_lon * channels, 3 * wind...]
  transfers between devices with their start and end apart: 18 -> 18, of which waited for: 2 -> 5; matrix products, arithmetic and copies ran while one was open for 49% -> 22% of each run, Pallas kernels for 4% -> 17%
where the time goes in v4:
time: 68.3 us; the launch traced here: 67.6 us
  starting transfers between devices  29.7 us (43%)
  Pallas kernels  11.6 us (17%)
  waiting for transfers between devices  8.9 us (13%)
  local copies, waits for them, and re-layouts  7.72 us (11%)
  other arithmetic  5.15 us (8%)
  matrix products  2.93 us (4%)
  between operations  1.61 us (2%)
    pallas_call x1, Pallas kernels, row_products(): pl.pallas_call(row_kernel, out_shape=(jax.ShapeDtypeStruct((weights.shape...  8.55 us
    ppermute x2, starting transfers between devices, padded_2(): lax.ppermute(tail, axis, [(i, (i + 1) % count) for i in range(ends)])  6.72 us
    ppermute x3, waiting for transfers between devices, lat_allreduce(): recv = lax.ppermute(mine, axis, [(i, i ^ d) for i in range(count)])  5.19 us
    ppermute x1, starting transfers between devices, body(): below = lax.ppermute(row, 'lat', [(i, i + 1) for i in range(count - 1)])  5.08 us
    ppermute x3, starting transfers between devices, body(): lax.ppermute(fields, 'lon', [(p, (p - d) % n_lon) for p in range(n_lon)])  4.66 us
    dot_general x1, local copies, waits for them, and re-layouts, body(): contrib = jnp.dot(grad_piece, matrix, preferred_element_type=jnp.float32)  4.13 us
    ppermute x3, starting transfers between devices, body(): lax.ppermute(part, 'lon', [(p, (p - d) % n_lon) for p in range(n_lon)])  3.46 us
    ppermute x2, starting transfers between devices, padded_2(): lax.ppermute(head, axis, [((i + 1) % count, i) for i in range(ends)])  3.45 us
  transfers between devices with their start and end apart: 18, of which 5 were waited for; matrix products, arithmetic and copies ran while one was open for 22% of the time, Pallas kernels for 17%

profile of v4, /device:TPU:1, one launch (start us, length us, event | category | flops | bytes accessed | tf_op | source)
XLA Modules:
  0.0 67.6 jit_solution(17028404408744031900)
XLA Ops:
  0.6 4.2 %collective-permute-start = (bf16[256,1,128]{2,0,1:T(8,128)(2,1)}, bf16[256,1,128]{2,0,1:T(8,128)(2,1)S(1)}, u32[]{:S(2)}, u32[]{:S(2)}) collective-permute-start(bf16[256,1,128]{2,0,1:T(8,128)(2,1)} %param.22), channel_id=1, source_target_pairs={{0,3},{1,0},{2,1},{3,2},{4,7},{5,4},{6,5},{7,6},{8,11},{9,8},{10,9... | collective-permute-start | bytes 196616 | tf_op jit(solution)/shard_map/ppermute | solution.py:152
  5.3 0.8 %dynamic-slice_bitcast_fusion.3 = (bf16[1,64,128]{2,1,0:T(8,128)(2,1)S(1)}, bf16[64,128]{1,0:T(8,128)(2,1)S(1)}, bf16[64,128]{1,0:T(8,128)(2,1)S(1)}, bf16[64,128]{1,0:T(8,128)(2,1)S(1)}) fusion(bf16[256,1,128]{2,0,1:T(8,128)(2,1)} %param.23, s32[]{:T(128)S(6)} %select_n.51, s32[]{:T(128)S(6)} %select_n.55, s32[]{:T(128)S(6)} %select_n.53, s32[]{:T(128)S(6)} %select_n.57), kind=kLoop, calls=%fused_computation.31 | loop fusion | bytes 131088 | tf_op jit(solution)/shard_map/stack | solution.py:170
  6.1 2.8 %collective-permute-start.5 = (bf16[64,128]{1,0:T(8,128)(2,1)S(1)}, bf16[64,128]{1,0:T(8,128)(2,1)S(1)}, u32[]{:S(2)}, u32[]{:S(2)}) collective-permute-start(bf16[64,128]{1,0:T(8,128)(2,1)S(1)} %get-tuple-element.102), channel_id=1, source_target_pairs={{0,3},{1,0},{2,1},{3,2},{4,7},{5,4},{6,5},{7,6},{8,11},{9,8},{10,9... | collective-permute-start | bytes 49160 | tf_op jit(solution)/shard_map/ppermute | solution.py:169
  8.9 0.6 collective-permute-start.6
  9.5 0.7 add_bitcast_fusion
  11.1 0.6 reshape.261.tap_ref
  11.8 3.1 %shard_map.100 = bf16[9,128,1152]{2,1,0:T(8,128)(2,1)} custom-call(f32[27,384]{1,0:T(8,128)} %reshape.261.tap_ref), custom_call_target="tpu_custom_call" | custom-call | tf_op jit(solution)/shard_map/pallas_call | solution.py:58
  14.9 4.1 %copy.17 = bf16[1152,1152]{1,0:T(8,128)(2,1)S(1)} copy(bf16[1152,1152]{0,1:T(8,128)(2,1)} %bitcast.53) | data formatting | bytes 5308416 | tf_op jit(solution)/shard_map/dot_general | solution.py:177
  19.0 1.6 %convolution_convert_fusion = bf16[128,9,256]{2,0,1:T(8,128)(2,1)S(1)} fusion(bf16[9,256,256]{2,1,0:T(8,128)(2,1)} %w_ref.1, bf16[256,1,128]{2,0,1:T(8,128)(2,1)S(1)} %copy-done.3), kind=kOutput, calls=%fused_computation | convolution fusion | flops 151289856 | bytes 1835008 | tf_op jit(solution)/shard_map/koc,oij->cikj/dot_general | solution.py:161
  20.7 1.1 %fusion.21 = f32[256,3,384]{2,0,1:T(8,128)S(1)} fusion(bf16[256,1152,1]{0,1,2:T(8,128)(2,1)S(1)} %bitcast.56, bf16[3,384,1152]{2,1,0:T(8,128)(2,1)S(1)} %bitcast.55), kind=kOutput, calls=%fused_computation.50 | convolution fusion | flops 679477248 | bytes 4423680 | tf_op jit(solution)/shard_map/dot_general | solution.py:177
  22.0 5.1 %collective-permute-start.3 = (bf16[256,512]{1,0:T(8,128)(2,1)S(1)}, bf16[256,512]{1,0:T(8,128)(2,1)S(1)}, u32[]{:S(2)}, u32[]{:S(2)}) collective-permute-start(bf16[256,512]{1,0:T(8,128)(2,1)S(1)} %bitcast.57), channel_id=1, source_target_pairs={{0,4},{4,8},{8,12},{1,5},{5,9},{9,13},{2,6},{6,10},{10,14},{3,7},{... | collective-permute-start | bytes 786440 | tf_op jit(solution)/shard_map/ppermute | solution.py:157
  27.1 1.9 %collective-permute-start.4 = (bf16[256,512]{1,0:T(8,128)(2,1)S(1)}, bf16[256,512]{1,0:T(8,128)(2,1)S(1)}, u32[]{:S(2)}, u32[]{:S(2)}) collective-permute-start(bf16[256,512]{1,0:T(8,128)(2,1)S(1)} %bitcast.58), channel_id=1, source_target_pairs={{4,0},{8,4},{12,8},{5,1},{9,5},{13,9},{6,2},{10,6},{14,10},{7,3},{... | collective-permute-start | bytes 786440 | tf_op jit(solution)/shard_map/ppermute | solution.py:158
  29.1 2.1 %collective-permute-start.8 = (f32[256,3,128]{2,0,1:T(8,128)S(1)}, f32[256,3,128]{2,0,1:T(8,128)S(1)}, u32[]{:S(2)}, u32[]{:S(2)}) collective-permute-start(f32[256,3,128]{2,0,1:T(8,128)S(1)} %get-tuple-element.93), channel_id=1, source_target_pairs={{0,1},{1,2},{2,3},{3,0},{4,5},{5,6},{6,7},{7,4},{8,9},{9,10},{10,1... | collective-permute-start | bytes 1179656 | tf_op jit(solution)/shard_map/ppermute | solution.py:19
  31.2 1.5 %collective-permute-start.9 = (f32[256,3,128]{2,0,1:T(8,128)S(1)}, f32[256,3,128]{2,0,1:T(8,128)S(1)}, u32[]{:S(2)}, u32[]{:S(2)}) collective-permute-start(f32[256,3,128]{2,0,1:T(8,128)S(1)} %get-tuple-element.94), channel_id=1, source_target_pairs={{1,0},{2,1},{3,2},{0,3},{5,4},{6,5},{7,6},{4,7},{9,8},{10,9},{11,1... | collective-permute-start | bytes 1179656 | tf_op jit(solution)/shard_map/ppermute | solution.py:21
  32.8 0.6 pad_maximum_fusion.4.up_ref
  33.4 1.7 %collective-permute-done.4 = bf16[256,512]{1,0:T(8,128)(2,1)S(1)} collective-permute-done((bf16[256,512]{1,0:T(8,128)(2,1)S(1)}, bf16[256,512]{1,0:T(8,128)(2,1)S(1)}, u32[]{:S(2)}, u32[]{:S(2)}) %collective-permute-start.4) | collective-permute-done | bytes 262176 | tf_op jit(solution)/shard_map/ppermute | solution.py:158
  35.1 1.1 %fusion.ext_ref = bf16[3,256,768]{2,1,0:T(8,128)(2,1)} fusion(bf16[1,256,512]{2,1,0:T(8,128)(2,1)S(1)} %bitcast.61, bf16[1,256,512]{2,1,0:T(8,128)(2,1)S(1)} %bitcast.59, bf16[1,256,512]{2,1,0:T(8,128)(2,1)S(1)} %bitcast.60), kind=kLoop, calls=%fused_computation.2 | loop fusion | flops 10616832 | bytes 1966080 | tf_op jit(solution)/shard_map/concatenate | solution.py:160
  36.1 8.6 %shard_map.101 = (bf16[256,128]{1,0:T(8,128)(2,1)}, f32[9,64,256]{2,1,0:T(8,128)}) custom-call(bf16[3,256,768]{2,1,0:T(8,128)(2,1)} %fusion.ext_ref, bf16[1152,1152]{1,0:T(8,128)(2,1)} %bitcast.54, bf16[9,256,256]{2,1,0:T(8,128)(2,1)} %w_ref.1, bf16[4,64,128]{2,1,0:T(8,128)(2,1)} %pad_maximum_fusion.4.up_ref), custom_call_target="tpu_custom_call" | custom-call | flops 3019898880 | bytes 5734400 | tf_op jit(solution)/shard_map/pallas_call | solution.py:133
  44.7 1.1 %constant_dynamic-slice_fusion.2 = (f32[9,16,256]{2,1,0:T(8,128)S(1)}, f32[9,16,256]{2,1,0:T(8,128)S(1)}, f32[9,16,256]{2,1,0:T(8,128)S(1)}) fusion(f32[9,64,256]{2,1,0:T(8,128)} %get-tuple-element.90, s32[]{:T(128)S(6)} %select_n.59, s32[]{:T(128)S(6)} %select_n.61, s32[]{:T(128)S(6)} %select_n.60), kind=kLoop, calls=%fused_computation.42 | loop fusion | bytes 884748 | tf_op jit(solution)/shard_map/dynamic_slice | solution.py:74
  45.9 0.5 collective-permute-start.13
  46.3 1.7 %collective-permute-start.14 = (f32[9,16,256]{2,1,0:T(8,128)S(1)}, f32[9,16,256]{2,1,0:T(8,128)S(1)}, u32[]{:S(2)}, u32[]{:S(2)}) collective-permute-start(f32[9,16,256]{2,1,0:T(8,128)S(1)} %get-tuple-element.96), channel_id=1, source_target_pairs={{0,12},{4,8},{8,4},{12,0},{1,13},{5,9},{9,5},{13,1},{2,14},{6,10},... | collective-permute-start | bytes 442376 | tf_op jit(solution)/shard_map/ppermute | solution.py:75
  48.0 0.5 collective-permute-done.9
  48.5 1.1 %fusion.4 = f32[256,3,128]{2,0,1:T(8,128)S(1)} fusion(f32[256,3,128]{2,0,1:T(8,128)S(1)} %collective-permute-done.9, f32[256,3,128]{2,0,1:T(8,128)S(1)} %collective-permute-done.8, f32[256,3,384]{2,0,1:T(8,128)} %copy-done.1), kind=kLoop, calls=%fused_computation.11 | loop fusion | flops 196608 | bytes 1572864 | tf_op jit(solution)/shard_map/add | solution.py:187
  49.6 4.6 %collective-permute-start.10 = (f32[256,1,128]{2,0,1:T(8,128)S(1)}, f32[256,1,128]{2,0,1:T(8,128)S(1)}, u32[]{:S(2)}, u32[]{:S(2)}) collective-permute-start(f32[256,1,128]{2,0,1:T(8,128)S(1)} %get-tuple-element.98), channel_id=1, source_target_pairs={{0,4},{4,8},{8,12},{1,5},{5,9},{9,13},{2,6},{6,10},{10,14},{3,7},{... | collective-permute-start | bytes 393224 | tf_op jit(solution)/shard_map/ppermute | solution.py:19
  54.2 1.9 %collective-permute-start.11 = (f32[256,1,128]{2,0,1:T(8,128)S(1)}, f32[256,1,128]{2,0,1:T(8,128)S(1)}, u32[]{:S(2)}, u32[]{:S(2)}) collective-permute-start(f32[256,1,128]{2,0,1:T(8,128)S(1)} %get-tuple-element.99), channel_id=1, source_target_pairs={{4,0},{8,4},{12,8},{5,1},{9,5},{13,9},{6,2},{10,6},{14,10},{7,3},{... | collective-permute-start | bytes 393224 | tf_op jit(solution)/shard_map/ppermute | solution.py:21
  56.2 1.0 %constant_dynamic-update-slice_fusion.7 = (f32[9,64,256]{2,1,0:T(8,128)S(1)}, f32[9,16,256]{2,1,0:T(8,128)S(1)}) fusion(f32[9,64,256]{2,1,0:T(8,128)S(1)} %broadcast_in_dim.25, s32[]{:T(128)S(6)} %select_n.58, f32[9,16,256]{2,1,0:T(8,128)S(1)} %collective-permute-done.13, f32[9,16,256]{2,1,0:T(8,128)S(1)} %collective-permute-done.14, ...), kind=kLoop, calls=%fused_computation.39 | loop fusion | flops 110592 | bytes 884740 | tf_op jit(solution)/shard_map/dynamic_update_slice | solution.py:80
  57.3 1.8 %collective-permute-start.16 = (f32[9,16,256]{2,1,0:T(8,128)S(1)}, f32[9,16,256]{2,1,0:T(8,128)S(1)}, u32[]{:S(2)}, u32[]{:S(2)}) collective-permute-start(f32[9,16,256]{2,1,0:T(8,128)S(1)} %get-tuple-element.92), channel_id=1, source_target_pairs={{0,8},{4,12},{8,0},{12,4},{1,9},{5,13},{9,1},{13,5},{2,10},{6,14},... | collective-permute-start | bytes 442376 | tf_op jit(solution)/shard_map/ppermute | solution.py:82
  59.4 1.5 %collective-permute-done.11 = f32[256,1,128]{2,0,1:T(8,128)S(1)} collective-permute-done((f32[256,1,128]{2,0,1:T(8,128)S(1)}, f32[256,1,128]{2,0,1:T(8,128)S(1)}, u32[]{:S(2)}, u32[]{:S(2)}) %collective-permute-start.11) | collective-permute-done | bytes 131104 | tf_op jit(solution)/shard_map/ppermute | solution.py:21
  60.9 0.7 fusion.6
  61.6 1.9 %collective-permute-done.16 = f32[9,16,256]{2,1,0:T(8,128)S(1)} collective-permute-done((f32[9,16,256]{2,1,0:T(8,128)S(1)}, f32[9,16,256]{2,1,0:T(8,128)S(1)}, u32[]{:S(2)}, u32[]{:S(2)}) %collective-permute-start.16) | collective-permute-done | bytes 147488 | tf_op jit(solution)/shard_map/ppermute | solution.py:82
  63.5 3.3 %collective-permute-done.17 = f32[9,16,256]{2,1,0:T(8,128)S(1)} collective-permute-done((f32[9,16,256]{2,1,0:T(8,128)S(1)}, f32[9,16,256]{2,1,0:T(8,128)S(1)}, u32[]{:S(2)}, u32[]{:S(2)}) %collective-permute-start.17) | collective-permute-done | bytes 147488 | tf_op jit(solution)/shard_map/ppermute | solution.py:82
  66.8 0.8 %copy-done.2 = f32[9,64,256]{2,1,0:T(8,128)} copy-done((f32[9,64,256]{2,1,0:T(8,128)}, f32[9,64,256]{2,1,0:T(8,128)S(1)}, u32[]{:S(2)}) %copy-start.2) | copy-done | bytes 589848
  (43 shorter events, 1.5 us)
Async XLA Ops:
  0.6 10.2 %copy-start = (bf16[1,9,3,2,64]{4,3,2,1,0:T(2,128)(2,1)S(1)}, bf16[1,9,3,2,64]{4,3,2,1,0:T(2,128)(2,1)}, u32[]{:S(2)}) copy-start(bf16[1,9,3,2,64]{4,3,2,1,0:T(2,128)(2,1)} %param.25) | copy-start | bytes 20740
  0.6 21.2 %collective-permute-start = (bf16[256,1,128]{2,0,1:T(8,128)(2,1)}, bf16[256,1,128]{2,0,1:T(8,128)(2,1)S(1)}, u32[]{:S(2)}, u32[]{:S(2)}) collective-permute-start(bf16[256,1,128]{2,0,1:T(8,128)(2,1)} %param.22), channel_id=1, source_target_pairs={{0,3},{1,0},{2,1},{3,2},{4,7},{5,4},{6,5},{7,6},{8,11},{9,8},{10,9... | collective-permute-start | bytes 196616 | tf_op jit(solution)/shard_map/ppermute | solution.py:152
  4.8 17.1 %collective-permute-start.1 = (bf16[256,1,128]{2,0,1:T(8,128)(2,1)}, bf16[256,1,128]{2,0,1:T(8,128)(2,1)S(1)}, u32[]{:S(2)}, u32[]{:S(2)}) collective-permute-start(bf16[256,1,128]{2,0,1:T(8,128)(2,1)} %param.22), channel_id=1, source_target_pairs={{0,2},{1,3},{2,0},{3,1},{4,6},{5,7},{6,4},{7,5},{8,10},{9,11},{10,... | collective-permute-start | bytes 196616 | tf_op jit(solution)/shard_map/ppermute | solution.py:152
  4.9 17.1 %collective-permute-start.2 = (bf16[256,1,128]{2,0,1:T(8,128)(2,1)}, bf16[256,1,128]{2,0,1:T(8,128)(2,1)S(1)}, u32[]{:S(2)}, u32[]{:S(2)}) collective-permute-start(bf16[256,1,128]{2,0,1:T(8,128)(2,1)} %param.22), channel_id=1, source_target_pairs={{0,1},{1,2},{2,3},{3,0},{4,5},{5,6},{6,7},{7,4},{8,9},{9,10},{10,1... | collective-permute-start | bytes 196616 | tf_op jit(solution)/shard_map/ppermute | solution.py:152
  6.1 23.0 %collective-permute-start.5 = (bf16[64,128]{1,0:T(8,128)(2,1)S(1)}, bf16[64,128]{1,0:T(8,128)(2,1)S(1)}, u32[]{:S(2)}, u32[]{:S(2)}) collective-permute-start(bf16[64,128]{1,0:T(8,128)(2,1)S(1)} %get-tuple-element.102), channel_id=1, source_target_pairs={{0,3},{1,0},{2,1},{3,2},{4,7},{5,4},{6,5},{7,6},{8,11},{9,8},{10,9... | collective-permute-start | bytes 49160 | tf_op jit(solution)/shard_map/ppermute | solution.py:169
  8.9 22.3 %collective-permute-start.6 = (bf16[64,128]{1,0:T(8,128)(2,1)S(1)}, bf16[64,128]{1,0:T(8,128)(2,1)S(1)}, u32[]{:S(2)}, u32[]{:S(2)}) collective-permute-start(bf16[64,128]{1,0:T(8,128)(2,1)S(1)} %get-tuple-element.101), channel_id=1, source_target_pairs={{0,2},{1,3},{2,0},{3,1},{4,6},{5,7},{6,4},{7,5},{8,10},{9,11},{10,... | collective-permute-start | bytes 49160 | tf_op jit(solution)/shard_map/ppermute | solution.py:169
  14.9 4.1 %copy-start.3 = (bf16[256,1,128]{2,0,1:T(8,128)(2,1)S(1)}, bf16[256,1,128]{2,0,1:T(8,128)(2,1)}, u32[]{:S(2)}) copy-start(bf16[256,1,128]{2,0,1:T(8,128)(2,1)} %param.23) | copy-start | bytes 196612
  20.6 1.1 %copy-start.4 = (bf16[256,1,128]{2,0,1:T(8,128)(2,1)S(1)}, bf16[256,1,128]{2,0,1:T(8,128)(2,1)}, u32[]{:S(2)}) copy-start(bf16[256,1,128]{2,0,1:T(8,128)(2,1)} %param.22) | copy-start | bytes 196612
  21.8 7.2 %copy-start.1 = (f32[256,3,384]{2,0,1:T(8,128)}, f32[256,3,384]{2,0,1:T(8,128)S(1)}, u32[]{:S(2)}) copy-start(f32[256,3,384]{2,0,1:T(8,128)S(1)} %fusion.21) | copy-start | bytes 3538948
  21.8 10.9 %collective-permute-start.7 = (bf16[64,128]{1,0:T(8,128)(2,1)S(1)}, bf16[64,128]{1,0:T(8,128)(2,1)S(1)}, u32[]{:S(2)}, u32[]{:S(2)}) collective-permute-start(bf16[64,128]{1,0:T(8,128)(2,1)S(1)} %get-tuple-element.103), channel_id=1, source_target_pairs={{0,1},{1,2},{2,3},{3,0},{4,5},{5,6},{6,7},{7,4},{8,9},{9,10},{10,1... | collective-permute-start | bytes 49160 | tf_op jit(solution)/shard_map/ppermute | solution.py:169
  22.0 11.4 %collective-permute-start.3 = (bf16[256,512]{1,0:T(8,128)(2,1)S(1)}, bf16[256,512]{1,0:T(8,128)(2,1)S(1)}, u32[]{:S(2)}, u32[]{:S(2)}) collective-permute-start(bf16[256,512]{1,0:T(8,128)(2,1)S(1)} %bitcast.57), channel_id=1, source_target_pairs={{0,4},{4,8},{8,12},{1,5},{5,9},{9,13},{2,6},{6,10},{10,14},{3,7},{... | collective-permute-start | bytes 786440 | tf_op jit(solution)/shard_map/ppermute | solution.py:157
  27.1 8.0 %collective-permute-start.4 = (bf16[256,512]{1,0:T(8,128)(2,1)S(1)}, bf16[256,512]{1,0:T(8,128)(2,1)S(1)}, u32[]{:S(2)}, u32[]{:S(2)}) collective-permute-start(bf16[256,512]{1,0:T(8,128)(2,1)S(1)} %bitcast.58), channel_id=1, source_target_pairs={{4,0},{8,4},{12,8},{5,1},{9,5},{13,9},{6,2},{10,6},{14,10},{7,3},{... | collective-permute-start | bytes 786440 | tf_op jit(solution)/shard_map/ppermute | solution.py:158
  29.1 18.9 %collective-permute-start.8 = (f32[256,3,128]{2,0,1:T(8,128)S(1)}, f32[256,3,128]{2,0,1:T(8,128)S(1)}, u32[]{:S(2)}, u32[]{:S(2)}) collective-permute-start(f32[256,3,128]{2,0,1:T(8,128)S(1)} %get-tuple-element.93), channel_id=1, source_target_pairs={{0,1},{1,2},{2,3},{3,0},{4,5},{5,6},{6,7},{7,4},{8,9},{9,10},{10,1... | collective-permute-start | bytes 1179656 | tf_op jit(solution)/shard_map/ppermute | solution.py:19
  31.2 17.3 %collective-permute-start.9 = (f32[256,3,128]{2,0,1:T(8,128)S(1)}, f32[256,3,128]{2,0,1:T(8,128)S(1)}, u32[]{:S(2)}, u32[]{:S(2)}) collective-permute-start(f32[256,3,128]{2,0,1:T(8,128)S(1)} %get-tuple-element.94), channel_id=1, source_target_pairs={{1,0},{2,1},{3,2},{0,3},{5,4},{6,5},{7,6},{4,7},{9,8},{10,9},{11,1... | collective-permute-start | bytes 1179656 | tf_op jit(solution)/shard_map/ppermute | solution.py:21
  45.8 10.3 %collective-permute-start.12 = (f32[9,16,256]{2,1,0:T(8,128)S(1)}, f32[9,16,256]{2,1,0:T(8,128)S(1)}, u32[]{:S(2)}, u32[]{:S(2)}) collective-permute-start(f32[9,16,256]{2,1,0:T(8,128)S(1)} %get-tuple-element.95), channel_id=1, source_target_pairs={{0,4},{4,0},{8,12},{12,8},{1,5},{5,1},{9,13},{13,9},{2,6},{6,2},{1... | collective-permute-start | bytes 442376 | tf_op jit(solution)/shard_map/ppermute | solution.py:75
  45.9 10.3 %collective-permute-start.13 = (f32[9,16,256]{2,1,0:T(8,128)S(1)}, f32[9,16,256]{2,1,0:T(8,128)S(1)}, u32[]{:S(2)}, u32[]{:S(2)}) collective-permute-start(f32[9,16,256]{2,1,0:T(8,128)S(1)} %get-tuple-element.97), channel_id=1, source_target_pairs={{0,8},{4,12},{8,0},{12,4},{1,9},{5,13},{9,1},{13,5},{2,10},{6,14},... | collective-permute-start | bytes 442376 | tf_op jit(solution)/shard_map/ppermute | solution.py:75
  46.3 9.8 %collective-permute-start.14 = (f32[9,16,256]{2,1,0:T(8,128)S(1)}, f32[9,16,256]{2,1,0:T(8,128)S(1)}, u32[]{:S(2)}, u32[]{:S(2)}) collective-permute-start(f32[9,16,256]{2,1,0:T(8,128)S(1)} %get-tuple-element.96), channel_id=1, source_target_pairs={{0,12},{4,8},{8,4},{12,0},{1,13},{5,9},{9,5},{13,1},{2,14},{6,10},... | collective-permute-start | bytes 442376 | tf_op jit(solution)/shard_map/ppermute | solution.py:75
  49.6 9.8 %collective-permute-start.10 = (f32[256,1,128]{2,0,1:T(8,128)S(1)}, f32[256,1,128]{2,0,1:T(8,128)S(1)}, u32[]{:S(2)}, u32[]{:S(2)}) collective-permute-start(f32[256,1,128]{2,0,1:T(8,128)S(1)} %get-tuple-element.98), channel_id=1, source_target_pairs={{0,4},{4,8},{8,12},{1,5},{5,9},{9,13},{2,6},{6,10},{10,14},{3,7},{... | collective-permute-start | bytes 393224 | tf_op jit(solution)/shard_map/ppermute | solution.py:19
  54.2 6.7 %collective-permute-start.11 = (f32[256,1,128]{2,0,1:T(8,128)S(1)}, f32[256,1,128]{2,0,1:T(8,128)S(1)}, u32[]{:S(2)}, u32[]{:S(2)}) collective-permute-start(f32[256,1,128]{2,0,1:T(8,128)S(1)} %get-tuple-element.99), channel_id=1, source_target_pairs={{4,0},{8,4},{12,8},{5,1},{9,5},{13,9},{6,2},{10,6},{14,10},{7,3},{... | collective-permute-start | bytes 393224 | tf_op jit(solution)/shard_map/ppermute | solution.py:21
  57.2 4.4 %collective-permute-start.15 = (f32[9,16,256]{2,1,0:T(8,128)S(1)}, f32[9,16,256]{2,1,0:T(8,128)S(1)}, u32[]{:S(2)}, u32[]{:S(2)}) collective-permute-start(f32[9,16,256]{2,1,0:T(8,128)S(1)} %get-tuple-element.92), channel_id=1, source_target_pairs={{0,4},{4,0},{8,12},{12,8},{1,5},{5,1},{9,13},{13,9},{2,6},{6,2},{1... | collective-permute-start | bytes 442376 | tf_op jit(solution)/shard_map/ppermute | solution.py:82
  57.3 6.2 %collective-permute-start.16 = (f32[9,16,256]{2,1,0:T(8,128)S(1)}, f32[9,16,256]{2,1,0:T(8,128)S(1)}, u32[]{:S(2)}, u32[]{:S(2)}) collective-permute-start(f32[9,16,256]{2,1,0:T(8,128)S(1)} %get-tuple-element.92), channel_id=1, source_target_pairs={{0,8},{4,12},{8,0},{12,4},{1,9},{5,13},{9,1},{13,5},{2,10},{6,14},... | collective-permute-start | bytes 442376 | tf_op jit(solution)/shard_map/ppermute | solution.py:82
  59.1 7.7 %collective-permute-start.17 = (f32[9,16,256]{2,1,0:T(8,128)S(1)}, f32[9,16,256]{2,1,0:T(8,128)S(1)}, u32[]{:S(2)}, u32[]{:S(2)}) collective-permute-start(f32[9,16,256]{2,1,0:T(8,128)S(1)} %get-tuple-element.92), channel_id=1, source_target_pairs={{0,12},{4,8},{8,4},{12,0},{1,13},{5,9},{9,5},{13,1},{2,14},{6,10},... | collective-permute-start | bytes 442376 | tf_op jit(solution)/shard_map/ppermute | solution.py:82
  66.8 0.8 %copy-start.2 = (f32[9,64,256]{2,1,0:T(8,128)}, f32[9,64,256]{2,1,0:T(8,128)S(1)}, u32[]{:S(2)}) copy-start(f32[9,64,256]{2,1,0:T(8,128)S(1)} %constant_dynamic-update-slice_fusion.4) | copy-start | bytes 1769476

commit v5 on v4

--- a/solution.py
+++ b/solution.py
@@ -64,24 +64,16 @@
 
 def lat_allreduce(x, axis, dim):
     count = lax.axis_size(axis)
-    steps = count.bit_length() - 1
-    if (1 << steps) != count or x.shape[dim] % count:
+    if x.shape[dim] % count:
         return lax.psum(x, axis)
-    index = lax.axis_index(axis)
     size = x.shape[dim] // count
-    parts = [lax.dynamic_slice_in_dim(x, index * size, size, axis=dim)]
-    for d in range(1, count):
-        send = lax.dynamic_slice_in_dim(x, (index ^ d) * size, size, axis=dim)
-        parts.append(lax.ppermute(send, axis, [(i, i ^ d) for i in range(count)]))
-    for s in range(steps):
-        parts = [parts[2 * e] + parts[2 * e + 1] for e in range(len(parts) // 2)]
+    gathered = lax.all_to_all(x, axis, dim, dim, tiled=True)
+    parts = [lax.slice_in_dim(gathered, s * size, (s + 1) * size, axis=dim) for s in range(count)]
+    while len(parts) > 1:
+        paired = [parts[2 * e] + parts[2 * e + 1] for e in range(len(parts) // 2)]
+        parts = paired + parts[2 * len(paired) :]
     mine = parts[0]
-    out = jnp.zeros(x.shape, x.dtype)
-    out = lax.dynamic_update_slice_in_dim(out, mine, index * size, axis=dim)
-    for d in range(1, count):
-        recv = lax.ppermute(mine, axis, [(i, i ^ d) for i in range(count)])
-        out = lax.dynamic_update_slice_in_dim(out, recv, (index ^ d) * size, axis=dim)
-    return out
+    return lax.all_to_all(jnp.concatenate([mine] * count, axis=dim), axis, dim, dim, tiled=True)
 
 
 def row_kernel(ext_ref, mt_ref, w_ref, up_ref, out_ref, gt_ref):
@@ -148,11 +140,21 @@
     lon_at = lax.axis_index("lon")
     tap_table = build_taps(filter_taps, cycle_counts, cycle_blocks).astype(jnp.bfloat16)
     matrix = toeplitz(tap_table[0], lon_cols)
-    blocks = [fields] + [
-        lax.ppermute(fields, "lon", [(p, (p - d) % n_lon) for p in range(n_lon)])
-        for d in range(1, n_lon)
-    ]
-    row = jnp.concatenate(blocks, axis=2)[:, 0]
+    o_block = upstream.shape[0] // n_lon
+    up_row = upstream[:, 0]
+    blocks = [fields[:, 0]]
+    up_parts = [lax.dynamic_slice_in_dim(up_row, lon_at * o_block, o_block, axis=0)]
+    for d in range(1, n_lon):
+        part = lax.dynamic_slice_in_dim(up_row, ((lon_at - d) % n_lon) * o_block, o_block, axis=0)
+        both = lax.ppermute(
+            jnp.concatenate([fields[:, 0], part], axis=0),
+            "lon",
+            [(p, (p - d) % n_lon) for p in range(n_lon)],
+        )
+        blocks.append(both[:channels])
+        up_parts.append(both[channels:])
+    up_rel = jnp.stack(up_parts, axis=0)
+    row = jnp.concatenate(blocks, axis=1)
     count = lax.axis_size("lat")
     below = lax.ppermute(row, "lat", [(i, i + 1) for i in range(count - 1)])
     above = lax.ppermute(row, "lat", [(i + 1, i) for i in range(count - 1)])
@@ -161,13 +163,6 @@
     response_grad = jnp.einsum(
         "koc,oij->cikj", weights, upstream, preferred_element_type=jnp.float32
     ).astype(jnp.bfloat16)
-    o_block = upstream.shape[0] // n_lon
-    up_row = upstream[:, 0]
-    up_parts = [lax.dynamic_slice_in_dim(up_row, lon_at * o_block, o_block, axis=0)]
-    for d in range(1, n_lon):
-        part = lax.dynamic_slice_in_dim(up_row, ((lon_at - d) % n_lon) * o_block, o_block, axis=0)
-        up_parts.append(lax.ppermute(part, "lon", [(p, (p - d) % n_lon) for p in range(n_lon)]))
-    up_rel = jnp.stack(up_parts, axis=0)
     out_row, grad_terms = row_products(ext, matrix, weights, up_rel)
     outputs = out_row[:, None, :]
     weight_grad = lat_allreduce(grad_terms, "lat", 1)

time: 68.3 us -> 86.6 us (1.27)
  waiting for transfers between devices: 8.9 us -> 25.9 us
  local copies, waits for them, and re-layouts: 7.72 us -> 9.3 us
  starting transfers between devices: 29.7 us -> 28.3 us
  other arithmetic: 5.15 us -> 6.3 us
    all_to_all x0 -> x2, waiting for transfers between devices: none -> 10.8 us  [the longest x1 10.8 us: lat_allreduce(): gathered = lax.all_to_all(x, axis, dim, dim, tiled=True)]
    all_to_all x0 -> x2, starting transfers between devices: none -> 7.86 us  [the longest x1 4.35 us: lat_allreduce(): lax.all_to_all(jnp.concatenate([mine] * count, axis=dim), axis, dim, dim,...]
    ppermute x12 -> x3, starting transfers between devices: 12.5 us -> 4.66 us  [body(): lax.ppermute(jnp.concatenate([fields[:, 0], part], axis=0), 'lon', [(p, (...]
    ppermute x2, waiting for transfers between devices: 0.01 us -> 7.86 us  [padded_2(): lax.ppermute(tail, axis, [(i, (i + 1) % count) for i in range(ends)])]
    ppermute x12 -> x3, waiting for transfers between devices: 5.22 us -> 0.01 us  [body(): lax.ppermute(jnp.concatenate([fields[:, 0], part], axis=0), 'lon', [(p, (...]
    ppermute x1, waiting for transfers between devices: 1.65 us -> 4.69 us  [body(): above = lax.ppermute(row, 'lat', [(i + 1, i) for i in range(count - 1)])]
    pallas_call x0 -> x1, local copies, waits for them, and re-layouts: none -> 2.43 us  [row_products(): pl.pallas_call(row_kernel, out_shape=(jax.ShapeDtypeStruct((weights.shape...]
    concatenate x0 -> x2, other arithmetic: none -> 2 us  [the longest x1 1.13 us: lat_allreduce(): jnp.concatenate([mine] * count, axis=dim)]
  transfers between devices with their start and end apart: 18 -> 11, of which waited for: 5 -> 5; matrix products, arithmetic and copies ran while one was open for 22% -> 17% of each run, Pallas kernels for 17% -> 14%
where the time goes in v5:
time: 86.6 us; the launch traced here: 85.9 us
  starting transfers between devices  28.3 us (33%)
  waiting for transfers between devices  25.9 us (30%)
  Pallas kernels  11.6 us (13%)
  local copies, waits for them, and re-layouts  9.3 us (11%)
  other arithmetic  6.3 us (7%)
  matrix products  2.93 us (3%)
  between operations  1.59 us (2%)
    all_to_all x1, waiting for transfers between devices, lat_allreduce(): gathered = lax.all_to_all(x, axis, dim, dim, tiled=True)  10.8 us
    pallas_call x1, Pallas kernels, row_products(): pl.pallas_call(row_kernel, out_shape=(jax.ShapeDtypeStruct((weights.shape...  8.55 us
    ppermute x2, waiting for transfers between devices, padded_2(): lax.ppermute(tail, axis, [(i, (i + 1) % count) for i in range(ends)])  7.86 us
    ppermute x2, starting transfers between devices, padded_2(): lax.ppermute(tail, axis, [(i, (i + 1) % count) for i in range(ends)])  5.79 us
    ppermute x1, starting transfers between devices, body(): below = lax.ppermute(row, 'lat', [(i, i + 1) for i in range(count - 1)])  5.08 us
    ppermute x1, waiting for transfers between devices, body(): above = lax.ppermute(row, 'lat', [(i + 1, i) for i in range(count - 1)])  4.69 us
    ppermute x3, starting transfers between devices, body(): lax.ppermute(jnp.concatenate([fields[:, 0], part], axis=0), 'lon', [(p, (...  4.66 us
    all_to_all x1, starting transfers between devices, lat_allreduce(): lax.all_to_all(jnp.concatenate([mine] * count, axis=dim), axis, dim, dim,...  4.35 us
  transfers between devices with their start and end apart: 11, of which 5 were waited for; matrix products, arithmetic and copies ran while one was open for 17% of the time, Pallas kernels for 14%

profile of v5, /device:TPU:1, one launch (start us, length us, event | category | flops | bytes accessed | tf_op | source)
XLA Modules:
  0.0 85.9 jit_solution(13808906847036159233)
XLA Ops:
  0.7 0.8 dynamic-slice_bitcast_fusion
  1.5 0.9 %pad_maximum_fusion.6 = (bf16[320,128]{1,0:T(8,128)(2,1)S(1)}, bf16[320,128]{1,0:T(8,128)(2,1)S(1)}, bf16[320,128]{1,0:T(8,128)(2,1)S(1)}) fusion(bf16[64,128]{1,0:T(8,128)(2,1)S(1)} %get-tuple-element.103, bf16[256,128]{1,0:T(8,128)(2,1)} %bitcast.63, bf16[64,128]{1,0:T(8,128)(2,1)S(1)} %get-tuple-element.102, bf16[64,128]{1,0:T(8,128)(2,1)S(1)} %get-tuple-element.101), kind=kLoop, calls=%fused_computation.24 | loop fusion | flops 409600 | bytes 360448 | tf_op jit(solution)/shard_map/concatenate | solution.py:150
  2.4 4.2 %collective-permute-start = (bf16[320,128]{1,0:T(8,128)(2,1)S(1)}, bf16[320,128]{1,0:T(8,128)(2,1)S(1)}, u32[]{:S(2)}, u32[]{:S(2)}) collective-permute-start(bf16[320,128]{1,0:T(8,128)(2,1)S(1)} %get-tuple-element.104), channel_id=1, source_target_pairs={{0,3},{1,0},{2,1},{3,2},{4,7},{5,4},{6,5},{7,6},{8,11},{9,8},{10,9... | collective-permute-start | bytes 245768 | tf_op jit(solution)/shard_map/ppermute | solution.py:149
  6.6 0.5 collective-permute-start.2
  7.0 0.7 add_bitcast_fusion
  8.4 0.2 fusion.3
  8.7 0.6 reshape.261.tap_ref
  9.3 3.1 %shard_map.100 = bf16[9,128,1152]{2,1,0:T(8,128)(2,1)} custom-call(f32[27,384]{1,0:T(8,128)} %reshape.261.tap_ref), custom_call_target="tpu_custom_call" | custom-call | tf_op jit(solution)/shard_map/pallas_call | solution.py:58
  12.4 4.1 %copy.22 = bf16[1152,1152]{1,0:T(8,128)(2,1)S(1)} copy(bf16[1152,1152]{0,1:T(8,128)(2,1)} %bitcast.57) | data formatting | bytes 5308416 | tf_op jit(solution)/shard_map/dot_general | solution.py:172
  16.6 1.6 %convolution_convert_fusion = bf16[128,9,256]{2,0,1:T(8,128)(2,1)S(1)} fusion(bf16[9,256,256]{2,1,0:T(8,128)(2,1)} %w_ref.1, bf16[256,1,128]{2,0,1:T(8,128)(2,1)S(1)} %copy-done.2), kind=kOutput, calls=%fused_computation | convolution fusion | flops 151289856 | bytes 1835008 | tf_op jit(solution)/shard_map/koc,oij->cikj/dot_general | solution.py:163
  18.2 1.1 %fusion.23 = f32[256,3,384]{2,0,1:T(8,128)S(1)} fusion(bf16[256,1152,1]{0,1,2:T(8,128)(2,1)S(1)} %bitcast.60, bf16[3,384,1152]{2,1,0:T(8,128)(2,1)S(1)} %bitcast.59), kind=kOutput, calls=%fused_computation.50 | convolution fusion | flops 679477248 | bytes 4423680 | tf_op jit(solution)/shard_map/dot_general | solution.py:172
  19.4 2.3 %collective-permute-start.5 = (f32[256,3,128]{2,0,1:T(8,128)S(1)}, f32[256,3,128]{2,0,1:T(8,128)S(1)}, u32[]{:S(2)}, u32[]{:S(2)}) collective-permute-start(f32[256,3,128]{2,0,1:T(8,128)S(1)} %get-tuple-element.94), channel_id=1, source_target_pairs={{0,1},{1,2},{2,3},{3,0},{4,5},{5,6},{6,7},{7,4},{8,9},{9,10},{10,1... | collective-permute-start | bytes 1179656 | tf_op jit(solution)/shard_map/ppermute | solution.py:19
  21.6 1.1 %collective-permute-start.6 = (f32[256,3,128]{2,0,1:T(8,128)S(1)}, f32[256,3,128]{2,0,1:T(8,128)S(1)}, u32[]{:S(2)}, u32[]{:S(2)}) collective-permute-start(f32[256,3,128]{2,0,1:T(8,128)S(1)} %get-tuple-element.95), channel_id=1, source_target_pairs={{1,0},{2,1},{3,2},{0,3},{5,4},{6,5},{7,6},{4,7},{9,8},{10,9},{11,1... | collective-permute-start | bytes 1179656 | tf_op jit(solution)/shard_map/ppermute | solution.py:21
  22.8 5.1 %collective-permute-start.3 = (bf16[256,512]{1,0:T(8,128)(2,1)S(1)}, bf16[256,512]{1,0:T(8,128)(2,1)S(1)}, u32[]{:S(2)}, u32[]{:S(2)}) collective-permute-start(bf16[256,512]{1,0:T(8,128)(2,1)S(1)} %get-tuple-element.99), channel_id=1, source_target_pairs={{0,4},{4,8},{8,12},{1,5},{5,9},{9,13},{2,6},{6,10},{10,14},{3,7},{... | collective-permute-start | bytes 786440 | tf_op jit(solution)/shard_map/ppermute | solution.py:159
  27.9 1.9 %collective-permute-start.4 = (bf16[256,512]{1,0:T(8,128)(2,1)S(1)}, bf16[256,512]{1,0:T(8,128)(2,1)S(1)}, u32[]{:S(2)}, u32[]{:S(2)}) collective-permute-start(bf16[256,512]{1,0:T(8,128)(2,1)S(1)} %get-tuple-element.99), channel_id=1, source_target_pairs={{4,0},{8,4},{12,8},{5,1},{9,5},{13,9},{6,2},{10,6},{14,10},{7,3},{... | collective-permute-start | bytes 786440 | tf_op jit(solution)/shard_map/ppermute | solution.py:160
  29.9 0.6 pad_maximum_fusion.9.up_ref
  30.5 0.7 collective-permute-done.3
  31.2 4.7 %collective-permute-done.4 = bf16[256,512]{1,0:T(8,128)(2,1)S(1)} collective-permute-done((bf16[256,512]{1,0:T(8,128)(2,1)S(1)}, bf16[256,512]{1,0:T(8,128)(2,1)S(1)}, u32[]{:S(2)}, u32[]{:S(2)}) %collective-permute-start.4) | collective-permute-done | bytes 262176 | tf_op jit(solution)/shard_map/ppermute | solution.py:160
  35.9 1.1 %fusion.ext_ref = bf16[3,256,768]{2,1,0:T(8,128)(2,1)} fusion(bf16[1,256,512]{2,1,0:T(8,128)(2,1)S(1)} %bitcast.62, bf16[1,256,512]{2,1,0:T(8,128)(2,1)S(1)} %get-tuple-element.98, bf16[1,256,512]{2,1,0:T(8,128)(2,1)S(1)} %bitcast.61), kind=kLoop, calls=%fused_computation.2 | loop fusion | flops 10616832 | bytes 1966080 | tf_op jit(solution)/shard_map/concatenate | solution.py:162
  37.0 8.6 %shard_map.101 = (bf16[256,128]{1,0:T(8,128)(2,1)}, f32[9,64,256]{2,1,0:T(8,128)}) custom-call(bf16[3,256,768]{2,1,0:T(8,128)(2,1)} %fusion.ext_ref, bf16[1152,1152]{1,0:T(8,128)(2,1)} %bitcast.58, bf16[9,256,256]{2,1,0:T(8,128)(2,1)} %w_ref.1, bf16[4,64,128]{2,1,0:T(8,128)(2,1)} %pad_maximum_fusion.9.up_ref), custom_call_target="tpu_custom_call" | custom-call | flops 3019898880 | bytes 5734400 | tf_op jit(solution)/shard_map/pallas_call | solution.py:125
  45.5 2.4 %copy.24 = f32[9,64,256]{2,0,1:T(8,128)} copy(f32[9,64,256]{2,1,0:T(8,128)} %get-tuple-element.90) | data formatting | bytes 1179648 | tf_op jit(solution)/shard_map/pallas_call | solution.py:125
  48.0 3.5 %all-to-all-start = ((f32[9,64,256]{2,0,1:T(8,128)}), f32[9,64,256]{2,0,1:T(8,128)S(1)}, u32[]{:S(2)}, u32[]{:S(2)}) async-start(f32[9,64,256]{2,0,1:T(8,128)} %copy.24), calls=%async_computation | async-start | bytes 2097152 | tf_op jit(solution)/shard_map/all_to_all | solution.py:70
  51.5 1.1 %fusion.4 = f32[256,3,128]{2,0,1:T(8,128)S(1)} fusion(f32[256,3,128]{2,0,1:T(8,128)S(1)} %collective-permute-done.6, f32[256,3,128]{2,0,1:T(8,128)S(1)} %collective-permute-done.5, f32[256,3,384]{2,0,1:T(8,128)} %copy-done.1), kind=kLoop, calls=%fused_computation.12 | loop fusion | flops 196608 | bytes 1572864 | tf_op jit(solution)/shard_map/add | solution.py:182
  52.5 10.8 %all-to-all-done = f32[9,64,256]{2,0,1:T(8,128)S(1)} async-done(((f32[9,64,256]{2,0,1:T(8,128)}), f32[9,64,256]{2,0,1:T(8,128)S(1)}, u32[]{:S(2)}, u32[]{:S(2)}) %all-to-all-start) | async-done | bytes 589856 | tf_op jit(solution)/shard_map/all_to_all | solution.py:70
  63.4 1.1 %pad_maximum_fusion.4 = f32[9,64,256]{2,0,1:T(8,128)} fusion(f32[9,16,256]{2,0,1:T(8,128)S(1)} %fusion.5), kind=kLoop, calls=%fused_computation.10 | loop fusion | flops 442368 | bytes 737280 | tf_op jit(solution)/shard_map/concatenate | solution.py:76
  64.5 4.4 %all-to-all-start.1 = ((f32[9,64,256]{2,0,1:T(8,128)}), f32[9,64,256]{2,0,1:T(8,128)S(1)}, u32[]{:S(2)}, u32[]{:S(2)}) async-start(f32[9,64,256]{2,0,1:T(8,128)} %pad_maximum_fusion.4), calls=%async_computation.1 | async-start | bytes 2097152 | tf_op jit(solution)/shard_map/all_to_all | solution.py:76
  68.9 3.5 %collective-permute-start.7 = (f32[256,1,128]{2,0,1:T(8,128)S(1)}, f32[256,1,128]{2,0,1:T(8,128)S(1)}, u32[]{:S(2)}, u32[]{:S(2)}) collective-permute-start(f32[256,1,128]{2,0,1:T(8,128)S(1)} %get-tuple-element.96), channel_id=1, source_target_pairs={{0,4},{4,8},{8,12},{1,5},{5,9},{9,13},{2,6},{6,10},{10,14},{3,7},{... | collective-permute-start | bytes 393224 | tf_op jit(solution)/shard_map/ppermute | solution.py:19
  72.5 1.9 %collective-permute-start.8 = (f32[256,1,128]{2,0,1:T(8,128)S(1)}, f32[256,1,128]{2,0,1:T(8,128)S(1)}, u32[]{:S(2)}, u32[]{:S(2)}) collective-permute-start(f32[256,1,128]{2,0,1:T(8,128)S(1)} %get-tuple-element.97), channel_id=1, source_target_pairs={{4,0},{8,4},{12,8},{5,1},{9,5},{13,9},{6,2},{10,6},{14,10},{7,3},{... | collective-permute-start | bytes 393224 | tf_op jit(solution)/shard_map/ppermute | solution.py:21
  74.4 7.9 %collective-permute-done.7 = f32[256,1,128]{2,0,1:T(8,128)S(1)} collective-permute-done((f32[256,1,128]{2,0,1:T(8,128)S(1)}, f32[256,1,128]{2,0,1:T(8,128)S(1)}, u32[]{:S(2)}, u32[]{:S(2)}) %collective-permute-start.7) | collective-permute-done | bytes 131104 | tf_op jit(solution)/shard_map/ppermute | solution.py:19
  82.3 1.8 %collective-permute-done.8 = f32[256,1,128]{2,0,1:T(8,128)S(1)} collective-permute-done((f32[256,1,128]{2,0,1:T(8,128)S(1)}, f32[256,1,128]{2,0,1:T(8,128)S(1)}, u32[]{:S(2)}, u32[]{:S(2)}) %collective-permute-start.8) | collective-permute-done | bytes 131104 | tf_op jit(solution)/shard_map/ppermute | solution.py:21
  84.1 0.7 fusion.7
  84.7 1.2 %copy.25 = f32[9,64,256]{2,1,0:T(8,128)} copy(f32[9,64,256]{2,0,1:T(8,128)S(1)} %all-to-all-done.1) | data formatting | bytes 1179648
  (29 shorter events, 0.4 us)
Async XLA Ops:
  0.6 7.8 %copy-start = (bf16[1,9,3,2,64]{4,3,2,1,0:T(2,128)(2,1)S(1)}, bf16[1,9,3,2,64]{4,3,2,1,0:T(2,128)(2,1)}, u32[]{:S(2)}) copy-start(bf16[1,9,3,2,64]{4,3,2,1,0:T(2,128)(2,1)} %param.25) | copy-start | bytes 20740
  2.4 20.3 %collective-permute-start = (bf16[320,128]{1,0:T(8,128)(2,1)S(1)}, bf16[320,128]{1,0:T(8,128)(2,1)S(1)}, u32[]{:S(2)}, u32[]{:S(2)}) collective-permute-start(bf16[320,128]{1,0:T(8,128)(2,1)S(1)} %get-tuple-element.104), channel_id=1, source_target_pairs={{0,3},{1,0},{2,1},{3,2},{4,7},{5,4},{6,5},{7,6},{8,11},{9,8},{10,9... | collective-permute-start | bytes 245768 | tf_op jit(solution)/shard_map/ppermute | solution.py:149
  6.6 16.1 %collective-permute-start.1 = (bf16[320,128]{1,0:T(8,128)(2,1)S(1)}, bf16[320,128]{1,0:T(8,128)(2,1)S(1)}, u32[]{:S(2)}, u32[]{:S(2)}) collective-permute-start(bf16[320,128]{1,0:T(8,128)(2,1)S(1)} %get-tuple-element.105), channel_id=1, source_target_pairs={{0,2},{1,3},{2,0},{3,1},{4,6},{5,7},{6,4},{7,5},{8,10},{9,11},{10,... | collective-permute-start | bytes 245768 | tf_op jit(solution)/shard_map/ppermute | solution.py:149
  6.6 16.2 %collective-permute-start.2 = (bf16[320,128]{1,0:T(8,128)(2,1)S(1)}, bf16[320,128]{1,0:T(8,128)(2,1)S(1)}, u32[]{:S(2)}, u32[]{:S(2)}) collective-permute-start(bf16[320,128]{1,0:T(8,128)(2,1)S(1)} %get-tuple-element.106), channel_id=1, source_target_pairs={{0,1},{1,2},{2,3},{3,0},{4,5},{5,6},{6,7},{7,4},{8,9},{9,10},{10,1... | collective-permute-start | bytes 245768 | tf_op jit(solution)/shard_map/ppermute | solution.py:149
  12.4 4.1 %copy-start.2 = (bf16[256,1,128]{2,0,1:T(8,128)(2,1)S(1)}, bf16[256,1,128]{2,0,1:T(8,128)(2,1)}, u32[]{:S(2)}) copy-start(bf16[256,1,128]{2,0,1:T(8,128)(2,1)} %param.23) | copy-start | bytes 196612
  18.2 4.6 %copy-start.3 = (bf16[256,1,128]{2,0,1:T(8,128)(2,1)S(1)}, bf16[256,1,128]{2,0,1:T(8,128)(2,1)}, u32[]{:S(2)}) copy-start(bf16[256,1,128]{2,0,1:T(8,128)(2,1)} %param.22) | copy-start | bytes 196612
  19.3 17.7 %copy-start.1 = (f32[256,3,384]{2,0,1:T(8,128)}, f32[256,3,384]{2,0,1:T(8,128)S(1)}, u32[]{:S(2)}) copy-start(f32[256,3,384]{2,0,1:T(8,128)S(1)} %fusion.23) | copy-start | bytes 3538948
  19.4 32.1 %collective-permute-start.5 = (f32[256,3,128]{2,0,1:T(8,128)S(1)}, f32[256,3,128]{2,0,1:T(8,128)S(1)}, u32[]{:S(2)}, u32[]{:S(2)}) collective-permute-start(f32[256,3,128]{2,0,1:T(8,128)S(1)} %get-tuple-element.94), channel_id=1, source_target_pairs={{0,1},{1,2},{2,3},{3,0},{4,5},{5,6},{6,7},{7,4},{8,9},{9,10},{10,1... | collective-permute-start | bytes 1179656 | tf_op jit(solution)/shard_map/ppermute | solution.py:19
  21.6 29.8 %collective-permute-start.6 = (f32[256,3,128]{2,0,1:T(8,128)S(1)}, f32[256,3,128]{2,0,1:T(8,128)S(1)}, u32[]{:S(2)}, u32[]{:S(2)}) collective-permute-start(f32[256,3,128]{2,0,1:T(8,128)S(1)} %get-tuple-element.95), channel_id=1, source_target_pairs={{1,0},{2,1},{3,2},{0,3},{5,4},{6,5},{7,6},{4,7},{9,8},{10,9},{11,1... | collective-permute-start | bytes 1179656 | tf_op jit(solution)/shard_map/ppermute | solution.py:21
  22.8 8.4 %collective-permute-start.3 = (bf16[256,512]{1,0:T(8,128)(2,1)S(1)}, bf16[256,512]{1,0:T(8,128)(2,1)S(1)}, u32[]{:S(2)}, u32[]{:S(2)}) collective-permute-start(bf16[256,512]{1,0:T(8,128)(2,1)S(1)} %get-tuple-element.99), channel_id=1, source_target_pairs={{0,4},{4,8},{8,12},{1,5},{5,9},{9,13},{2,6},{6,10},{10,14},{3,7},{... | collective-permute-start | bytes 786440 | tf_op jit(solution)/shard_map/ppermute | solution.py:159
  27.9 8.0 %collective-permute-start.4 = (bf16[256,512]{1,0:T(8,128)(2,1)S(1)}, bf16[256,512]{1,0:T(8,128)(2,1)S(1)}, u32[]{:S(2)}, u32[]{:S(2)}) collective-permute-start(bf16[256,512]{1,0:T(8,128)(2,1)S(1)} %get-tuple-element.99), channel_id=1, source_target_pairs={{4,0},{8,4},{12,8},{5,1},{9,5},{13,9},{6,2},{10,6},{14,10},{7,3},{... | collective-permute-start | bytes 786440 | tf_op jit(solution)/shard_map/ppermute | solution.py:160
  48.0 15.4 %all-to-all-start = ((f32[9,64,256]{2,0,1:T(8,128)}), f32[9,64,256]{2,0,1:T(8,128)S(1)}, u32[]{:S(2)}, u32[]{:S(2)}) async-start(f32[9,64,256]{2,0,1:T(8,128)} %copy.24), calls=%async_computation | async-start | bytes 2097152 | tf_op jit(solution)/shard_map/all_to_all | solution.py:70
  64.5 20.2 %all-to-all-start.1 = ((f32[9,64,256]{2,0,1:T(8,128)}), f32[9,64,256]{2,0,1:T(8,128)S(1)}, u32[]{:S(2)}, u32[]{:S(2)}) async-start(f32[9,64,256]{2,0,1:T(8,128)} %pad_maximum_fusion.4), calls=%async_computation.1 | async-start | bytes 2097152 | tf_op jit(solution)/shard_map/all_to_all | solution.py:76
  68.9 13.3 %collective-permute-start.7 = (f32[256,1,128]{2,0,1:T(8,128)S(1)}, f32[256,1,128]{2,0,1:T(8,128)S(1)}, u32[]{:S(2)}, u32[]{:S(2)}) collective-permute-start(f32[256,1,128]{2,0,1:T(8,128)S(1)} %get-tuple-element.96), channel_id=1, source_target_pairs={{0,4},{4,8},{8,12},{1,5},{5,9},{9,13},{2,6},{6,10},{10,14},{3,7},{... | collective-permute-start | bytes 393224 | tf_op jit(solution)/shard_map/ppermute | solution.py:19
  72.5 11.6 %collective-permute-start.8 = (f32[256,1,128]{2,0,1:T(8,128)S(1)}, f32[256,1,128]{2,0,1:T(8,128)S(1)}, u32[]{:S(2)}, u32[]{:S(2)}) collective-permute-start(f32[256,1,128]{2,0,1:T(8,128)S(1)} %get-tuple-element.97), channel_id=1, source_target_pairs={{4,0},{8,4},{12,8},{5,1},{9,5},{13,9},{6,2},{10,6},{14,10},{7,3},{... | collective-permute-start | bytes 393224 | tf_op jit(solution)/shard_map/ppermute | solution.py:21

commit v6 on v5

--- a/solution.py
+++ b/solution.py
@@ -38,42 +38,61 @@
     return jnp.einsum("ikrst,istu->ikru", filter_taps.astype(jnp.float32), onehot)
 
 
-def toeplitz_kernel(tap_ref, out_ref):
+def toeplitz_kernel(tap_ref, grad_ref, out_ref, contrib_ref):
     kernels, lon_cols, width = out_ref.shape
     window_len = tap_ref.shape[1]
     stencil_rows = width // window_len
+    acc = None
     for k in range(kernels):
         for r in range(stencil_rows):
             row = tap_ref[pl.ds(k * stencil_rows + r, 1), :]
             tiled = jnp.broadcast_to(row, (lon_cols, window_len))
             rolled = pltpu.roll(tiled, 0, 1, stride=1, stride_axis=0)
             out_ref[k, :, pl.ds(r * window_len, window_len)] = rolled.astype(out_ref.dtype)
-
-
-def toeplitz(tap_row, out_width):
+        term = jnp.dot(
+            grad_ref[:, pl.ds(k * lon_cols, lon_cols)],
+            out_ref[k],
+            preferred_element_type=jnp.float32,
+        )
+        acc = term if acc is None else acc + term
+    contrib_ref[...] = acc
+
+
+def toeplitz(tap_row, out_width, grad_piece):
     kernels, stencil_rows, reach = tap_row.shape
     window_len = out_width + reach
     padded = jnp.pad(tap_row.astype(jnp.float32), ((0, 0), (0, 0), (0, window_len - reach)))
     padded = padded.reshape(kernels * stencil_rows, window_len)
-    out = pl.pallas_call(
+    out, contrib = pl.pallas_call(
         toeplitz_kernel,
-        out_shape=jax.ShapeDtypeStruct((kernels, out_width, stencil_rows * window_len), jnp.bfloat16),
-    )(padded)
-    return out.reshape(kernels * out_width, stencil_rows * window_len)
+        out_shape=(
+            jax.ShapeDtypeStruct((kernels, out_width, stencil_rows * window_len), jnp.bfloat16),
+            jax.ShapeDtypeStruct((grad_piece.shape[0], stencil_rows * window_len), jnp.float32),
+        ),
+    )(padded, grad_piece)
+    return out.reshape(kernels * out_width, stencil_rows * window_len), contrib
 
 
 def lat_allreduce(x, axis, dim):
     count = lax.axis_size(axis)
-    if x.shape[dim] % count:
+    steps = count.bit_length() - 1
+    if (1 << steps) != count or x.shape[dim] % count:
         return lax.psum(x, axis)
+    index = lax.axis_index(axis)
     size = x.shape[dim] // count
-    gathered = lax.all_to_all(x, axis, dim, dim, tiled=True)
-    parts = [lax.slice_in_dim(gathered, s * size, (s + 1) * size, axis=dim) for s in range(count)]
-    while len(parts) > 1:
-        paired = [parts[2 * e] + parts[2 * e + 1] for e in range(len(parts) // 2)]
-        parts = paired + parts[2 * len(paired) :]
+    parts = [lax.dynamic_slice_in_dim(x, index * size, size, axis=dim)]
+    for d in range(1, count):
+        send = lax.dynamic_slice_in_dim(x, (index ^ d) * size, size, axis=dim)
+        parts.append(lax.ppermute(send, axis, [(i, i ^ d) for i in range(count)]))
+    for s in range(steps):
+        parts = [parts[2 * e] + parts[2 * e + 1] for e in range(len(parts) // 2)]
     mine = parts[0]
-    return lax.all_to_all(jnp.concatenate([mine] * count, axis=dim), axis, dim, dim, tiled=True)
+    out = jnp.zeros(x.shape, x.dtype)
+    out = lax.dynamic_update_slice_in_dim(out, mine, index * size, axis=dim)
+    for d in range(1, count):
+        recv = lax.ppermute(mine, axis, [(i, i ^ d) for i in range(count)])
+        out = lax.dynamic_update_slice_in_dim(out, recv, (index ^ d) * size, axis=dim)
+    return out
 
 
 def row_kernel(ext_ref, mt_ref, w_ref, up_ref, out_ref, gt_ref):
@@ -139,7 +158,11 @@
     n_lon = lax.axis_size("lon")
     lon_at = lax.axis_index("lon")
     tap_table = build_taps(filter_taps, cycle_counts, cycle_blocks).astype(jnp.bfloat16)
-    matrix = toeplitz(tap_table[0], lon_cols)
+    response_grad = jnp.einsum(
+        "koc,oij->cikj", weights, upstream, preferred_element_type=jnp.float32
+    ).astype(jnp.bfloat16)
+    grad_piece = response_grad[:, 0].reshape(channels, kernels * lon_cols)
+    matrix, contrib = toeplitz(tap_table[0], lon_cols, grad_piece)
     o_block = upstream.shape[0] // n_lon
     up_row = upstream[:, 0]
     blocks = [fields[:, 0]]
@@ -160,16 +183,11 @@
     above = lax.ppermute(row, "lat", [(i + 1, i) for i in range(count - 1)])
     rows = jnp.stack([below, row, above], axis=0)
     ext = jnp.concatenate([rows[:, :, rows.shape[2] - HALO :], rows, rows[:, :, :HALO]], axis=2)
-    response_grad = jnp.einsum(
-        "koc,oij->cikj", weights, upstream, preferred_element_type=jnp.float32
-    ).astype(jnp.bfloat16)
     out_row, grad_terms = row_products(ext, matrix, weights, up_rel)
     outputs = out_row[:, None, :]
     weight_grad = lat_allreduce(grad_terms, "lat", 1)
     accumulated = jnp.zeros((channels, lat_rows + 2, window_len), jnp.float32)
     cycle_row = 0
-    grad_piece = response_grad[:, cycle_row].reshape(channels, kernels * lon_cols)
-    contrib = jnp.dot(grad_piece, matrix, preferred_element_type=jnp.float32)
     accumulated = accumulated.at[:, cycle_row : cycle_row + 3].add(
         contrib.reshape(channels, 3, window_len)
     )

time: 86.6 us -> 63.9 us (0.74)
  waiting for transfers between devices: 25.9 us -> 12 us
  starting transfers between devices: 28.3 us -> 24.1 us
  other arithmetic: 6.3 us -> 3.8 us
  local copies, waits for them, and re-layouts: 9.3 us -> 6.99 us
  Pallas kernels: 11.6 us -> 12.9 us
  matrix products: 2.93 us -> 1.86 us
    all_to_all x2 -> x0, waiting for transfers between devices: 10.8 us -> none  [the longest x1 10.8 us: lat_allreduce(): gathered = lax.all_to_all(x, axis, dim, dim, tiled=True)]
    all_to_all x2 -> x0, starting transfers between devices: 7.86 us -> none  [the longest x1 4.35 us: lat_allreduce(): lax.all_to_all(jnp.concatenate([mine] * count, axis=dim), axis, dim, dim,...]
    ppermute x2, waiting for transfers between devices: 7.86 us -> 0.01 us  [padded_2(): lax.ppermute(tail, axis, [(i, (i + 1) % count) for i in range(ends)])]
    ppermute x0 -> x6, waiting for transfers between devices: none -> 6.61 us  [the longest x3 6.22 us: lat_allreduce(): recv = lax.ppermute(mine, axis, [(i, i ^ d) for i in range(count)])]
    ppermute x0 -> x6, starting transfers between devices: none -> 4.82 us  [the longest x3 2.91 us: lat_allreduce(): recv = lax.ppermute(mine, axis, [(i, i ^ d) for i in range(count)])]
    dot_general x1 -> x0, local copies, waits for them, and re-layouts: 4.13 us -> none  [body(): contrib = jnp.dot(grad_piece, matrix, preferred_element_type=jnp.float32)]
    ppermute x2, waiting for transfers between devices: 1.83 us -> 0.01 us  [padded_2(): lax.ppermute(head, axis, [((i + 1) % count, i) for i in range(ends)])]
    ppermute x2, starting transfers between devices: 5.79 us -> 4.17 us  [padded_2(): lax.ppermute(tail, axis, [(i, (i + 1) % count) for i in range(ends)])]
  transfers between devices with their start and end apart: 11 -> 15, of which waited for: 5 -> 5; matrix products, arithmetic and copies ran while one was open for 17% -> 16% of each run, Pallas kernels for 14% -> 20%
where the time goes in v6:
time: 63.9 us; the launch traced here: 63.3 us
  starting transfers between devices  24.1 us (38%)
  Pallas kernels  12.9 us (20%)
  waiting for transfers between devices  12 us (19%)
  local copies, waits for them, and re-layouts  6.99 us (11%)
  other arithmetic  3.8 us (6%)
  matrix products  1.86 us (3%)
  between operations  1.62 us (3%)
    pallas_call x1, Pallas kernels, row_products(): pl.pallas_call(row_kernel, out_shape=(jax.ShapeDtypeStruct((weights.shape...  8.55 us
    ppermute x3, waiting for transfers between devices, lat_allreduce(): recv = lax.ppermute(mine, axis, [(i, i ^ d) for i in range(count)])  6.22 us
    ppermute x1, starting transfers between devices, body(): below = lax.ppermute(row, 'lat', [(i, i + 1) for i in range(count - 1)])  5.08 us
    ppermute x1, waiting for transfers between devices, body(): above = lax.ppermute(row, 'lat', [(i + 1, i) for i in range(count - 1)])  4.69 us
    ppermute x3, starting transfers between devices, body(): lax.ppermute(jnp.concatenate([fields[:, 0], part], axis=0), 'lon', [(p, (...  4.66 us
    pallas_call x1, Pallas kernels, toeplitz(): pl.pallas_call(toeplitz_kernel, out_shape=(jax.ShapeDtypeStruct((kernels,...  4.32 us
    ppermute x2, starting transfers between devices, padded_2(): lax.ppermute(tail, axis, [(i, (i + 1) % count) for i in range(ends)])  4.17 us
    ppermute x2, starting transfers between devices, padded_2(): lax.ppermute(head, axis, [((i + 1) % count, i) for i in range(ends)])  3.47 us
  transfers between devices with their start and end apart: 15, of which 5 were waited for; matrix products, arithmetic and copies ran while one was open for 16% of the time, Pallas kernels for 20%

profile of v6, /device:TPU:1, one launch (start us, length us, event | category | flops | bytes accessed | tf_op | source)
XLA Modules:
  0.0 63.3 jit_solution(2922901110351469448)
XLA Ops:
  0.7 0.8 %dynamic-slice_bitcast_fusion = (bf16[1,64,128]{2,1,0:T(8,128)(2,1)S(1)}, bf16[64,128]{1,0:T(8,128)(2,1)S(1)}, bf16[64,128]{1,0:T(8,128)(2,1)S(1)}, bf16[64,128]{1,0:T(8,128)(2,1)S(1)}) fusion(bf16[256,1,128]{2,0,1:T(8,128)(2,1)} %param.23, s32[]{:T(128)S(6)} %select_n.57, s32[]{:T(128)S(6)} %select_n.55, s32[]{:T(128)S(6)} %select_n.53, s32[]{:T(128)S(6)} %select_n.51), kind=kLoop, calls=%fused_computation.35 | loop fusion | bytes 131088 | tf_op jit(solution)/shard_map/stack | solution.py:179
  1.5 0.9 %pad_maximum_fusion.5 = (bf16[320,128]{1,0:T(8,128)(2,1)S(1)}, bf16[320,128]{1,0:T(8,128)(2,1)S(1)}, bf16[320,128]{1,0:T(8,128)(2,1)S(1)}) fusion(bf16[64,128]{1,0:T(8,128)(2,1)S(1)} %get-tuple-element.112, bf16[256,128]{1,0:T(8,128)(2,1)} %bitcast.56, bf16[64,128]{1,0:T(8,128)(2,1)S(1)} %get-tuple-element.111, bf16[64,128]{1,0:T(8,128)(2,1)S(1)} %get-tuple-element.110), kind=kLoop, calls=%fused_computation.21 | loop fusion | flops 409600 | bytes 360448 | tf_op jit(solution)/shard_map/concatenate | solution.py:173
  2.4 4.2 %collective-permute-start = (bf16[320,128]{1,0:T(8,128)(2,1)S(1)}, bf16[320,128]{1,0:T(8,128)(2,1)S(1)}, u32[]{:S(2)}, u32[]{:S(2)}) collective-permute-start(bf16[320,128]{1,0:T(8,128)(2,1)S(1)} %get-tuple-element.113), channel_id=1, source_target_pairs={{0,3},{1,0},{2,1},{3,2},{4,7},{5,4},{6,5},{7,6},{8,11},{9,8},{10,9... | collective-permute-start | bytes 245768 | tf_op jit(solution)/shard_map/ppermute | solution.py:172
  6.6 0.5 collective-permute-start.2
  7.0 1.7 %convolution_convert_fusion = bf16[128,9,256]{2,0,1:T(8,128)(2,1)S(1)} fusion(bf16[9,256,256]{2,1,0:T(8,128)(2,1)} %w_ref.1, bf16[256,1,128]{2,0,1:T(8,128)(2,1)} %param.23), kind=kOutput, calls=%fused_computation | convolution fusion | flops 151289856 | bytes 1835008 | tf_op jit(solution)/shard_map/koc,oij->cikj/dot_general | solution.py:161
  8.7 1.1 %copy.19.grad_ref = bf16[256,1152]{1,0:T(8,128)(2,1)} copy(bf16[256,1152]{0,1:T(8,128)(2,1)S(1)} %bitcast.53) | data formatting | bytes 1179648 | tf_op jit(solution)/shard_map/reshape;squeeze | solution.py:164
  10.5 0.2 fusion.3
  10.8 0.6 %reshape.252.tap_ref = f32[27,384]{1,0:T(8,128)} reshape(f32[9,3,384]{2,1,0:T(4,128)S(1)} %copy.17) | data formatting | bytes 82944 | tf_op jit(solution)/shard_map/reshape | solution.py:65
  11.4 4.3 %shard_map.100 = (bf16[9,128,1152]{2,1,0:T(8,128)(2,1)}, f32[256,1152]{1,0:T(8,128)}) custom-call(f32[27,384]{1,0:T(8,128)} %reshape.252.tap_ref, bf16[256,1152]{1,0:T(8,128)(2,1)} %copy.19.grad_ref), custom_call_target="tpu_custom_call" | custom-call | tf_op jit(solution)/shard_map/pallas_call | solution.py:66
  15.7 1.6 %copy.20 = f32[256,1152]{0,1:T(8,128)S(1)} copy(f32[256,1152]{1,0:T(8,128)} %get-tuple-element.93) | data formatting | bytes 2359296 | tf_op jit(solution)/shard_map/pallas_call | solution.py:66
  17.5 2.3 %collective-permute-start.5 = (f32[256,3,128]{0,2,1:T(8,128)S(1)}, f32[256,3,128]{0,2,1:T(8,128)S(1)}, u32[]{:S(2)}, u32[]{:S(2)}) collective-permute-start(f32[256,3,128]{0,2,1:T(8,128)S(1)} %get-tuple-element.100), channel_id=1, source_target_pairs={{0,1},{1,2},{2,3},{3,0},{4,5},{5,6},{6,7},{7,4},{8,9},{9,10},{10,1... | collective-permute-start | bytes 1179656 | tf_op jit(solution)/shard_map/ppermute | solution.py:19
  19.7 1.1 %collective-permute-start.6 = (f32[256,3,128]{0,2,1:T(8,128)S(1)}, f32[256,3,128]{0,2,1:T(8,128)S(1)}, u32[]{:S(2)}, u32[]{:S(2)}) collective-permute-start(f32[256,3,128]{0,2,1:T(8,128)S(1)} %get-tuple-element.101), channel_id=1, source_target_pairs={{1,0},{2,1},{3,2},{0,3},{5,4},{6,5},{7,6},{4,7},{9,8},{10,9},{11,1... | collective-permute-start | bytes 1179656 | tf_op jit(solution)/shard_map/ppermute | solution.py:21
  20.9 5.1 %collective-permute-start.3 = (bf16[256,512]{1,0:T(8,128)(2,1)S(1)}, bf16[256,512]{1,0:T(8,128)(2,1)S(1)}, u32[]{:S(2)}, u32[]{:S(2)}) collective-permute-start(bf16[256,512]{1,0:T(8,128)(2,1)S(1)} %get-tuple-element.108), channel_id=1, source_target_pairs={{0,4},{4,8},{8,12},{1,5},{5,9},{9,13},{2,6},{6,10},{10,14},{3,7},{... | collective-permute-start | bytes 786440 | tf_op jit(solution)/shard_map/ppermute | solution.py:182
  26.0 1.9 %collective-permute-start.4 = (bf16[256,512]{1,0:T(8,128)(2,1)S(1)}, bf16[256,512]{1,0:T(8,128)(2,1)S(1)}, u32[]{:S(2)}, u32[]{:S(2)}) collective-permute-start(bf16[256,512]{1,0:T(8,128)(2,1)S(1)} %get-tuple-element.108), channel_id=1, source_target_pairs={{4,0},{8,4},{12,8},{5,1},{9,5},{13,9},{6,2},{10,6},{14,10},{7,3},{... | collective-permute-start | bytes 786440 | tf_op jit(solution)/shard_map/ppermute | solution.py:183
  27.9 0.6 %pad_maximum_fusion.8.up_ref = bf16[4,64,128]{2,1,0:T(8,128)(2,1)} fusion(bf16[1,64,128]{2,1,0:T(8,128)(2,1)S(1)} %slice_bitcast_fusion, bf16[1,64,128]{2,1,0:T(8,128)(2,1)S(1)} %slice_bitcast_fusion.1, bf16[1,64,128]{2,1,0:T(8,128)(2,1)S(1)} %slice_bitcast_fusion.2, bf16[1,64,128]{2,1,0:T(8,128)(2,1)S(1)} %get-tuple-element.109), kind=kLoop, calls=%fused_computation.24 | loop fusion | flops 98304 | bytes 131072 | tf_op jit(solution)/shard_map/stack | solution.py:179
  28.6 0.7 %collective-permute-done.3 = bf16[256,512]{1,0:T(8,128)(2,1)S(1)} collective-permute-done((bf16[256,512]{1,0:T(8,128)(2,1)S(1)}, bf16[256,512]{1,0:T(8,128)(2,1)S(1)}, u32[]{:S(2)}, u32[]{:S(2)}) %collective-permute-start.3) | collective-permute-done | bytes 262176 | tf_op jit(solution)/shard_map/ppermute | solution.py:182
  29.3 4.7 %collective-permute-done.4 = bf16[256,512]{1,0:T(8,128)(2,1)S(1)} collective-permute-done((bf16[256,512]{1,0:T(8,128)(2,1)S(1)}, bf16[256,512]{1,0:T(8,128)(2,1)S(1)}, u32[]{:S(2)}, u32[]{:S(2)}) %collective-permute-start.4) | collective-permute-done | bytes 262176 | tf_op jit(solution)/shard_map/ppermute | solution.py:183
  34.0 1.1 %fusion.ext_ref = bf16[3,256,768]{2,1,0:T(8,128)(2,1)} fusion(bf16[1,256,512]{2,1,0:T(8,128)(2,1)S(1)} %bitcast.55, bf16[1,256,512]{2,1,0:T(8,128)(2,1)S(1)} %get-tuple-element.107, bf16[1,256,512]{2,1,0:T(8,128)(2,1)S(1)} %bitcast.54), kind=kLoop, calls=%fused_computation.2 | loop fusion | flops 10616832 | bytes 1966080 | tf_op jit(solution)/shard_map/concatenate | solution.py:185
  35.1 8.5 %shard_map.101 = (bf16[256,128]{1,0:T(8,128)(2,1)}, f32[9,64,256]{2,1,0:T(8,128)}) custom-call(bf16[3,256,768]{2,1,0:T(8,128)(2,1)} %fusion.ext_ref, bf16[1152,1152]{1,0:T(8,128)(2,1)} %bitcast.58, bf16[9,256,256]{2,1,0:T(8,128)(2,1)} %w_ref.1, bf16[4,64,128]{2,1,0:T(8,128)(2,1)} %pad_maximum_fusion.8.up_ref), custom_call_target="tpu_custom_call" | custom-call | flops 3019898880 | bytes 5734400 | tf_op jit(solution)/shard_map/pallas_call | solution.py:144
  43.6 1.1 %constant_dynamic-slice_fusion.2 = (f32[9,16,256]{2,1,0:T(8,128)S(1)}, f32[9,16,256]{2,1,0:T(8,128)S(1)}, f32[9,16,256]{2,1,0:T(8,128)S(1)}) fusion(f32[9,64,256]{2,1,0:T(8,128)} %get-tuple-element.94, s32[]{:T(128)S(6)} %select_n.59, s32[]{:T(128)S(6)} %select_n.61, s32[]{:T(128)S(6)} %select_n.60), kind=kLoop, calls=%fused_computation.45 | loop fusion | bytes 884748 | tf_op jit(solution)/shard_map/dynamic_slice | solution.py:85
  44.9 1.8 %collective-permute-start.9 = (f32[9,16,256]{2,1,0:T(8,128)S(1)}, f32[9,16,256]{2,1,0:T(8,128)S(1)}, u32[]{:S(2)}, u32[]{:S(2)}) collective-permute-start(f32[9,16,256]{2,1,0:T(8,128)S(1)} %get-tuple-element.102), channel_id=1, source_target_pairs={{0,4},{4,0},{8,12},{12,8},{1,5},{5,1},{9,13},{13,9},{2,6},{6,2},{1... | collective-permute-start | bytes 442376 | tf_op jit(solution)/shard_map/ppermute | solution.py:86
  46.7 1.9 %collective-permute-start.7 = (f32[256,1,128]{0,2,1:T(8,128)S(1)}, f32[256,1,128]{0,2,1:T(8,128)S(1)}, u32[]{:S(2)}, u32[]{:S(2)}) collective-permute-start(f32[256,1,128]{0,2,1:T(8,128)S(1)} %get-tuple-element.105), channel_id=1, source_target_pairs={{0,4},{4,8},{8,12},{1,5},{5,9},{9,13},{2,6},{6,10},{10,14},{3,7},{... | collective-permute-start | bytes 393224 | tf_op jit(solution)/shard_map/ppermute | solution.py:19
  48.7 2.4 %collective-permute-start.8 = (f32[256,1,128]{0,2,1:T(8,128)S(1)}, f32[256,1,128]{0,2,1:T(8,128)S(1)}, u32[]{:S(2)}, u32[]{:S(2)}) collective-permute-start(f32[256,1,128]{0,2,1:T(8,128)S(1)} %get-tuple-element.106), channel_id=1, source_target_pairs={{4,0},{8,4},{12,8},{5,1},{9,5},{13,9},{6,2},{10,6},{14,10},{7,3},{... | collective-permute-start | bytes 393224 | tf_op jit(solution)/shard_map/ppermute | solution.py:21
  51.1 0.4 collective-permute-done.11
  51.5 1.0 %constant_dynamic-update-slice_fusion.3 = (f32[9,64,256]{2,1,0:T(8,128)S(1)}, f32[9,16,256]{2,1,0:T(8,128)S(1)}) fusion(f32[9,64,256]{2,1,0:T(8,128)S(1)} %broadcast_in_dim.25, s32[]{:T(128)S(6)} %select_n.58, f32[9,16,256]{2,1,0:T(8,128)S(1)} %collective-permute-done.10, f32[9,16,256]{2,1,0:T(8,128)S(1)} %collective-permute-done.11, ...), kind=kLoop, calls=%fused_computation.42 | loop fusion | flops 110592 | bytes 884740 | tf_op jit(solution)/shard_map/dynamic_update_slice | solution.py:91
  52.5 1.2 %collective-permute-start.12 = (f32[9,16,256]{2,1,0:T(8,128)S(1)}, f32[9,16,256]{2,1,0:T(8,128)S(1)}, u32[]{:S(2)}, u32[]{:S(2)}) collective-permute-start(f32[9,16,256]{2,1,0:T(8,128)S(1)} %get-tuple-element.99), channel_id=1, source_target_pairs={{0,4},{4,0},{8,12},{12,8},{1,5},{5,1},{9,13},{13,9},{2,6},{6,2},{1... | collective-permute-start | bytes 442376 | tf_op jit(solution)/shard_map/ppermute | solution.py:93
  53.7 1.5 %collective-permute-start.13 = (f32[9,16,256]{2,1,0:T(8,128)S(1)}, f32[9,16,256]{2,1,0:T(8,128)S(1)}, u32[]{:S(2)}, u32[]{:S(2)}) collective-permute-start(f32[9,16,256]{2,1,0:T(8,128)S(1)} %get-tuple-element.99), channel_id=1, source_target_pairs={{0,8},{4,12},{8,0},{12,4},{1,9},{5,13},{9,1},{13,5},{2,10},{6,14},... | collective-permute-start | bytes 442376 | tf_op jit(solution)/shard_map/ppermute | solution.py:93
  55.2 0.2 collective-permute-start.14
  55.5 0.7 %copy.21 = bf16[256,1,128]{2,0,1:T(8,128)(2,1)} copy(bf16[256,1,128]{0,2,1:T(8,128)(2,1)S(1)} %fusion.6) | data formatting | bytes 131072
  56.2 2.9 %collective-permute-done.13 = f32[9,16,256]{2,1,0:T(8,128)S(1)} collective-permute-done((f32[9,16,256]{2,1,0:T(8,128)S(1)}, f32[9,16,256]{2,1,0:T(8,128)S(1)}, u32[]{:S(2)}, u32[]{:S(2)}) %collective-permute-start.13) | collective-permute-done | bytes 147488 | tf_op jit(solution)/shard_map/ppermute | solution.py:93
  59.1 3.3 %collective-permute-done.14 = f32[9,16,256]{2,1,0:T(8,128)S(1)} collective-permute-done((f32[9,16,256]{2,1,0:T(8,128)S(1)}, f32[9,16,256]{2,1,0:T(8,128)S(1)}, u32[]{:S(2)}, u32[]{:S(2)}) %collective-permute-start.14) | collective-permute-done | bytes 147488 | tf_op jit(solution)/shard_map/ppermute | solution.py:93
  62.5 0.8 %copy-done.1 = f32[9,64,256]{2,1,0:T(8,128)} copy-done((f32[9,64,256]{2,1,0:T(8,128)}, f32[9,64,256]{2,1,0:T(8,128)S(1)}, u32[]{:S(2)}) %copy-start.1) | copy-done | bytes 589848
  (40 shorter events, 0.7 us)
Async XLA Ops:
  0.6 9.9 %copy-start = (bf16[1,9,3,2,64]{4,3,2,1,0:T(2,128)(2,1)S(1)}, bf16[1,9,3,2,64]{4,3,2,1,0:T(2,128)(2,1)}, u32[]{:S(2)}) copy-start(bf16[1,9,3,2,64]{4,3,2,1,0:T(2,128)(2,1)} %param.25) | copy-start | bytes 20740
  2.4 18.4 %collective-permute-start = (bf16[320,128]{1,0:T(8,128)(2,1)S(1)}, bf16[320,128]{1,0:T(8,128)(2,1)S(1)}, u32[]{:S(2)}, u32[]{:S(2)}) collective-permute-start(bf16[320,128]{1,0:T(8,128)(2,1)S(1)} %get-tuple-element.113), channel_id=1, source_target_pairs={{0,3},{1,0},{2,1},{3,2},{4,7},{5,4},{6,5},{7,6},{8,11},{9,8},{10,9... | collective-permute-start | bytes 245768 | tf_op jit(solution)/shard_map/ppermute | solution.py:172
  6.6 14.2 %collective-permute-start.1 = (bf16[320,128]{1,0:T(8,128)(2,1)S(1)}, bf16[320,128]{1,0:T(8,128)(2,1)S(1)}, u32[]{:S(2)}, u32[]{:S(2)}) collective-permute-start(bf16[320,128]{1,0:T(8,128)(2,1)S(1)} %get-tuple-element.114), channel_id=1, source_target_pairs={{0,2},{1,3},{2,0},{3,1},{4,6},{5,7},{6,4},{7,5},{8,10},{9,11},{10,... | collective-permute-start | bytes 245768 | tf_op jit(solution)/shard_map/ppermute | solution.py:172
  6.6 3.2 %copy-start.3 = (s32[1,2]{1,0:T(1,128)S(1)}, s32[1,2]{1,0:T(1,128)}, u32[]{:S(2)}) copy-start(s32[1,2]{1,0:T(1,128)} %param.27) | copy-start | bytes 28
  6.6 14.2 %collective-permute-start.2 = (bf16[320,128]{1,0:T(8,128)(2,1)S(1)}, bf16[320,128]{1,0:T(8,128)(2,1)S(1)}, u32[]{:S(2)}, u32[]{:S(2)}) collective-permute-start(bf16[320,128]{1,0:T(8,128)(2,1)S(1)} %get-tuple-element.115), channel_id=1, source_target_pairs={{0,1},{1,2},{2,3},{3,0},{4,5},{5,6},{6,7},{7,4},{8,9},{9,10},{10,1... | collective-permute-start | bytes 245768 | tf_op jit(solution)/shard_map/ppermute | solution.py:172
  17.4 3.5 %copy-start.2 = (bf16[256,1,128]{2,0,1:T(8,128)(2,1)S(1)}, bf16[256,1,128]{2,0,1:T(8,128)(2,1)}, u32[]{:S(2)}) copy-start(bf16[256,1,128]{2,0,1:T(8,128)(2,1)} %param.22) | copy-start | bytes 196612
  17.5 29.2 %collective-permute-start.5 = (f32[256,3,128]{0,2,1:T(8,128)S(1)}, f32[256,3,128]{0,2,1:T(8,128)S(1)}, u32[]{:S(2)}, u32[]{:S(2)}) collective-permute-start(f32[256,3,128]{0,2,1:T(8,128)S(1)} %get-tuple-element.100), channel_id=1, source_target_pairs={{0,1},{1,2},{2,3},{3,0},{4,5},{5,6},{6,7},{7,4},{8,9},{9,10},{10,1... | collective-permute-start | bytes 1179656 | tf_op jit(solution)/shard_map/ppermute | solution.py:19
  19.7 26.9 %collective-permute-start.6 = (f32[256,3,128]{0,2,1:T(8,128)S(1)}, f32[256,3,128]{0,2,1:T(8,128)S(1)}, u32[]{:S(2)}, u32[]{:S(2)}) collective-permute-start(f32[256,3,128]{0,2,1:T(8,128)S(1)} %get-tuple-element.101), channel_id=1, source_target_pairs={{1,0},{2,1},{3,2},{0,3},{5,4},{6,5},{7,6},{4,7},{9,8},{10,9},{11,1... | collective-permute-start | bytes 1179656 | tf_op jit(solution)/shard_map/ppermute | solution.py:21
  20.9 8.4 %collective-permute-start.3 = (bf16[256,512]{1,0:T(8,128)(2,1)S(1)}, bf16[256,512]{1,0:T(8,128)(2,1)S(1)}, u32[]{:S(2)}, u32[]{:S(2)}) collective-permute-start(bf16[256,512]{1,0:T(8,128)(2,1)S(1)} %get-tuple-element.108), channel_id=1, source_target_pairs={{0,4},{4,8},{8,12},{1,5},{5,9},{9,13},{2,6},{6,10},{10,14},{3,7},{... | collective-permute-start | bytes 786440 | tf_op jit(solution)/shard_map/ppermute | solution.py:182
  26.0 8.0 %collective-permute-start.4 = (bf16[256,512]{1,0:T(8,128)(2,1)S(1)}, bf16[256,512]{1,0:T(8,128)(2,1)S(1)}, u32[]{:S(2)}, u32[]{:S(2)}) collective-permute-start(bf16[256,512]{1,0:T(8,128)(2,1)S(1)} %get-tuple-element.108), channel_id=1, source_target_pairs={{4,0},{8,4},{12,8},{5,1},{9,5},{13,9},{6,2},{10,6},{14,10},{7,3},{... | collective-permute-start | bytes 786440 | tf_op jit(solution)/shard_map/ppermute | solution.py:183
  44.7 6.4 %collective-permute-start.10 = (f32[9,16,256]{2,1,0:T(8,128)S(1)}, f32[9,16,256]{2,1,0:T(8,128)S(1)}, u32[]{:S(2)}, u32[]{:S(2)}) collective-permute-start(f32[9,16,256]{2,1,0:T(8,128)S(1)} %get-tuple-element.104), channel_id=1, source_target_pairs={{0,8},{4,12},{8,0},{12,4},{1,9},{5,13},{9,1},{13,5},{2,10},{6,14},... | collective-permute-start | bytes 442376 | tf_op jit(solution)/shard_map/ppermute | solution.py:86
  44.8 6.7 %collective-permute-start.11 = (f32[9,16,256]{2,1,0:T(8,128)S(1)}, f32[9,16,256]{2,1,0:T(8,128)S(1)}, u32[]{:S(2)}, u32[]{:S(2)}) collective-permute-start(f32[9,16,256]{2,1,0:T(8,128)S(1)} %get-tuple-element.103), channel_id=1, source_target_pairs={{0,12},{4,8},{8,4},{12,0},{1,13},{5,9},{9,5},{13,1},{2,14},{6,10},... | collective-permute-start | bytes 442376 | tf_op jit(solution)/shard_map/ppermute | solution.py:86
  44.9 6.6 %collective-permute-start.9 = (f32[9,16,256]{2,1,0:T(8,128)S(1)}, f32[9,16,256]{2,1,0:T(8,128)S(1)}, u32[]{:S(2)}, u32[]{:S(2)}) collective-permute-start(f32[9,16,256]{2,1,0:T(8,128)S(1)} %get-tuple-element.102), channel_id=1, source_target_pairs={{0,4},{4,0},{8,12},{12,8},{1,5},{5,1},{9,13},{13,9},{2,6},{6,2},{1... | collective-permute-start | bytes 442376 | tf_op jit(solution)/shard_map/ppermute | solution.py:86
  46.7 8.7 %collective-permute-start.7 = (f32[256,1,128]{0,2,1:T(8,128)S(1)}, f32[256,1,128]{0,2,1:T(8,128)S(1)}, u32[]{:S(2)}, u32[]{:S(2)}) collective-permute-start(f32[256,1,128]{0,2,1:T(8,128)S(1)} %get-tuple-element.105), channel_id=1, source_target_pairs={{0,4},{4,8},{8,12},{1,5},{5,9},{9,13},{2,6},{6,10},{10,14},{3,7},{... | collective-permute-start | bytes 393224 | tf_op jit(solution)/shard_map/ppermute | solution.py:19
  48.7 6.8 %collective-permute-start.8 = (f32[256,1,128]{0,2,1:T(8,128)S(1)}, f32[256,1,128]{0,2,1:T(8,128)S(1)}, u32[]{:S(2)}, u32[]{:S(2)}) collective-permute-start(f32[256,1,128]{0,2,1:T(8,128)S(1)} %get-tuple-element.106), channel_id=1, source_target_pairs={{4,0},{8,4},{12,8},{5,1},{9,5},{13,9},{6,2},{10,6},{14,10},{7,3},{... | collective-permute-start | bytes 393224 | tf_op jit(solution)/shard_map/ppermute | solution.py:21
  52.5 3.7 %collective-permute-start.12 = (f32[9,16,256]{2,1,0:T(8,128)S(1)}, f32[9,16,256]{2,1,0:T(8,128)S(1)}, u32[]{:S(2)}, u32[]{:S(2)}) collective-permute-start(f32[9,16,256]{2,1,0:T(8,128)S(1)} %get-tuple-element.99), channel_id=1, source_target_pairs={{0,4},{4,0},{8,12},{12,8},{1,5},{5,1},{9,13},{13,9},{2,6},{6,2},{1... | collective-permute-start | bytes 442376 | tf_op jit(solution)/shard_map/ppermute | solution.py:93
  53.7 5.4 %collective-permute-start.13 = (f32[9,16,256]{2,1,0:T(8,128)S(1)}, f32[9,16,256]{2,1,0:T(8,128)S(1)}, u32[]{:S(2)}, u32[]{:S(2)}) collective-permute-start(f32[9,16,256]{2,1,0:T(8,128)S(1)} %get-tuple-element.99), channel_id=1, source_target_pairs={{0,8},{4,12},{8,0},{12,4},{1,9},{5,13},{9,1},{13,5},{2,10},{6,14},... | collective-permute-start | bytes 442376 | tf_op jit(solution)/shard_map/ppermute | solution.py:93
  55.2 7.3 %collective-permute-start.14 = (f32[9,16,256]{2,1,0:T(8,128)S(1)}, f32[9,16,256]{2,1,0:T(8,128)S(1)}, u32[]{:S(2)}, u32[]{:S(2)}) collective-permute-start(f32[9,16,256]{2,1,0:T(8,128)S(1)} %get-tuple-element.99), channel_id=1, source_target_pairs={{0,12},{4,8},{8,4},{12,0},{1,13},{5,9},{9,5},{13,1},{2,14},{6,10},... | collective-permute-start | bytes 442376 | tf_op jit(solution)/shard_map/ppermute | solution.py:93
  62.5 0.8 %copy-start.1 = (f32[9,64,256]{2,1,0:T(8,128)}, f32[9,64,256]{2,1,0:T(8,128)S(1)}, u32[]{:S(2)}) copy-start(f32[9,64,256]{2,1,0:T(8,128)S(1)} %constant_dynamic-update-slice_fusion) | copy-start | bytes 1769476

commit v7 on v6

--- a/solution.py
+++ b/solution.py
@@ -96,7 +96,7 @@
 
 
 def row_kernel(ext_ref, mt_ref, w_ref, up_ref, out_ref, gt_ref):
-    stencil_rows, channels, _ = ext_ref.shape
+    stencil_rows, _, channels = ext_ref.shape
     n_blocks, o_block, lon_cols = up_ref.shape
     kernels = w_ref.shape[0]
     window_len = mt_ref.shape[1] // stencil_rows
@@ -105,41 +105,39 @@
     for d in range(n_blocks):
         acc = None
         for r in range(stencil_rows):
-            win = ext_ref[r, :, pl.ds(d * lon_cols, window_len)]
-            part = lax.dot_general(
-                win,
+            part = jnp.dot(
                 mt_ref[:, pl.ds(r * window_len, window_len)],
-                contract_last,
+                ext_ref[r, pl.ds(d * lon_cols, window_len), :],
                 preferred_element_type=jnp.float32,
             )
             acc = part if acc is None else acc + part
-        resp = acc.astype(jnp.bfloat16)
+        resp_t = acc.astype(jnp.bfloat16)
         up_d = up_ref[d]
         for k in range(kernels):
-            resp_k = resp[:, k * lon_cols : (k + 1) * lon_cols]
-            gt_ref[k] += lax.dot_general(
-                up_d, resp_k, contract_last, preferred_element_type=jnp.float32
+            gt_ref[k] += jnp.dot(
+                up_d, resp_t[k * lon_cols : (k + 1) * lon_cols], preferred_element_type=jnp.float32
             )
         if d == 0:
             total = None
             for k in range(kernels):
-                term = jnp.dot(
+                term = lax.dot_general(
                     w_ref[k],
-                    resp[:, k * lon_cols : (k + 1) * lon_cols],
+                    resp_t[k * lon_cols : (k + 1) * lon_cols],
+                    contract_last,
                     preferred_element_type=jnp.float32,
                 )
                 total = term if total is None else total + term
             out_ref[...] = total.astype(out_ref.dtype)
 
 
-def row_products(ext, matrix, weights, up_rel):
-    stencil_rows, channels, _ = ext.shape
+def row_products(ext_t, matrix, weights, up_rel):
+    stencil_rows, _, channels = ext_t.shape
     n_blocks, o_block, lon_cols = up_rel.shape
     kernels = weights.shape[0]
     flops = 2 * n_blocks * channels * matrix.shape[0] * matrix.shape[1]
     flops += 2 * n_blocks * kernels * o_block * lon_cols * channels
     flops += 2 * kernels * weights.shape[1] * channels * lon_cols
-    nbytes = 2 * (ext.size + matrix.size + weights.size + up_rel.size)
+    nbytes = 2 * (ext_t.size + matrix.size + weights.size + up_rel.size)
     nbytes += 2 * weights.shape[1] * lon_cols + 4 * kernels * o_block * channels
     return pl.pallas_call(
         row_kernel,
@@ -148,7 +146,7 @@
             jax.ShapeDtypeStruct((kernels, o_block, channels), jnp.float32),
         ),
         cost_estimate=pl.CostEstimate(flops=flops, transcendentals=0, bytes_accessed=nbytes),
-    )(ext, matrix, weights, up_rel)
+    )(ext_t, matrix, weights, up_rel)
 
 
 def body(fields, upstream, weights, filter_taps, cycle_counts, cycle_blocks):
@@ -162,7 +160,6 @@
         "koc,oij->cikj", weights, upstream, preferred_element_type=jnp.float32
     ).astype(jnp.bfloat16)
     grad_piece = response_grad[:, 0].reshape(channels, kernels * lon_cols)
-    matrix, contrib = toeplitz(tap_table[0], lon_cols, grad_piece)
     o_block = upstream.shape[0] // n_lon
     up_row = upstream[:, 0]
     blocks = [fields[:, 0]]
@@ -178,12 +175,14 @@
         up_parts.append(both[channels:])
     up_rel = jnp.stack(up_parts, axis=0)
     row = jnp.concatenate(blocks, axis=1)
+    row, tap_row, grad_piece = lax.optimization_barrier((row, tap_table[0], grad_piece))
     count = lax.axis_size("lat")
     below = lax.ppermute(row, "lat", [(i, i + 1) for i in range(count - 1)])
     above = lax.ppermute(row, "lat", [(i + 1, i) for i in range(count - 1)])
-    rows = jnp.stack([below, row, above], axis=0)
-    ext = jnp.concatenate([rows[:, :, rows.shape[2] - HALO :], rows, rows[:, :, :HALO]], axis=2)
-    out_row, grad_terms = row_products(ext, matrix, weights, up_rel)
+    matrix, contrib = toeplitz(tap_row, lon_cols, grad_piece)
+    rows = jnp.stack([below, row, above], axis=0).transpose(0, 2, 1)
+    ext_t = jnp.concatenate([rows[:, rows.shape[1] - HALO :], rows, rows[:, :HALO]], axis=1)
+    out_row, grad_terms = row_products(ext_t, matrix, weights, up_rel)
     outputs = out_row[:, None, :]
     weight_grad = lat_allreduce(grad_terms, "lat", 1)
     accumulated = jnp.zeros((channels, lat_rows + 2, window_len), jnp.float32)

time: 63.9 us -> 65 us (1.017)
  local copies, waits for them, and re-layouts: 6.99 us -> 9.26 us
  waiting for transfers between devices: 12 us -> 10.3 us
  Pallas kernels: 12.9 us -> 13.9 us
    ppermute x1, waiting for transfers between devices: 4.69 us -> 0.01 us  [body(): above = lax.ppermute(row, 'lat', [(i + 1, i) for i in range(count - 1)])]
    ppermute x2, waiting for transfers between devices: 0.01 us -> 2.73 us  [padded_2(): lax.ppermute(tail, axis, [(i, (i + 1) % count) for i in range(ends)])]
    ppermute x1, starting transfers between devices: 5.08 us -> 3.01 us  [body(): below = lax.ppermute(row, 'lat', [(i, i + 1) for i in range(count - 1)])]
    ppermute x2, starting transfers between devices: 3.47 us -> 5.3 us  [padded_2(): lax.ppermute(head, axis, [((i + 1) % count, i) for i in range(ends)])]
    ppermute x3, waiting for transfers between devices: 0.01 us -> 1.73 us  [body(): lax.ppermute(jnp.concatenate([fields[:, 0], part], axis=0), 'lon', [(p, (...]
    concatenate x0 -> x1, local copies, waits for them, and re-layouts: none -> 1.45 us  [body(): jnp.concatenate([rows[:, rows.shape[1] - HALO:], rows, rows[:, :HALO]], a...]
    another operation x1 -> x0, local copies, waits for them, and re-layouts: 1.06 us -> none  [body(): grad_piece = response_grad[:, 0].reshape(channels, kernels * lon_cols)]
    optimization_barrier x0 -> x1, local copies, waits for them, and re-layouts: none -> 1.05 us  [body(): lax.optimization_barrier((row, tap_table[0], grad_piece))]
  transfers between devices with their start and end apart: 15 -> 15, of which waited for: 5 -> 4; matrix products, arithmetic and copies ran while one was open for 16% -> 19% of each run, Pallas kernels for 20% -> 22%
where the time goes in v7:
time: 65 us; the launch traced here: 64.5 us
  starting transfers between devices  24 us (37%)
  Pallas kernels  13.9 us (21%)
  waiting for transfers between devices  10.3 us (16%)
  local copies, waits for them, and re-layouts  9.26 us (14%)
  other arithmetic  3.55 us (5%)
  matrix products  1.89 us (3%)
  between operations  1.62 us (2%)
    pallas_call x1, Pallas kernels, row_products(): pl.pallas_call(row_kernel, out_shape=(jax.ShapeDtypeStruct((weights.shape...  9.56 us
    ppermute x3, waiting for transfers between devices, lat_allreduce(): recv = lax.ppermute(mine, axis, [(i, i ^ d) for i in range(count)])  5.86 us
    ppermute x3, starting transfers between devices, body(): lax.ppermute(jnp.concatenate([fields[:, 0], part], axis=0), 'lon', [(p, (...  5.56 us
    ppermute x2, starting transfers between devices, padded_2(): lax.ppermute(head, axis, [((i + 1) % count, i) for i in range(ends)])  5.3 us
    pallas_call x1, Pallas kernels, toeplitz(): pl.pallas_call(toeplitz_kernel, out_shape=(jax.ShapeDtypeStruct((kernels,...  4.33 us
    ppermute x2, starting transfers between devices, padded_2(): lax.ppermute(tail, axis, [(i, (i + 1) % count) for i in range(ends)])  3.3 us
    ppermute x1, starting transfers between devices, body(): below = lax.ppermute(row, 'lat', [(i, i + 1) for i in range(count - 1)])  3.01 us
    ppermute x2, waiting for transfers between devices, padded_2(): lax.ppermute(tail, axis, [(i, (i + 1) % count) for i in range(ends)])  2.73 us
  transfers between devices with their start and end apart: 15, of which 4 were waited for; matrix products, arithmetic and copies ran while one was open for 19% of the time, Pallas kernels for 22%

profile of v7, /device:TPU:1, one launch (start us, length us, event | category | flops | bytes accessed | tf_op | source)
XLA Modules:
  0.0 64.5 jit_solution(14241525417784513798)
XLA Ops:
  0.7 0.8 %dynamic-slice_bitcast_fusion = (bf16[1,64,128]{2,1,0:T(8,128)(2,1)S(1)}, bf16[64,128]{1,0:T(8,128)(2,1)S(1)}, bf16[64,128]{1,0:T(8,128)(2,1)S(1)}, bf16[64,128]{1,0:T(8,128)(2,1)S(1)}) fusion(bf16[256,1,128]{2,0,1:T(8,128)(2,1)} %param.23, s32[]{:T(128)S(6)} %select_n.57, s32[]{:T(128)S(6)} %select_n.55, s32[]{:T(128)S(6)} %select_n.53, s32[]{:T(128)S(6)} %select_n.51), kind=kLoop, calls=%fused_computation.31 | loop fusion | bytes 131088 | tf_op jit(solution)/shard_map/stack | solution.py:176
  1.5 0.9 %pad_maximum_fusion.2 = (bf16[320,128]{1,0:T(8,128)(2,1)S(1)}, bf16[320,128]{1,0:T(8,128)(2,1)S(1)}, bf16[320,128]{1,0:T(8,128)(2,1)S(1)}) fusion(bf16[64,128]{1,0:T(8,128)(2,1)S(1)} %get-tuple-element.118, bf16[256,128]{1,0:T(8,128)(2,1)} %bitcast.58, bf16[64,128]{1,0:T(8,128)(2,1)S(1)} %get-tuple-element.117, bf16[64,128]{1,0:T(8,128)(2,1)S(1)} %get-tuple-element.116), kind=kLoop, calls=%fused_computation.17 | loop fusion | flops 409600 | bytes 360448 | tf_op jit(solution)/shard_map/concatenate | solution.py:170
  2.4 2.2 %collective-permute-start.2 = (bf16[320,128]{1,0:T(8,128)(2,1)S(1)}, bf16[320,128]{1,0:T(8,128)(2,1)S(1)}, u32[]{:S(2)}, u32[]{:S(2)}) collective-permute-start(bf16[320,128]{1,0:T(8,128)(2,1)S(1)} %get-tuple-element.121), channel_id=1, source_target_pairs={{0,1},{1,2},{2,3},{3,0},{4,5},{5,6},{6,7},{7,4},{8,9},{9,10},{10,1... | collective-permute-start | bytes 245768 | tf_op jit(solution)/shard_map/ppermute | solution.py:169
  4.5 2.3 %collective-permute-start.1 = (bf16[320,128]{1,0:T(8,128)(2,1)S(1)}, bf16[320,128]{1,0:T(8,128)(2,1)S(1)}, u32[]{:S(2)}, u32[]{:S(2)}) collective-permute-start(bf16[320,128]{1,0:T(8,128)(2,1)S(1)} %get-tuple-element.120), channel_id=1, source_target_pairs={{0,2},{1,3},{2,0},{3,1},{4,6},{5,7},{6,4},{7,5},{8,10},{9,11},{10,... | collective-permute-start | bytes 245768 | tf_op jit(solution)/shard_map/ppermute | solution.py:169
  6.9 1.1 %collective-permute-start = (bf16[320,128]{1,0:T(8,128)(2,1)S(1)}, bf16[320,128]{1,0:T(8,128)(2,1)S(1)}, u32[]{:S(2)}, u32[]{:S(2)}) collective-permute-start(bf16[320,128]{1,0:T(8,128)(2,1)S(1)} %get-tuple-element.119), channel_id=1, source_target_pairs={{0,3},{1,0},{2,1},{3,2},{4,7},{5,4},{6,5},{7,6},{8,11},{9,8},{10,9... | collective-permute-start | bytes 245768 | tf_op jit(solution)/shard_map/ppermute | solution.py:169
  7.9 0.7 %add_bitcast_fusion = s32[2]{0:T(128)S(1)} fusion(s32[1,2]{1,0:T(1,128)} %param.27), kind=kLoop, calls=%fused_computation.44 | loop fusion | flops 4 | bytes 16 | tf_op jit(solution)/shard_map/add | solution.py:32
  9.3 1.7 %convolution_convert_fusion = bf16[128,9,256]{2,0,1:T(8,128)(2,1)S(1)} fusion(bf16[9,256,256]{2,1,0:T(8,128)(2,1)} %w_ref.1, bf16[256,1,128]{2,0,1:T(8,128)(2,1)} %param.23), kind=kOutput, calls=%fused_computation | convolution fusion | flops 151289856 | bytes 1835008 | tf_op jit(solution)/shard_map/koc,oij->cikj/dot_general | solution.py:159
  11.0 0.2 fusion.1
  11.3 1.7 %collective-permute-done.1 = bf16[320,128]{1,0:T(8,128)(2,1)S(1)} collective-permute-done((bf16[320,128]{1,0:T(8,128)(2,1)S(1)}, bf16[320,128]{1,0:T(8,128)(2,1)S(1)}, u32[]{:S(2)}, u32[]{:S(2)}) %collective-permute-start.1) | collective-permute-done | bytes 81952 | tf_op jit(solution)/shard_map/ppermute | solution.py:169
  13.1 2.7 %collective-permute-start.4 = (bf16[256,512]{1,0:T(8,128)(2,1)S(1)}, bf16[256,512]{1,0:T(8,128)(2,1)S(1)}, u32[]{:S(2)}, u32[]{:S(2)}) collective-permute-start(bf16[256,512]{1,0:T(8,128)(2,1)S(1)} %pad_maximum_fusion.1), channel_id=1, source_target_pairs={{4,0},{8,4},{12,8},{5,1},{9,5},{13,9},{6,2},{10,6},{14,10},{7,3},{... | collective-permute-start | bytes 786440 | tf_op jit(solution)/shard_map/ppermute | solution.py:181
  15.8 3.0 %collective-permute-start.3 = (bf16[256,512]{1,0:T(8,128)(2,1)S(1)}, bf16[256,512]{1,0:T(8,128)(2,1)S(1)}, u32[]{:S(2)}, u32[]{:S(2)}) collective-permute-start(bf16[256,512]{1,0:T(8,128)(2,1)S(1)} %pad_maximum_fusion.1), channel_id=1, source_target_pairs={{0,4},{4,8},{8,12},{1,5},{5,9},{9,13},{2,6},{6,10},{10,14},{3,7},{... | collective-permute-start | bytes 786440 | tf_op jit(solution)/shard_map/ppermute | solution.py:180
  18.8 0.6 reshape.252.tap_ref
  19.5 1.1 %copy.20.grad_ref = bf16[256,1152]{1,0:T(8,128)(2,1)} copy(bf16[256,1152]{0,1:T(8,128)(2,1)S(1)} %bitcast.54) | data formatting | bytes 1179648 | tf_op jit(solution)/shard_map/optimization_barrier | solution.py:178
  20.5 4.3 %shard_map.100 = (bf16[9,128,1152]{2,1,0:T(8,128)(2,1)}, f32[256,1152]{1,0:T(8,128)}) custom-call(f32[27,384]{1,0:T(8,128)} %reshape.252.tap_ref, bf16[256,1152]{1,0:T(8,128)(2,1)} %copy.20.grad_ref), custom_call_target="tpu_custom_call" | custom-call | tf_op jit(solution)/shard_map/pallas_call | solution.py:66
  24.9 1.6 %copy.22 = f32[256,1152]{0,1:T(8,128)S(1)} copy(f32[256,1152]{1,0:T(8,128)} %get-tuple-element.99) | data formatting | bytes 2359296 | tf_op jit(solution)/shard_map/pallas_call | solution.py:66
  26.5 0.8 %fusion.17 = (f32[256,3,128]{0,2,1:T(8,128)S(1)}, f32[256,3,128]{0,2,1:T(8,128)}) fusion(f32[256,3,384]{0,2,1:T(8,128)S(1)} %bitcast.52), kind=kLoop, calls=%fused_computation.47 | loop fusion | bytes 1572864 | tf_op jit(solution)/shard_map/slice | solution.py:194
  27.3 3.0 %collective-permute-start.6 = (f32[256,3,128]{0,2,1:T(8,128)}, f32[256,3,128]{0,2,1:T(8,128)S(1)}, u32[]{:S(2)}, u32[]{:S(2)}) collective-permute-start(f32[256,3,128]{0,2,1:T(8,128)} %get-tuple-element.107), channel_id=1, source_target_pairs={{1,0},{2,1},{3,2},{0,3},{5,4},{6,5},{7,6},{4,7},{9,8},{10,9},{11,1... | collective-permute-start | bytes 1179656 | tf_op jit(solution)/shard_map/ppermute | solution.py:21
  30.4 0.6 pad_maximum_fusion.5.up_ref
  31.3 1.4 %copy.21.ext_ref = bf16[3,768,256]{2,1,0:T(8,128)(2,1)} copy(bf16[3,768,256]{1,2,0:T(8,128)(2,1)S(1)} %pad_maximum_fusion) | data formatting | bytes 2359296 | tf_op jit(solution)/shard_map/concatenate | solution.py:184
  32.8 9.6 %shard_map.101 = (bf16[256,128]{1,0:T(8,128)(2,1)}, f32[9,64,256]{2,1,0:T(8,128)}) custom-call(bf16[3,768,256]{2,1,0:T(8,128)(2,1)} %copy.21.ext_ref, bf16[1152,1152]{1,0:T(8,128)(2,1)} %bitcast.60, bf16[9,256,256]{2,1,0:T(8,128)(2,1)} %w_ref.1, bf16[4,64,128]{2,1,0:T(8,128)(2,1)} %pad_maximum_fusion.5.up_ref), custom_call_target="tpu_custom_call" | custom-call | flops 3019898880 | bytes 5734400 | tf_op jit(solution)/shard_map/pallas_call | solution.py:142
  42.3 1.1 %constant_dynamic-slice_fusion.2 = (f32[9,16,256]{2,1,0:T(8,128)S(1)}, f32[9,16,256]{2,1,0:T(8,128)S(1)}, f32[9,16,256]{2,1,0:T(8,128)S(1)}) fusion(f32[9,64,256]{2,1,0:T(8,128)} %get-tuple-element.100, s32[]{:T(128)S(6)} %select_n.59, s32[]{:T(128)S(6)} %select_n.61, s32[]{:T(128)S(6)} %select_n.60), kind=kLoop, calls=%fused_computation.41 | loop fusion | bytes 884748 | tf_op jit(solution)/shard_map/dynamic_slice | solution.py:85
  43.5 1.3 %collective-permute-start.11 = (f32[9,16,256]{2,1,0:T(8,128)S(1)}, f32[9,16,256]{2,1,0:T(8,128)S(1)}, u32[]{:S(2)}, u32[]{:S(2)}) collective-permute-start(f32[9,16,256]{2,1,0:T(8,128)S(1)} %get-tuple-element.111), channel_id=1, source_target_pairs={{0,12},{4,8},{8,4},{12,0},{1,13},{5,9},{9,5},{13,1},{2,14},{6,10},... | collective-permute-start | bytes 442376 | tf_op jit(solution)/shard_map/ppermute | solution.py:86
  44.8 0.5 collective-permute-start.9
  45.4 2.7 %collective-permute-done.5 = f32[256,3,128]{0,2,1:T(8,128)S(1)} collective-permute-done((f32[256,3,128]{0,2,1:T(8,128)S(1)}, f32[256,3,128]{0,2,1:T(8,128)S(1)}, u32[]{:S(2)}, u32[]{:S(2)}) %collective-permute-start.5) | collective-permute-done | bytes 393248 | tf_op jit(solution)/shard_map/ppermute | solution.py:19
  48.2 2.3 %collective-permute-start.8 = (f32[256,1,128]{0,2,1:T(8,128)S(1)}, f32[256,1,128]{0,2,1:T(8,128)S(1)}, u32[]{:S(2)}, u32[]{:S(2)}) collective-permute-start(f32[256,1,128]{0,2,1:T(8,128)S(1)} %get-tuple-element.114), channel_id=1, source_target_pairs={{4,0},{8,4},{12,8},{5,1},{9,5},{13,9},{6,2},{10,6},{14,10},{7,3},{... | collective-permute-start | bytes 393224 | tf_op jit(solution)/shard_map/ppermute | solution.py:21
  50.5 3.3 %collective-permute-start.7 = (f32[256,1,128]{0,2,1:T(8,128)S(1)}, f32[256,1,128]{0,2,1:T(8,128)S(1)}, u32[]{:S(2)}, u32[]{:S(2)}) collective-permute-start(f32[256,1,128]{0,2,1:T(8,128)S(1)} %get-tuple-element.113), channel_id=1, source_target_pairs={{0,4},{4,8},{8,12},{1,5},{5,9},{9,13},{2,6},{6,10},{10,14},{3,7},{... | collective-permute-start | bytes 393224 | tf_op jit(solution)/shard_map/ppermute | solution.py:19
  53.8 1.0 %constant_dynamic-update-slice_fusion.3 = (f32[9,64,256]{2,1,0:T(8,128)S(1)}, f32[9,16,256]{2,1,0:T(8,128)S(1)}) fusion(f32[9,64,256]{2,1,0:T(8,128)S(1)} %broadcast_in_dim.25, s32[]{:T(128)S(6)} %select_n.58, f32[9,16,256]{2,1,0:T(8,128)S(1)} %collective-permute-done.10, f32[9,16,256]{2,1,0:T(8,128)S(1)} %collective-permute-done.11, ...), kind=kLoop, calls=%fused_computation.38 | loop fusion | flops 110592 | bytes 884740 | tf_op jit(solution)/shard_map/dynamic_update_slice | solution.py:91
  55.0 2.0 %collective-permute-start.14 = (f32[9,16,256]{2,1,0:T(8,128)S(1)}, f32[9,16,256]{2,1,0:T(8,128)S(1)}, u32[]{:S(2)}, u32[]{:S(2)}) collective-permute-start(f32[9,16,256]{2,1,0:T(8,128)S(1)} %get-tuple-element.105), channel_id=1, source_target_pairs={{0,12},{4,8},{8,4},{12,0},{1,13},{5,9},{9,5},{13,1},{2,14},{6,10},... | collective-permute-start | bytes 442376 | tf_op jit(solution)/shard_map/ppermute | solution.py:93
  57.1 0.7 %copy.23 = bf16[256,1,128]{2,0,1:T(8,128)(2,1)} copy(bf16[256,1,128]{0,2,1:T(8,128)(2,1)S(1)} %fusion.4) | data formatting | bytes 131072
  57.8 2.1 %collective-permute-done.13 = f32[9,16,256]{2,1,0:T(8,128)S(1)} collective-permute-done((f32[9,16,256]{2,1,0:T(8,128)S(1)}, f32[9,16,256]{2,1,0:T(8,128)S(1)}, u32[]{:S(2)}, u32[]{:S(2)}) %collective-permute-start.13) | collective-permute-done | bytes 147488 | tf_op jit(solution)/shard_map/ppermute | solution.py:93
  60.0 3.7 %collective-permute-done.14 = f32[9,16,256]{2,1,0:T(8,128)S(1)} collective-permute-done((f32[9,16,256]{2,1,0:T(8,128)S(1)}, f32[9,16,256]{2,1,0:T(8,128)S(1)}, u32[]{:S(2)}, u32[]{:S(2)}) %collective-permute-start.14) | collective-permute-done | bytes 147488 | tf_op jit(solution)/shard_map/ppermute | solution.py:93
  63.7 0.8 %copy-done.1 = f32[9,64,256]{2,1,0:T(8,128)} copy-done((f32[9,64,256]{2,1,0:T(8,128)}, f32[9,64,256]{2,1,0:T(8,128)S(1)}, u32[]{:S(2)}) %copy-start.1) | copy-done | bytes 589848
  (41 shorter events, 1.0 us)
Async XLA Ops:
  0.6 10.4 %copy-start = (bf16[1,9,3,2,64]{4,3,2,1,0:T(2,128)(2,1)S(1)}, bf16[1,9,3,2,64]{4,3,2,1,0:T(2,128)(2,1)}, u32[]{:S(2)}) copy-start(bf16[1,9,3,2,64]{4,3,2,1,0:T(2,128)(2,1)} %param.25) | copy-start | bytes 20740
  2.4 8.9 %collective-permute-start.2 = (bf16[320,128]{1,0:T(8,128)(2,1)S(1)}, bf16[320,128]{1,0:T(8,128)(2,1)S(1)}, u32[]{:S(2)}, u32[]{:S(2)}) collective-permute-start(bf16[320,128]{1,0:T(8,128)(2,1)S(1)} %get-tuple-element.121), channel_id=1, source_target_pairs={{0,1},{1,2},{2,3},{3,0},{4,5},{5,6},{6,7},{7,4},{8,9},{9,10},{10,1... | collective-permute-start | bytes 245768 | tf_op jit(solution)/shard_map/ppermute | solution.py:169
  4.5 8.4 %collective-permute-start.1 = (bf16[320,128]{1,0:T(8,128)(2,1)S(1)}, bf16[320,128]{1,0:T(8,128)(2,1)S(1)}, u32[]{:S(2)}, u32[]{:S(2)}) collective-permute-start(bf16[320,128]{1,0:T(8,128)(2,1)S(1)} %get-tuple-element.120), channel_id=1, source_target_pairs={{0,2},{1,3},{2,0},{3,1},{4,6},{5,7},{6,4},{7,5},{8,10},{9,11},{10,... | collective-permute-start | bytes 245768 | tf_op jit(solution)/shard_map/ppermute | solution.py:169
  6.9 6.1 %collective-permute-start = (bf16[320,128]{1,0:T(8,128)(2,1)S(1)}, bf16[320,128]{1,0:T(8,128)(2,1)S(1)}, u32[]{:S(2)}, u32[]{:S(2)}) collective-permute-start(bf16[320,128]{1,0:T(8,128)(2,1)S(1)} %get-tuple-element.119), channel_id=1, source_target_pairs={{0,3},{1,0},{2,1},{3,2},{4,7},{5,4},{6,5},{7,6},{8,11},{9,8},{10,9... | collective-permute-start | bytes 245768 | tf_op jit(solution)/shard_map/ppermute | solution.py:169
  9.3 3.7 %copy-start.2 = (bf16[256,1,128]{2,0,1:T(8,128)(2,1)S(1)}, bf16[256,1,128]{2,0,1:T(8,128)(2,1)}, u32[]{:S(2)}) copy-start(bf16[256,1,128]{2,0,1:T(8,128)(2,1)} %param.22) | copy-start | bytes 196612
  13.1 18.0 %collective-permute-start.4 = (bf16[256,512]{1,0:T(8,128)(2,1)S(1)}, bf16[256,512]{1,0:T(8,128)(2,1)S(1)}, u32[]{:S(2)}, u32[]{:S(2)}) collective-permute-start(bf16[256,512]{1,0:T(8,128)(2,1)S(1)} %pad_maximum_fusion.1), channel_id=1, source_target_pairs={{4,0},{8,4},{12,8},{5,1},{9,5},{13,9},{6,2},{10,6},{14,10},{7,3},{... | collective-permute-start | bytes 786440 | tf_op jit(solution)/shard_map/ppermute | solution.py:181
  15.8 15.3 %collective-permute-start.3 = (bf16[256,512]{1,0:T(8,128)(2,1)S(1)}, bf16[256,512]{1,0:T(8,128)(2,1)S(1)}, u32[]{:S(2)}, u32[]{:S(2)}) collective-permute-start(bf16[256,512]{1,0:T(8,128)(2,1)S(1)} %pad_maximum_fusion.1), channel_id=1, source_target_pairs={{0,4},{4,8},{8,12},{1,5},{5,9},{9,13},{2,6},{6,10},{10,14},{3,7},{... | collective-permute-start | bytes 786440 | tf_op jit(solution)/shard_map/ppermute | solution.py:180
  27.3 18.0 %collective-permute-start.6 = (f32[256,3,128]{0,2,1:T(8,128)}, f32[256,3,128]{0,2,1:T(8,128)S(1)}, u32[]{:S(2)}, u32[]{:S(2)}) collective-permute-start(f32[256,3,128]{0,2,1:T(8,128)} %get-tuple-element.107), channel_id=1, source_target_pairs={{1,0},{2,1},{3,2},{0,3},{5,4},{6,5},{7,6},{4,7},{9,8},{10,9},{11,1... | collective-permute-start | bytes 1179656 | tf_op jit(solution)/shard_map/ppermute | solution.py:21
  30.4 17.7 %collective-permute-start.5 = (f32[256,3,128]{0,2,1:T(8,128)S(1)}, f32[256,3,128]{0,2,1:T(8,128)S(1)}, u32[]{:S(2)}, u32[]{:S(2)}) collective-permute-start(f32[256,3,128]{0,2,1:T(8,128)S(1)} %get-tuple-element.106), channel_id=1, source_target_pairs={{0,1},{1,2},{2,3},{3,0},{4,5},{5,6},{6,7},{7,4},{8,9},{9,10},{10,1... | collective-permute-start | bytes 1179656 | tf_op jit(solution)/shard_map/ppermute | solution.py:19
  43.4 10.3 %collective-permute-start.10 = (f32[9,16,256]{2,1,0:T(8,128)S(1)}, f32[9,16,256]{2,1,0:T(8,128)S(1)}, u32[]{:S(2)}, u32[]{:S(2)}) collective-permute-start(f32[9,16,256]{2,1,0:T(8,128)S(1)} %get-tuple-element.112), channel_id=1, source_target_pairs={{0,8},{4,12},{8,0},{12,4},{1,9},{5,13},{9,1},{13,5},{2,10},{6,14},... | collective-permute-start | bytes 442376 | tf_op jit(solution)/shard_map/ppermute | solution.py:86
  43.5 10.3 %collective-permute-start.11 = (f32[9,16,256]{2,1,0:T(8,128)S(1)}, f32[9,16,256]{2,1,0:T(8,128)S(1)}, u32[]{:S(2)}, u32[]{:S(2)}) collective-permute-start(f32[9,16,256]{2,1,0:T(8,128)S(1)} %get-tuple-element.111), channel_id=1, source_target_pairs={{0,12},{4,8},{8,4},{12,0},{1,13},{5,9},{9,5},{13,1},{2,14},{6,10},... | collective-permute-start | bytes 442376 | tf_op jit(solution)/shard_map/ppermute | solution.py:86
  44.8 9.0 %collective-permute-start.9 = (f32[9,16,256]{2,1,0:T(8,128)S(1)}, f32[9,16,256]{2,1,0:T(8,128)S(1)}, u32[]{:S(2)}, u32[]{:S(2)}) collective-permute-start(f32[9,16,256]{2,1,0:T(8,128)S(1)} %get-tuple-element.110), channel_id=1, source_target_pairs={{0,4},{4,0},{8,12},{12,8},{1,5},{5,1},{9,13},{13,9},{2,6},{6,2},{1... | collective-permute-start | bytes 442376 | tf_op jit(solution)/shard_map/ppermute | solution.py:86
  48.2 8.8 %collective-permute-start.8 = (f32[256,1,128]{0,2,1:T(8,128)S(1)}, f32[256,1,128]{0,2,1:T(8,128)S(1)}, u32[]{:S(2)}, u32[]{:S(2)}) collective-permute-start(f32[256,1,128]{0,2,1:T(8,128)S(1)} %get-tuple-element.114), channel_id=1, source_target_pairs={{4,0},{8,4},{12,8},{5,1},{9,5},{13,9},{6,2},{10,6},{14,10},{7,3},{... | collective-permute-start | bytes 393224 | tf_op jit(solution)/shard_map/ppermute | solution.py:21
  50.5 6.6 %collective-permute-start.7 = (f32[256,1,128]{0,2,1:T(8,128)S(1)}, f32[256,1,128]{0,2,1:T(8,128)S(1)}, u32[]{:S(2)}, u32[]{:S(2)}) collective-permute-start(f32[256,1,128]{0,2,1:T(8,128)S(1)} %get-tuple-element.113), channel_id=1, source_target_pairs={{0,4},{4,8},{8,12},{1,5},{5,9},{9,13},{2,6},{6,10},{10,14},{3,7},{... | collective-permute-start | bytes 393224 | tf_op jit(solution)/shard_map/ppermute | solution.py:19
  54.8 3.0 %collective-permute-start.12 = (f32[9,16,256]{2,1,0:T(8,128)S(1)}, f32[9,16,256]{2,1,0:T(8,128)S(1)}, u32[]{:S(2)}, u32[]{:S(2)}) collective-permute-start(f32[9,16,256]{2,1,0:T(8,128)S(1)} %get-tuple-element.105), channel_id=1, source_target_pairs={{0,4},{4,0},{8,12},{12,8},{1,5},{5,1},{9,13},{13,9},{2,6},{6,2},{1... | collective-permute-start | bytes 442376 | tf_op jit(solution)/shard_map/ppermute | solution.py:93
  54.9 5.1 %collective-permute-start.13 = (f32[9,16,256]{2,1,0:T(8,128)S(1)}, f32[9,16,256]{2,1,0:T(8,128)S(1)}, u32[]{:S(2)}, u32[]{:S(2)}) collective-permute-start(f32[9,16,256]{2,1,0:T(8,128)S(1)} %get-tuple-element.105), channel_id=1, source_target_pairs={{0,8},{4,12},{8,0},{12,4},{1,9},{5,13},{9,1},{13,5},{2,10},{6,14},... | collective-permute-start | bytes 442376 | tf_op jit(solution)/shard_map/ppermute | solution.py:93
  55.0 8.7 %collective-permute-start.14 = (f32[9,16,256]{2,1,0:T(8,128)S(1)}, f32[9,16,256]{2,1,0:T(8,128)S(1)}, u32[]{:S(2)}, u32[]{:S(2)}) collective-permute-start(f32[9,16,256]{2,1,0:T(8,128)S(1)} %get-tuple-element.105), channel_id=1, source_target_pairs={{0,12},{4,8},{8,4},{12,0},{1,13},{5,9},{9,5},{13,1},{2,14},{6,10},... | collective-permute-start | bytes 442376 | tf_op jit(solution)/shard_map/ppermute | solution.py:93
  63.7 0.8 %copy-start.1 = (f32[9,64,256]{2,1,0:T(8,128)}, f32[9,64,256]{2,1,0:T(8,128)S(1)}, u32[]{:S(2)}) copy-start(f32[9,64,256]{2,1,0:T(8,128)S(1)} %constant_dynamic-update-slice_fusion) | copy-start | bytes 1769476

commit v8 on v6

--- a/solution.py
+++ b/solution.py
@@ -162,7 +162,6 @@
         "koc,oij->cikj", weights, upstream, preferred_element_type=jnp.float32
     ).astype(jnp.bfloat16)
     grad_piece = response_grad[:, 0].reshape(channels, kernels * lon_cols)
-    matrix, contrib = toeplitz(tap_table[0], lon_cols, grad_piece)
     o_block = upstream.shape[0] // n_lon
     up_row = upstream[:, 0]
     blocks = [fields[:, 0]]
@@ -178,9 +177,11 @@
         up_parts.append(both[channels:])
     up_rel = jnp.stack(up_parts, axis=0)
     row = jnp.concatenate(blocks, axis=1)
+    row, tap_row, grad_piece = lax.optimization_barrier((row, tap_table[0], grad_piece))
     count = lax.axis_size("lat")
     below = lax.ppermute(row, "lat", [(i, i + 1) for i in range(count - 1)])
     above = lax.ppermute(row, "lat", [(i + 1, i) for i in range(count - 1)])
+    matrix, contrib = toeplitz(tap_row, lon_cols, grad_piece)
     rows = jnp.stack([below, row, above], axis=0)
     ext = jnp.concatenate([rows[:, :, rows.shape[2] - HALO :], rows, rows[:, :, :HALO]], axis=2)
     out_row, grad_terms = row_products(ext, matrix, weights, up_rel)

time: 63.9 us -> 65.3 us (1.022)
  local copies, waits for them, and re-layouts: 6.99 us -> 10.4 us
  waiting for transfers between devices: 12 us -> 9.39 us
  other arithmetic: 3.8 us -> 4.46 us
    ppermute x1, waiting for transfers between devices: 4.69 us -> 0.01 us  [body(): above = lax.ppermute(row, 'lat', [(i + 1, i) for i in range(count - 1)])]
    another operation x4, local copies, waits for them, and re-layouts: 0.79 us -> 3.55 us  [body(): up_rel = jnp.stack(up_parts, axis=0)]
    ppermute x2, waiting for transfers between devices: 0.01 us -> 2.39 us  [padded_2(): lax.ppermute(tail, axis, [(i, (i + 1) % count) for i in range(ends)])]
    ppermute x1, starting transfers between devices: 5.08 us -> 3.01 us  [body(): below = lax.ppermute(row, 'lat', [(i, i + 1) for i in range(count - 1)])]
    ppermute x2, starting transfers between devices: 3.47 us -> 5.4 us  [padded_2(): lax.ppermute(head, axis, [((i + 1) % count, i) for i in range(ends)])]
    ppermute x3, waiting for transfers between devices: 0.01 us -> 1.12 us  [body(): lax.ppermute(jnp.concatenate([fields[:, 0], part], axis=0), 'lon', [(p, (...]
    another operation x1 -> x0, local copies, waits for them, and re-layouts: 1.06 us -> none  [body(): grad_piece = response_grad[:, 0].reshape(channels, kernels * lon_cols)]
    optimization_barrier x0 -> x1, local copies, waits for them, and re-layouts: none -> 1.05 us  [body(): lax.optimization_barrier((row, tap_table[0], grad_piece))]
  transfers between devices with their start and end apart: 15 -> 15, of which waited for: 5 -> 4; matrix products, arithmetic and copies ran while one was open for 16% -> 20% of each run, Pallas kernels for 20% -> 20%
where the time goes in v8:
time: 65.3 us; the launch traced here: 64.6 us
  starting transfers between devices  24 us (37%)
  Pallas kernels  12.9 us (20%)
  local copies, waits for them, and re-layouts  10.4 us (16%)
  waiting for transfers between devices  9.39 us (14%)
  other arithmetic  4.46 us (7%)
  matrix products  1.89 us (3%)
  between operations  1.63 us (2%)
    pallas_call x1, Pallas kernels, row_products(): pl.pallas_call(row_kernel, out_shape=(jax.ShapeDtypeStruct((weights.shape...  8.55 us
    ppermute x3, waiting for transfers between devices, lat_allreduce(): recv = lax.ppermute(mine, axis, [(i, i ^ d) for i in range(count)])  5.86 us
    ppermute x3, starting transfers between devices, body(): lax.ppermute(jnp.concatenate([fields[:, 0], part], axis=0), 'lon', [(p, (...  5.56 us
    ppermute x2, starting transfers between devices, padded_2(): lax.ppermute(head, axis, [((i + 1) % count, i) for i in range(ends)])  5.4 us
    pallas_call x1, Pallas kernels, toeplitz(): pl.pallas_call(toeplitz_kernel, out_shape=(jax.ShapeDtypeStruct((kernels,...  4.33 us
    another operation x4, local copies, waits for them, and re-layouts, body(): up_rel = jnp.stack(up_parts, axis=0)  3.55 us
    ppermute x2, starting transfers between devices, padded_2(): lax.ppermute(tail, axis, [(i, (i + 1) % count) for i in range(ends)])  3.26 us
    ppermute x1, starting transfers between devices, body(): below = lax.ppermute(row, 'lat', [(i, i + 1) for i in range(count - 1)])  3.01 us
  transfers between devices with their start and end apart: 15, of which 4 were waited for; matrix products, arithmetic and copies ran while one was open for 20% of the time, Pallas kernels for 20%

profile of v8, /device:TPU:1, one launch (start us, length us, event | category | flops | bytes accessed | tf_op | source)
XLA Modules:
  0.0 64.6 jit_solution(5552952187186004474)
XLA Ops:
  0.7 1.4 %dynamic-slice_bitcast_fusion = (bf16[1,64,128]{2,1,0:T(8,128)(2,1)}, bf16[64,128]{1,0:T(8,128)(2,1)S(1)}, bf16[64,128]{1,0:T(8,128)(2,1)S(1)}, bf16[64,128]{1,0:T(8,128)(2,1)S(1)}) fusion(bf16[256,1,128]{2,0,1:T(8,128)(2,1)} %param.23, s32[]{:T(128)S(6)} %select_n.57, s32[]{:T(128)S(6)} %select_n.55, s32[]{:T(128)S(6)} %select_n.53, s32[]{:T(128)S(6)} %select_n.51), kind=kLoop, calls=%fused_computation.35 | loop fusion | bytes 131088 | tf_op jit(solution)/shard_map/stack | solution.py:178
  2.1 0.9 %pad_maximum_fusion.5 = (bf16[320,128]{1,0:T(8,128)(2,1)S(1)}, bf16[320,128]{1,0:T(8,128)(2,1)S(1)}, bf16[320,128]{1,0:T(8,128)(2,1)S(1)}) fusion(bf16[64,128]{1,0:T(8,128)(2,1)S(1)} %get-tuple-element.116, bf16[256,128]{1,0:T(8,128)(2,1)} %bitcast.56, bf16[64,128]{1,0:T(8,128)(2,1)S(1)} %get-tuple-element.115, bf16[64,128]{1,0:T(8,128)(2,1)S(1)} %get-tuple-element.114), kind=kLoop, calls=%fused_computation.21 | loop fusion | flops 409600 | bytes 360448 | tf_op jit(solution)/shard_map/concatenate | solution.py:172
  3.0 2.2 %collective-permute-start.2 = (bf16[320,128]{1,0:T(8,128)(2,1)S(1)}, bf16[320,128]{1,0:T(8,128)(2,1)S(1)}, u32[]{:S(2)}, u32[]{:S(2)}) collective-permute-start(bf16[320,128]{1,0:T(8,128)(2,1)S(1)} %get-tuple-element.119), channel_id=1, source_target_pairs={{0,1},{1,2},{2,3},{3,0},{4,5},{5,6},{6,7},{7,4},{8,9},{9,10},{10,1... | collective-permute-start | bytes 245768 | tf_op jit(solution)/shard_map/ppermute | solution.py:171
  5.2 2.3 %collective-permute-start.1 = (bf16[320,128]{1,0:T(8,128)(2,1)S(1)}, bf16[320,128]{1,0:T(8,128)(2,1)S(1)}, u32[]{:S(2)}, u32[]{:S(2)}) collective-permute-start(bf16[320,128]{1,0:T(8,128)(2,1)S(1)} %get-tuple-element.118), channel_id=1, source_target_pairs={{0,2},{1,3},{2,0},{3,1},{4,6},{5,7},{6,4},{7,5},{8,10},{9,11},{10,... | collective-permute-start | bytes 245768 | tf_op jit(solution)/shard_map/ppermute | solution.py:171
  7.5 1.1 %collective-permute-start = (bf16[320,128]{1,0:T(8,128)(2,1)S(1)}, bf16[320,128]{1,0:T(8,128)(2,1)S(1)}, u32[]{:S(2)}, u32[]{:S(2)}) collective-permute-start(bf16[320,128]{1,0:T(8,128)(2,1)S(1)} %get-tuple-element.117), channel_id=1, source_target_pairs={{0,3},{1,0},{2,1},{3,2},{4,7},{5,4},{6,5},{7,6},{8,11},{9,8},{10,9... | collective-permute-start | bytes 245768 | tf_op jit(solution)/shard_map/ppermute | solution.py:171
  8.5 0.7 %add_bitcast_fusion = s32[2]{0:T(128)S(1)} fusion(s32[1,2]{1,0:T(1,128)} %param.27), kind=kLoop, calls=%fused_computation.48 | loop fusion | flops 4 | bytes 16 | tf_op jit(solution)/shard_map/add | solution.py:32
  9.9 1.7 %convolution_convert_fusion = bf16[128,9,256]{2,0,1:T(8,128)(2,1)S(1)} fusion(bf16[9,256,256]{2,1,0:T(8,128)(2,1)} %w_ref.1, bf16[256,1,128]{2,0,1:T(8,128)(2,1)} %param.23), kind=kOutput, calls=%fused_computation | convolution fusion | flops 151289856 | bytes 1835008 | tf_op jit(solution)/shard_map/koc,oij->cikj/dot_general | solution.py:161
  12.5 1.1 %collective-permute-done.1 = bf16[320,128]{1,0:T(8,128)(2,1)S(1)} collective-permute-done((bf16[320,128]{1,0:T(8,128)(2,1)S(1)}, bf16[320,128]{1,0:T(8,128)(2,1)S(1)}, u32[]{:S(2)}, u32[]{:S(2)}) %collective-permute-start.1) | collective-permute-done | bytes 81952 | tf_op jit(solution)/shard_map/ppermute | solution.py:171
  13.7 2.7 %collective-permute-start.4 = (bf16[256,512]{1,0:T(8,128)(2,1)S(1)}, bf16[256,512]{1,0:T(8,128)(2,1)S(1)}, u32[]{:S(2)}, u32[]{:S(2)}) collective-permute-start(bf16[256,512]{1,0:T(8,128)(2,1)S(1)} %pad_maximum_fusion.4), channel_id=1, source_target_pairs={{4,0},{8,4},{12,8},{5,1},{9,5},{13,9},{6,2},{10,6},{14,10},{7,3},{... | collective-permute-start | bytes 786440 | tf_op jit(solution)/shard_map/ppermute | solution.py:183
  16.4 3.0 %collective-permute-start.3 = (bf16[256,512]{1,0:T(8,128)(2,1)S(1)}, bf16[256,512]{1,0:T(8,128)(2,1)S(1)}, u32[]{:S(2)}, u32[]{:S(2)}) collective-permute-start(bf16[256,512]{1,0:T(8,128)(2,1)S(1)} %pad_maximum_fusion.4), channel_id=1, source_target_pairs={{0,4},{4,8},{8,12},{1,5},{5,9},{9,13},{2,6},{6,10},{10,14},{3,7},{... | collective-permute-start | bytes 786440 | tf_op jit(solution)/shard_map/ppermute | solution.py:182
  19.4 0.6 reshape.252.tap_ref
  20.1 1.1 %copy.19.grad_ref = bf16[256,1152]{1,0:T(8,128)(2,1)} copy(bf16[256,1152]{0,1:T(8,128)(2,1)S(1)} %bitcast.52) | data formatting | bytes 1179648 | tf_op jit(solution)/shard_map/optimization_barrier | solution.py:180
  21.1 4.3 %shard_map.100 = (bf16[9,128,1152]{2,1,0:T(8,128)(2,1)}, f32[256,1152]{1,0:T(8,128)}) custom-call(f32[27,384]{1,0:T(8,128)} %reshape.252.tap_ref, bf16[256,1152]{1,0:T(8,128)(2,1)} %copy.19.grad_ref), custom_call_target="tpu_custom_call" | custom-call | tf_op jit(solution)/shard_map/pallas_call | solution.py:66
  25.5 1.6 %copy.20 = f32[256,1152]{0,1:T(8,128)S(1)} copy(f32[256,1152]{1,0:T(8,128)} %get-tuple-element.99) | data formatting | bytes 2359296 | tf_op jit(solution)/shard_map/pallas_call | solution.py:66
  27.2 3.1 %collective-permute-start.6 = (f32[256,3,128]{0,2,1:T(8,128)S(1)}, f32[256,3,128]{0,2,1:T(8,128)S(1)}, u32[]{:S(2)}, u32[]{:S(2)}) collective-permute-start(f32[256,3,128]{0,2,1:T(8,128)S(1)} %get-tuple-element.107), channel_id=1, source_target_pairs={{1,0},{2,1},{3,2},{0,3},{5,4},{6,5},{7,6},{4,7},{9,8},{10,9},{11,1... | collective-permute-start | bytes 1179656 | tf_op jit(solution)/shard_map/ppermute | solution.py:21
  30.3 0.7 %slice_bitcast_fusion = bf16[1,64,128]{2,1,0:T(8,128)(2,1)S(1)} fusion(bf16[320,128]{1,0:T(8,128)(2,1)} %copy-done.3), kind=kLoop, calls=%fused_computation.32 | loop fusion | bytes 32768 | tf_op jit(solution)/shard_map/stack | solution.py:178
  31.0 0.7 %slice_bitcast_fusion.1 = bf16[1,64,128]{2,1,0:T(8,128)(2,1)S(1)} fusion(bf16[320,128]{1,0:T(8,128)(2,1)} %copy-done.4), kind=kLoop, calls=%fused_computation.33 | loop fusion | bytes 32768 | tf_op jit(solution)/shard_map/stack | solution.py:178
  31.8 0.7 %slice_bitcast_fusion.2 = bf16[1,64,128]{2,1,0:T(8,128)(2,1)S(1)} fusion(bf16[320,128]{1,0:T(8,128)(2,1)} %copy-done.5), kind=kLoop, calls=%fused_computation.34 | loop fusion | bytes 32768 | tf_op jit(solution)/shard_map/stack | solution.py:178
  32.5 0.6 pad_maximum_fusion.8.up_ref
  33.1 1.1 %fusion.ext_ref = bf16[3,256,768]{2,1,0:T(8,128)(2,1)} fusion(bf16[1,256,512]{2,1,0:T(8,128)(2,1)S(1)} %bitcast.54, bf16[1,256,512]{2,1,0:T(8,128)(2,1)S(1)} %bitcast.53, bf16[1,256,512]{2,1,0:T(8,128)(2,1)S(1)} %bitcast.55), kind=kLoop, calls=%fused_computation.2 | loop fusion | flops 10616832 | bytes 1966080 | tf_op jit(solution)/shard_map/concatenate | solution.py:186
  34.2 8.5 %shard_map.101 = (bf16[256,128]{1,0:T(8,128)(2,1)}, f32[9,64,256]{2,1,0:T(8,128)}) custom-call(bf16[3,256,768]{2,1,0:T(8,128)(2,1)} %fusion.ext_ref, bf16[1152,1152]{1,0:T(8,128)(2,1)} %bitcast.58, bf16[9,256,256]{2,1,0:T(8,128)(2,1)} %w_ref.1, bf16[4,64,128]{2,1,0:T(8,128)(2,1)} %pad_maximum_fusion.8.up_ref), custom_call_target="tpu_custom_call" | custom-call | flops 3019898880 | bytes 5734400 | tf_op jit(solution)/shard_map/pallas_call | solution.py:144
  42.8 1.1 %constant_dynamic-slice_fusion.2 = (f32[9,16,256]{2,1,0:T(8,128)S(1)}, f32[9,16,256]{2,1,0:T(8,128)S(1)}, f32[9,16,256]{2,1,0:T(8,128)S(1)}) fusion(f32[9,64,256]{2,1,0:T(8,128)} %get-tuple-element.100, s32[]{:T(128)S(6)} %select_n.59, s32[]{:T(128)S(6)} %select_n.61, s32[]{:T(128)S(6)} %select_n.60), kind=kLoop, calls=%fused_computation.45 | loop fusion | bytes 884748 | tf_op jit(solution)/shard_map/dynamic_slice | solution.py:85
  43.9 1.3 %collective-permute-start.11 = (f32[9,16,256]{2,1,0:T(8,128)S(1)}, f32[9,16,256]{2,1,0:T(8,128)S(1)}, u32[]{:S(2)}, u32[]{:S(2)}) collective-permute-start(f32[9,16,256]{2,1,0:T(8,128)S(1)} %get-tuple-element.109), channel_id=1, source_target_pairs={{0,12},{4,8},{8,4},{12,0},{1,13},{5,9},{9,5},{13,1},{2,14},{6,10},... | collective-permute-start | bytes 442376 | tf_op jit(solution)/shard_map/ppermute | solution.py:86
  45.8 2.4 %collective-permute-done.5 = f32[256,3,128]{0,2,1:T(8,128)S(1)} collective-permute-done((f32[256,3,128]{0,2,1:T(8,128)S(1)}, f32[256,3,128]{0,2,1:T(8,128)S(1)}, u32[]{:S(2)}, u32[]{:S(2)}) %collective-permute-start.5) | collective-permute-done | bytes 393248 | tf_op jit(solution)/shard_map/ppermute | solution.py:19
  48.3 2.3 %collective-permute-start.8 = (f32[256,1,128]{0,2,1:T(8,128)S(1)}, f32[256,1,128]{0,2,1:T(8,128)S(1)}, u32[]{:S(2)}, u32[]{:S(2)}) collective-permute-start(f32[256,1,128]{0,2,1:T(8,128)S(1)} %get-tuple-element.112), channel_id=1, source_target_pairs={{4,0},{8,4},{12,8},{5,1},{9,5},{13,9},{6,2},{10,6},{14,10},{7,3},{... | collective-permute-start | bytes 393224 | tf_op jit(solution)/shard_map/ppermute | solution.py:21
  50.6 3.3 %collective-permute-start.7 = (f32[256,1,128]{0,2,1:T(8,128)S(1)}, f32[256,1,128]{0,2,1:T(8,128)S(1)}, u32[]{:S(2)}, u32[]{:S(2)}) collective-permute-start(f32[256,1,128]{0,2,1:T(8,128)S(1)} %get-tuple-element.111), channel_id=1, source_target_pairs={{0,4},{4,8},{8,12},{1,5},{5,9},{9,13},{2,6},{6,10},{10,14},{3,7},{... | collective-permute-start | bytes 393224 | tf_op jit(solution)/shard_map/ppermute | solution.py:19
  53.9 1.0 %constant_dynamic-update-slice_fusion.3 = (f32[9,64,256]{2,1,0:T(8,128)S(1)}, f32[9,16,256]{2,1,0:T(8,128)S(1)}) fusion(f32[9,64,256]{2,1,0:T(8,128)S(1)} %broadcast_in_dim.25, s32[]{:T(128)S(6)} %select_n.58, f32[9,16,256]{2,1,0:T(8,128)S(1)} %collective-permute-done.10, f32[9,16,256]{2,1,0:T(8,128)S(1)} %collective-permute-done.11, ...), kind=kLoop, calls=%fused_computation.42 | loop fusion | flops 110592 | bytes 884740 | tf_op jit(solution)/shard_map/dynamic_update_slice | solution.py:91
  55.1 2.0 %collective-permute-start.14 = (f32[9,16,256]{2,1,0:T(8,128)S(1)}, f32[9,16,256]{2,1,0:T(8,128)S(1)}, u32[]{:S(2)}, u32[]{:S(2)}) collective-permute-start(f32[9,16,256]{2,1,0:T(8,128)S(1)} %get-tuple-element.105), channel_id=1, source_target_pairs={{0,12},{4,8},{8,4},{12,0},{1,13},{5,9},{9,5},{13,1},{2,14},{6,10},... | collective-permute-start | bytes 442376 | tf_op jit(solution)/shard_map/ppermute | solution.py:93
  57.2 0.7 %copy.21 = bf16[256,1,128]{2,0,1:T(8,128)(2,1)} copy(bf16[256,1,128]{0,2,1:T(8,128)(2,1)S(1)} %fusion.6) | data formatting | bytes 131072
  57.9 2.1 %collective-permute-done.13 = f32[9,16,256]{2,1,0:T(8,128)S(1)} collective-permute-done((f32[9,16,256]{2,1,0:T(8,128)S(1)}, f32[9,16,256]{2,1,0:T(8,128)S(1)}, u32[]{:S(2)}, u32[]{:S(2)}) %collective-permute-start.13) | collective-permute-done | bytes 147488 | tf_op jit(solution)/shard_map/ppermute | solution.py:93
  60.1 3.7 %collective-permute-done.14 = f32[9,16,256]{2,1,0:T(8,128)S(1)} collective-permute-done((f32[9,16,256]{2,1,0:T(8,128)S(1)}, f32[9,16,256]{2,1,0:T(8,128)S(1)}, u32[]{:S(2)}, u32[]{:S(2)}) %collective-permute-start.14) | collective-permute-done | bytes 147488 | tf_op jit(solution)/shard_map/ppermute | solution.py:93
  63.8 0.8 %copy-done.1 = f32[9,64,256]{2,1,0:T(8,128)} copy-done((f32[9,64,256]{2,1,0:T(8,128)}, f32[9,64,256]{2,1,0:T(8,128)S(1)}, u32[]{:S(2)}) %copy-start.1) | copy-done | bytes 589848
  (46 shorter events, 2.1 us)
Async XLA Ops:
  0.6 11.0 %copy-start = (bf16[1,9,3,2,64]{4,3,2,1,0:T(2,128)(2,1)S(1)}, bf16[1,9,3,2,64]{4,3,2,1,0:T(2,128)(2,1)}, u32[]{:S(2)}) copy-start(bf16[1,9,3,2,64]{4,3,2,1,0:T(2,128)(2,1)} %param.25) | copy-start | bytes 20740
  3.0 8.9 %collective-permute-start.2 = (bf16[320,128]{1,0:T(8,128)(2,1)S(1)}, bf16[320,128]{1,0:T(8,128)(2,1)S(1)}, u32[]{:S(2)}, u32[]{:S(2)}) collective-permute-start(bf16[320,128]{1,0:T(8,128)(2,1)S(1)} %get-tuple-element.119), channel_id=1, source_target_pairs={{0,1},{1,2},{2,3},{3,0},{4,5},{5,6},{6,7},{7,4},{8,9},{9,10},{10,1... | collective-permute-start | bytes 245768 | tf_op jit(solution)/shard_map/ppermute | solution.py:171
  5.2 8.4 %collective-permute-start.1 = (bf16[320,128]{1,0:T(8,128)(2,1)S(1)}, bf16[320,128]{1,0:T(8,128)(2,1)S(1)}, u32[]{:S(2)}, u32[]{:S(2)}) collective-permute-start(bf16[320,128]{1,0:T(8,128)(2,1)S(1)} %get-tuple-element.118), channel_id=1, source_target_pairs={{0,2},{1,3},{2,0},{3,1},{4,6},{5,7},{6,4},{7,5},{8,10},{9,11},{10,... | collective-permute-start | bytes 245768 | tf_op jit(solution)/shard_map/ppermute | solution.py:171
  7.5 6.1 %collective-permute-start = (bf16[320,128]{1,0:T(8,128)(2,1)S(1)}, bf16[320,128]{1,0:T(8,128)(2,1)S(1)}, u32[]{:S(2)}, u32[]{:S(2)}) collective-permute-start(bf16[320,128]{1,0:T(8,128)(2,1)S(1)} %get-tuple-element.117), channel_id=1, source_target_pairs={{0,3},{1,0},{2,1},{3,2},{4,7},{5,4},{6,5},{7,6},{8,11},{9,8},{10,9... | collective-permute-start | bytes 245768 | tf_op jit(solution)/shard_map/ppermute | solution.py:171
  9.9 3.7 %copy-start.2 = (bf16[256,1,128]{2,0,1:T(8,128)(2,1)S(1)}, bf16[256,1,128]{2,0,1:T(8,128)(2,1)}, u32[]{:S(2)}) copy-start(bf16[256,1,128]{2,0,1:T(8,128)(2,1)} %param.22) | copy-start | bytes 196612
  11.8 0.6 copy-start.3
  13.6 11.9 %copy-start.4 = (bf16[320,128]{1,0:T(8,128)(2,1)}, bf16[320,128]{1,0:T(8,128)(2,1)S(1)}, u32[]{:S(2)}) copy-start(bf16[320,128]{1,0:T(8,128)(2,1)S(1)} %collective-permute-done.1) | copy-start | bytes 245764
  13.6 11.9 %copy-start.5 = (bf16[320,128]{1,0:T(8,128)(2,1)}, bf16[320,128]{1,0:T(8,128)(2,1)S(1)}, u32[]{:S(2)}) copy-start(bf16[320,128]{1,0:T(8,128)(2,1)S(1)} %collective-permute-done) | copy-start | bytes 245764
  13.7 19.4 %collective-permute-start.4 = (bf16[256,512]{1,0:T(8,128)(2,1)S(1)}, bf16[256,512]{1,0:T(8,128)(2,1)S(1)}, u32[]{:S(2)}, u32[]{:S(2)}) collective-permute-start(bf16[256,512]{1,0:T(8,128)(2,1)S(1)} %pad_maximum_fusion.4), channel_id=1, source_target_pairs={{4,0},{8,4},{12,8},{5,1},{9,5},{13,9},{6,2},{10,6},{14,10},{7,3},{... | collective-permute-start | bytes 786440 | tf_op jit(solution)/shard_map/ppermute | solution.py:183
  16.4 16.7 %collective-permute-start.3 = (bf16[256,512]{1,0:T(8,128)(2,1)S(1)}, bf16[256,512]{1,0:T(8,128)(2,1)S(1)}, u32[]{:S(2)}, u32[]{:S(2)}) collective-permute-start(bf16[256,512]{1,0:T(8,128)(2,1)S(1)} %pad_maximum_fusion.4), channel_id=1, source_target_pairs={{0,4},{4,8},{8,12},{1,5},{5,9},{9,13},{2,6},{6,10},{10,14},{3,7},{... | collective-permute-start | bytes 786440 | tf_op jit(solution)/shard_map/ppermute | solution.py:182
  27.1 5.4 %copy-start.6 = (bf16[1,64,128]{2,1,0:T(8,128)(2,1)S(1)}, bf16[1,64,128]{2,1,0:T(8,128)(2,1)}, u32[]{:S(2)}) copy-start(bf16[1,64,128]{2,1,0:T(8,128)(2,1)} %get-tuple-element.113) | copy-start | bytes 49156
  27.2 18.6 %collective-permute-start.6 = (f32[256,3,128]{0,2,1:T(8,128)S(1)}, f32[256,3,128]{0,2,1:T(8,128)S(1)}, u32[]{:S(2)}, u32[]{:S(2)}) collective-permute-start(f32[256,3,128]{0,2,1:T(8,128)S(1)} %get-tuple-element.107), channel_id=1, source_target_pairs={{1,0},{2,1},{3,2},{0,3},{5,4},{6,5},{7,6},{4,7},{9,8},{10,9},{11,1... | collective-permute-start | bytes 1179656 | tf_op jit(solution)/shard_map/ppermute | solution.py:21
  30.3 17.9 %collective-permute-start.5 = (f32[256,3,128]{0,2,1:T(8,128)S(1)}, f32[256,3,128]{0,2,1:T(8,128)S(1)}, u32[]{:S(2)}, u32[]{:S(2)}) collective-permute-start(f32[256,3,128]{0,2,1:T(8,128)S(1)} %get-tuple-element.106), channel_id=1, source_target_pairs={{0,1},{1,2},{2,3},{3,0},{4,5},{5,6},{6,7},{7,4},{8,9},{9,10},{10,1... | collective-permute-start | bytes 1179656 | tf_op jit(solution)/shard_map/ppermute | solution.py:19
  43.9 10.0 %collective-permute-start.10 = (f32[9,16,256]{2,1,0:T(8,128)S(1)}, f32[9,16,256]{2,1,0:T(8,128)S(1)}, u32[]{:S(2)}, u32[]{:S(2)}) collective-permute-start(f32[9,16,256]{2,1,0:T(8,128)S(1)} %get-tuple-element.110), channel_id=1, source_target_pairs={{0,8},{4,12},{8,0},{12,4},{1,9},{5,13},{9,1},{13,5},{2,10},{6,14},... | collective-permute-start | bytes 442376 | tf_op jit(solution)/shard_map/ppermute | solution.py:86
  43.9 9.9 %collective-permute-start.11 = (f32[9,16,256]{2,1,0:T(8,128)S(1)}, f32[9,16,256]{2,1,0:T(8,128)S(1)}, u32[]{:S(2)}, u32[]{:S(2)}) collective-permute-start(f32[9,16,256]{2,1,0:T(8,128)S(1)} %get-tuple-element.109), channel_id=1, source_target_pairs={{0,12},{4,8},{8,4},{12,0},{1,13},{5,9},{9,5},{13,1},{2,14},{6,10},... | collective-permute-start | bytes 442376 | tf_op jit(solution)/shard_map/ppermute | solution.py:86
  45.2 8.6 %collective-permute-start.9 = (f32[9,16,256]{2,1,0:T(8,128)S(1)}, f32[9,16,256]{2,1,0:T(8,128)S(1)}, u32[]{:S(2)}, u32[]{:S(2)}) collective-permute-start(f32[9,16,256]{2,1,0:T(8,128)S(1)} %get-tuple-element.108), channel_id=1, source_target_pairs={{0,4},{4,0},{8,12},{12,8},{1,5},{5,1},{9,13},{13,9},{2,6},{6,2},{1... | collective-permute-start | bytes 442376 | tf_op jit(solution)/shard_map/ppermute | solution.py:86
  48.3 8.8 %collective-permute-start.8 = (f32[256,1,128]{0,2,1:T(8,128)S(1)}, f32[256,1,128]{0,2,1:T(8,128)S(1)}, u32[]{:S(2)}, u32[]{:S(2)}) collective-permute-start(f32[256,1,128]{0,2,1:T(8,128)S(1)} %get-tuple-element.112), channel_id=1, source_target_pairs={{4,0},{8,4},{12,8},{5,1},{9,5},{13,9},{6,2},{10,6},{14,10},{7,3},{... | collective-permute-start | bytes 393224 | tf_op jit(solution)/shard_map/ppermute | solution.py:21
  50.6 6.5 %collective-permute-start.7 = (f32[256,1,128]{0,2,1:T(8,128)S(1)}, f32[256,1,128]{0,2,1:T(8,128)S(1)}, u32[]{:S(2)}, u32[]{:S(2)}) collective-permute-start(f32[256,1,128]{0,2,1:T(8,128)S(1)} %get-tuple-element.111), channel_id=1, source_target_pairs={{0,4},{4,8},{8,12},{1,5},{5,9},{9,13},{2,6},{6,10},{10,14},{3,7},{... | collective-permute-start | bytes 393224 | tf_op jit(solution)/shard_map/ppermute | solution.py:19
  54.9 3.0 %collective-permute-start.12 = (f32[9,16,256]{2,1,0:T(8,128)S(1)}, f32[9,16,256]{2,1,0:T(8,128)S(1)}, u32[]{:S(2)}, u32[]{:S(2)}) collective-permute-start(f32[9,16,256]{2,1,0:T(8,128)S(1)} %get-tuple-element.105), channel_id=1, source_target_pairs={{0,4},{4,0},{8,12},{12,8},{1,5},{5,1},{9,13},{13,9},{2,6},{6,2},{1... | collective-permute-start | bytes 442376 | tf_op jit(solution)/shard_map/ppermute | solution.py:93
  55.0 5.1 %collective-permute-start.13 = (f32[9,16,256]{2,1,0:T(8,128)S(1)}, f32[9,16,256]{2,1,0:T(8,128)S(1)}, u32[]{:S(2)}, u32[]{:S(2)}) collective-permute-start(f32[9,16,256]{2,1,0:T(8,128)S(1)} %get-tuple-element.105), channel_id=1, source_target_pairs={{0,8},{4,12},{8,0},{12,4},{1,9},{5,13},{9,1},{13,5},{2,10},{6,14},... | collective-permute-start | bytes 442376 | tf_op jit(solution)/shard_map/ppermute | solution.py:93
  55.1 8.7 %collective-permute-start.14 = (f32[9,16,256]{2,1,0:T(8,128)S(1)}, f32[9,16,256]{2,1,0:T(8,128)S(1)}, u32[]{:S(2)}, u32[]{:S(2)}) collective-permute-start(f32[9,16,256]{2,1,0:T(8,128)S(1)} %get-tuple-element.105), channel_id=1, source_target_pairs={{0,12},{4,8},{8,4},{12,0},{1,13},{5,9},{9,5},{13,1},{2,14},{6,10},... | collective-permute-start | bytes 442376 | tf_op jit(solution)/shard_map/ppermute | solution.py:93
  63.8 0.8 %copy-start.1 = (f32[9,64,256]{2,1,0:T(8,128)}, f32[9,64,256]{2,1,0:T(8,128)S(1)}, u32[]{:S(2)}) copy-start(f32[9,64,256]{2,1,0:T(8,128)S(1)} %constant_dynamic-update-slice_fusion) | copy-start | bytes 1769476

commit v9 on v6

--- a/solution.py
+++ b/solution.py
@@ -186,23 +186,17 @@
     out_row, grad_terms = row_products(ext, matrix, weights, up_rel)
     outputs = out_row[:, None, :]
     weight_grad = lat_allreduce(grad_terms, "lat", 1)
-    accumulated = jnp.zeros((channels, lat_rows + 2, window_len), jnp.float32)
-    cycle_row = 0
-    accumulated = accumulated.at[:, cycle_row : cycle_row + 3].add(
-        contrib.reshape(channels, 3, window_len)
-    )
-    rim_columns = jnp.concatenate(
-        [accumulated[:, :, :HALO], accumulated[:, :, HALO + lon_cols :]], axis=2
-    )
-    arrived = padded_2(rim_columns, (("lon", 2),), HALO, True)
-    interior = accumulated[:, :, HALO : HALO + lon_cols]
-    interior = interior.at[:, :, :HALO].add(arrived[:, :, :HALO])
-    interior = interior.at[:, :, lon_cols - HALO :].add(arrived[:, :, 3 * HALO :])
-    edge_rows = jnp.stack([interior[:, 0], interior[:, lat_rows + 1]], axis=1)
-    arrived = padded_2(edge_rows, (("lat", 1),), 1, False)
-    result = interior[:, 1 : lat_rows + 1]
-    result = result.at[:, 0].add(arrived[:, 0])
-    result = result.at[:, lat_rows - 1].add(arrived[:, 3])
+    terms = contrib.reshape(channels, 3, window_len)
+    count = lax.axis_size("lat")
+    from_below = lax.ppermute(terms[:, 2], "lat", [(i, i + 1) for i in range(count - 1)])
+    from_above = lax.ppermute(terms[:, 0], "lat", [(i + 1, i) for i in range(count - 1)])
+    own = terms[:, 1] + from_below + from_above
+    rims = jnp.stack([own[:, :HALO], own[:, HALO + lon_cols :]], axis=1)
+    arrived = padded_2(rims, (("lon", 1),), 1, True)
+    result = own[:, HALO : HALO + lon_cols]
+    result = result.at[:, :HALO].add(arrived[:, 0])
+    result = result.at[:, lon_cols - HALO :].add(arrived[:, 3])
+    result = result[:, None, :]
     return (outputs, result.astype(jnp.bfloat16), weight_grad)
 
 

time: 63.9 us -> 65.6 us (1.027)
  starting transfers between devices: 24.1 us -> 25.3 us
    ppermute x0 -> x2, starting transfers between devices: none -> 6.44 us  [the longest x1 4.52 us: body(): lax.ppermute(terms[:, 2], 'lat', [(i, i + 1) for i in range(count - 1)])]
    ppermute x2 -> x1, starting transfers between devices: 3.47 us -> 1.07 us  [padded_2(): lax.ppermute(head, axis, [((i + 1) % count, i) for i in range(ends)])]
    ppermute x2 -> x1, starting transfers between devices: 4.17 us -> 2.24 us  [padded_2(): lax.ppermute(tail, axis, [(i, (i + 1) % count) for i in range(ends)])]
    ppermute x1, starting transfers between devices: 5.08 us -> 3.64 us  [body(): below = lax.ppermute(row, 'lat', [(i, i + 1) for i in range(count - 1)])]
    ppermute x2 -> x1, waiting for transfers between devices: 0.01 us -> 1.14 us  [padded_2(): lax.ppermute(head, axis, [((i + 1) % count, i) for i in range(ends)])]
    ppermute x3, waiting for transfers between devices: 6.22 us -> 5.1 us  [lat_allreduce(): recv = lax.ppermute(mine, axis, [(i, i ^ d) for i in range(count)])]
    ppermute x3, waiting for transfers between devices: 0.4 us -> 1.22 us  [lat_allreduce(): parts.append(lax.ppermute(send, axis, [(i, i ^ d) for i in range(count)]))]
  transfers between devices with their start and end apart: 15 -> 15, of which waited for: 5 -> 7; matrix products, arithmetic and copies ran while one was open for 16% -> 16% of each run, Pallas kernels for 20% -> 20%
where the time goes in v9:
time: 65.6 us; the launch traced here: 65 us
  starting transfers between devices  25.3 us (39%)
  Pallas kernels  12.9 us (20%)
  waiting for transfers between devices  12.6 us (19%)
  local copies, waits for them, and re-layouts  6.97 us (11%)
  other arithmetic  3.8 us (6%)
  matrix products  1.86 us (3%)
  between operations  1.64 us (2%)
    pallas_call x1, Pallas kernels, row_products(): pl.pallas_call(row_kernel, out_shape=(jax.ShapeDtypeStruct((weights.shape...  8.55 us
    ppermute x3, waiting for transfers between devices, lat_allreduce(): recv = lax.ppermute(mine, axis, [(i, i ^ d) for i in range(count)])  5.1 us
    ppermute x3, starting transfers between devices, body(): lax.ppermute(jnp.concatenate([fields[:, 0], part], axis=0), 'lon', [(p, (...  4.66 us
    ppermute x1, starting transfers between devices, body(): lax.ppermute(terms[:, 2], 'lat', [(i, i + 1) for i in range(count - 1)])  4.52 us
    ppermute x1, waiting for transfers between devices, body(): above = lax.ppermute(row, 'lat', [(i + 1, i) for i in range(count - 1)])  4.4 us
    pallas_call x1, Pallas kernels, toeplitz(): pl.pallas_call(toeplitz_kernel, out_shape=(jax.ShapeDtypeStruct((kernels,...  4.32 us
    ppermute x1, starting transfers between devices, body(): below = lax.ppermute(row, 'lat', [(i, i + 1) for i in range(count - 1)])  3.64 us
    ppermute x3, starting transfers between devices, lat_allreduce(): recv = lax.ppermute(mine, axis, [(i, i ^ d) for i in range(count)])  3.36 us
  transfers between devices with their start and end apart: 15, of which 7 were waited for; matrix products, arithmetic and copies ran while one was open for 16% of the time, Pallas kernels for 20%

profile of v9, /device:TPU:1, one launch (start us, length us, event | category | flops | bytes accessed | tf_op | source)
XLA Modules:
  0.0 65.0 jit_solution(13731759217851939121)
XLA Ops:
  0.7 0.8 %dynamic-slice_bitcast_fusion = (bf16[1,64,128]{2,1,0:T(8,128)(2,1)S(1)}, bf16[64,128]{1,0:T(8,128)(2,1)S(1)}, bf16[64,128]{1,0:T(8,128)(2,1)S(1)}, bf16[64,128]{1,0:T(8,128)(2,1)S(1)}) fusion(bf16[256,1,128]{2,0,1:T(8,128)(2,1)} %param.15, s32[]{:T(128)S(6)} %select_n.57, s32[]{:T(128)S(6)} %select_n.55, s32[]{:T(128)S(6)} %select_n.53, s32[]{:T(128)S(6)} %select_n.51), kind=kLoop, calls=%fused_computation.41 | loop fusion | bytes 131088 | tf_op jit(solution)/shard_map/stack | solution.py:179
  1.5 0.9 %pad_maximum_fusion.5 = (bf16[320,128]{1,0:T(8,128)(2,1)S(1)}, bf16[320,128]{1,0:T(8,128)(2,1)S(1)}, bf16[320,128]{1,0:T(8,128)(2,1)S(1)}) fusion(bf16[64,128]{1,0:T(8,128)(2,1)S(1)} %get-tuple-element.68, bf16[256,128]{1,0:T(8,128)(2,1)} %bitcast.80, bf16[64,128]{1,0:T(8,128)(2,1)S(1)} %get-tuple-element.67, bf16[64,128]{1,0:T(8,128)(2,1)S(1)} %get-tuple-element.66), kind=kLoop, calls=%fused_computation.26 | loop fusion | flops 409600 | bytes 360448 | tf_op jit(solution)/shard_map/concatenate | solution.py:173
  2.4 4.2 %collective-permute-start = (bf16[320,128]{1,0:T(8,128)(2,1)S(1)}, bf16[320,128]{1,0:T(8,128)(2,1)S(1)}, u32[]{:S(2)}, u32[]{:S(2)}) collective-permute-start(bf16[320,128]{1,0:T(8,128)(2,1)S(1)} %get-tuple-element.69), channel_id=1, source_target_pairs={{0,3},{1,0},{2,1},{3,2},{4,7},{5,4},{6,5},{7,6},{8,11},{9,8},{10,9... | collective-permute-start | bytes 245768 | tf_op jit(solution)/shard_map/ppermute | solution.py:172
  6.6 0.5 collective-permute-start.2
  7.0 1.7 %convolution_convert_fusion = bf16[128,9,256]{2,0,1:T(8,128)(2,1)S(1)} fusion(bf16[9,256,256]{2,1,0:T(8,128)(2,1)} %w_ref.1, bf16[256,1,128]{2,0,1:T(8,128)(2,1)} %param.15), kind=kOutput, calls=%fused_computation | convolution fusion | flops 151289856 | bytes 1835008 | tf_op jit(solution)/shard_map/koc,oij->cikj/dot_general | solution.py:161
  8.7 1.1 %copy.19.grad_ref = bf16[256,1152]{1,0:T(8,128)(2,1)} copy(bf16[256,1152]{0,1:T(8,128)(2,1)S(1)} %bitcast.77) | data formatting | bytes 1179648 | tf_op jit(solution)/shard_map/reshape;squeeze | solution.py:164
  10.8 0.6 reshape.159.tap_ref
  11.4 4.3 %shard_map.95 = (bf16[9,128,1152]{2,1,0:T(8,128)(2,1)}, f32[256,1152]{1,0:T(8,128)}) custom-call(f32[27,384]{1,0:T(8,128)} %reshape.159.tap_ref, bf16[256,1152]{1,0:T(8,128)(2,1)} %copy.19.grad_ref), custom_call_target="tpu_custom_call" | custom-call | tf_op jit(solution)/shard_map/pallas_call | solution.py:66
  15.7 1.6 %copy.20 = f32[256,1152]{0,1:T(8,128)S(1)} copy(f32[256,1152]{1,0:T(8,128)} %get-tuple-element.49) | data formatting | bytes 2359296 | tf_op jit(solution)/shard_map/pallas_call | solution.py:66
  17.4 4.5 %collective-permute-start.5 = (f32[256,384]{0,1:T(8,128)S(1)}, f32[256,384]{0,1:T(8,128)S(1)}, u32[]{:S(2)}, u32[]{:S(2)}) collective-permute-start(f32[256,384]{0,1:T(8,128)S(1)} %get-tuple-element.56), channel_id=1, source_target_pairs={{0,4},{4,8},{8,12},{1,5},{5,9},{9,13},{2,6},{6,10},{10,14},{3,7},{... | collective-permute-start | bytes 1179656 | tf_op jit(solution)/shard_map/ppermute | solution.py:191
  22.0 1.9 %collective-permute-start.6 = (f32[256,384]{0,1:T(8,128)S(1)}, f32[256,384]{0,1:T(8,128)S(1)}, u32[]{:S(2)}, u32[]{:S(2)}) collective-permute-start(f32[256,384]{0,1:T(8,128)S(1)} %get-tuple-element.57), channel_id=1, source_target_pairs={{4,0},{8,4},{12,8},{5,1},{9,5},{13,9},{6,2},{10,6},{14,10},{7,3},{... | collective-permute-start | bytes 1179656 | tf_op jit(solution)/shard_map/ppermute | solution.py:192
  24.0 3.6 %collective-permute-start.3 = (bf16[256,512]{1,0:T(8,128)(2,1)S(1)}, bf16[256,512]{1,0:T(8,128)(2,1)S(1)}, u32[]{:S(2)}, u32[]{:S(2)}) collective-permute-start(bf16[256,512]{1,0:T(8,128)(2,1)S(1)} %get-tuple-element.64), channel_id=1, source_target_pairs={{0,4},{4,8},{8,12},{1,5},{5,9},{9,13},{2,6},{6,10},{10,14},{3,7},{... | collective-permute-start | bytes 786440 | tf_op jit(solution)/shard_map/ppermute | solution.py:182
  27.7 1.9 %collective-permute-start.4 = (bf16[256,512]{1,0:T(8,128)(2,1)S(1)}, bf16[256,512]{1,0:T(8,128)(2,1)S(1)}, u32[]{:S(2)}, u32[]{:S(2)}) collective-permute-start(bf16[256,512]{1,0:T(8,128)(2,1)S(1)} %get-tuple-element.64), channel_id=1, source_target_pairs={{4,0},{8,4},{12,8},{5,1},{9,5},{13,9},{6,2},{10,6},{14,10},{7,3},{... | collective-permute-start | bytes 786440 | tf_op jit(solution)/shard_map/ppermute | solution.py:183
  29.7 0.6 pad_maximum_fusion.8.up_ref
  30.3 0.7 %collective-permute-done.3 = bf16[256,512]{1,0:T(8,128)(2,1)S(1)} collective-permute-done((bf16[256,512]{1,0:T(8,128)(2,1)S(1)}, bf16[256,512]{1,0:T(8,128)(2,1)S(1)}, u32[]{:S(2)}, u32[]{:S(2)}) %collective-permute-start.3) | collective-permute-done | bytes 262176 | tf_op jit(solution)/shard_map/ppermute | solution.py:182
  31.0 4.4 %collective-permute-done.4 = bf16[256,512]{1,0:T(8,128)(2,1)S(1)} collective-permute-done((bf16[256,512]{1,0:T(8,128)(2,1)S(1)}, bf16[256,512]{1,0:T(8,128)(2,1)S(1)}, u32[]{:S(2)}, u32[]{:S(2)}) %collective-permute-start.4) | collective-permute-done | bytes 262176 | tf_op jit(solution)/shard_map/ppermute | solution.py:183
  35.4 1.1 %fusion.ext_ref = bf16[3,256,768]{2,1,0:T(8,128)(2,1)} fusion(bf16[1,256,512]{2,1,0:T(8,128)(2,1)S(1)} %bitcast.79, bf16[1,256,512]{2,1,0:T(8,128)(2,1)S(1)} %get-tuple-element.63, bf16[1,256,512]{2,1,0:T(8,128)(2,1)S(1)} %bitcast.78), kind=kLoop, calls=%fused_computation.2 | loop fusion | flops 10616832 | bytes 1966080 | tf_op jit(solution)/shard_map/concatenate | solution.py:185
  36.5 8.6 %shard_map.96 = (bf16[256,128]{1,0:T(8,128)(2,1)}, f32[9,64,256]{2,1,0:T(8,128)}) custom-call(bf16[3,256,768]{2,1,0:T(8,128)(2,1)} %fusion.ext_ref, bf16[1152,1152]{1,0:T(8,128)(2,1)} %bitcast.82, bf16[9,256,256]{2,1,0:T(8,128)(2,1)} %w_ref.1, bf16[4,64,128]{2,1,0:T(8,128)(2,1)} %pad_maximum_fusion.8.up_ref), custom_call_target="tpu_custom_call" | custom-call | flops 3019898880 | bytes 5734400 | tf_op jit(solution)/shard_map/pallas_call | solution.py:144
  45.0 1.1 %constant_dynamic-slice_fusion.2 = (f32[9,16,256]{2,1,0:T(8,128)S(1)}, f32[9,16,256]{2,1,0:T(8,128)S(1)}, f32[9,16,256]{2,1,0:T(8,128)S(1)}) fusion(f32[9,64,256]{2,1,0:T(8,128)} %get-tuple-element.50, s32[]{:T(128)S(6)} %select_n.59, s32[]{:T(128)S(6)} %select_n.61, s32[]{:T(128)S(6)} %select_n.60), kind=kLoop, calls=%fused_computation.51 | loop fusion | bytes 884748 | tf_op jit(solution)/shard_map/dynamic_slice | solution.py:85
  46.3 1.8 %collective-permute-start.9 = (f32[9,16,256]{2,1,0:T(8,128)S(1)}, f32[9,16,256]{2,1,0:T(8,128)S(1)}, u32[]{:S(2)}, u32[]{:S(2)}) collective-permute-start(f32[9,16,256]{2,1,0:T(8,128)S(1)} %get-tuple-element.58), channel_id=1, source_target_pairs={{0,4},{4,0},{8,12},{12,8},{1,5},{5,1},{9,13},{13,9},{2,6},{6,2},{1... | collective-permute-start | bytes 442376 | tf_op jit(solution)/shard_map/ppermute | solution.py:86
  48.2 2.2 %collective-permute-start.7 = (f32[256,1,128]{0,2,1:T(8,128)S(1)}, f32[256,1,128]{0,2,1:T(8,128)S(1)}, u32[]{:S(2)}, u32[]{:S(2)}) collective-permute-start(f32[256,1,128]{0,2,1:T(8,128)S(1)} %get-tuple-element.61), channel_id=1, source_target_pairs={{0,1},{1,2},{2,3},{3,0},{4,5},{5,6},{6,7},{7,4},{8,9},{9,10},{10,1... | collective-permute-start | bytes 393224 | tf_op jit(solution)/shard_map/ppermute | solution.py:19
  50.4 1.1 %collective-permute-start.8 = (f32[256,1,128]{0,2,1:T(8,128)S(1)}, f32[256,1,128]{0,2,1:T(8,128)S(1)}, u32[]{:S(2)}, u32[]{:S(2)}) collective-permute-start(f32[256,1,128]{0,2,1:T(8,128)S(1)} %get-tuple-element.62), channel_id=1, source_target_pairs={{1,0},{2,1},{3,2},{0,3},{5,4},{6,5},{7,6},{4,7},{9,8},{10,9},{11,1... | collective-permute-start | bytes 393224 | tf_op jit(solution)/shard_map/ppermute | solution.py:21
  51.7 1.0 %collective-permute-done.11 = f32[9,16,256]{2,1,0:T(8,128)S(1)} collective-permute-done((f32[9,16,256]{2,1,0:T(8,128)S(1)}, f32[9,16,256]{2,1,0:T(8,128)S(1)}, u32[]{:S(2)}, u32[]{:S(2)}) %collective-permute-start.11) | collective-permute-done | bytes 147488 | tf_op jit(solution)/shard_map/ppermute | solution.py:86
  52.7 1.0 %constant_dynamic-update-slice_fusion.3 = (f32[9,64,256]{2,1,0:T(8,128)S(1)}, f32[9,16,256]{2,1,0:T(8,128)S(1)}) fusion(f32[9,64,256]{2,1,0:T(8,128)S(1)} %broadcast_in_dim.25, s32[]{:T(128)S(6)} %select_n.58, f32[9,16,256]{2,1,0:T(8,128)S(1)} %collective-permute-done.10, f32[9,16,256]{2,1,0:T(8,128)S(1)} %collective-permute-done.11, ...), kind=kLoop, calls=%fused_computation.48 | loop fusion | flops 110592 | bytes 884740 | tf_op jit(solution)/shard_map/dynamic_update_slice | solution.py:91
  53.7 1.7 %collective-permute-start.12 = (f32[9,16,256]{2,1,0:T(8,128)S(1)}, f32[9,16,256]{2,1,0:T(8,128)S(1)}, u32[]{:S(2)}, u32[]{:S(2)}) collective-permute-start(f32[9,16,256]{2,1,0:T(8,128)S(1)} %get-tuple-element.55), channel_id=1, source_target_pairs={{0,4},{4,0},{8,12},{12,8},{1,5},{5,1},{9,13},{13,9},{2,6},{6,2},{1... | collective-permute-start | bytes 442376 | tf_op jit(solution)/shard_map/ppermute | solution.py:93
  55.4 1.0 %collective-permute-start.13 = (f32[9,16,256]{2,1,0:T(8,128)S(1)}, f32[9,16,256]{2,1,0:T(8,128)S(1)}, u32[]{:S(2)}, u32[]{:S(2)}) collective-permute-start(f32[9,16,256]{2,1,0:T(8,128)S(1)} %get-tuple-element.55), channel_id=1, source_target_pairs={{0,8},{4,12},{8,0},{12,4},{1,9},{5,13},{9,1},{13,5},{2,10},{6,14},... | collective-permute-start | bytes 442376 | tf_op jit(solution)/shard_map/ppermute | solution.py:93
  56.4 0.7 %collective-permute-start.14 = (f32[9,16,256]{2,1,0:T(8,128)S(1)}, f32[9,16,256]{2,1,0:T(8,128)S(1)}, u32[]{:S(2)}, u32[]{:S(2)}) collective-permute-start(f32[9,16,256]{2,1,0:T(8,128)S(1)} %get-tuple-element.55), channel_id=1, source_target_pairs={{0,12},{4,8},{8,4},{12,0},{1,13},{5,9},{9,5},{13,1},{2,14},{6,10},... | collective-permute-start | bytes 442376 | tf_op jit(solution)/shard_map/ppermute | solution.py:93
  57.1 1.1 %collective-permute-done.8 = f32[256,1,128]{0,2,1:T(8,128)S(1)} collective-permute-done((f32[256,1,128]{0,2,1:T(8,128)S(1)}, f32[256,1,128]{0,2,1:T(8,128)S(1)}, u32[]{:S(2)}, u32[]{:S(2)}) %collective-permute-start.8) | collective-permute-done | bytes 131104 | tf_op jit(solution)/shard_map/ppermute | solution.py:21
  58.3 0.7 %copy.21 = bf16[256,1,128]{2,0,1:T(8,128)(2,1)} copy(bf16[256,1,128]{0,2,1:T(8,128)(2,1)S(1)} %fusion.12) | data formatting | bytes 131072
  59.0 1.8 %collective-permute-done.13 = f32[9,16,256]{2,1,0:T(8,128)S(1)} collective-permute-done((f32[9,16,256]{2,1,0:T(8,128)S(1)}, f32[9,16,256]{2,1,0:T(8,128)S(1)}, u32[]{:S(2)}, u32[]{:S(2)}) %collective-permute-start.13) | collective-permute-done | bytes 147488 | tf_op jit(solution)/shard_map/ppermute | solution.py:93
  60.8 3.3 %collective-permute-done.14 = f32[9,16,256]{2,1,0:T(8,128)S(1)} collective-permute-done((f32[9,16,256]{2,1,0:T(8,128)S(1)}, f32[9,16,256]{2,1,0:T(8,128)S(1)}, u32[]{:S(2)}, u32[]{:S(2)}) %collective-permute-start.14) | collective-permute-done | bytes 147488 | tf_op jit(solution)/shard_map/ppermute | solution.py:93
  64.2 0.8 %copy-done.1 = f32[9,64,256]{2,1,0:T(8,128)} copy-done((f32[9,64,256]{2,1,0:T(8,128)}, f32[9,64,256]{2,1,0:T(8,128)S(1)}, u32[]{:S(2)}) %copy-start.1) | copy-done | bytes 589848
  (40 shorter events, 1.0 us)
Async XLA Ops:
  0.6 9.9 %copy-start = (bf16[1,9,3,2,64]{4,3,2,1,0:T(2,128)(2,1)S(1)}, bf16[1,9,3,2,64]{4,3,2,1,0:T(2,128)(2,1)}, u32[]{:S(2)}) copy-start(bf16[1,9,3,2,64]{4,3,2,1,0:T(2,128)(2,1)} %param.17) | copy-start | bytes 20740
  2.4 21.5 %collective-permute-start = (bf16[320,128]{1,0:T(8,128)(2,1)S(1)}, bf16[320,128]{1,0:T(8,128)(2,1)S(1)}, u32[]{:S(2)}, u32[]{:S(2)}) collective-permute-start(bf16[320,128]{1,0:T(8,128)(2,1)S(1)} %get-tuple-element.69), channel_id=1, source_target_pairs={{0,3},{1,0},{2,1},{3,2},{4,7},{5,4},{6,5},{7,6},{8,11},{9,8},{10,9... | collective-permute-start | bytes 245768 | tf_op jit(solution)/shard_map/ppermute | solution.py:172
  6.6 17.4 %collective-permute-start.1 = (bf16[320,128]{1,0:T(8,128)(2,1)S(1)}, bf16[320,128]{1,0:T(8,128)(2,1)S(1)}, u32[]{:S(2)}, u32[]{:S(2)}) collective-permute-start(bf16[320,128]{1,0:T(8,128)(2,1)S(1)} %get-tuple-element.70), channel_id=1, source_target_pairs={{0,2},{1,3},{2,0},{3,1},{4,6},{5,7},{6,4},{7,5},{8,10},{9,11},{10,... | collective-permute-start | bytes 245768 | tf_op jit(solution)/shard_map/ppermute | solution.py:172
  6.6 3.2 %copy-start.3 = (s32[1,2]{1,0:T(1,128)S(1)}, s32[1,2]{1,0:T(1,128)}, u32[]{:S(2)}) copy-start(s32[1,2]{1,0:T(1,128)} %param.19) | copy-start | bytes 28
  6.6 17.4 %collective-permute-start.2 = (bf16[320,128]{1,0:T(8,128)(2,1)S(1)}, bf16[320,128]{1,0:T(8,128)(2,1)S(1)}, u32[]{:S(2)}, u32[]{:S(2)}) collective-permute-start(bf16[320,128]{1,0:T(8,128)(2,1)S(1)} %get-tuple-element.71), channel_id=1, source_target_pairs={{0,1},{1,2},{2,3},{3,0},{4,5},{5,6},{6,7},{7,4},{8,9},{9,10},{10,1... | collective-permute-start | bytes 245768 | tf_op jit(solution)/shard_map/ppermute | solution.py:172
  17.4 6.6 %copy-start.2 = (bf16[256,1,128]{2,0,1:T(8,128)(2,1)S(1)}, bf16[256,1,128]{2,0,1:T(8,128)(2,1)}, u32[]{:S(2)}) copy-start(bf16[256,1,128]{2,0,1:T(8,128)(2,1)} %param.14) | copy-start | bytes 196612
  17.4 30.6 %collective-permute-start.5 = (f32[256,384]{0,1:T(8,128)S(1)}, f32[256,384]{0,1:T(8,128)S(1)}, u32[]{:S(2)}, u32[]{:S(2)}) collective-permute-start(f32[256,384]{0,1:T(8,128)S(1)} %get-tuple-element.56), channel_id=1, source_target_pairs={{0,4},{4,8},{8,12},{1,5},{5,9},{9,13},{2,6},{6,10},{10,14},{3,7},{... | collective-permute-start | bytes 1179656 | tf_op jit(solution)/shard_map/ppermute | solution.py:191
  22.0 26.1 %collective-permute-start.6 = (f32[256,384]{0,1:T(8,128)S(1)}, f32[256,384]{0,1:T(8,128)S(1)}, u32[]{:S(2)}, u32[]{:S(2)}) collective-permute-start(f32[256,384]{0,1:T(8,128)S(1)} %get-tuple-element.57), channel_id=1, source_target_pairs={{4,0},{8,4},{12,8},{5,1},{9,5},{13,9},{6,2},{10,6},{14,10},{7,3},{... | collective-permute-start | bytes 1179656 | tf_op jit(solution)/shard_map/ppermute | solution.py:192
  24.0 6.9 %collective-permute-start.3 = (bf16[256,512]{1,0:T(8,128)(2,1)S(1)}, bf16[256,512]{1,0:T(8,128)(2,1)S(1)}, u32[]{:S(2)}, u32[]{:S(2)}) collective-permute-start(bf16[256,512]{1,0:T(8,128)(2,1)S(1)} %get-tuple-element.64), channel_id=1, source_target_pairs={{0,4},{4,8},{8,12},{1,5},{5,9},{9,13},{2,6},{6,10},{10,14},{3,7},{... | collective-permute-start | bytes 786440 | tf_op jit(solution)/shard_map/ppermute | solution.py:182
  27.7 7.7 %collective-permute-start.4 = (bf16[256,512]{1,0:T(8,128)(2,1)S(1)}, bf16[256,512]{1,0:T(8,128)(2,1)S(1)}, u32[]{:S(2)}, u32[]{:S(2)}) collective-permute-start(bf16[256,512]{1,0:T(8,128)(2,1)S(1)} %get-tuple-element.64), channel_id=1, source_target_pairs={{4,0},{8,4},{12,8},{5,1},{9,5},{13,9},{6,2},{10,6},{14,10},{7,3},{... | collective-permute-start | bytes 786440 | tf_op jit(solution)/shard_map/ppermute | solution.py:183
  46.1 5.5 %collective-permute-start.10 = (f32[9,16,256]{2,1,0:T(8,128)S(1)}, f32[9,16,256]{2,1,0:T(8,128)S(1)}, u32[]{:S(2)}, u32[]{:S(2)}) collective-permute-start(f32[9,16,256]{2,1,0:T(8,128)S(1)} %get-tuple-element.60), channel_id=1, source_target_pairs={{0,8},{4,12},{8,0},{12,4},{1,9},{5,13},{9,1},{13,5},{2,10},{6,14},... | collective-permute-start | bytes 442376 | tf_op jit(solution)/shard_map/ppermute | solution.py:86
  46.2 6.5 %collective-permute-start.11 = (f32[9,16,256]{2,1,0:T(8,128)S(1)}, f32[9,16,256]{2,1,0:T(8,128)S(1)}, u32[]{:S(2)}, u32[]{:S(2)}) collective-permute-start(f32[9,16,256]{2,1,0:T(8,128)S(1)} %get-tuple-element.59), channel_id=1, source_target_pairs={{0,12},{4,8},{8,4},{12,0},{1,13},{5,9},{9,5},{13,1},{2,14},{6,10},... | collective-permute-start | bytes 442376 | tf_op jit(solution)/shard_map/ppermute | solution.py:86
  46.3 6.4 %collective-permute-start.9 = (f32[9,16,256]{2,1,0:T(8,128)S(1)}, f32[9,16,256]{2,1,0:T(8,128)S(1)}, u32[]{:S(2)}, u32[]{:S(2)}) collective-permute-start(f32[9,16,256]{2,1,0:T(8,128)S(1)} %get-tuple-element.58), channel_id=1, source_target_pairs={{0,4},{4,0},{8,12},{12,8},{1,5},{5,1},{9,13},{13,9},{2,6},{6,2},{1... | collective-permute-start | bytes 442376 | tf_op jit(solution)/shard_map/ppermute | solution.py:86
  48.2 8.9 %collective-permute-start.7 = (f32[256,1,128]{0,2,1:T(8,128)S(1)}, f32[256,1,128]{0,2,1:T(8,128)S(1)}, u32[]{:S(2)}, u32[]{:S(2)}) collective-permute-start(f32[256,1,128]{0,2,1:T(8,128)S(1)} %get-tuple-element.61), channel_id=1, source_target_pairs={{0,1},{1,2},{2,3},{3,0},{4,5},{5,6},{6,7},{7,4},{8,9},{9,10},{10,1... | collective-permute-start | bytes 393224 | tf_op jit(solution)/shard_map/ppermute | solution.py:19
  50.4 7.8 %collective-permute-start.8 = (f32[256,1,128]{0,2,1:T(8,128)S(1)}, f32[256,1,128]{0,2,1:T(8,128)S(1)}, u32[]{:S(2)}, u32[]{:S(2)}) collective-permute-start(f32[256,1,128]{0,2,1:T(8,128)S(1)} %get-tuple-element.62), channel_id=1, source_target_pairs={{1,0},{2,1},{3,2},{0,3},{5,4},{6,5},{7,6},{4,7},{9,8},{10,9},{11,1... | collective-permute-start | bytes 393224 | tf_op jit(solution)/shard_map/ppermute | solution.py:21
  53.7 5.3 %collective-permute-start.12 = (f32[9,16,256]{2,1,0:T(8,128)S(1)}, f32[9,16,256]{2,1,0:T(8,128)S(1)}, u32[]{:S(2)}, u32[]{:S(2)}) collective-permute-start(f32[9,16,256]{2,1,0:T(8,128)S(1)} %get-tuple-element.55), channel_id=1, source_target_pairs={{0,4},{4,0},{8,12},{12,8},{1,5},{5,1},{9,13},{13,9},{2,6},{6,2},{1... | collective-permute-start | bytes 442376 | tf_op jit(solution)/shard_map/ppermute | solution.py:93
  55.4 5.4 %collective-permute-start.13 = (f32[9,16,256]{2,1,0:T(8,128)S(1)}, f32[9,16,256]{2,1,0:T(8,128)S(1)}, u32[]{:S(2)}, u32[]{:S(2)}) collective-permute-start(f32[9,16,256]{2,1,0:T(8,128)S(1)} %get-tuple-element.55), channel_id=1, source_target_pairs={{0,8},{4,12},{8,0},{12,4},{1,9},{5,13},{9,1},{13,5},{2,10},{6,14},... | collective-permute-start | bytes 442376 | tf_op jit(solution)/shard_map/ppermute | solution.py:93
  56.4 7.7 %collective-permute-start.14 = (f32[9,16,256]{2,1,0:T(8,128)S(1)}, f32[9,16,256]{2,1,0:T(8,128)S(1)}, u32[]{:S(2)}, u32[]{:S(2)}) collective-permute-start(f32[9,16,256]{2,1,0:T(8,128)S(1)} %get-tuple-element.55), channel_id=1, source_target_pairs={{0,12},{4,8},{8,4},{12,0},{1,13},{5,9},{9,5},{13,1},{2,14},{6,10},... | collective-permute-start | bytes 442376 | tf_op jit(solution)/shard_map/ppermute | solution.py:93
  64.1 0.8 %copy-start.1 = (f32[9,64,256]{2,1,0:T(8,128)}, f32[9,64,256]{2,1,0:T(8,128)S(1)}, u32[]{:S(2)}) copy-start(f32[9,64,256]{2,1,0:T(8,128)S(1)} %constant_dynamic-update-slice_fusion) | copy-start | bytes 1769476

commit v10 on v9

--- a/solution.py
+++ b/solution.py
@@ -165,38 +165,55 @@
     matrix, contrib = toeplitz(tap_table[0], lon_cols, grad_piece)
     o_block = upstream.shape[0] // n_lon
     up_row = upstream[:, 0]
+    terms = contrib.reshape(channels, 3, window_len)
+    left_rim = terms[:, :, :HALO].reshape(3 * channels, HALO)
+    right_rim = terms[:, :, HALO + lon_cols :].reshape(3 * channels, HALO)
+    interior = terms[:, :, HALO : HALO + lon_cols]
     blocks = [fields[:, 0]]
     up_parts = [lax.dynamic_slice_in_dim(up_row, lon_at * o_block, o_block, axis=0)]
     for d in range(1, n_lon):
         part = lax.dynamic_slice_in_dim(up_row, ((lon_at - d) % n_lon) * o_block, o_block, axis=0)
-        both = lax.ppermute(
-            jnp.concatenate([fields[:, 0], part], axis=0),
-            "lon",
-            [(p, (p - d) % n_lon) for p in range(n_lon)],
+        pieces = [fields[:, 0].astype(jnp.float32), part.astype(jnp.float32)]
+        if d == 1:
+            pieces.append(left_rim)
+        if d == n_lon - 1:
+            pieces.append(right_rim)
+        got = lax.ppermute(
+            jnp.concatenate(pieces, axis=0), "lon", [(p, (p - d) % n_lon) for p in range(n_lon)]
         )
-        blocks.append(both[:channels])
-        up_parts.append(both[channels:])
+        blocks.append(got[:channels].astype(jnp.bfloat16))
+        up_parts.append(got[channels : channels + o_block].astype(jnp.bfloat16))
+        at = channels + o_block
+        if d == 1:
+            rim = got[at : at + 3 * channels].reshape(channels, 3, HALO)
+            interior = interior.at[:, :, lon_cols - HALO :].add(rim)
+            at += 3 * channels
+        if d == n_lon - 1:
+            rim = got[at : at + 3 * channels].reshape(channels, 3, HALO)
+            interior = interior.at[:, :, :HALO].add(rim)
     up_rel = jnp.stack(up_parts, axis=0)
     row = jnp.concatenate(blocks, axis=1)
+    width = row.shape[1]
     count = lax.axis_size("lat")
-    below = lax.ppermute(row, "lat", [(i, i + 1) for i in range(count - 1)])
-    above = lax.ppermute(row, "lat", [(i + 1, i) for i in range(count - 1)])
-    rows = jnp.stack([below, row, above], axis=0)
-    ext = jnp.concatenate([rows[:, :, rows.shape[2] - HALO :], rows, rows[:, :, :HALO]], axis=2)
+    below = lax.ppermute(
+        jnp.concatenate([row.astype(jnp.float32), interior[:, 2]], axis=1),
+        "lat",
+        [(i, i + 1) for i in range(count - 1)],
+    )
+    above = lax.ppermute(
+        jnp.concatenate([row.astype(jnp.float32), interior[:, 0]], axis=1),
+        "lat",
+        [(i + 1, i) for i in range(count - 1)],
+    )
+    result = interior[:, 1] + below[:, width:] + above[:, width:]
+    result = result[:, None, :]
+    rows = jnp.stack(
+        [below[:, :width].astype(jnp.bfloat16), row, above[:, :width].astype(jnp.bfloat16)], axis=0
+    )
+    ext = jnp.concatenate([rows[:, :, width - HALO :], rows, rows[:, :, :HALO]], axis=2)
     out_row, grad_terms = row_products(ext, matrix, weights, up_rel)
     outputs = out_row[:, None, :]
     weight_grad = lat_allreduce(grad_terms, "lat", 1)
-    terms = contrib.reshape(channels, 3, window_len)
-    count = lax.axis_size("lat")
-    from_below = lax.ppermute(terms[:, 2], "lat", [(i, i + 1) for i in range(count - 1)])
-    from_above = lax.ppermute(terms[:, 0], "lat", [(i + 1, i) for i in range(count - 1)])
-    own = terms[:, 1] + from_below + from_above
-    rims = jnp.stack([own[:, :HALO], own[:, HALO + lon_cols :]], axis=1)
-    arrived = padded_2(rims, (("lon", 1),), 1, True)
-    result = own[:, HALO : HALO + lon_cols]
-    result = result.at[:, :HALO].add(arrived[:, 0])
-    result = result.at[:, lon_cols - HALO :].add(arrived[:, 3])
-    result = result[:, None, :]
     return (outputs, result.astype(jnp.bfloat16), weight_grad)
 
 

time: 65.6 us -> 95.3 us (1.45)
  waiting for transfers between devices: 12.6 us -> 46.9 us
  starting transfers between devices: 25.3 us -> 17 us
  other arithmetic: 3.8 us -> 6.12 us
  local copies, waits for them, and re-layouts: 6.97 us -> 8.32 us
    ppermute x9 -> x5, waiting for transfers between devices: 6.24 us -> 33.9 us  [the longest x3 24.6 us: body(): lax.ppermute(jnp.concatenate(pieces, axis=0), 'lon', [(p, (p - d) % n_lon...]
    ppermute x9 -> x5, starting transfers between devices: 20 us -> 12.7 us  [the longest x1 6.1 us: body(): lax.ppermute(jnp.concatenate([row.astype(jnp.float32), interior[:, 2]], a...]
    ppermute x3, waiting for transfers between devices: 1.22 us -> 7.28 us  [lat_allreduce(): parts.append(lax.ppermute(send, axis, [(i, i ^ d) for i in range(count)]))]
    slice x3 -> x10, local copies, waits for them, and re-layouts: 0.02 us -> 1.33 us  [the longest x5 0.75 us: body(): blocks.append(got[:channels].astype(jnp.bfloat16))]
    ppermute x3, starting transfers between devices: 3.36 us -> 2.35 us  [lat_allreduce(): recv = lax.ppermute(mine, axis, [(i, i ^ d) for i in range(count)])]
    concatenate x2 -> x4, other arithmetic: 1.96 us -> 2.08 us  [the longest x1 1.11 us: body(): jnp.concatenate([rows[:, :, width - HALO:], rows, rows[:, :, :HALO]], axi...]
  transfers between devices with their start and end apart: 15 -> 11, of which waited for: 7 -> 7; matrix products, arithmetic and copies ran while one was open for 16% -> 2% of each run, Pallas kernels for 20% -> 0%
where the time goes in v10:
time: 95.3 us; the launch traced here: 94.8 us
  waiting for transfers between devices  46.9 us (49%)
  starting transfers between devices  17 us (18%)
  Pallas kernels  12.9 us (14%)
  local copies, waits for them, and re-layouts  8.32 us (9%)
  other arithmetic  6.12 us (6%)
  matrix products  1.86 us (2%)
  between operations  1.74 us (2%)
    ppermute x3, waiting for transfers between devices, body(): lax.ppermute(jnp.concatenate(pieces, axis=0), 'lon', [(p, (p - d) % n_lon...  24.6 us
    pallas_call x1, Pallas kernels, row_products(): pl.pallas_call(row_kernel, out_shape=(jax.ShapeDtypeStruct((weights.shape...  8.55 us
    ppermute x3, waiting for transfers between devices, lat_allreduce(): parts.append(lax.ppermute(send, axis, [(i, i ^ d) for i in range(count)]))  7.28 us
    ppermute x1, starting transfers between devices, body(): lax.ppermute(jnp.concatenate([row.astype(jnp.float32), interior[:, 2]], a...  6.1 us
    ppermute x3, waiting for transfers between devices, lat_allreduce(): recv = lax.ppermute(mine, axis, [(i, i ^ d) for i in range(count)])  5.75 us
    ppermute x1, waiting for transfers between devices, body(): lax.ppermute(jnp.concatenate([row.astype(jnp.float32), interior[:, 2]], a...  4.89 us
    ppermute x3, starting transfers between devices, body(): lax.ppermute(jnp.concatenate(pieces, axis=0), 'lon', [(p, (p - d) % n_lon...  4.67 us
    ppermute x1, waiting for transfers between devices, body(): lax.ppermute(jnp.concatenate([row.astype(jnp.float32), interior[:, 0]], a...  4.38 us
  transfers between devices with their start and end apart: 11, of which 7 were waited for; matrix products, arithmetic and copies ran while one was open for 2% of the time, Pallas kernels for 0%

profile of v10, /device:TPU:1, one launch (start us, length us, event | category | flops | bytes accessed | tf_op | source)
XLA Modules:
  0.0 94.8 jit_solution(6098337897986859960)
XLA Ops:
  1.4 0.7 add_bitcast_fusion
  2.4 0.6 reshape.190.tap_ref
  3.0 0.8 bitcast_convert_fusion.3
  3.9 1.7 %convolution_convert_fusion = bf16[128,9,256]{2,0,1:T(8,128)(2,1)S(1)} fusion(bf16[9,256,256]{2,1,0:T(8,128)(2,1)} %w_ref.1, bf16[256,1,128]{2,0,1:T(8,128)(2,1)} %param.15), kind=kOutput, calls=%fused_computation | convolution fusion | flops 151289856 | bytes 1835008 | tf_op jit(solution)/shard_map/koc,oij->cikj/dot_general | solution.py:161
  5.5 1.1 %copy.16.grad_ref = bf16[256,1152]{1,0:T(8,128)(2,1)} copy(bf16[256,1152]{0,1:T(8,128)(2,1)S(1)} %bitcast.70) | data formatting | bytes 1179648 | tf_op jit(solution)/shard_map/reshape;squeeze | solution.py:164
  6.6 4.3 %shard_map.95 = (bf16[9,128,1152]{2,1,0:T(8,128)(2,1)}, f32[256,1152]{1,0:T(8,128)}) custom-call(f32[27,384]{1,0:T(8,128)} %reshape.190.tap_ref, bf16[256,1152]{1,0:T(8,128)(2,1)} %copy.16.grad_ref), custom_call_target="tpu_custom_call" | custom-call | tf_op jit(solution)/shard_map/pallas_call | solution.py:66
  10.9 1.6 %copy.17 = f32[256,1152]{0,1:T(8,128)S(1)} copy(f32[256,1152]{1,0:T(8,128)} %get-tuple-element.47) | data formatting | bytes 2359296 | tf_op jit(solution)/shard_map/pallas_call | solution.py:66
  12.6 0.2 copy.19
  13.7 0.9 fusion.4
  14.6 4.2 %collective-permute-start = (f32[1088,128]{1,0:T(8,128)}, f32[1088,128]{1,0:T(8,128)S(1)}, u32[]{:S(2)}, u32[]{:S(2)}) collective-permute-start(f32[1088,128]{1,0:T(8,128)} %get-tuple-element.65), channel_id=1, source_target_pairs={{0,3},{1,0},{2,1},{3,2},{4,7},{5,4},{6,5},{7,6},{8,11},{9,8},{10,9... | collective-permute-start | bytes 1671176 | tf_op jit(solution)/shard_map/ppermute | solution.py:181
  18.8 0.5 collective-permute-start.1
  19.5 24.6 %collective-permute-done.1 = bf16[320,128]{1,0:T(8,128)(2,1)S(1)} collective-permute-done((bf16[320,128]{1,0:T(8,128)(2,1)S(1)}, bf16[320,128]{1,0:T(8,128)(2,1)S(1)}, u32[]{:S(2)}, u32[]{:S(2)}) %collective-permute-start.1) | collective-permute-done | bytes 81952 | tf_op jit(solution)/shard_map/ppermute | solution.py:181
  44.3 0.4 copy-done.5
  45.1 0.7 slice-done
  46.1 6.1 %collective-permute-start.3 = (f32[256,640]{1,0:T(8,128)S(1)}, f32[256,640]{1,0:T(8,128)S(1)}, u32[]{:S(2)}, u32[]{:S(2)}) collective-permute-start(f32[256,640]{1,0:T(8,128)S(1)} %get-tuple-element.59), channel_id=1, source_target_pairs={{0,4},{4,8},{8,12},{1,5},{5,9},{9,13},{2,6},{6,10},{10,14},{3,7},{... | collective-permute-start | bytes 1966088 | tf_op jit(solution)/shard_map/ppermute | solution.py:198
  52.2 1.9 %collective-permute-start.4 = (f32[256,640]{1,0:T(8,128)S(1)}, f32[256,640]{1,0:T(8,128)S(1)}, u32[]{:S(2)}, u32[]{:S(2)}) collective-permute-start(f32[256,640]{1,0:T(8,128)S(1)} %get-tuple-element.60), channel_id=1, source_target_pairs={{4,0},{8,4},{12,8},{5,1},{9,5},{13,9},{6,2},{10,6},{14,10},{7,3},{... | collective-permute-start | bytes 1966088 | tf_op jit(solution)/shard_map/ppermute | solution.py:203
  54.2 0.6 pad_maximum_fusion.10.up_ref
  54.8 4.9 %collective-permute-done.3 = f32[256,640]{1,0:T(8,128)S(1)} collective-permute-done((f32[256,640]{1,0:T(8,128)S(1)}, f32[256,640]{1,0:T(8,128)S(1)}, u32[]{:S(2)}, u32[]{:S(2)}) %collective-permute-start.3) | collective-permute-done | bytes 655392 | tf_op jit(solution)/shard_map/ppermute | solution.py:198
  59.7 4.4 %collective-permute-done.4 = f32[256,640]{1,0:T(8,128)S(1)} collective-permute-done((f32[256,640]{1,0:T(8,128)S(1)}, f32[256,640]{1,0:T(8,128)S(1)}, u32[]{:S(2)}, u32[]{:S(2)}) %collective-permute-start.4) | collective-permute-done | bytes 655392 | tf_op jit(solution)/shard_map/ppermute | solution.py:203
  64.2 1.1 %fusion.ext_ref = bf16[3,256,768]{2,1,0:T(8,128)(2,1)} fusion(bf16[1,256,512]{2,1,0:T(8,128)(2,1)S(1)} %fusion.7, bf16[1,256,512]{2,1,0:T(8,128)(2,1)S(1)} %get-tuple-element.63, bf16[1,256,512]{2,1,0:T(8,128)(2,1)S(1)} %fusion.6), kind=kLoop, calls=%fused_computation.2 | loop fusion | flops 10616832 | bytes 1966080 | tf_op jit(solution)/shard_map/concatenate | solution.py:213
  65.3 8.5 %shard_map.96 = (bf16[256,128]{1,0:T(8,128)(2,1)}, f32[9,64,256]{2,1,0:T(8,128)}) custom-call(bf16[3,256,768]{2,1,0:T(8,128)(2,1)} %fusion.ext_ref, bf16[1152,1152]{1,0:T(8,128)(2,1)} %bitcast.72, bf16[9,256,256]{2,1,0:T(8,128)(2,1)} %w_ref.1, bf16[4,64,128]{2,1,0:T(8,128)(2,1)} %pad_maximum_fusion.10.up_ref), custom_call_target="tpu_custom_call" | custom-call | flops 3019898880 | bytes 5734400 | tf_op jit(solution)/shard_map/pallas_call | solution.py:144
  73.8 1.1 %constant_dynamic-slice_fusion.2 = (f32[9,16,256]{2,1,0:T(8,128)S(1)}, f32[9,16,256]{2,1,0:T(8,128)S(1)}, f32[9,16,256]{2,1,0:T(8,128)S(1)}) fusion(f32[9,64,256]{2,1,0:T(8,128)} %get-tuple-element.50, s32[]{:T(128)S(6)} %select_n.59, s32[]{:T(128)S(6)} %select_n.61, s32[]{:T(128)S(6)} %select_n.60), kind=kLoop, calls=%fused_computation.59 | loop fusion | bytes 884748 | tf_op jit(solution)/shard_map/dynamic_slice | solution.py:85
  75.1 1.8 %collective-permute-start.6 = (f32[9,16,256]{2,1,0:T(8,128)S(1)}, f32[9,16,256]{2,1,0:T(8,128)S(1)}, u32[]{:S(2)}, u32[]{:S(2)}) collective-permute-start(f32[9,16,256]{2,1,0:T(8,128)S(1)} %get-tuple-element.58), channel_id=1, source_target_pairs={{0,8},{4,12},{8,0},{12,4},{1,9},{5,13},{9,1},{13,5},{2,10},{6,14},... | collective-permute-start | bytes 442376 | tf_op jit(solution)/shard_map/ppermute | solution.py:86
  76.9 4.3 %collective-permute-done.7 = f32[9,16,256]{2,1,0:T(8,128)S(1)} collective-permute-done((f32[9,16,256]{2,1,0:T(8,128)S(1)}, f32[9,16,256]{2,1,0:T(8,128)S(1)}, u32[]{:S(2)}, u32[]{:S(2)}) %collective-permute-start.7) | collective-permute-done | bytes 147488 | tf_op jit(solution)/shard_map/ppermute | solution.py:86
  81.2 2.9 %collective-permute-done.6 = f32[9,16,256]{2,1,0:T(8,128)S(1)} collective-permute-done((f32[9,16,256]{2,1,0:T(8,128)S(1)}, f32[9,16,256]{2,1,0:T(8,128)S(1)}, u32[]{:S(2)}, u32[]{:S(2)}) %collective-permute-start.6) | collective-permute-done | bytes 147488 | tf_op jit(solution)/shard_map/ppermute | solution.py:86
  84.2 1.0 %constant_dynamic-update-slice_fusion.3 = (f32[9,64,256]{2,1,0:T(8,128)S(1)}, f32[9,16,256]{2,1,0:T(8,128)S(1)}) fusion(f32[9,64,256]{2,1,0:T(8,128)S(1)} %broadcast_in_dim.25, s32[]{:T(128)S(6)} %select_n.58, f32[9,16,256]{2,1,0:T(8,128)S(1)} %collective-permute-done.6, f32[9,16,256]{2,1,0:T(8,128)S(1)} %collective-permute-done.7, ...), kind=kLoop, calls=%fused_computation.56 | loop fusion | flops 110592 | bytes 884740 | tf_op jit(solution)/shard_map/dynamic_update_slice | solution.py:91
  85.2 0.7 collective-permute-start.8
  86.0 0.7 fusion.13
  86.6 1.6 %collective-permute-start.10 = (f32[9,16,256]{2,1,0:T(8,128)S(1)}, f32[9,16,256]{2,1,0:T(8,128)S(1)}, u32[]{:S(2)}, u32[]{:S(2)}) collective-permute-start(f32[9,16,256]{2,1,0:T(8,128)S(1)} %get-tuple-element.52), channel_id=1, source_target_pairs={{0,12},{4,8},{8,4},{12,0},{1,13},{5,9},{9,5},{13,1},{2,14},{6,10},... | collective-permute-start | bytes 442376 | tf_op jit(solution)/shard_map/ppermute | solution.py:93
  88.2 1.8 %collective-permute-done.9 = f32[9,16,256]{2,1,0:T(8,128)S(1)} collective-permute-done((f32[9,16,256]{2,1,0:T(8,128)S(1)}, f32[9,16,256]{2,1,0:T(8,128)S(1)}, u32[]{:S(2)}, u32[]{:S(2)}) %collective-permute-start.9) | collective-permute-done | bytes 147488 | tf_op jit(solution)/shard_map/ppermute | solution.py:93
  90.0 4.0 %collective-permute-done.10 = f32[9,16,256]{2,1,0:T(8,128)S(1)} collective-permute-done((f32[9,16,256]{2,1,0:T(8,128)S(1)}, f32[9,16,256]{2,1,0:T(8,128)S(1)}, u32[]{:S(2)}, u32[]{:S(2)}) %collective-permute-start.10) | collective-permute-done | bytes 147488 | tf_op jit(solution)/shard_map/ppermute | solution.py:93
  94.0 0.8 copy-done.1
  (57 shorter events, 2.6 us)
Async XLA Ops:
  0.6 1.5 %copy-start = (bf16[1,9,3,2,64]{4,3,2,1,0:T(2,128)(2,1)S(1)}, bf16[1,9,3,2,64]{4,3,2,1,0:T(2,128)(2,1)}, u32[]{:S(2)}) copy-start(bf16[1,9,3,2,64]{4,3,2,1,0:T(2,128)(2,1)} %param.17) | copy-start | bytes 20740
  12.9 0.8 copy-start.7
  14.6 29.5 %collective-permute-start = (f32[1088,128]{1,0:T(8,128)}, f32[1088,128]{1,0:T(8,128)S(1)}, u32[]{:S(2)}, u32[]{:S(2)}) collective-permute-start(f32[1088,128]{1,0:T(8,128)} %get-tuple-element.65), channel_id=1, source_target_pairs={{0,3},{1,0},{2,1},{3,2},{4,7},{5,4},{6,5},{7,6},{8,11},{9,8},{10,9... | collective-permute-start | bytes 1671176 | tf_op jit(solution)/shard_map/ppermute | solution.py:181
  18.8 25.9 %collective-permute-start.2 = (f32[1088,128]{1,0:T(8,128)S(1)}, f32[1088,128]{1,0:T(8,128)S(1)}, u32[]{:S(2)}, u32[]{:S(2)}) collective-permute-start(f32[1088,128]{1,0:T(8,128)S(1)} %get-tuple-element.66), channel_id=1, source_target_pairs={{0,1},{1,2},{2,3},{3,0},{4,5},{5,6},{6,7},{7,4},{8,9},{9,10},{10,1... | collective-permute-start | bytes 1671176 | tf_op jit(solution)/shard_map/ppermute | solution.py:181
  18.8 25.3 %collective-permute-start.1 = (bf16[320,128]{1,0:T(8,128)(2,1)S(1)}, bf16[320,128]{1,0:T(8,128)(2,1)S(1)}, u32[]{:S(2)}, u32[]{:S(2)}) collective-permute-start(bf16[320,128]{1,0:T(8,128)(2,1)S(1)} %pad_maximum_fusion.9), channel_id=1, source_target_pairs={{0,2},{1,3},{2,0},{3,1},{4,6},{5,7},{6,4},{7,5},{8,10},{9,11},{10,... | collective-permute-start | bytes 245768 | tf_op jit(solution)/shard_map/ppermute | solution.py:181
  44.1 0.6 copy-start.5
  44.1 0.7 copy-start.2
  45.0 0.8 slice-start
  45.0 0.9 copy-start.4
  45.0 0.9 slice-start.1
  46.0 6.2 %copy-start.6 = (bf16[320,128]{1,0:T(8,128)(2,1)S(1)}, bf16[320,128]{1,0:T(8,128)(2,1)}, u32[]{:S(2)}) copy-start(bf16[320,128]{1,0:T(8,128)(2,1)} %copy-done.5) | copy-start | bytes 245764
  46.0 8.2 %copy-start.3 = (bf16[1088,128]{1,0:T(8,128)(2,1)S(1)}, bf16[1088,128]{1,0:T(8,128)(2,1)}, u32[]{:S(2)}) copy-start(bf16[1088,128]{1,0:T(8,128)(2,1)} %copy-done.2) | copy-start | bytes 835588
  46.1 13.6 %collective-permute-start.3 = (f32[256,640]{1,0:T(8,128)S(1)}, f32[256,640]{1,0:T(8,128)S(1)}, u32[]{:S(2)}, u32[]{:S(2)}) collective-permute-start(f32[256,640]{1,0:T(8,128)S(1)} %get-tuple-element.59), channel_id=1, source_target_pairs={{0,4},{4,8},{8,12},{1,5},{5,9},{9,13},{2,6},{6,10},{10,14},{3,7},{... | collective-permute-start | bytes 1966088 | tf_op jit(solution)/shard_map/ppermute | solution.py:198
  52.2 11.9 %collective-permute-start.4 = (f32[256,640]{1,0:T(8,128)S(1)}, f32[256,640]{1,0:T(8,128)S(1)}, u32[]{:S(2)}, u32[]{:S(2)}) collective-permute-start(f32[256,640]{1,0:T(8,128)S(1)} %get-tuple-element.60), channel_id=1, source_target_pairs={{4,0},{8,4},{12,8},{5,1},{9,5},{13,9},{6,2},{10,6},{14,10},{7,3},{... | collective-permute-start | bytes 1966088 | tf_op jit(solution)/shard_map/ppermute | solution.py:203
  74.9 1.9 %collective-permute-start.5 = (f32[9,16,256]{2,1,0:T(8,128)S(1)}, f32[9,16,256]{2,1,0:T(8,128)S(1)}, u32[]{:S(2)}, u32[]{:S(2)}) collective-permute-start(f32[9,16,256]{2,1,0:T(8,128)S(1)} %get-tuple-element.56), channel_id=1, source_target_pairs={{0,4},{4,0},{8,12},{12,8},{1,5},{5,1},{9,13},{13,9},{2,6},{6,2},{1... | collective-permute-start | bytes 442376 | tf_op jit(solution)/shard_map/ppermute | solution.py:86
  75.0 6.2 %collective-permute-start.7 = (f32[9,16,256]{2,1,0:T(8,128)S(1)}, f32[9,16,256]{2,1,0:T(8,128)S(1)}, u32[]{:S(2)}, u32[]{:S(2)}) collective-permute-start(f32[9,16,256]{2,1,0:T(8,128)S(1)} %get-tuple-element.57), channel_id=1, source_target_pairs={{0,12},{4,8},{8,4},{12,0},{1,13},{5,9},{9,5},{13,1},{2,14},{6,10},... | collective-permute-start | bytes 442376 | tf_op jit(solution)/shard_map/ppermute | solution.py:86
  75.1 9.1 %collective-permute-start.6 = (f32[9,16,256]{2,1,0:T(8,128)S(1)}, f32[9,16,256]{2,1,0:T(8,128)S(1)}, u32[]{:S(2)}, u32[]{:S(2)}) collective-permute-start(f32[9,16,256]{2,1,0:T(8,128)S(1)} %get-tuple-element.58), channel_id=1, source_target_pairs={{0,8},{4,12},{8,0},{12,4},{1,9},{5,13},{9,1},{13,5},{2,10},{6,14},... | collective-permute-start | bytes 442376 | tf_op jit(solution)/shard_map/ppermute | solution.py:86
  85.2 4.8 %collective-permute-start.9 = (f32[9,16,256]{2,1,0:T(8,128)S(1)}, f32[9,16,256]{2,1,0:T(8,128)S(1)}, u32[]{:S(2)}, u32[]{:S(2)}) collective-permute-start(f32[9,16,256]{2,1,0:T(8,128)S(1)} %get-tuple-element.52), channel_id=1, source_target_pairs={{0,8},{4,12},{8,0},{12,4},{1,9},{5,13},{9,1},{13,5},{2,10},{6,14},... | collective-permute-start | bytes 442376 | tf_op jit(solution)/shard_map/ppermute | solution.py:93
  85.2 2.9 %collective-permute-start.8 = (f32[9,16,256]{2,1,0:T(8,128)S(1)}, f32[9,16,256]{2,1,0:T(8,128)S(1)}, u32[]{:S(2)}, u32[]{:S(2)}) collective-permute-start(f32[9,16,256]{2,1,0:T(8,128)S(1)} %get-tuple-element.52), channel_id=1, source_target_pairs={{0,4},{4,0},{8,12},{12,8},{1,5},{5,1},{9,13},{13,9},{2,6},{6,2},{1... | collective-permute-start | bytes 442376 | tf_op jit(solution)/shard_map/ppermute | solution.py:93
  86.6 7.3 %collective-permute-start.10 = (f32[9,16,256]{2,1,0:T(8,128)S(1)}, f32[9,16,256]{2,1,0:T(8,128)S(1)}, u32[]{:S(2)}, u32[]{:S(2)}) collective-permute-start(f32[9,16,256]{2,1,0:T(8,128)S(1)} %get-tuple-element.52), channel_id=1, source_target_pairs={{0,12},{4,8},{8,4},{12,0},{1,13},{5,9},{9,5},{13,1},{2,14},{6,10},... | collective-permute-start | bytes 442376 | tf_op jit(solution)/shard_map/ppermute | solution.py:93
  94.0 0.8 copy-start.1

commit v11 on v6

--- a/solution.py
+++ b/solution.py
@@ -73,26 +73,33 @@
     return out.reshape(kernels * out_width, stencil_rows * window_len), contrib
 
 
+def group_allreduce(x, axis, dim, stride, count):
+    size = lax.axis_size(axis)
+    parts = [x]
+    for e in range(1, count):
+        parts.append(lax.ppermute(x, axis, [(i, i ^ (stride * e)) for i in range(size)]))
+    while len(parts) > 1:
+        parts = [parts[2 * e] + parts[2 * e + 1] for e in range(len(parts) // 2)]
+    return parts[0]
+
+
 def lat_allreduce(x, axis, dim):
     count = lax.axis_size(axis)
     steps = count.bit_length() - 1
-    if (1 << steps) != count or x.shape[dim] % count:
+    if (1 << steps) != count or x.shape[dim] % 2 or count < 4:
         return lax.psum(x, axis)
     index = lax.axis_index(axis)
-    size = x.shape[dim] // count
-    parts = [lax.dynamic_slice_in_dim(x, index * size, size, axis=dim)]
-    for d in range(1, count):
-        send = lax.dynamic_slice_in_dim(x, (index ^ d) * size, size, axis=dim)
-        parts.append(lax.ppermute(send, axis, [(i, i ^ d) for i in range(count)]))
-    for s in range(steps):
-        parts = [parts[2 * e] + parts[2 * e + 1] for e in range(len(parts) // 2)]
-    mine = parts[0]
+    partner = [(i, i ^ 1) for i in range(count)]
+    half = x.shape[dim] // 2
+    bit = index & 1
+    keep = lax.dynamic_slice_in_dim(x, bit * half, half, axis=dim)
+    send = lax.dynamic_slice_in_dim(x, (1 - bit) * half, half, axis=dim)
+    mine = keep + lax.ppermute(send, axis, partner)
+    mine = group_allreduce(mine, axis, dim, 2, count // 2)
+    other = lax.ppermute(mine, axis, partner)
     out = jnp.zeros(x.shape, x.dtype)
-    out = lax.dynamic_update_slice_in_dim(out, mine, index * size, axis=dim)
-    for d in range(1, count):
-        recv = lax.ppermute(mine, axis, [(i, i ^ d) for i in range(count)])
-        out = lax.dynamic_update_slice_in_dim(out, recv, (index ^ d) * size, axis=dim)
-    return out
+    out = lax.dynamic_update_slice_in_dim(out, mine, bit * half, axis=dim)
+    return lax.dynamic_update_slice_in_dim(out, other, (1 - bit) * half, axis=dim)
 
 
 def row_kernel(ext_ref, mt_ref, w_ref, up_ref, out_ref, gt_ref):

time: 63.9 us -> 73.3 us (1.15)
  waiting for transfers between devices: 12 us -> 26 us
  starting transfers between devices: 24.1 us -> 18.9 us
    ppermute x2, waiting for transfers between devices: 0.01 us -> 13.2 us  [padded_2(): lax.ppermute(head, axis, [((i + 1) % count, i) for i in range(ends)])]
    ppermute x2, waiting for transfers between devices: 0.01 us -> 7.66 us  [padded_2(): lax.ppermute(tail, axis, [(i, (i + 1) % count) for i in range(ends)])]
    ppermute x6 -> x3, waiting for transfers between devices: 6.61 us -> 0.01 us  [the longest x1 0.01 us: lat_allreduce(): mine = keep + lax.ppermute(send, axis, partner)]
    ppermute x6 -> x3, starting transfers between devices: 4.82 us -> 0.14 us  [the longest x1 0.07 us: group_allreduce(): lax.ppermute(x, axis, [(i, i ^ stride * e) for i in range(size)])]
    add x0 -> x1, other arithmetic: none -> 1 us  [lat_allreduce(): mine = keep + lax.ppermute(send, axis, partner)]
    dynamic_update_slice x1, other arithmetic: 0.97 us -> 0.05 us  [lat_allreduce(): out = lax.dynamic_update_slice_in_dim(out, mine, bit * half, axis=dim)]
    unnamed x9 -> x11, local copies, waits for them, and re-layouts: 1.56 us -> 1.56 us
  transfers between devices with their start and end apart: 15 -> 12, of which waited for: 5 -> 5; matrix products, arithmetic and copies ran while one was open for 16% -> 11% of each run, Pallas kernels for 20% -> 6%
where the time goes in v11:
time: 73.3 us; the launch traced here: 72.9 us
  waiting for transfers between devices  26 us (35%)
  starting transfers between devices  18.9 us (26%)
  Pallas kernels  12.9 us (18%)
  local copies, waits for them, and re-layouts  7.69 us (10%)
  other arithmetic  3.9 us (5%)
  matrix products  1.87 us (3%)
  between operations  1.63 us (2%)
    ppermute x2, waiting for transfers between devices, padded_2(): lax.ppermute(head, axis, [((i + 1) % count, i) for i in range(ends)])  13.2 us
    pallas_call x1, Pallas kernels, row_products(): pl.pallas_call(row_kernel, out_shape=(jax.ShapeDtypeStruct((weights.shape...  8.55 us
    ppermute x2, waiting for transfers between devices, padded_2(): lax.ppermute(tail, axis, [(i, (i + 1) % count) for i in range(ends)])  7.66 us
    ppermute x3, starting transfers between devices, body(): lax.ppermute(jnp.concatenate([fields[:, 0], part], axis=0), 'lon', [(p, (...  4.66 us
    ppermute x1, starting transfers between devices, body(): below = lax.ppermute(row, 'lat', [(i, i + 1) for i in range(count - 1)])  4.52 us
    ppermute x2, starting transfers between devices, padded_2(): lax.ppermute(tail, axis, [(i, (i + 1) % count) for i in range(ends)])  4.52 us
    ppermute x1, waiting for transfers between devices, body(): above = lax.ppermute(row, 'lat', [(i + 1, i) for i in range(count - 1)])  4.4 us
    pallas_call x1, Pallas kernels, toeplitz(): pl.pallas_call(toeplitz_kernel, out_shape=(jax.ShapeDtypeStruct((kernels,...  4.32 us
  transfers between devices with their start and end apart: 12, of which 5 were waited for; matrix products, arithmetic and copies ran while one was open for 11% of the time, Pallas kernels for 6%

profile of v11, /device:TPU:1, one launch (start us, length us, event | category | flops | bytes accessed | tf_op | source)
XLA Modules:
  0.0 72.9 jit_solution(14491797497127261193)
XLA Ops:
  0.7 0.8 %dynamic-slice_bitcast_fusion = (bf16[1,64,128]{2,1,0:T(8,128)(2,1)S(1)}, bf16[64,128]{1,0:T(8,128)(2,1)S(1)}, bf16[64,128]{1,0:T(8,128)(2,1)S(1)}, bf16[64,128]{1,0:T(8,128)(2,1)S(1)}) fusion(bf16[256,1,128]{2,0,1:T(8,128)(2,1)} %param.23, s32[]{:T(128)S(6)} %select_n.49, s32[]{:T(128)S(6)} %select_n.47, s32[]{:T(128)S(6)} %select_n.45, s32[]{:T(128)S(6)} %select_n.43), kind=kLoop, calls=%fused_computation.35 | loop fusion | bytes 131088 | tf_op jit(solution)/shard_map/stack | solution.py:186
  1.5 0.9 %pad_maximum_fusion.5 = (bf16[320,128]{1,0:T(8,128)(2,1)S(1)}, bf16[320,128]{1,0:T(8,128)(2,1)S(1)}, bf16[320,128]{1,0:T(8,128)(2,1)S(1)}) fusion(bf16[64,128]{1,0:T(8,128)(2,1)S(1)} %get-tuple-element.109, bf16[256,128]{1,0:T(8,128)(2,1)} %bitcast.56, bf16[64,128]{1,0:T(8,128)(2,1)S(1)} %get-tuple-element.108, bf16[64,128]{1,0:T(8,128)(2,1)S(1)} %get-tuple-element.107), kind=kLoop, calls=%fused_computation.21 | loop fusion | flops 409600 | bytes 360448 | tf_op jit(solution)/shard_map/concatenate | solution.py:180
  2.4 4.2 %collective-permute-start = (bf16[320,128]{1,0:T(8,128)(2,1)S(1)}, bf16[320,128]{1,0:T(8,128)(2,1)S(1)}, u32[]{:S(2)}, u32[]{:S(2)}) collective-permute-start(bf16[320,128]{1,0:T(8,128)(2,1)S(1)} %get-tuple-element.110), channel_id=1, source_target_pairs={{0,3},{1,0},{2,1},{3,2},{4,7},{5,4},{6,5},{7,6},{8,11},{9,8},{10,9... | collective-permute-start | bytes 245768 | tf_op jit(solution)/shard_map/ppermute | solution.py:179
  6.6 0.5 collective-permute-start.2
  7.0 1.7 %convolution_convert_fusion = bf16[128,9,256]{2,0,1:T(8,128)(2,1)S(1)} fusion(bf16[9,256,256]{2,1,0:T(8,128)(2,1)} %w_ref.1, bf16[256,1,128]{2,0,1:T(8,128)(2,1)} %param.23), kind=kOutput, calls=%fused_computation | convolution fusion | flops 151289856 | bytes 1835008 | tf_op jit(solution)/shard_map/koc,oij->cikj/dot_general | solution.py:168
  8.7 1.1 %copy.19.grad_ref = bf16[256,1152]{1,0:T(8,128)(2,1)} copy(bf16[256,1152]{0,1:T(8,128)(2,1)S(1)} %bitcast.53) | data formatting | bytes 1179648 | tf_op jit(solution)/shard_map/reshape;squeeze | solution.py:171
  9.8 0.1 iota_add_fusion
  10.5 0.2 fusion.3
  10.8 0.6 reshape.252.tap_ref
  11.4 4.3 %shard_map.100 = (bf16[9,128,1152]{2,1,0:T(8,128)(2,1)}, f32[256,1152]{1,0:T(8,128)}) custom-call(f32[27,384]{1,0:T(8,128)} %reshape.252.tap_ref, bf16[256,1152]{1,0:T(8,128)(2,1)} %copy.19.grad_ref), custom_call_target="tpu_custom_call" | custom-call | tf_op jit(solution)/shard_map/pallas_call | solution.py:66
  15.7 1.7 %copy.20 = f32[256,1152]{0,1:T(8,128)S(1)} copy(f32[256,1152]{1,0:T(8,128)} %get-tuple-element.93) | data formatting | bytes 2359296 | tf_op jit(solution)/shard_map/pallas_call | solution.py:66
  17.5 4.5 %collective-permute-start.3 = (bf16[256,512]{1,0:T(8,128)(2,1)S(1)}, bf16[256,512]{1,0:T(8,128)(2,1)S(1)}, u32[]{:S(2)}, u32[]{:S(2)}) collective-permute-start(bf16[256,512]{1,0:T(8,128)(2,1)S(1)} %get-tuple-element.105), channel_id=1, source_target_pairs={{0,4},{4,8},{8,12},{1,5},{5,9},{9,13},{2,6},{6,10},{10,14},{3,7},{... | collective-permute-start | bytes 786440 | tf_op jit(solution)/shard_map/ppermute | solution.py:189
  22.1 1.9 %collective-permute-start.4 = (bf16[256,512]{1,0:T(8,128)(2,1)S(1)}, bf16[256,512]{1,0:T(8,128)(2,1)S(1)}, u32[]{:S(2)}, u32[]{:S(2)}) collective-permute-start(bf16[256,512]{1,0:T(8,128)(2,1)S(1)} %get-tuple-element.105), channel_id=1, source_target_pairs={{4,0},{8,4},{12,8},{5,1},{9,5},{13,9},{6,2},{10,6},{14,10},{7,3},{... | collective-permute-start | bytes 786440 | tf_op jit(solution)/shard_map/ppermute | solution.py:190
  24.0 0.6 pad_maximum_fusion.8.up_ref
  24.7 0.7 collective-permute-done.3
  25.4 4.4 %collective-permute-done.4 = bf16[256,512]{1,0:T(8,128)(2,1)S(1)} collective-permute-done((bf16[256,512]{1,0:T(8,128)(2,1)S(1)}, bf16[256,512]{1,0:T(8,128)(2,1)S(1)}, u32[]{:S(2)}, u32[]{:S(2)}) %collective-permute-start.4) | collective-permute-done | bytes 262176 | tf_op jit(solution)/shard_map/ppermute | solution.py:190
  29.8 1.1 %fusion.ext_ref = bf16[3,256,768]{2,1,0:T(8,128)(2,1)} fusion(bf16[1,256,512]{2,1,0:T(8,128)(2,1)S(1)} %bitcast.55, bf16[1,256,512]{2,1,0:T(8,128)(2,1)S(1)} %get-tuple-element.104, bf16[1,256,512]{2,1,0:T(8,128)(2,1)S(1)} %bitcast.54), kind=kLoop, calls=%fused_computation.2 | loop fusion | flops 10616832 | bytes 1966080 | tf_op jit(solution)/shard_map/concatenate | solution.py:192
  30.9 8.6 %shard_map.101 = (bf16[256,128]{1,0:T(8,128)(2,1)}, f32[9,64,256]{2,1,0:T(8,128)}) custom-call(bf16[3,256,768]{2,1,0:T(8,128)(2,1)} %fusion.ext_ref, bf16[1152,1152]{1,0:T(8,128)(2,1)} %bitcast.58, bf16[9,256,256]{2,1,0:T(8,128)(2,1)} %w_ref.1, bf16[4,64,128]{2,1,0:T(8,128)(2,1)} %pad_maximum_fusion.8.up_ref), custom_call_target="tpu_custom_call" | custom-call | flops 3019898880 | bytes 5734400 | tf_op jit(solution)/shard_map/pallas_call | solution.py:151
  39.4 1.8 %constant_dynamic-slice_fusion = f32[9,32,256]{2,1,0:T(8,128)} fusion(f32[9,64,256]{2,1,0:T(8,128)} %get-tuple-element.94, s32[]{:T(128)S(6)} %select_n.51), kind=kLoop, calls=%fused_computation.41 | loop fusion | bytes 589828 | tf_op jit(solution)/shard_map/dynamic_slice | solution.py:96
  41.2 0.1 fusion.20
  41.3 2.2 %collective-permute-start.5 = (f32[256,3,128]{0,2,1:T(8,128)S(1)}, f32[256,3,128]{0,2,1:T(8,128)S(1)}, u32[]{:S(2)}, u32[]{:S(2)}) collective-permute-start(f32[256,3,128]{0,2,1:T(8,128)S(1)} %get-tuple-element.100), channel_id=1, source_target_pairs={{0,1},{1,2},{2,3},{3,0},{4,5},{5,6},{6,7},{7,4},{8,9},{9,10},{10,1... | collective-permute-start | bytes 1179656 | tf_op jit(solution)/shard_map/ppermute | solution.py:19
  43.5 1.1 %collective-permute-start.6 = (f32[256,3,128]{0,2,1:T(8,128)S(1)}, f32[256,3,128]{0,2,1:T(8,128)S(1)}, u32[]{:S(2)}, u32[]{:S(2)}) collective-permute-start(f32[256,3,128]{0,2,1:T(8,128)S(1)} %get-tuple-element.101), channel_id=1, source_target_pairs={{1,0},{2,1},{3,2},{0,3},{5,4},{6,5},{7,6},{4,7},{9,8},{10,9},{11,1... | collective-permute-start | bytes 1179656 | tf_op jit(solution)/shard_map/ppermute | solution.py:21
  44.6 1.0 %dynamic-slice_add_fusion = f32[9,32,256]{2,1,0:T(8,128)S(1)} fusion(f32[9,32,256]{2,1,0:T(8,128)} %collective-permute-done.9, f32[9,64,256]{2,1,0:T(8,128)S(1)} %copy-done.1, s32[]{:T(128)S(6)} %select_n.50), kind=kLoop, calls=%fused_computation.12 | loop fusion | flops 73728 | bytes 884740 | tf_op jit(solution)/shard_map/add | solution.py:97
  45.6 0.1 collective-permute-start.10
  45.7 7.7 %collective-permute-done.5 = f32[256,3,128]{0,2,1:T(8,128)S(1)} collective-permute-done((f32[256,3,128]{0,2,1:T(8,128)S(1)}, f32[256,3,128]{0,2,1:T(8,128)S(1)}, u32[]{:S(2)}, u32[]{:S(2)}) %collective-permute-start.5) | collective-permute-done | bytes 393248 | tf_op jit(solution)/shard_map/ppermute | solution.py:19
  53.3 9.2 %collective-permute-done.6 = f32[256,3,128]{0,2,1:T(8,128)S(1)} collective-permute-done((f32[256,3,128]{0,2,1:T(8,128)S(1)}, f32[256,3,128]{0,2,1:T(8,128)S(1)}, u32[]{:S(2)}, u32[]{:S(2)}) %collective-permute-start.6) | collective-permute-done | bytes 393248 | tf_op jit(solution)/shard_map/ppermute | solution.py:21
  62.6 0.1 fusion.4
  62.7 2.3 %collective-permute-start.7 = (f32[256,1,128]{0,2,1:T(8,128)S(1)}, f32[256,1,128]{0,2,1:T(8,128)S(1)}, u32[]{:S(2)}, u32[]{:S(2)}) collective-permute-start(f32[256,1,128]{0,2,1:T(8,128)S(1)} %get-tuple-element.102), channel_id=1, source_target_pairs={{0,4},{4,8},{8,12},{1,5},{5,9},{9,13},{2,6},{6,10},{10,14},{3,7},{... | collective-permute-start | bytes 393224 | tf_op jit(solution)/shard_map/ppermute | solution.py:19
  65.0 2.1 %collective-permute-start.8 = (f32[256,1,128]{0,2,1:T(8,128)S(1)}, f32[256,1,128]{0,2,1:T(8,128)S(1)}, u32[]{:S(2)}, u32[]{:S(2)}) collective-permute-start(f32[256,1,128]{0,2,1:T(8,128)S(1)} %get-tuple-element.103), channel_id=1, source_target_pairs={{4,0},{8,4},{12,8},{5,1},{9,5},{13,9},{6,2},{10,6},{14,10},{7,3},{... | collective-permute-start | bytes 393224 | tf_op jit(solution)/shard_map/ppermute | solution.py:21
  67.2 4.0 %collective-permute-done.8 = f32[256,1,128]{0,2,1:T(8,128)S(1)} collective-permute-done((f32[256,1,128]{0,2,1:T(8,128)S(1)}, f32[256,1,128]{0,2,1:T(8,128)S(1)}, u32[]{:S(2)}, u32[]{:S(2)}) %collective-permute-start.8) | collective-permute-done | bytes 131104 | tf_op jit(solution)/shard_map/ppermute | solution.py:21
  71.3 0.7 %copy.21 = bf16[256,1,128]{2,0,1:T(8,128)(2,1)} copy(bf16[256,1,128]{0,2,1:T(8,128)(2,1)S(1)} %fusion.6) | data formatting | bytes 131072
  72.0 0.8 %copy-done.2 = f32[9,64,256]{2,1,0:T(8,128)} copy-done((f32[9,64,256]{2,1,0:T(8,128)}, f32[9,64,256]{2,1,0:T(8,128)S(1)}, u32[]{:S(2)}) %copy-start.2) | copy-done | bytes 589848
  (35 shorter events, 0.4 us)
Async XLA Ops:
  0.6 9.9 %copy-start = (bf16[1,9,3,2,64]{4,3,2,1,0:T(2,128)(2,1)S(1)}, bf16[1,9,3,2,64]{4,3,2,1,0:T(2,128)(2,1)}, u32[]{:S(2)}) copy-start(bf16[1,9,3,2,64]{4,3,2,1,0:T(2,128)(2,1)} %param.25) | copy-start | bytes 20740
  2.4 15.0 %collective-permute-start = (bf16[320,128]{1,0:T(8,128)(2,1)S(1)}, bf16[320,128]{1,0:T(8,128)(2,1)S(1)}, u32[]{:S(2)}, u32[]{:S(2)}) collective-permute-start(bf16[320,128]{1,0:T(8,128)(2,1)S(1)} %get-tuple-element.110), channel_id=1, source_target_pairs={{0,3},{1,0},{2,1},{3,2},{4,7},{5,4},{6,5},{7,6},{8,11},{9,8},{10,9... | collective-permute-start | bytes 245768 | tf_op jit(solution)/shard_map/ppermute | solution.py:179
  6.6 10.9 %collective-permute-start.1 = (bf16[320,128]{1,0:T(8,128)(2,1)S(1)}, bf16[320,128]{1,0:T(8,128)(2,1)S(1)}, u32[]{:S(2)}, u32[]{:S(2)}) collective-permute-start(bf16[320,128]{1,0:T(8,128)(2,1)S(1)} %get-tuple-element.111), channel_id=1, source_target_pairs={{0,2},{1,3},{2,0},{3,1},{4,6},{5,7},{6,4},{7,5},{8,10},{9,11},{10,... | collective-permute-start | bytes 245768 | tf_op jit(solution)/shard_map/ppermute | solution.py:179
  6.6 10.9 %collective-permute-start.2 = (bf16[320,128]{1,0:T(8,128)(2,1)S(1)}, bf16[320,128]{1,0:T(8,128)(2,1)S(1)}, u32[]{:S(2)}, u32[]{:S(2)}) collective-permute-start(bf16[320,128]{1,0:T(8,128)(2,1)S(1)} %get-tuple-element.112), channel_id=1, source_target_pairs={{0,1},{1,2},{2,3},{3,0},{4,5},{5,6},{6,7},{7,4},{8,9},{9,10},{10,1... | collective-permute-start | bytes 245768 | tf_op jit(solution)/shard_map/ppermute | solution.py:179
  7.0 2.7 %copy-start.4 = (s32[1,2]{1,0:T(1,128)S(1)}, s32[1,2]{1,0:T(1,128)}, u32[]{:S(2)}) copy-start(s32[1,2]{1,0:T(1,128)} %param.27) | copy-start | bytes 28
  15.7 1.8 %copy-start.3 = (bf16[256,1,128]{2,0,1:T(8,128)(2,1)S(1)}, bf16[256,1,128]{2,0,1:T(8,128)(2,1)}, u32[]{:S(2)}) copy-start(bf16[256,1,128]{2,0,1:T(8,128)(2,1)} %param.22) | copy-start | bytes 196612
  17.5 7.8 %collective-permute-start.3 = (bf16[256,512]{1,0:T(8,128)(2,1)S(1)}, bf16[256,512]{1,0:T(8,128)(2,1)S(1)}, u32[]{:S(2)}, u32[]{:S(2)}) collective-permute-start(bf16[256,512]{1,0:T(8,128)(2,1)S(1)} %get-tuple-element.105), channel_id=1, source_target_pairs={{0,4},{4,8},{8,12},{1,5},{5,9},{9,13},{2,6},{6,10},{10,14},{3,7},{... | collective-permute-start | bytes 786440 | tf_op jit(solution)/shard_map/ppermute | solution.py:189
  22.1 7.7 %collective-permute-start.4 = (bf16[256,512]{1,0:T(8,128)(2,1)S(1)}, bf16[256,512]{1,0:T(8,128)(2,1)S(1)}, u32[]{:S(2)}, u32[]{:S(2)}) collective-permute-start(bf16[256,512]{1,0:T(8,128)(2,1)S(1)} %get-tuple-element.105), channel_id=1, source_target_pairs={{4,0},{8,4},{12,8},{5,1},{9,5},{13,9},{6,2},{10,6},{14,10},{7,3},{... | collective-permute-start | bytes 786440 | tf_op jit(solution)/shard_map/ppermute | solution.py:190
  39.4 5.2 %copy-start.1 = (f32[9,64,256]{2,1,0:T(8,128)S(1)}, f32[9,64,256]{2,1,0:T(8,128)}, u32[]{:S(2)}) copy-start(f32[9,64,256]{2,1,0:T(8,128)} %get-tuple-element.94) | copy-start | bytes 1769476
  41.2 3.4 %collective-permute-start.9 = (f32[9,32,256]{2,1,0:T(8,128)}, f32[9,32,256]{2,1,0:T(8,128)}, u32[]{:S(2)}, u32[]{:S(2)}) collective-permute-start(f32[9,32,256]{2,1,0:T(8,128)} %constant_dynamic-slice_fusion), channel_id=1, source_target_pairs={{0,4},{4,0},{8,12},{12,8},{1,5},{5,1},{9,13},{13,9},{2,6},{6,2},{1... | collective-permute-start | bytes 884744 | tf_op jit(solution)/shard_map/ppermute | solution.py:97
  41.3 12.1 %collective-permute-start.5 = (f32[256,3,128]{0,2,1:T(8,128)S(1)}, f32[256,3,128]{0,2,1:T(8,128)S(1)}, u32[]{:S(2)}, u32[]{:S(2)}) collective-permute-start(f32[256,3,128]{0,2,1:T(8,128)S(1)} %get-tuple-element.100), channel_id=1, source_target_pairs={{0,1},{1,2},{2,3},{3,0},{4,5},{5,6},{6,7},{7,4},{8,9},{9,10},{10,1... | collective-permute-start | bytes 1179656 | tf_op jit(solution)/shard_map/ppermute | solution.py:19
  43.5 19.0 %collective-permute-start.6 = (f32[256,3,128]{0,2,1:T(8,128)S(1)}, f32[256,3,128]{0,2,1:T(8,128)S(1)}, u32[]{:S(2)}, u32[]{:S(2)}) collective-permute-start(f32[256,3,128]{0,2,1:T(8,128)S(1)} %get-tuple-element.101), channel_id=1, source_target_pairs={{1,0},{2,1},{3,2},{0,3},{5,4},{6,5},{7,6},{4,7},{9,8},{10,9},{11,1... | collective-permute-start | bytes 1179656 | tf_op jit(solution)/shard_map/ppermute | solution.py:21
  45.6 21.4 %collective-permute-start.10 = (f32[9,32,256]{2,1,0:T(8,128)S(1)}, f32[9,32,256]{2,1,0:T(8,128)S(1)}, u32[]{:S(2)}, u32[]{:S(2)}) collective-permute-start(f32[9,32,256]{2,1,0:T(8,128)S(1)} %dynamic-slice_add_fusion), channel_id=1, source_target_pairs={{0,8},{4,12},{8,0},{12,4},{1,9},{5,13},{9,1},{13,5},{2,10},{6,14},... | collective-permute-start | bytes 884744 | tf_op jit(solution)/shard_map/ppermute | solution.py:80
  62.7 4.5 %collective-permute-start.7 = (f32[256,1,128]{0,2,1:T(8,128)S(1)}, f32[256,1,128]{0,2,1:T(8,128)S(1)}, u32[]{:S(2)}, u32[]{:S(2)}) collective-permute-start(f32[256,1,128]{0,2,1:T(8,128)S(1)} %get-tuple-element.102), channel_id=1, source_target_pairs={{0,4},{4,8},{8,12},{1,5},{5,9},{9,13},{2,6},{6,10},{10,14},{3,7},{... | collective-permute-start | bytes 393224 | tf_op jit(solution)/shard_map/ppermute | solution.py:19
  65.0 6.3 %collective-permute-start.8 = (f32[256,1,128]{0,2,1:T(8,128)S(1)}, f32[256,1,128]{0,2,1:T(8,128)S(1)}, u32[]{:S(2)}, u32[]{:S(2)}) collective-permute-start(f32[256,1,128]{0,2,1:T(8,128)S(1)} %get-tuple-element.103), channel_id=1, source_target_pairs={{4,0},{8,4},{12,8},{5,1},{9,5},{13,9},{6,2},{10,6},{14,10},{7,3},{... | collective-permute-start | bytes 393224 | tf_op jit(solution)/shard_map/ppermute | solution.py:21
  67.1 4.9 %collective-permute-start.11 = (f32[9,32,256]{2,1,0:T(8,128)S(1)}, f32[9,32,256]{2,1,0:T(8,128)S(1)}, u32[]{:S(2)}, u32[]{:S(2)}) collective-permute-start(f32[9,32,256]{2,1,0:T(8,128)S(1)} %get-tuple-element.99), channel_id=1, source_target_pairs={{0,4},{4,0},{8,12},{12,8},{1,5},{5,1},{9,13},{13,9},{2,6},{6,2},{1... | collective-permute-start | bytes 884744 | tf_op jit(solution)/shard_map/ppermute | solution.py:99
  72.0 0.8 %copy-start.2 = (f32[9,64,256]{2,1,0:T(8,128)}, f32[9,64,256]{2,1,0:T(8,128)S(1)}, u32[]{:S(2)}) copy-start(f32[9,64,256]{2,1,0:T(8,128)S(1)} %constant_dynamic-update-slice_fusion) | copy-start | bytes 1769476

commit v12 on v6

--- a/solution.py
+++ b/solution.py
@@ -95,23 +95,20 @@
     return out
 
 
-def row_kernel(ext_ref, mt_ref, w_ref, up_ref, out_ref, gt_ref):
+def row_kernel(ext_ref, mt_ref, w_ref, up_ref, out_ref, gt_ref, m_ref):
     stencil_rows, channels, _ = ext_ref.shape
     n_blocks, o_block, lon_cols = up_ref.shape
     kernels = w_ref.shape[0]
     window_len = mt_ref.shape[1] // stencil_rows
     contract_last = (((1,), (1,)), ((), ()))
     gt_ref[...] = jnp.zeros(gt_ref.shape, gt_ref.dtype)
+    for r in range(stencil_rows):
+        m_ref[r] = mt_ref[:, pl.ds(r * window_len, window_len)].T
     for d in range(n_blocks):
         acc = None
         for r in range(stencil_rows):
             win = ext_ref[r, :, pl.ds(d * lon_cols, window_len)]
-            part = lax.dot_general(
-                win,
-                mt_ref[:, pl.ds(r * window_len, window_len)],
-                contract_last,
-                preferred_element_type=jnp.float32,
-            )
+            part = jnp.dot(win, m_ref[r], preferred_element_type=jnp.float32)
             acc = part if acc is None else acc + part
         resp = acc.astype(jnp.bfloat16)
         up_d = up_ref[d]
@@ -147,6 +144,7 @@
             jax.ShapeDtypeStruct((weights.shape[1], lon_cols), jnp.bfloat16),
             jax.ShapeDtypeStruct((kernels, o_block, channels), jnp.float32),
         ),
+        scratch_shapes=[pltpu.VMEM((stencil_rows, matrix.shape[1] // stencil_rows, matrix.shape[0]), matrix.dtype)],
         cost_estimate=pl.CostEstimate(flops=flops, transcendentals=0, bytes_accessed=nbytes),
     )(ext, matrix, weights, up_rel)
 

time: 63.9 us -> 63.9 us (level)
  no operation moved by 1% of the time
where the time goes in v12:
time: 63.9 us; the launch traced here: 63.3 us
  starting transfers between devices  24.1 us (38%)
  Pallas kernels  12.9 us (20%)
  waiting for transfers between devices  12 us (19%)
  local copies, waits for them, and re-layouts  6.99 us (11%)
  other arithmetic  3.8 us (6%)
  matrix products  1.86 us (3%)
  between operations  1.62 us (3%)
    pallas_call x1, Pallas kernels, row_products(): pl.pallas_call(row_kernel, out_shape=(jax.ShapeDtypeStruct((weights.shape...  8.6 us
    ppermute x3, waiting for transfers between devices, lat_allreduce(): recv = lax.ppermute(mine, axis, [(i, i ^ d) for i in range(count)])  6.21 us
    ppermute x1, starting transfers between devices, body(): below = lax.ppermute(row, 'lat', [(i, i + 1) for i in range(count - 1)])  5.08 us
    ppermute x1, waiting for transfers between devices, body(): above = lax.ppermute(row, 'lat', [(i + 1, i) for i in range(count - 1)])  4.69 us
    ppermute x3, starting transfers between devices, body(): lax.ppermute(jnp.concatenate([fields[:, 0], part], axis=0), 'lon', [(p, (...  4.66 us
    pallas_call x1, Pallas kernels, toeplitz(): pl.pallas_call(toeplitz_kernel, out_shape=(jax.ShapeDtypeStruct((kernels,...  4.32 us
    ppermute x2, starting transfers between devices, padded_2(): lax.ppermute(tail, axis, [(i, (i + 1) % count) for i in range(ends)])  4.17 us
    ppermute x2, starting transfers between devices, padded_2(): lax.ppermute(head, axis, [((i + 1) % count, i) for i in range(ends)])  3.47 us
  transfers between devices with their start and end apart: 15, of which 5 were waited for; matrix products, arithmetic and copies ran while one was open for 16% of the time, Pallas kernels for 20%

profile of v12, /device:TPU:1, one launch (start us, length us, event | category | flops | bytes accessed | tf_op | source)
XLA Modules:
  0.0 63.3 jit_solution(14831420741219731991)
XLA Ops:
  0.7 0.8 %dynamic-slice_bitcast_fusion = (bf16[1,64,128]{2,1,0:T(8,128)(2,1)S(1)}, bf16[64,128]{1,0:T(8,128)(2,1)S(1)}, bf16[64,128]{1,0:T(8,128)(2,1)S(1)}, bf16[64,128]{1,0:T(8,128)(2,1)S(1)}) fusion(bf16[256,1,128]{2,0,1:T(8,128)(2,1)} %param.23, s32[]{:T(128)S(6)} %select_n.57, s32[]{:T(128)S(6)} %select_n.55, s32[]{:T(128)S(6)} %select_n.53, s32[]{:T(128)S(6)} %select_n.51), kind=kLoop, calls=%fused_computation.35 | loop fusion | bytes 131088 | tf_op jit(solution)/shard_map/stack | solution.py:177
  1.5 0.9 %pad_maximum_fusion.5 = (bf16[320,128]{1,0:T(8,128)(2,1)S(1)}, bf16[320,128]{1,0:T(8,128)(2,1)S(1)}, bf16[320,128]{1,0:T(8,128)(2,1)S(1)}) fusion(bf16[64,128]{1,0:T(8,128)(2,1)S(1)} %get-tuple-element.112, bf16[256,128]{1,0:T(8,128)(2,1)} %bitcast.56, bf16[64,128]{1,0:T(8,128)(2,1)S(1)} %get-tuple-element.111, bf16[64,128]{1,0:T(8,128)(2,1)S(1)} %get-tuple-element.110), kind=kLoop, calls=%fused_computation.21 | loop fusion | flops 409600 | bytes 360448 | tf_op jit(solution)/shard_map/concatenate | solution.py:171
  2.4 4.2 %collective-permute-start = (bf16[320,128]{1,0:T(8,128)(2,1)S(1)}, bf16[320,128]{1,0:T(8,128)(2,1)S(1)}, u32[]{:S(2)}, u32[]{:S(2)}) collective-permute-start(bf16[320,128]{1,0:T(8,128)(2,1)S(1)} %get-tuple-element.113), channel_id=1, source_target_pairs={{0,3},{1,0},{2,1},{3,2},{4,7},{5,4},{6,5},{7,6},{8,11},{9,8},{10,9... | collective-permute-start | bytes 245768 | tf_op jit(solution)/shard_map/ppermute | solution.py:170
  6.6 0.5 collective-permute-start.2
  7.0 1.7 %convolution_convert_fusion = bf16[128,9,256]{2,0,1:T(8,128)(2,1)S(1)} fusion(bf16[9,256,256]{2,1,0:T(8,128)(2,1)} %w_ref.1, bf16[256,1,128]{2,0,1:T(8,128)(2,1)} %param.23), kind=kOutput, calls=%fused_computation | convolution fusion | flops 151289856 | bytes 1835008 | tf_op jit(solution)/shard_map/koc,oij->cikj/dot_general | solution.py:159
  8.7 1.1 %copy.19.grad_ref = bf16[256,1152]{1,0:T(8,128)(2,1)} copy(bf16[256,1152]{0,1:T(8,128)(2,1)S(1)} %bitcast.53) | data formatting | bytes 1179648 | tf_op jit(solution)/shard_map/reshape;squeeze | solution.py:162
  10.5 0.2 fusion.3
  10.8 0.6 %reshape.252.tap_ref = f32[27,384]{1,0:T(8,128)} reshape(f32[9,3,384]{2,1,0:T(4,128)S(1)} %copy.17) | data formatting | bytes 82944 | tf_op jit(solution)/shard_map/reshape | solution.py:65
  11.4 4.3 %shard_map.100 = (bf16[9,128,1152]{2,1,0:T(8,128)(2,1)}, f32[256,1152]{1,0:T(8,128)}) custom-call(f32[27,384]{1,0:T(8,128)} %reshape.252.tap_ref, bf16[256,1152]{1,0:T(8,128)(2,1)} %copy.19.grad_ref), custom_call_target="tpu_custom_call" | custom-call | tf_op jit(solution)/shard_map/pallas_call | solution.py:66
  15.7 1.6 %copy.20 = f32[256,1152]{0,1:T(8,128)S(1)} copy(f32[256,1152]{1,0:T(8,128)} %get-tuple-element.93) | data formatting | bytes 2359296 | tf_op jit(solution)/shard_map/pallas_call | solution.py:66
  17.5 2.3 %collective-permute-start.5 = (f32[256,3,128]{0,2,1:T(8,128)S(1)}, f32[256,3,128]{0,2,1:T(8,128)S(1)}, u32[]{:S(2)}, u32[]{:S(2)}) collective-permute-start(f32[256,3,128]{0,2,1:T(8,128)S(1)} %get-tuple-element.100), channel_id=1, source_target_pairs={{0,1},{1,2},{2,3},{3,0},{4,5},{5,6},{6,7},{7,4},{8,9},{9,10},{10,1... | collective-permute-start | bytes 1179656 | tf_op jit(solution)/shard_map/ppermute | solution.py:19
  19.7 1.1 %collective-permute-start.6 = (f32[256,3,128]{0,2,1:T(8,128)S(1)}, f32[256,3,128]{0,2,1:T(8,128)S(1)}, u32[]{:S(2)}, u32[]{:S(2)}) collective-permute-start(f32[256,3,128]{0,2,1:T(8,128)S(1)} %get-tuple-element.101), channel_id=1, source_target_pairs={{1,0},{2,1},{3,2},{0,3},{5,4},{6,5},{7,6},{4,7},{9,8},{10,9},{11,1... | collective-permute-start | bytes 1179656 | tf_op jit(solution)/shard_map/ppermute | solution.py:21
  20.9 5.1 %collective-permute-start.3 = (bf16[256,512]{1,0:T(8,128)(2,1)S(1)}, bf16[256,512]{1,0:T(8,128)(2,1)S(1)}, u32[]{:S(2)}, u32[]{:S(2)}) collective-permute-start(bf16[256,512]{1,0:T(8,128)(2,1)S(1)} %get-tuple-element.108), channel_id=1, source_target_pairs={{0,4},{4,8},{8,12},{1,5},{5,9},{9,13},{2,6},{6,10},{10,14},{3,7},{... | collective-permute-start | bytes 786440 | tf_op jit(solution)/shard_map/ppermute | solution.py:180
  26.0 1.9 %collective-permute-start.4 = (bf16[256,512]{1,0:T(8,128)(2,1)S(1)}, bf16[256,512]{1,0:T(8,128)(2,1)S(1)}, u32[]{:S(2)}, u32[]{:S(2)}) collective-permute-start(bf16[256,512]{1,0:T(8,128)(2,1)S(1)} %get-tuple-element.108), channel_id=1, source_target_pairs={{4,0},{8,4},{12,8},{5,1},{9,5},{13,9},{6,2},{10,6},{14,10},{7,3},{... | collective-permute-start | bytes 786440 | tf_op jit(solution)/shard_map/ppermute | solution.py:181
  27.9 0.6 %pad_maximum_fusion.8.up_ref = bf16[4,64,128]{2,1,0:T(8,128)(2,1)} fusion(bf16[1,64,128]{2,1,0:T(8,128)(2,1)S(1)} %slice_bitcast_fusion, bf16[1,64,128]{2,1,0:T(8,128)(2,1)S(1)} %slice_bitcast_fusion.1, bf16[1,64,128]{2,1,0:T(8,128)(2,1)S(1)} %slice_bitcast_fusion.2, bf16[1,64,128]{2,1,0:T(8,128)(2,1)S(1)} %get-tuple-element.109), kind=kLoop, calls=%fused_computation.24 | loop fusion | flops 98304 | bytes 131072 | tf_op jit(solution)/shard_map/stack | solution.py:177
  28.6 0.7 %collective-permute-done.3 = bf16[256,512]{1,0:T(8,128)(2,1)S(1)} collective-permute-done((bf16[256,512]{1,0:T(8,128)(2,1)S(1)}, bf16[256,512]{1,0:T(8,128)(2,1)S(1)}, u32[]{:S(2)}, u32[]{:S(2)}) %collective-permute-start.3) | collective-permute-done | bytes 262176 | tf_op jit(solution)/shard_map/ppermute | solution.py:180
  29.3 4.7 %collective-permute-done.4 = bf16[256,512]{1,0:T(8,128)(2,1)S(1)} collective-permute-done((bf16[256,512]{1,0:T(8,128)(2,1)S(1)}, bf16[256,512]{1,0:T(8,128)(2,1)S(1)}, u32[]{:S(2)}, u32[]{:S(2)}) %collective-permute-start.4) | collective-permute-done | bytes 262176 | tf_op jit(solution)/shard_map/ppermute | solution.py:181
  34.0 1.1 %fusion.ext_ref = bf16[3,256,768]{2,1,0:T(8,128)(2,1)} fusion(bf16[1,256,512]{2,1,0:T(8,128)(2,1)S(1)} %bitcast.55, bf16[1,256,512]{2,1,0:T(8,128)(2,1)S(1)} %get-tuple-element.107, bf16[1,256,512]{2,1,0:T(8,128)(2,1)S(1)} %bitcast.54), kind=kLoop, calls=%fused_computation.2 | loop fusion | flops 10616832 | bytes 1966080 | tf_op jit(solution)/shard_map/concatenate | solution.py:183
  35.1 8.6 %shard_map.101 = (bf16[256,128]{1,0:T(8,128)(2,1)}, f32[9,64,256]{2,1,0:T(8,128)}) custom-call(bf16[3,256,768]{2,1,0:T(8,128)(2,1)} %fusion.ext_ref, bf16[1152,1152]{1,0:T(8,128)(2,1)} %bitcast.58, bf16[9,256,256]{2,1,0:T(8,128)(2,1)} %w_ref.1, bf16[4,64,128]{2,1,0:T(8,128)(2,1)} %pad_maximum_fusion.8.up_ref), custom_call_target="tpu_custom_call" | custom-call | flops 3019898880 | bytes 5734400 | tf_op jit(solution)/shard_map/pallas_call | solution.py:141
  43.7 1.1 %constant_dynamic-slice_fusion.2 = (f32[9,16,256]{2,1,0:T(8,128)S(1)}, f32[9,16,256]{2,1,0:T(8,128)S(1)}, f32[9,16,256]{2,1,0:T(8,128)S(1)}) fusion(f32[9,64,256]{2,1,0:T(8,128)} %get-tuple-element.94, s32[]{:T(128)S(6)} %select_n.59, s32[]{:T(128)S(6)} %select_n.61, s32[]{:T(128)S(6)} %select_n.60), kind=kLoop, calls=%fused_computation.45 | loop fusion | bytes 884748 | tf_op jit(solution)/shard_map/dynamic_slice | solution.py:85
  44.9 1.8 %collective-permute-start.9 = (f32[9,16,256]{2,1,0:T(8,128)S(1)}, f32[9,16,256]{2,1,0:T(8,128)S(1)}, u32[]{:S(2)}, u32[]{:S(2)}) collective-permute-start(f32[9,16,256]{2,1,0:T(8,128)S(1)} %get-tuple-element.102), channel_id=1, source_target_pairs={{0,4},{4,0},{8,12},{12,8},{1,5},{5,1},{9,13},{13,9},{2,6},{6,2},{1... | collective-permute-start | bytes 442376 | tf_op jit(solution)/shard_map/ppermute | solution.py:86
  46.8 1.9 %collective-permute-start.7 = (f32[256,1,128]{0,2,1:T(8,128)S(1)}, f32[256,1,128]{0,2,1:T(8,128)S(1)}, u32[]{:S(2)}, u32[]{:S(2)}) collective-permute-start(f32[256,1,128]{0,2,1:T(8,128)S(1)} %get-tuple-element.105), channel_id=1, source_target_pairs={{0,4},{4,8},{8,12},{1,5},{5,9},{9,13},{2,6},{6,10},{10,14},{3,7},{... | collective-permute-start | bytes 393224 | tf_op jit(solution)/shard_map/ppermute | solution.py:19
  48.7 2.4 %collective-permute-start.8 = (f32[256,1,128]{0,2,1:T(8,128)S(1)}, f32[256,1,128]{0,2,1:T(8,128)S(1)}, u32[]{:S(2)}, u32[]{:S(2)}) collective-permute-start(f32[256,1,128]{0,2,1:T(8,128)S(1)} %get-tuple-element.106), channel_id=1, source_target_pairs={{4,0},{8,4},{12,8},{5,1},{9,5},{13,9},{6,2},{10,6},{14,10},{7,3},{... | collective-permute-start | bytes 393224 | tf_op jit(solution)/shard_map/ppermute | solution.py:21
  51.1 0.4 collective-permute-done.11
  51.6 1.0 %constant_dynamic-update-slice_fusion.3 = (f32[9,64,256]{2,1,0:T(8,128)S(1)}, f32[9,16,256]{2,1,0:T(8,128)S(1)}) fusion(f32[9,64,256]{2,1,0:T(8,128)S(1)} %broadcast_in_dim.25, s32[]{:T(128)S(6)} %select_n.58, f32[9,16,256]{2,1,0:T(8,128)S(1)} %collective-permute-done.10, f32[9,16,256]{2,1,0:T(8,128)S(1)} %collective-permute-done.11, ...), kind=kLoop, calls=%fused_computation.42 | loop fusion | flops 110592 | bytes 884740 | tf_op jit(solution)/shard_map/dynamic_update_slice | solution.py:91
  52.6 1.2 %collective-permute-start.12 = (f32[9,16,256]{2,1,0:T(8,128)S(1)}, f32[9,16,256]{2,1,0:T(8,128)S(1)}, u32[]{:S(2)}, u32[]{:S(2)}) collective-permute-start(f32[9,16,256]{2,1,0:T(8,128)S(1)} %get-tuple-element.99), channel_id=1, source_target_pairs={{0,4},{4,0},{8,12},{12,8},{1,5},{5,1},{9,13},{13,9},{2,6},{6,2},{1... | collective-permute-start | bytes 442376 | tf_op jit(solution)/shard_map/ppermute | solution.py:93
  53.8 1.5 %collective-permute-start.13 = (f32[9,16,256]{2,1,0:T(8,128)S(1)}, f32[9,16,256]{2,1,0:T(8,128)S(1)}, u32[]{:S(2)}, u32[]{:S(2)}) collective-permute-start(f32[9,16,256]{2,1,0:T(8,128)S(1)} %get-tuple-element.99), channel_id=1, source_target_pairs={{0,8},{4,12},{8,0},{12,4},{1,9},{5,13},{9,1},{13,5},{2,10},{6,14},... | collective-permute-start | bytes 442376 | tf_op jit(solution)/shard_map/ppermute | solution.py:93
  55.2 0.3 collective-permute-start.14
  55.5 0.7 %copy.21 = bf16[256,1,128]{2,0,1:T(8,128)(2,1)} copy(bf16[256,1,128]{0,2,1:T(8,128)(2,1)S(1)} %fusion.6) | data formatting | bytes 131072
  56.3 2.9 %collective-permute-done.13 = f32[9,16,256]{2,1,0:T(8,128)S(1)} collective-permute-done((f32[9,16,256]{2,1,0:T(8,128)S(1)}, f32[9,16,256]{2,1,0:T(8,128)S(1)}, u32[]{:S(2)}, u32[]{:S(2)}) %collective-permute-start.13) | collective-permute-done | bytes 147488 | tf_op jit(solution)/shard_map/ppermute | solution.py:93
  59.2 3.3 %collective-permute-done.14 = f32[9,16,256]{2,1,0:T(8,128)S(1)} collective-permute-done((f32[9,16,256]{2,1,0:T(8,128)S(1)}, f32[9,16,256]{2,1,0:T(8,128)S(1)}, u32[]{:S(2)}, u32[]{:S(2)}) %collective-permute-start.14) | collective-permute-done | bytes 147488 | tf_op jit(solution)/shard_map/ppermute | solution.py:93
  62.5 0.8 %copy-done.1 = f32[9,64,256]{2,1,0:T(8,128)} copy-done((f32[9,64,256]{2,1,0:T(8,128)}, f32[9,64,256]{2,1,0:T(8,128)S(1)}, u32[]{:S(2)}) %copy-start.1) | copy-done | bytes 589848
  (40 shorter events, 0.7 us)
Async XLA Ops:
  0.6 9.9 %copy-start = (bf16[1,9,3,2,64]{4,3,2,1,0:T(2,128)(2,1)S(1)}, bf16[1,9,3,2,64]{4,3,2,1,0:T(2,128)(2,1)}, u32[]{:S(2)}) copy-start(bf16[1,9,3,2,64]{4,3,2,1,0:T(2,128)(2,1)} %param.25) | copy-start | bytes 20740
  2.4 18.4 %collective-permute-start = (bf16[320,128]{1,0:T(8,128)(2,1)S(1)}, bf16[320,128]{1,0:T(8,128)(2,1)S(1)}, u32[]{:S(2)}, u32[]{:S(2)}) collective-permute-start(bf16[320,128]{1,0:T(8,128)(2,1)S(1)} %get-tuple-element.113), channel_id=1, source_target_pairs={{0,3},{1,0},{2,1},{3,2},{4,7},{5,4},{6,5},{7,6},{8,11},{9,8},{10,9... | collective-permute-start | bytes 245768 | tf_op jit(solution)/shard_map/ppermute | solution.py:170
  6.6 14.2 %collective-permute-start.1 = (bf16[320,128]{1,0:T(8,128)(2,1)S(1)}, bf16[320,128]{1,0:T(8,128)(2,1)S(1)}, u32[]{:S(2)}, u32[]{:S(2)}) collective-permute-start(bf16[320,128]{1,0:T(8,128)(2,1)S(1)} %get-tuple-element.114), channel_id=1, source_target_pairs={{0,2},{1,3},{2,0},{3,1},{4,6},{5,7},{6,4},{7,5},{8,10},{9,11},{10,... | collective-permute-start | bytes 245768 | tf_op jit(solution)/shard_map/ppermute | solution.py:170
  6.6 3.2 %copy-start.3 = (s32[1,2]{1,0:T(1,128)S(1)}, s32[1,2]{1,0:T(1,128)}, u32[]{:S(2)}) copy-start(s32[1,2]{1,0:T(1,128)} %param.27) | copy-start | bytes 28
  6.6 14.2 %collective-permute-start.2 = (bf16[320,128]{1,0:T(8,128)(2,1)S(1)}, bf16[320,128]{1,0:T(8,128)(2,1)S(1)}, u32[]{:S(2)}, u32[]{:S(2)}) collective-permute-start(bf16[320,128]{1,0:T(8,128)(2,1)S(1)} %get-tuple-element.115), channel_id=1, source_target_pairs={{0,1},{1,2},{2,3},{3,0},{4,5},{5,6},{6,7},{7,4},{8,9},{9,10},{10,1... | collective-permute-start | bytes 245768 | tf_op jit(solution)/shard_map/ppermute | solution.py:170
  17.4 3.5 %copy-start.2 = (bf16[256,1,128]{2,0,1:T(8,128)(2,1)S(1)}, bf16[256,1,128]{2,0,1:T(8,128)(2,1)}, u32[]{:S(2)}) copy-start(bf16[256,1,128]{2,0,1:T(8,128)(2,1)} %param.22) | copy-start | bytes 196612
  17.5 29.2 %collective-permute-start.5 = (f32[256,3,128]{0,2,1:T(8,128)S(1)}, f32[256,3,128]{0,2,1:T(8,128)S(1)}, u32[]{:S(2)}, u32[]{:S(2)}) collective-permute-start(f32[256,3,128]{0,2,1:T(8,128)S(1)} %get-tuple-element.100), channel_id=1, source_target_pairs={{0,1},{1,2},{2,3},{3,0},{4,5},{5,6},{6,7},{7,4},{8,9},{9,10},{10,1... | collective-permute-start | bytes 1179656 | tf_op jit(solution)/shard_map/ppermute | solution.py:19
  19.7 27.0 %collective-permute-start.6 = (f32[256,3,128]{0,2,1:T(8,128)S(1)}, f32[256,3,128]{0,2,1:T(8,128)S(1)}, u32[]{:S(2)}, u32[]{:S(2)}) collective-permute-start(f32[256,3,128]{0,2,1:T(8,128)S(1)} %get-tuple-element.101), channel_id=1, source_target_pairs={{1,0},{2,1},{3,2},{0,3},{5,4},{6,5},{7,6},{4,7},{9,8},{10,9},{11,1... | collective-permute-start | bytes 1179656 | tf_op jit(solution)/shard_map/ppermute | solution.py:21
  20.9 8.4 %collective-permute-start.3 = (bf16[256,512]{1,0:T(8,128)(2,1)S(1)}, bf16[256,512]{1,0:T(8,128)(2,1)S(1)}, u32[]{:S(2)}, u32[]{:S(2)}) collective-permute-start(bf16[256,512]{1,0:T(8,128)(2,1)S(1)} %get-tuple-element.108), channel_id=1, source_target_pairs={{0,4},{4,8},{8,12},{1,5},{5,9},{9,13},{2,6},{6,10},{10,14},{3,7},{... | collective-permute-start | bytes 786440 | tf_op jit(solution)/shard_map/ppermute | solution.py:180
  26.0 8.0 %collective-permute-start.4 = (bf16[256,512]{1,0:T(8,128)(2,1)S(1)}, bf16[256,512]{1,0:T(8,128)(2,1)S(1)}, u32[]{:S(2)}, u32[]{:S(2)}) collective-permute-start(bf16[256,512]{1,0:T(8,128)(2,1)S(1)} %get-tuple-element.108), channel_id=1, source_target_pairs={{4,0},{8,4},{12,8},{5,1},{9,5},{13,9},{6,2},{10,6},{14,10},{7,3},{... | collective-permute-start | bytes 786440 | tf_op jit(solution)/shard_map/ppermute | solution.py:181
  44.7 6.4 %collective-permute-start.10 = (f32[9,16,256]{2,1,0:T(8,128)S(1)}, f32[9,16,256]{2,1,0:T(8,128)S(1)}, u32[]{:S(2)}, u32[]{:S(2)}) collective-permute-start(f32[9,16,256]{2,1,0:T(8,128)S(1)} %get-tuple-element.104), channel_id=1, source_target_pairs={{0,8},{4,12},{8,0},{12,4},{1,9},{5,13},{9,1},{13,5},{2,10},{6,14},... | collective-permute-start | bytes 442376 | tf_op jit(solution)/shard_map/ppermute | solution.py:86
  44.8 6.7 %collective-permute-start.11 = (f32[9,16,256]{2,1,0:T(8,128)S(1)}, f32[9,16,256]{2,1,0:T(8,128)S(1)}, u32[]{:S(2)}, u32[]{:S(2)}) collective-permute-start(f32[9,16,256]{2,1,0:T(8,128)S(1)} %get-tuple-element.103), channel_id=1, source_target_pairs={{0,12},{4,8},{8,4},{12,0},{1,13},{5,9},{9,5},{13,1},{2,14},{6,10},... | collective-permute-start | bytes 442376 | tf_op jit(solution)/shard_map/ppermute | solution.py:86
  44.9 6.6 %collective-permute-start.9 = (f32[9,16,256]{2,1,0:T(8,128)S(1)}, f32[9,16,256]{2,1,0:T(8,128)S(1)}, u32[]{:S(2)}, u32[]{:S(2)}) collective-permute-start(f32[9,16,256]{2,1,0:T(8,128)S(1)} %get-tuple-element.102), channel_id=1, source_target_pairs={{0,4},{4,0},{8,12},{12,8},{1,5},{5,1},{9,13},{13,9},{2,6},{6,2},{1... | collective-permute-start | bytes 442376 | tf_op jit(solution)/shard_map/ppermute | solution.py:86
  46.8 8.7 %collective-permute-start.7 = (f32[256,1,128]{0,2,1:T(8,128)S(1)}, f32[256,1,128]{0,2,1:T(8,128)S(1)}, u32[]{:S(2)}, u32[]{:S(2)}) collective-permute-start(f32[256,1,128]{0,2,1:T(8,128)S(1)} %get-tuple-element.105), channel_id=1, source_target_pairs={{0,4},{4,8},{8,12},{1,5},{5,9},{9,13},{2,6},{6,10},{10,14},{3,7},{... | collective-permute-start | bytes 393224 | tf_op jit(solution)/shard_map/ppermute | solution.py:19
  48.7 6.8 %collective-permute-start.8 = (f32[256,1,128]{0,2,1:T(8,128)S(1)}, f32[256,1,128]{0,2,1:T(8,128)S(1)}, u32[]{:S(2)}, u32[]{:S(2)}) collective-permute-start(f32[256,1,128]{0,2,1:T(8,128)S(1)} %get-tuple-element.106), channel_id=1, source_target_pairs={{4,0},{8,4},{12,8},{5,1},{9,5},{13,9},{6,2},{10,6},{14,10},{7,3},{... | collective-permute-start | bytes 393224 | tf_op jit(solution)/shard_map/ppermute | solution.py:21
  52.6 3.7 %collective-permute-start.12 = (f32[9,16,256]{2,1,0:T(8,128)S(1)}, f32[9,16,256]{2,1,0:T(8,128)S(1)}, u32[]{:S(2)}, u32[]{:S(2)}) collective-permute-start(f32[9,16,256]{2,1,0:T(8,128)S(1)} %get-tuple-element.99), channel_id=1, source_target_pairs={{0,4},{4,0},{8,12},{12,8},{1,5},{5,1},{9,13},{13,9},{2,6},{6,2},{1... | collective-permute-start | bytes 442376 | tf_op jit(solution)/shard_map/ppermute | solution.py:93
  53.8 5.4 %collective-permute-start.13 = (f32[9,16,256]{2,1,0:T(8,128)S(1)}, f32[9,16,256]{2,1,0:T(8,128)S(1)}, u32[]{:S(2)}, u32[]{:S(2)}) collective-permute-start(f32[9,16,256]{2,1,0:T(8,128)S(1)} %get-tuple-element.99), channel_id=1, source_target_pairs={{0,8},{4,12},{8,0},{12,4},{1,9},{5,13},{9,1},{13,5},{2,10},{6,14},... | collective-permute-start | bytes 442376 | tf_op jit(solution)/shard_map/ppermute | solution.py:93
  55.2 7.3 %collective-permute-start.14 = (f32[9,16,256]{2,1,0:T(8,128)S(1)}, f32[9,16,256]{2,1,0:T(8,128)S(1)}, u32[]{:S(2)}, u32[]{:S(2)}) collective-permute-start(f32[9,16,256]{2,1,0:T(8,128)S(1)} %get-tuple-element.99), channel_id=1, source_target_pairs={{0,12},{4,8},{8,4},{12,0},{1,13},{5,9},{9,5},{13,1},{2,14},{6,10},... | collective-permute-start | bytes 442376 | tf_op jit(solution)/shard_map/ppermute | solution.py:93
  62.5 0.8 %copy-start.1 = (f32[9,64,256]{2,1,0:T(8,128)}, f32[9,64,256]{2,1,0:T(8,128)S(1)}, u32[]{:S(2)}) copy-start(f32[9,64,256]{2,1,0:T(8,128)S(1)} %constant_dynamic-update-slice_fusion) | copy-start | bytes 1769476

commit v13 on v12

--- a/solution.py
+++ b/solution.py
@@ -95,44 +95,48 @@
     return out
 
 
-def row_kernel(ext_ref, mt_ref, w_ref, up_ref, out_ref, gt_ref, m_ref):
+def row_kernel(ext_ref, mt_ref, w_ref, upt_ref, out_ref, gt_ref, m_ref, rs_ref):
     stencil_rows, channels, _ = ext_ref.shape
-    n_blocks, o_block, lon_cols = up_ref.shape
+    n_blocks, lon_cols, o_block = upt_ref.shape
     kernels = w_ref.shape[0]
     window_len = mt_ref.shape[1] // stencil_rows
-    contract_last = (((1,), (1,)), ((), ()))
-    gt_ref[...] = jnp.zeros(gt_ref.shape, gt_ref.dtype)
+    acc = None
     for r in range(stencil_rows):
-        m_ref[r] = mt_ref[:, pl.ds(r * window_len, window_len)].T
-    for d in range(n_blocks):
-        acc = None
-        for r in range(stencil_rows):
-            win = ext_ref[r, :, pl.ds(d * lon_cols, window_len)]
-            part = jnp.dot(win, m_ref[r], preferred_element_type=jnp.float32)
-            acc = part if acc is None else acc + part
-        resp = acc.astype(jnp.bfloat16)
-        up_d = up_ref[d]
-        for k in range(kernels):
-            resp_k = resp[:, k * lon_cols : (k + 1) * lon_cols]
-            gt_ref[k] += lax.dot_general(
-                up_d, resp_k, contract_last, preferred_element_type=jnp.float32
-            )
-        if d == 0:
-            total = None
-            for k in range(kernels):
-                term = jnp.dot(
-                    w_ref[k],
-                    resp[:, k * lon_cols : (k + 1) * lon_cols],
-                    preferred_element_type=jnp.float32,
-                )
-                total = term if total is None else total + term
-            out_ref[...] = total.astype(out_ref.dtype)
+        m_ref[...] = mt_ref[:, pl.ds(r * window_len, window_len)].T
+        wins = jnp.concatenate(
+            [ext_ref[r, :, pl.ds(d * lon_cols, window_len)] for d in range(n_blocks)], axis=0
+        )
+        part = jnp.dot(wins, m_ref[...], preferred_element_type=jnp.float32)
+        acc = part if acc is None else acc + part
+    rs_ref[...] = acc.astype(jnp.bfloat16)
+    up_t = upt_ref[...].reshape(n_blocks * lon_cols, o_block)
+    for k in range(kernels):
+        lhs = jnp.concatenate(
+            [
+                rs_ref[pl.ds(d * channels, channels), pl.ds(k * lon_cols, lon_cols)]
+                for d in range(n_blocks)
+            ],
+            axis=1,
+        )
+        grad_t = jnp.dot(lhs, up_t, preferred_element_type=jnp.float32)
+        gt_ref[k] = grad_t.T
+    total = None
+    for k in range(kernels):
+        term = jnp.dot(
+            w_ref[k],
+            rs_ref[pl.ds(0, channels), pl.ds(k * lon_cols, lon_cols)],
+            preferred_element_type=jnp.float32,
+        )
+        total = term if total is None else total + term
+    out_ref[...] = total.astype(out_ref.dtype)
 
 
 def row_products(ext, matrix, weights, up_rel):
     stencil_rows, channels, _ = ext.shape
     n_blocks, o_block, lon_cols = up_rel.shape
     kernels = weights.shape[0]
+    up_t = jnp.swapaxes(up_rel, 1, 2)
+    window_len = matrix.shape[1] // stencil_rows
     flops = 2 * n_blocks * channels * matrix.shape[0] * matrix.shape[1]
     flops += 2 * n_blocks * kernels * o_block * lon_cols * channels
     flops += 2 * kernels * weights.shape[1] * channels * lon_cols
@@ -144,9 +148,12 @@
             jax.ShapeDtypeStruct((weights.shape[1], lon_cols), jnp.bfloat16),
             jax.ShapeDtypeStruct((kernels, o_block, channels), jnp.float32),
         ),
-        scratch_shapes=[pltpu.VMEM((stencil_rows, matrix.shape[1] // stencil_rows, matrix.shape[0]), matrix.dtype)],
+        scratch_shapes=[
+            pltpu.VMEM((window_len, matrix.shape[0]), matrix.dtype),
+            pltpu.VMEM((n_blocks * channels, matrix.shape[0]), jnp.bfloat16),
+        ],
         cost_estimate=pl.CostEstimate(flops=flops, transcendentals=0, bytes_accessed=nbytes),
-    )(ext, matrix, weights, up_rel)
+    )(ext, matrix, weights, up_t)
 
 
 def body(fields, upstream, weights, filter_taps, cycle_counts, cycle_blocks):

time: 63.9 us -> 65.6 us (1.027)
  local copies, waits for them, and re-layouts: 6.99 us -> 10.7 us
  other arithmetic: 3.8 us -> 2.04 us
    concatenate x0 -> x1, local copies, waits for them, and re-layouts: none -> 1.53 us  [body(): jnp.concatenate([rows[:, :, rows.shape[2] - HALO:], rows, rows[:, :, :HAL...]
    dynamic_slice x0 -> x5, local copies, waits for them, and re-layouts: none -> 1.25 us  [the longest x2 0.9 us: body(): lax.dynamic_slice_in_dim(up_row, lon_at * o_block, o_block, axis=0)]
    concatenate x1, other arithmetic: 1.09 us -> 0.12 us  [body(): jnp.concatenate([rows[:, :, rows.shape[2] - HALO:], rows, rows[:, :, :HAL...]
    unnamed x9 -> x8, local copies, waits for them, and re-layouts: 1.56 us -> 2.5 us
    concatenate x1, other arithmetic: 0.87 us -> 0.03 us  [body(): jnp.concatenate([fields[:, 0], part], axis=0)]
    another operation x4 -> x3, local copies, waits for them, and re-layouts: 0.79 us -> 0.01 us  [body(): up_rel = jnp.stack(up_parts, axis=0)]
    slice x1, local copies, waits for them, and re-layouts: 0.08 us -> 0.83 us  [body(): accumulated[:, :, HALO + lon_cols:]]
    transpose x0 -> x1, other arithmetic: none -> 0.69 us  [row_products(): up_t = jnp.swapaxes(up_rel, 1, 2)]
  transfers between devices with their start and end apart: 15 -> 15, of which waited for: 5 -> 5; matrix products, arithmetic and copies ran while one was open for 16% -> 18% of each run, Pallas kernels for 20% -> 20%
where the time goes in v13:
time: 65.6 us; the launch traced here: 65 us
  starting transfers between devices  24.1 us (37%)
  Pallas kernels  12.7 us (19%)
  waiting for transfers between devices  12 us (18%)
  local copies, waits for them, and re-layouts  10.7 us (16%)
  other arithmetic  2.04 us (3%)
  matrix products  1.86 us (3%)
  between operations  1.66 us (3%)
    pallas_call x1, Pallas kernels, row_products(): pl.pallas_call(row_kernel, out_shape=(jax.ShapeDtypeStruct((weights.shape...  8.37 us
    ppermute x3, waiting for transfers between devices, lat_allreduce(): recv = lax.ppermute(mine, axis, [(i, i ^ d) for i in range(count)])  6.21 us
    ppermute x1, starting transfers between devices, body(): below = lax.ppermute(row, 'lat', [(i, i + 1) for i in range(count - 1)])  5.08 us
    ppermute x1, waiting for transfers between devices, body(): above = lax.ppermute(row, 'lat', [(i + 1, i) for i in range(count - 1)])  4.69 us
    ppermute x3, starting transfers between devices, body(): lax.ppermute(jnp.concatenate([fields[:, 0], part], axis=0), 'lon', [(p, (...  4.66 us
    pallas_call x1, Pallas kernels, toeplitz(): pl.pallas_call(toeplitz_kernel, out_shape=(jax.ShapeDtypeStruct((kernels,...  4.33 us
    ppermute x2, starting transfers between devices, padded_2(): lax.ppermute(tail, axis, [(i, (i + 1) % count) for i in range(ends)])  4.12 us
    ppermute x2, starting transfers between devices, padded_2(): lax.ppermute(head, axis, [((i + 1) % count, i) for i in range(ends)])  3.48 us
  transfers between devices with their start and end apart: 15, of which 5 were waited for; matrix products, arithmetic and copies ran while one was open for 18% of the time, Pallas kernels for 20%

profile of v13, /device:TPU:1, one launch (start us, length us, event | category | flops | bytes accessed | tf_op | source)
XLA Modules:
  0.0 65.0 jit_solution(16529807017559666655)
XLA Ops:
  0.7 0.8 %constant_dynamic-slice_fusion.3 = (bf16[64,1,128]{2,0,1:T(8,128)(2,1)S(1)}, bf16[64,1,128]{2,0,1:T(8,128)(2,1)S(1)}, bf16[64,1,128]{2,0,1:T(8,128)(2,1)S(1)}, bf16[64,1,128]{2,0,1:T(8,128)(2,1)S(1)}) fusion(bf16[256,1,128]{2,0,1:T(8,128)(2,1)} %param.23, s32[]{:T(128)S(6)} %select_n.57, s32[]{:T(128)S(6)} %select_n.55, s32[]{:T(128)S(6)} %select_n.53, ...), kind=kLoop, calls=%fused_computation.42 | loop fusion | bytes 131088 | tf_op jit(solution)/shard_map/dynamic_slice | solution.py:174
  1.9 0.9 %copy.22 = bf16[256,1,128]{0,2,1:T(8,128)(2,1)S(1)} copy(bf16[256,1,128]{2,0,1:T(8,128)(2,1)} %param.22) | data formatting | bytes 131072 | tf_op args[0]
  2.9 4.2 %collective-permute-start = (bf16[320,128]{0,1:T(8,128)(2,1)S(1)}, bf16[320,128]{0,1:T(8,128)(2,1)S(1)}, u32[]{:S(2)}, u32[]{:S(2)}) collective-permute-start(bf16[320,128]{0,1:T(8,128)(2,1)S(1)} %get-tuple-element.113), channel_id=1, source_target_pairs={{0,3},{1,0},{2,1},{3,2},{4,7},{5,4},{6,5},{7,6},{8,11},{9,8},{10,9... | collective-permute-start | bytes 245768 | tf_op jit(solution)/shard_map/ppermute | solution.py:177
  7.1 0.5 collective-permute-start.2
  7.5 1.7 %convolution_convert_fusion = bf16[128,9,256]{2,0,1:T(8,128)(2,1)S(1)} fusion(bf16[9,256,256]{2,1,0:T(8,128)(2,1)} %w_ref.1, bf16[256,1,128]{2,0,1:T(8,128)(2,1)} %param.23), kind=kOutput, calls=%fused_computation | convolution fusion | flops 151289856 | bytes 1835008 | tf_op jit(solution)/shard_map/koc,oij->cikj/dot_general | solution.py:166
  9.2 1.1 %copy.29.grad_ref = bf16[256,1152]{1,0:T(8,128)(2,1)} copy(bf16[256,1152]{0,1:T(8,128)(2,1)S(1)} %bitcast.51) | data formatting | bytes 1179648 | tf_op jit(solution)/shard_map/reshape;squeeze | solution.py:169
  11.2 0.6 reshape.252.tap_ref
  11.9 4.3 %shard_map.100 = (bf16[9,128,1152]{2,1,0:T(8,128)(2,1)}, f32[256,1152]{1,0:T(8,128)}) custom-call(f32[27,384]{1,0:T(8,128)} %reshape.252.tap_ref, bf16[256,1152]{1,0:T(8,128)(2,1)} %copy.29.grad_ref), custom_call_target="tpu_custom_call" | custom-call | tf_op jit(solution)/shard_map/pallas_call | solution.py:66
  16.2 1.6 %copy.32 = f32[256,1152]{0,1:T(8,128)S(1)} copy(f32[256,1152]{1,0:T(8,128)} %get-tuple-element.93) | data formatting | bytes 2359296 | tf_op jit(solution)/shard_map/pallas_call | solution.py:66
  17.9 0.8 %fusion.20 = (f32[256,3,128]{0,2,1:T(8,128)}, f32[256,3,128]{0,2,1:T(8,128)S(1)}) fusion(f32[256,3,384]{0,2,1:T(8,128)S(1)} %bitcast.49), kind=kLoop, calls=%fused_computation.52 | loop fusion | bytes 1572864 | tf_op jit(solution)/shard_map/slice | solution.py:200
  18.7 2.2 %collective-permute-start.5 = (f32[256,3,128]{0,2,1:T(8,128)}, f32[256,3,128]{0,2,1:T(8,128)S(1)}, u32[]{:S(2)}, u32[]{:S(2)}) collective-permute-start(f32[256,3,128]{0,2,1:T(8,128)} %get-tuple-element.100), channel_id=1, source_target_pairs={{0,1},{1,2},{2,3},{3,0},{4,5},{5,6},{6,7},{7,4},{8,9},{9,10},{10,1... | collective-permute-start | bytes 1179656 | tf_op jit(solution)/shard_map/ppermute | solution.py:19
  20.9 1.1 %collective-permute-start.6 = (f32[256,3,128]{0,2,1:T(8,128)S(1)}, f32[256,3,128]{0,2,1:T(8,128)S(1)}, u32[]{:S(2)}, u32[]{:S(2)}) collective-permute-start(f32[256,3,128]{0,2,1:T(8,128)S(1)} %get-tuple-element.101), channel_id=1, source_target_pairs={{1,0},{2,1},{3,2},{0,3},{5,4},{6,5},{7,6},{4,7},{9,8},{10,9},{11,1... | collective-permute-start | bytes 1179656 | tf_op jit(solution)/shard_map/ppermute | solution.py:21
  22.2 5.1 %collective-permute-start.3 = (bf16[256,512]{0,1:T(8,128)(2,1)S(1)}, bf16[256,512]{0,1:T(8,128)(2,1)S(1)}, u32[]{:S(2)}, u32[]{:S(2)}) collective-permute-start(bf16[256,512]{0,1:T(8,128)(2,1)S(1)} %get-tuple-element.108), channel_id=1, source_target_pairs={{0,4},{4,8},{8,12},{1,5},{5,9},{9,13},{2,6},{6,10},{10,14},{3,7},{... | collective-permute-start | bytes 786440 | tf_op jit(solution)/shard_map/ppermute | solution.py:187
  27.3 1.9 %collective-permute-start.4 = (bf16[256,512]{0,1:T(8,128)(2,1)S(1)}, bf16[256,512]{0,1:T(8,128)(2,1)S(1)}, u32[]{:S(2)}, u32[]{:S(2)}) collective-permute-start(bf16[256,512]{0,1:T(8,128)(2,1)S(1)} %get-tuple-element.108), channel_id=1, source_target_pairs={{4,0},{8,4},{12,8},{5,1},{9,5},{13,9},{6,2},{10,6},{14,10},{7,3},{... | collective-permute-start | bytes 786440 | tf_op jit(solution)/shard_map/ppermute | solution.py:188
  29.3 0.7 %maximum_bitcast_fusion.upt_ref = bf16[4,128,64]{2,1,0:T(8,128)(2,1)} fusion(bf16[1,64,128]{1,2,0:T(8,128)(2,1)S(1)} %slice_bitcast_fusion, bf16[1,64,128]{1,2,0:T(8,128)(2,1)S(1)} %slice_bitcast_fusion.1, bf16[1,64,128]{1,2,0:T(8,128)(2,1)S(1)} %slice_bitcast_fusion.2, bf16[1,64,128]{1,2,0:T(8,128)(2,1)S(1)} %bitcast.59), kind=kLoop, calls=%fused_computation.17 | loop fusion | flops 98304 | bytes 131072 | tf_op jit(solution)/shard_map/transpose | solution.py:138
  29.9 0.6 collective-permute-done.3
  30.6 4.7 %collective-permute-done.4 = bf16[256,512]{0,1:T(8,128)(2,1)S(1)} collective-permute-done((bf16[256,512]{0,1:T(8,128)(2,1)S(1)}, bf16[256,512]{0,1:T(8,128)(2,1)S(1)}, u32[]{:S(2)}, u32[]{:S(2)}) %collective-permute-start.4) | collective-permute-done | bytes 262176 | tf_op jit(solution)/shard_map/ppermute | solution.py:188
  35.4 1.5 %copy.31.ext_ref = bf16[3,256,768]{2,1,0:T(8,128)(2,1)} copy(bf16[3,256,768]{1,2,0:T(8,128)(2,1)S(1)} %fusion) | data formatting | bytes 2359296 | tf_op jit(solution)/shard_map/concatenate | solution.py:190
  36.9 8.4 %shard_map.101 = (bf16[256,128]{1,0:T(8,128)(2,1)}, f32[9,64,256]{2,1,0:T(8,128)}) custom-call(bf16[3,256,768]{2,1,0:T(8,128)(2,1)} %copy.31.ext_ref, bf16[1152,1152]{1,0:T(8,128)(2,1)} %bitcast.60, bf16[9,256,256]{2,1,0:T(8,128)(2,1)} %w_ref.1, bf16[4,128,64]{2,1,0:T(8,128)(2,1)} %maximum_bitcast_fusion.upt_ref), custom_call_target="tpu_custom_call" | custom-call | flops 3019898880 | bytes 5734400 | tf_op jit(solution)/shard_map/pallas_call | solution.py:145
  45.3 1.1 %constant_dynamic-slice_fusion.2 = (f32[9,16,256]{2,1,0:T(8,128)S(1)}, f32[9,16,256]{2,1,0:T(8,128)S(1)}, f32[9,16,256]{2,1,0:T(8,128)S(1)}) fusion(f32[9,64,256]{2,1,0:T(8,128)} %get-tuple-element.94, s32[]{:T(128)S(6)} %select_n.59, s32[]{:T(128)S(6)} %select_n.61, s32[]{:T(128)S(6)} %select_n.60), kind=kLoop, calls=%fused_computation.41 | loop fusion | bytes 884748 | tf_op jit(solution)/shard_map/dynamic_slice | solution.py:85
  46.6 1.8 %collective-permute-start.9 = (f32[9,16,256]{2,1,0:T(8,128)S(1)}, f32[9,16,256]{2,1,0:T(8,128)S(1)}, u32[]{:S(2)}, u32[]{:S(2)}) collective-permute-start(f32[9,16,256]{2,1,0:T(8,128)S(1)} %get-tuple-element.102), channel_id=1, source_target_pairs={{0,4},{4,0},{8,12},{12,8},{1,5},{5,1},{9,13},{13,9},{2,6},{6,2},{1... | collective-permute-start | bytes 442376 | tf_op jit(solution)/shard_map/ppermute | solution.py:86
  48.4 1.9 %collective-permute-start.7 = (f32[256,1,128]{0,2,1:T(8,128)S(1)}, f32[256,1,128]{0,2,1:T(8,128)S(1)}, u32[]{:S(2)}, u32[]{:S(2)}) collective-permute-start(f32[256,1,128]{0,2,1:T(8,128)S(1)} %get-tuple-element.105), channel_id=1, source_target_pairs={{0,4},{4,8},{8,12},{1,5},{5,9},{9,13},{2,6},{6,10},{10,14},{3,7},{... | collective-permute-start | bytes 393224 | tf_op jit(solution)/shard_map/ppermute | solution.py:19
  50.4 2.4 %collective-permute-start.8 = (f32[256,1,128]{0,2,1:T(8,128)S(1)}, f32[256,1,128]{0,2,1:T(8,128)S(1)}, u32[]{:S(2)}, u32[]{:S(2)}) collective-permute-start(f32[256,1,128]{0,2,1:T(8,128)S(1)} %get-tuple-element.106), channel_id=1, source_target_pairs={{4,0},{8,4},{12,8},{5,1},{9,5},{13,9},{6,2},{10,6},{14,10},{7,3},{... | collective-permute-start | bytes 393224 | tf_op jit(solution)/shard_map/ppermute | solution.py:21
  52.8 0.4 collective-permute-done.11
  53.2 1.0 %constant_dynamic-update-slice_fusion.3 = (f32[9,64,256]{2,1,0:T(8,128)S(1)}, f32[9,16,256]{2,1,0:T(8,128)S(1)}) fusion(f32[9,64,256]{2,1,0:T(8,128)S(1)} %broadcast_in_dim.25, s32[]{:T(128)S(6)} %select_n.58, f32[9,16,256]{2,1,0:T(8,128)S(1)} %collective-permute-done.10, f32[9,16,256]{2,1,0:T(8,128)S(1)} %collective-permute-done.11, ...), kind=kLoop, calls=%fused_computation.38 | loop fusion | flops 110592 | bytes 884740 | tf_op jit(solution)/shard_map/dynamic_update_slice | solution.py:91
  54.2 1.2 %collective-permute-start.12 = (f32[9,16,256]{2,1,0:T(8,128)S(1)}, f32[9,16,256]{2,1,0:T(8,128)S(1)}, u32[]{:S(2)}, u32[]{:S(2)}) collective-permute-start(f32[9,16,256]{2,1,0:T(8,128)S(1)} %get-tuple-element.99), channel_id=1, source_target_pairs={{0,4},{4,0},{8,12},{12,8},{1,5},{5,1},{9,13},{13,9},{2,6},{6,2},{1... | collective-permute-start | bytes 442376 | tf_op jit(solution)/shard_map/ppermute | solution.py:93
  55.4 1.5 %collective-permute-start.13 = (f32[9,16,256]{2,1,0:T(8,128)S(1)}, f32[9,16,256]{2,1,0:T(8,128)S(1)}, u32[]{:S(2)}, u32[]{:S(2)}) collective-permute-start(f32[9,16,256]{2,1,0:T(8,128)S(1)} %get-tuple-element.99), channel_id=1, source_target_pairs={{0,8},{4,12},{8,0},{12,4},{1,9},{5,13},{9,1},{13,5},{2,10},{6,14},... | collective-permute-start | bytes 442376 | tf_op jit(solution)/shard_map/ppermute | solution.py:93
  56.9 0.3 collective-permute-start.14
  57.2 0.7 %copy.33 = bf16[256,1,128]{2,0,1:T(8,128)(2,1)} copy(bf16[256,1,128]{0,2,1:T(8,128)(2,1)S(1)} %fusion.6) | data formatting | bytes 131072
  57.9 2.9 %collective-permute-done.13 = f32[9,16,256]{2,1,0:T(8,128)S(1)} collective-permute-done((f32[9,16,256]{2,1,0:T(8,128)S(1)}, f32[9,16,256]{2,1,0:T(8,128)S(1)}, u32[]{:S(2)}, u32[]{:S(2)}) %collective-permute-start.13) | collective-permute-done | bytes 147488 | tf_op jit(solution)/shard_map/ppermute | solution.py:93
  60.8 3.3 %collective-permute-done.14 = f32[9,16,256]{2,1,0:T(8,128)S(1)} collective-permute-done((f32[9,16,256]{2,1,0:T(8,128)S(1)}, f32[9,16,256]{2,1,0:T(8,128)S(1)}, u32[]{:S(2)}, u32[]{:S(2)}) %collective-permute-start.14) | collective-permute-done | bytes 147488 | tf_op jit(solution)/shard_map/ppermute | solution.py:93
  64.2 0.8 %copy-done.1 = f32[9,64,256]{2,1,0:T(8,128)} copy-done((f32[9,64,256]{2,1,0:T(8,128)}, f32[9,64,256]{2,1,0:T(8,128)S(1)}, u32[]{:S(2)}) %copy-start.1) | copy-done | bytes 589848
  (44 shorter events, 1.4 us)
Async XLA Ops:
  0.6 10.4 %copy-start = (bf16[1,9,3,2,64]{4,3,2,1,0:T(2,128)(2,1)S(1)}, bf16[1,9,3,2,64]{4,3,2,1,0:T(2,128)(2,1)}, u32[]{:S(2)}) copy-start(bf16[1,9,3,2,64]{4,3,2,1,0:T(2,128)(2,1)} %param.25) | copy-start | bytes 20740
  2.9 19.2 %collective-permute-start = (bf16[320,128]{0,1:T(8,128)(2,1)S(1)}, bf16[320,128]{0,1:T(8,128)(2,1)S(1)}, u32[]{:S(2)}, u32[]{:S(2)}) collective-permute-start(bf16[320,128]{0,1:T(8,128)(2,1)S(1)} %get-tuple-element.113), channel_id=1, source_target_pairs={{0,3},{1,0},{2,1},{3,2},{4,7},{5,4},{6,5},{7,6},{8,11},{9,8},{10,9... | collective-permute-start | bytes 245768 | tf_op jit(solution)/shard_map/ppermute | solution.py:177
  7.1 15.1 %collective-permute-start.1 = (bf16[320,128]{0,1:T(8,128)(2,1)S(1)}, bf16[320,128]{0,1:T(8,128)(2,1)S(1)}, u32[]{:S(2)}, u32[]{:S(2)}) collective-permute-start(bf16[320,128]{0,1:T(8,128)(2,1)S(1)} %get-tuple-element.114), channel_id=1, source_target_pairs={{0,2},{1,3},{2,0},{3,1},{4,6},{5,7},{6,4},{7,5},{8,10},{9,11},{10,... | collective-permute-start | bytes 245768 | tf_op jit(solution)/shard_map/ppermute | solution.py:177
  7.1 3.2 %copy-start.2 = (s32[1,2]{1,0:T(1,128)S(1)}, s32[1,2]{1,0:T(1,128)}, u32[]{:S(2)}) copy-start(s32[1,2]{1,0:T(1,128)} %param.27) | copy-start | bytes 28
  7.1 15.1 %collective-permute-start.2 = (bf16[320,128]{0,1:T(8,128)(2,1)S(1)}, bf16[320,128]{0,1:T(8,128)(2,1)S(1)}, u32[]{:S(2)}, u32[]{:S(2)}) collective-permute-start(bf16[320,128]{0,1:T(8,128)(2,1)S(1)} %get-tuple-element.115), channel_id=1, source_target_pairs={{0,1},{1,2},{2,3},{3,0},{4,5},{5,6},{6,7},{7,4},{8,9},{9,10},{10,1... | collective-permute-start | bytes 245768 | tf_op jit(solution)/shard_map/ppermute | solution.py:177
  18.7 29.6 %collective-permute-start.5 = (f32[256,3,128]{0,2,1:T(8,128)}, f32[256,3,128]{0,2,1:T(8,128)S(1)}, u32[]{:S(2)}, u32[]{:S(2)}) collective-permute-start(f32[256,3,128]{0,2,1:T(8,128)} %get-tuple-element.100), channel_id=1, source_target_pairs={{0,1},{1,2},{2,3},{3,0},{4,5},{5,6},{6,7},{7,4},{8,9},{9,10},{10,1... | collective-permute-start | bytes 1179656 | tf_op jit(solution)/shard_map/ppermute | solution.py:19
  20.9 27.4 %collective-permute-start.6 = (f32[256,3,128]{0,2,1:T(8,128)S(1)}, f32[256,3,128]{0,2,1:T(8,128)S(1)}, u32[]{:S(2)}, u32[]{:S(2)}) collective-permute-start(f32[256,3,128]{0,2,1:T(8,128)S(1)} %get-tuple-element.101), channel_id=1, source_target_pairs={{1,0},{2,1},{3,2},{0,3},{5,4},{6,5},{7,6},{4,7},{9,8},{10,9},{11,1... | collective-permute-start | bytes 1179656 | tf_op jit(solution)/shard_map/ppermute | solution.py:21
  22.2 8.4 %collective-permute-start.3 = (bf16[256,512]{0,1:T(8,128)(2,1)S(1)}, bf16[256,512]{0,1:T(8,128)(2,1)S(1)}, u32[]{:S(2)}, u32[]{:S(2)}) collective-permute-start(bf16[256,512]{0,1:T(8,128)(2,1)S(1)} %get-tuple-element.108), channel_id=1, source_target_pairs={{0,4},{4,8},{8,12},{1,5},{5,9},{9,13},{2,6},{6,10},{10,14},{3,7},{... | collective-permute-start | bytes 786440 | tf_op jit(solution)/shard_map/ppermute | solution.py:187
  27.3 8.0 %collective-permute-start.4 = (bf16[256,512]{0,1:T(8,128)(2,1)S(1)}, bf16[256,512]{0,1:T(8,128)(2,1)S(1)}, u32[]{:S(2)}, u32[]{:S(2)}) collective-permute-start(bf16[256,512]{0,1:T(8,128)(2,1)S(1)} %get-tuple-element.108), channel_id=1, source_target_pairs={{4,0},{8,4},{12,8},{5,1},{9,5},{13,9},{6,2},{10,6},{14,10},{7,3},{... | collective-permute-start | bytes 786440 | tf_op jit(solution)/shard_map/ppermute | solution.py:188
  46.4 6.4 %collective-permute-start.10 = (f32[9,16,256]{2,1,0:T(8,128)S(1)}, f32[9,16,256]{2,1,0:T(8,128)S(1)}, u32[]{:S(2)}, u32[]{:S(2)}) collective-permute-start(f32[9,16,256]{2,1,0:T(8,128)S(1)} %get-tuple-element.104), channel_id=1, source_target_pairs={{0,8},{4,12},{8,0},{12,4},{1,9},{5,13},{9,1},{13,5},{2,10},{6,14},... | collective-permute-start | bytes 442376 | tf_op jit(solution)/shard_map/ppermute | solution.py:86
  46.5 6.7 %collective-permute-start.11 = (f32[9,16,256]{2,1,0:T(8,128)S(1)}, f32[9,16,256]{2,1,0:T(8,128)S(1)}, u32[]{:S(2)}, u32[]{:S(2)}) collective-permute-start(f32[9,16,256]{2,1,0:T(8,128)S(1)} %get-tuple-element.103), channel_id=1, source_target_pairs={{0,12},{4,8},{8,4},{12,0},{1,13},{5,9},{9,5},{13,1},{2,14},{6,10},... | collective-permute-start | bytes 442376 | tf_op jit(solution)/shard_map/ppermute | solution.py:86
  46.6 6.6 %collective-permute-start.9 = (f32[9,16,256]{2,1,0:T(8,128)S(1)}, f32[9,16,256]{2,1,0:T(8,128)S(1)}, u32[]{:S(2)}, u32[]{:S(2)}) collective-permute-start(f32[9,16,256]{2,1,0:T(8,128)S(1)} %get-tuple-element.102), channel_id=1, source_target_pairs={{0,4},{4,0},{8,12},{12,8},{1,5},{5,1},{9,13},{13,9},{2,6},{6,2},{1... | collective-permute-start | bytes 442376 | tf_op jit(solution)/shard_map/ppermute | solution.py:86
  48.4 8.7 %collective-permute-start.7 = (f32[256,1,128]{0,2,1:T(8,128)S(1)}, f32[256,1,128]{0,2,1:T(8,128)S(1)}, u32[]{:S(2)}, u32[]{:S(2)}) collective-permute-start(f32[256,1,128]{0,2,1:T(8,128)S(1)} %get-tuple-element.105), channel_id=1, source_target_pairs={{0,4},{4,8},{8,12},{1,5},{5,9},{9,13},{2,6},{6,10},{10,14},{3,7},{... | collective-permute-start | bytes 393224 | tf_op jit(solution)/shard_map/ppermute | solution.py:19
  50.4 6.8 %collective-permute-start.8 = (f32[256,1,128]{0,2,1:T(8,128)S(1)}, f32[256,1,128]{0,2,1:T(8,128)S(1)}, u32[]{:S(2)}, u32[]{:S(2)}) collective-permute-start(f32[256,1,128]{0,2,1:T(8,128)S(1)} %get-tuple-element.106), channel_id=1, source_target_pairs={{4,0},{8,4},{12,8},{5,1},{9,5},{13,9},{6,2},{10,6},{14,10},{7,3},{... | collective-permute-start | bytes 393224 | tf_op jit(solution)/shard_map/ppermute | solution.py:21
  54.2 3.7 %collective-permute-start.12 = (f32[9,16,256]{2,1,0:T(8,128)S(1)}, f32[9,16,256]{2,1,0:T(8,128)S(1)}, u32[]{:S(2)}, u32[]{:S(2)}) collective-permute-start(f32[9,16,256]{2,1,0:T(8,128)S(1)} %get-tuple-element.99), channel_id=1, source_target_pairs={{0,4},{4,0},{8,12},{12,8},{1,5},{5,1},{9,13},{13,9},{2,6},{6,2},{1... | collective-permute-start | bytes 442376 | tf_op jit(solution)/shard_map/ppermute | solution.py:93
  55.4 5.4 %collective-permute-start.13 = (f32[9,16,256]{2,1,0:T(8,128)S(1)}, f32[9,16,256]{2,1,0:T(8,128)S(1)}, u32[]{:S(2)}, u32[]{:S(2)}) collective-permute-start(f32[9,16,256]{2,1,0:T(8,128)S(1)} %get-tuple-element.99), channel_id=1, source_target_pairs={{0,8},{4,12},{8,0},{12,4},{1,9},{5,13},{9,1},{13,5},{2,10},{6,14},... | collective-permute-start | bytes 442376 | tf_op jit(solution)/shard_map/ppermute | solution.py:93
  56.9 7.3 %collective-permute-start.14 = (f32[9,16,256]{2,1,0:T(8,128)S(1)}, f32[9,16,256]{2,1,0:T(8,128)S(1)}, u32[]{:S(2)}, u32[]{:S(2)}) collective-permute-start(f32[9,16,256]{2,1,0:T(8,128)S(1)} %get-tuple-element.99), channel_id=1, source_target_pairs={{0,12},{4,8},{8,4},{12,0},{1,13},{5,9},{9,5},{13,1},{2,14},{6,10},... | collective-permute-start | bytes 442376 | tf_op jit(solution)/shard_map/ppermute | solution.py:93
  64.2 0.8 %copy-start.1 = (f32[9,64,256]{2,1,0:T(8,128)}, f32[9,64,256]{2,1,0:T(8,128)S(1)}, u32[]{:S(2)}) copy-start(f32[9,64,256]{2,1,0:T(8,128)S(1)} %constant_dynamic-update-slice_fusion) | copy-start | bytes 1769476

commit v14 on v12

--- a/solution.py
+++ b/solution.py
@@ -95,44 +95,57 @@
     return out
 
 
-def row_kernel(ext_ref, mt_ref, w_ref, up_ref, out_ref, gt_ref, m_ref):
-    stencil_rows, channels, _ = ext_ref.shape
+def row_kernel(ext_ref, mt_ref, w_ref, up_ref, out_ref, gt_ref, acc_ref):
+    _, channels, _ = ext_ref.shape
     n_blocks, o_block, lon_cols = up_ref.shape
     kernels = w_ref.shape[0]
-    window_len = mt_ref.shape[1] // stencil_rows
+    window_len = mt_ref.shape[1]
     contract_last = (((1,), (1,)), ((), ()))
-    gt_ref[...] = jnp.zeros(gt_ref.shape, gt_ref.dtype)
-    for r in range(stencil_rows):
-        m_ref[r] = mt_ref[:, pl.ds(r * window_len, window_len)].T
+    r = pl.program_id(0)
+
+    @pl.when(r == 0)
+    def _():
+        acc_ref[...] = jnp.zeros(acc_ref.shape, acc_ref.dtype)
+
     for d in range(n_blocks):
-        acc = None
-        for r in range(stencil_rows):
-            win = ext_ref[r, :, pl.ds(d * lon_cols, window_len)]
-            part = jnp.dot(win, m_ref[r], preferred_element_type=jnp.float32)
-            acc = part if acc is None else acc + part
-        resp = acc.astype(jnp.bfloat16)
-        up_d = up_ref[d]
-        for k in range(kernels):
-            resp_k = resp[:, k * lon_cols : (k + 1) * lon_cols]
-            gt_ref[k] += lax.dot_general(
-                up_d, resp_k, contract_last, preferred_element_type=jnp.float32
-            )
-        if d == 0:
-            total = None
+        win = ext_ref[0, :, pl.ds(d * lon_cols, window_len)]
+        acc_ref[d] += lax.dot_general(
+            win, mt_ref[...], contract_last, preferred_element_type=jnp.float32
+        )
+
+    @pl.when(r == pl.num_programs(0) - 1)
+    def _():
+        grads = [None] * kernels
+        for d in range(n_blocks):
+            resp = acc_ref[d].astype(jnp.bfloat16)
+            up_d = up_ref[d]
             for k in range(kernels):
-                term = jnp.dot(
-                    w_ref[k],
+                term = lax.dot_general(
+                    up_d,
                     resp[:, k * lon_cols : (k + 1) * lon_cols],
+                    contract_last,
                     preferred_element_type=jnp.float32,
                 )
-                total = term if total is None else total + term
-            out_ref[...] = total.astype(out_ref.dtype)
+                grads[k] = term if grads[k] is None else grads[k] + term
+            if d == 0:
+                total = None
+                for k in range(kernels):
+                    term = jnp.dot(
+                        w_ref[k],
+                        resp[:, k * lon_cols : (k + 1) * lon_cols],
+                        preferred_element_type=jnp.float32,
+                    )
+                    total = term if total is None else total + term
+                out_ref[...] = total.astype(out_ref.dtype)
+        for k in range(kernels):
+            gt_ref[k] = grads[k]
 
 
 def row_products(ext, matrix, weights, up_rel):
-    stencil_rows, channels, _ = ext.shape
+    stencil_rows, channels, ext_width = ext.shape
     n_blocks, o_block, lon_cols = up_rel.shape
     kernels = weights.shape[0]
+    window_len = matrix.shape[1] // stencil_rows
     flops = 2 * n_blocks * channels * matrix.shape[0] * matrix.shape[1]
     flops += 2 * n_blocks * kernels * o_block * lon_cols * channels
     flops += 2 * kernels * weights.shape[1] * channels * lon_cols
@@ -140,11 +153,23 @@
     nbytes += 2 * weights.shape[1] * lon_cols + 4 * kernels * o_block * channels
     return pl.pallas_call(
         row_kernel,
+        grid=(stencil_rows,),
+        in_specs=[
+            pl.BlockSpec((1, channels, ext_width), lambda r: (r, 0, 0)),
+            pl.BlockSpec((matrix.shape[0], window_len), lambda r: (0, r)),
+            pl.BlockSpec(weights.shape, lambda r: (0, 0, 0)),
+            pl.BlockSpec(up_rel.shape, lambda r: (0, 0, 0)),
+        ],
+        out_specs=[
+            pl.BlockSpec((weights.shape[1], lon_cols), lambda r: (0, 0)),
+            pl.BlockSpec((kernels, o_block, channels), lambda r: (0, 0, 0)),
+        ],
         out_shape=(
             jax.ShapeDtypeStruct((weights.shape[1], lon_cols), jnp.bfloat16),
             jax.ShapeDtypeStruct((kernels, o_block, channels), jnp.float32),
         ),
-        scratch_shapes=[pltpu.VMEM((stencil_rows, matrix.shape[1] // stencil_rows, matrix.shape[0]), matrix.dtype)],
+        scratch_shapes=[pltpu.VMEM((n_blocks, channels, matrix.shape[0]), jnp.float32)],
+        compiler_params=pltpu.CompilerParams(dimension_semantics=("arbitrary",)),
         cost_estimate=pl.CostEstimate(flops=flops, transcendentals=0, bytes_accessed=nbytes),
     )(ext, matrix, weights, up_rel)
 

time: 63.9 us -> 64.1 us (level)
  transfers between devices with their start and end apart: 15 -> 15, of which waited for: 5 -> 5; matrix products, arithmetic and copies ran while one was open for 16% -> 16% of each run, Pallas kernels for 20% -> 21%
where the time goes in v14:
time: 64.1 us; the launch traced here: 63.5 us
  starting transfers between devices  24.1 us (38%)
  Pallas kernels  13.1 us (20%)
  waiting for transfers between devices  12 us (19%)
  local copies, waits for them, and re-layouts  6.99 us (11%)
  other arithmetic  3.8 us (6%)
  matrix products  1.86 us (3%)
  between operations  1.62 us (3%)
    pallas_call x1, Pallas kernels, row_products(): pl.pallas_call(row_kernel, grid=(stencil_rows,), in_specs=[pl.BlockSpec((...  8.8 us
    ppermute x3, waiting for transfers between devices, lat_allreduce(): recv = lax.ppermute(mine, axis, [(i, i ^ d) for i in range(count)])  6.21 us
    ppermute x1, starting transfers between devices, body(): below = lax.ppermute(row, 'lat', [(i, i + 1) for i in range(count - 1)])  5.08 us
    ppermute x1, waiting for transfers between devices, body(): above = lax.ppermute(row, 'lat', [(i + 1, i) for i in range(count - 1)])  4.69 us
    ppermute x3, starting transfers between devices, body(): lax.ppermute(jnp.concatenate([fields[:, 0], part], axis=0), 'lon', [(p, (...  4.66 us
    pallas_call x1, Pallas kernels, toeplitz(): pl.pallas_call(toeplitz_kernel, out_shape=(jax.ShapeDtypeStruct((kernels,...  4.32 us
    ppermute x2, starting transfers between devices, padded_2(): lax.ppermute(tail, axis, [(i, (i + 1) % count) for i in range(ends)])  4.17 us
    ppermute x2, starting transfers between devices, padded_2(): lax.ppermute(head, axis, [((i + 1) % count, i) for i in range(ends)])  3.47 us
  transfers between devices with their start and end apart: 15, of which 5 were waited for; matrix products, arithmetic and copies ran while one was open for 16% of the time, Pallas kernels for 21%

profile of v14, /device:TPU:1, one launch (start us, length us, event | category | flops | bytes accessed | tf_op | source)
XLA Modules:
  0.0 63.5 jit_solution(6458266758146949420)
XLA Ops:
  0.7 0.8 %dynamic-slice_bitcast_fusion = (bf16[1,64,128]{2,1,0:T(8,128)(2,1)S(1)}, bf16[64,128]{1,0:T(8,128)(2,1)S(1)}, bf16[64,128]{1,0:T(8,128)(2,1)S(1)}, bf16[64,128]{1,0:T(8,128)(2,1)S(1)}) fusion(bf16[256,1,128]{2,0,1:T(8,128)(2,1)} %param.23, s32[]{:T(128)S(6)} %select_n.57, s32[]{:T(128)S(6)} %select_n.55, s32[]{:T(128)S(6)} %select_n.53, s32[]{:T(128)S(6)} %select_n.51), kind=kLoop, calls=%fused_computation.35 | loop fusion | bytes 131088 | tf_op jit(solution)/shard_map/stack | solution.py:202
  1.5 0.9 %pad_maximum_fusion.5 = (bf16[320,128]{1,0:T(8,128)(2,1)S(1)}, bf16[320,128]{1,0:T(8,128)(2,1)S(1)}, bf16[320,128]{1,0:T(8,128)(2,1)S(1)}) fusion(bf16[64,128]{1,0:T(8,128)(2,1)S(1)} %get-tuple-element.112, bf16[256,128]{1,0:T(8,128)(2,1)} %bitcast.56, bf16[64,128]{1,0:T(8,128)(2,1)S(1)} %get-tuple-element.111, bf16[64,128]{1,0:T(8,128)(2,1)S(1)} %get-tuple-element.110), kind=kLoop, calls=%fused_computation.21 | loop fusion | flops 409600 | bytes 360448 | tf_op jit(solution)/shard_map/concatenate | solution.py:196
  2.4 4.2 %collective-permute-start = (bf16[320,128]{1,0:T(8,128)(2,1)S(1)}, bf16[320,128]{1,0:T(8,128)(2,1)S(1)}, u32[]{:S(2)}, u32[]{:S(2)}) collective-permute-start(bf16[320,128]{1,0:T(8,128)(2,1)S(1)} %get-tuple-element.113), channel_id=1, source_target_pairs={{0,3},{1,0},{2,1},{3,2},{4,7},{5,4},{6,5},{7,6},{8,11},{9,8},{10,9... | collective-permute-start | bytes 245768 | tf_op jit(solution)/shard_map/ppermute | solution.py:195
  6.6 0.5 collective-permute-start.2
  7.0 1.7 %convolution_convert_fusion = bf16[128,9,256]{2,0,1:T(8,128)(2,1)S(1)} fusion(bf16[9,256,256]{2,1,0:T(8,128)(2,1)} %w_ref.1, bf16[256,1,128]{2,0,1:T(8,128)(2,1)} %param.23), kind=kOutput, calls=%fused_computation | convolution fusion | flops 151289856 | bytes 1835008 | tf_op jit(solution)/shard_map/koc,oij->cikj/dot_general | solution.py:184
  8.7 1.1 %copy.19.grad_ref = bf16[256,1152]{1,0:T(8,128)(2,1)} copy(bf16[256,1152]{0,1:T(8,128)(2,1)S(1)} %bitcast.53) | data formatting | bytes 1179648 | tf_op jit(solution)/shard_map/reshape;squeeze | solution.py:187
  10.5 0.2 fusion.3
  10.8 0.6 %reshape.252.tap_ref = f32[27,384]{1,0:T(8,128)} reshape(f32[9,3,384]{2,1,0:T(4,128)S(1)} %copy.17) | data formatting | bytes 82944 | tf_op jit(solution)/shard_map/reshape | solution.py:65
  11.4 4.3 %shard_map.100 = (bf16[9,128,1152]{2,1,0:T(8,128)(2,1)}, f32[256,1152]{1,0:T(8,128)}) custom-call(f32[27,384]{1,0:T(8,128)} %reshape.252.tap_ref, bf16[256,1152]{1,0:T(8,128)(2,1)} %copy.19.grad_ref), custom_call_target="tpu_custom_call" | custom-call | tf_op jit(solution)/shard_map/pallas_call | solution.py:66
  15.7 1.6 %copy.20 = f32[256,1152]{0,1:T(8,128)S(1)} copy(f32[256,1152]{1,0:T(8,128)} %get-tuple-element.93) | data formatting | bytes 2359296 | tf_op jit(solution)/shard_map/pallas_call | solution.py:66
  17.5 2.3 %collective-permute-start.5 = (f32[256,3,128]{0,2,1:T(8,128)S(1)}, f32[256,3,128]{0,2,1:T(8,128)S(1)}, u32[]{:S(2)}, u32[]{:S(2)}) collective-permute-start(f32[256,3,128]{0,2,1:T(8,128)S(1)} %get-tuple-element.100), channel_id=1, source_target_pairs={{0,1},{1,2},{2,3},{3,0},{4,5},{5,6},{6,7},{7,4},{8,9},{9,10},{10,1... | collective-permute-start | bytes 1179656 | tf_op jit(solution)/shard_map/ppermute | solution.py:19
  19.7 1.1 %collective-permute-start.6 = (f32[256,3,128]{0,2,1:T(8,128)S(1)}, f32[256,3,128]{0,2,1:T(8,128)S(1)}, u32[]{:S(2)}, u32[]{:S(2)}) collective-permute-start(f32[256,3,128]{0,2,1:T(8,128)S(1)} %get-tuple-element.101), channel_id=1, source_target_pairs={{1,0},{2,1},{3,2},{0,3},{5,4},{6,5},{7,6},{4,7},{9,8},{10,9},{11,1... | collective-permute-start | bytes 1179656 | tf_op jit(solution)/shard_map/ppermute | solution.py:21
  20.9 5.1 %collective-permute-start.3 = (bf16[256,512]{1,0:T(8,128)(2,1)S(1)}, bf16[256,512]{1,0:T(8,128)(2,1)S(1)}, u32[]{:S(2)}, u32[]{:S(2)}) collective-permute-start(bf16[256,512]{1,0:T(8,128)(2,1)S(1)} %get-tuple-element.108), channel_id=1, source_target_pairs={{0,4},{4,8},{8,12},{1,5},{5,9},{9,13},{2,6},{6,10},{10,14},{3,7},{... | collective-permute-start | bytes 786440 | tf_op jit(solution)/shard_map/ppermute | solution.py:205
  26.0 1.9 %collective-permute-start.4 = (bf16[256,512]{1,0:T(8,128)(2,1)S(1)}, bf16[256,512]{1,0:T(8,128)(2,1)S(1)}, u32[]{:S(2)}, u32[]{:S(2)}) collective-permute-start(bf16[256,512]{1,0:T(8,128)(2,1)S(1)} %get-tuple-element.108), channel_id=1, source_target_pairs={{4,0},{8,4},{12,8},{5,1},{9,5},{13,9},{6,2},{10,6},{14,10},{7,3},{... | collective-permute-start | bytes 786440 | tf_op jit(solution)/shard_map/ppermute | solution.py:206
  27.9 0.6 %pad_maximum_fusion.8.up_ref = bf16[4,64,128]{2,1,0:T(8,128)(2,1)} fusion(bf16[1,64,128]{2,1,0:T(8,128)(2,1)S(1)} %slice_bitcast_fusion, bf16[1,64,128]{2,1,0:T(8,128)(2,1)S(1)} %slice_bitcast_fusion.1, bf16[1,64,128]{2,1,0:T(8,128)(2,1)S(1)} %slice_bitcast_fusion.2, bf16[1,64,128]{2,1,0:T(8,128)(2,1)S(1)} %get-tuple-element.109), kind=kLoop, calls=%fused_computation.24 | loop fusion | flops 98304 | bytes 131072 | tf_op jit(solution)/shard_map/stack | solution.py:202
  28.6 0.7 %collective-permute-done.3 = bf16[256,512]{1,0:T(8,128)(2,1)S(1)} collective-permute-done((bf16[256,512]{1,0:T(8,128)(2,1)S(1)}, bf16[256,512]{1,0:T(8,128)(2,1)S(1)}, u32[]{:S(2)}, u32[]{:S(2)}) %collective-permute-start.3) | collective-permute-done | bytes 262176 | tf_op jit(solution)/shard_map/ppermute | solution.py:205
  29.3 4.7 %collective-permute-done.4 = bf16[256,512]{1,0:T(8,128)(2,1)S(1)} collective-permute-done((bf16[256,512]{1,0:T(8,128)(2,1)S(1)}, bf16[256,512]{1,0:T(8,128)(2,1)S(1)}, u32[]{:S(2)}, u32[]{:S(2)}) %collective-permute-start.4) | collective-permute-done | bytes 262176 | tf_op jit(solution)/shard_map/ppermute | solution.py:206
  34.0 1.1 %fusion.ext_ref = bf16[3,256,768]{2,1,0:T(8,128)(2,1)} fusion(bf16[1,256,512]{2,1,0:T(8,128)(2,1)S(1)} %bitcast.55, bf16[1,256,512]{2,1,0:T(8,128)(2,1)S(1)} %get-tuple-element.107, bf16[1,256,512]{2,1,0:T(8,128)(2,1)S(1)} %bitcast.54), kind=kLoop, calls=%fused_computation.2 | loop fusion | flops 10616832 | bytes 1966080 | tf_op jit(solution)/shard_map/concatenate | solution.py:208
  35.1 8.8 %shard_map.101 = (bf16[256,128]{1,0:T(8,128)(2,1)}, f32[9,64,256]{2,1,0:T(8,128)}) custom-call(bf16[3,256,768]{2,1,0:T(8,128)(2,1)} %fusion.ext_ref, bf16[1152,1152]{1,0:T(8,128)(2,1)} %bitcast.58, bf16[9,256,256]{2,1,0:T(8,128)(2,1)} %w_ref.1, bf16[4,64,128]{2,1,0:T(8,128)(2,1)} %pad_maximum_fusion.8.up_ref), custom_call_target="tpu_custom_call" | custom-call | flops 3019898880 | bytes 5734400 | tf_op jit(solution)/shard_map/pallas_call | solution.py:154
  43.9 1.1 %constant_dynamic-slice_fusion.2 = (f32[9,16,256]{2,1,0:T(8,128)S(1)}, f32[9,16,256]{2,1,0:T(8,128)S(1)}, f32[9,16,256]{2,1,0:T(8,128)S(1)}) fusion(f32[9,64,256]{2,1,0:T(8,128)} %get-tuple-element.94, s32[]{:T(128)S(6)} %select_n.59, s32[]{:T(128)S(6)} %select_n.61, s32[]{:T(128)S(6)} %select_n.60), kind=kLoop, calls=%fused_computation.45 | loop fusion | bytes 884748 | tf_op jit(solution)/shard_map/dynamic_slice | solution.py:85
  45.1 1.8 %collective-permute-start.9 = (f32[9,16,256]{2,1,0:T(8,128)S(1)}, f32[9,16,256]{2,1,0:T(8,128)S(1)}, u32[]{:S(2)}, u32[]{:S(2)}) collective-permute-start(f32[9,16,256]{2,1,0:T(8,128)S(1)} %get-tuple-element.102), channel_id=1, source_target_pairs={{0,4},{4,0},{8,12},{12,8},{1,5},{5,1},{9,13},{13,9},{2,6},{6,2},{1... | collective-permute-start | bytes 442376 | tf_op jit(solution)/shard_map/ppermute | solution.py:86
  47.0 1.9 %collective-permute-start.7 = (f32[256,1,128]{0,2,1:T(8,128)S(1)}, f32[256,1,128]{0,2,1:T(8,128)S(1)}, u32[]{:S(2)}, u32[]{:S(2)}) collective-permute-start(f32[256,1,128]{0,2,1:T(8,128)S(1)} %get-tuple-element.105), channel_id=1, source_target_pairs={{0,4},{4,8},{8,12},{1,5},{5,9},{9,13},{2,6},{6,10},{10,14},{3,7},{... | collective-permute-start | bytes 393224 | tf_op jit(solution)/shard_map/ppermute | solution.py:19
  48.9 2.4 %collective-permute-start.8 = (f32[256,1,128]{0,2,1:T(8,128)S(1)}, f32[256,1,128]{0,2,1:T(8,128)S(1)}, u32[]{:S(2)}, u32[]{:S(2)}) collective-permute-start(f32[256,1,128]{0,2,1:T(8,128)S(1)} %get-tuple-element.106), channel_id=1, source_target_pairs={{4,0},{8,4},{12,8},{5,1},{9,5},{13,9},{6,2},{10,6},{14,10},{7,3},{... | collective-permute-start | bytes 393224 | tf_op jit(solution)/shard_map/ppermute | solution.py:21
  51.3 0.4 collective-permute-done.11
  51.8 1.0 %constant_dynamic-update-slice_fusion.3 = (f32[9,64,256]{2,1,0:T(8,128)S(1)}, f32[9,16,256]{2,1,0:T(8,128)S(1)}) fusion(f32[9,64,256]{2,1,0:T(8,128)S(1)} %broadcast_in_dim.25, s32[]{:T(128)S(6)} %select_n.58, f32[9,16,256]{2,1,0:T(8,128)S(1)} %collective-permute-done.10, f32[9,16,256]{2,1,0:T(8,128)S(1)} %collective-permute-done.11, ...), kind=kLoop, calls=%fused_computation.42 | loop fusion | flops 110592 | bytes 884740 | tf_op jit(solution)/shard_map/dynamic_update_slice | solution.py:91
  52.8 1.2 %collective-permute-start.12 = (f32[9,16,256]{2,1,0:T(8,128)S(1)}, f32[9,16,256]{2,1,0:T(8,128)S(1)}, u32[]{:S(2)}, u32[]{:S(2)}) collective-permute-start(f32[9,16,256]{2,1,0:T(8,128)S(1)} %get-tuple-element.99), channel_id=1, source_target_pairs={{0,4},{4,0},{8,12},{12,8},{1,5},{5,1},{9,13},{13,9},{2,6},{6,2},{1... | collective-permute-start | bytes 442376 | tf_op jit(solution)/shard_map/ppermute | solution.py:93
  53.9 1.5 %collective-permute-start.13 = (f32[9,16,256]{2,1,0:T(8,128)S(1)}, f32[9,16,256]{2,1,0:T(8,128)S(1)}, u32[]{:S(2)}, u32[]{:S(2)}) collective-permute-start(f32[9,16,256]{2,1,0:T(8,128)S(1)} %get-tuple-element.99), channel_id=1, source_target_pairs={{0,8},{4,12},{8,0},{12,4},{1,9},{5,13},{9,1},{13,5},{2,10},{6,14},... | collective-permute-start | bytes 442376 | tf_op jit(solution)/shard_map/ppermute | solution.py:93
  55.4 0.3 collective-permute-start.14
  55.7 0.7 %copy.21 = bf16[256,1,128]{2,0,1:T(8,128)(2,1)} copy(bf16[256,1,128]{0,2,1:T(8,128)(2,1)S(1)} %fusion.6) | data formatting | bytes 131072
  56.5 2.9 %collective-permute-done.13 = f32[9,16,256]{2,1,0:T(8,128)S(1)} collective-permute-done((f32[9,16,256]{2,1,0:T(8,128)S(1)}, f32[9,16,256]{2,1,0:T(8,128)S(1)}, u32[]{:S(2)}, u32[]{:S(2)}) %collective-permute-start.13) | collective-permute-done | bytes 147488 | tf_op jit(solution)/shard_map/ppermute | solution.py:93
  59.4 3.3 %collective-permute-done.14 = f32[9,16,256]{2,1,0:T(8,128)S(1)} collective-permute-done((f32[9,16,256]{2,1,0:T(8,128)S(1)}, f32[9,16,256]{2,1,0:T(8,128)S(1)}, u32[]{:S(2)}, u32[]{:S(2)}) %collective-permute-start.14) | collective-permute-done | bytes 147488 | tf_op jit(solution)/shard_map/ppermute | solution.py:93
  62.7 0.8 %copy-done.1 = f32[9,64,256]{2,1,0:T(8,128)} copy-done((f32[9,64,256]{2,1,0:T(8,128)}, f32[9,64,256]{2,1,0:T(8,128)S(1)}, u32[]{:S(2)}) %copy-start.1) | copy-done | bytes 589848
  (40 shorter events, 0.7 us)
Async XLA Ops:
  0.6 9.9 %copy-start = (bf16[1,9,3,2,64]{4,3,2,1,0:T(2,128)(2,1)S(1)}, bf16[1,9,3,2,64]{4,3,2,1,0:T(2,128)(2,1)}, u32[]{:S(2)}) copy-start(bf16[1,9,3,2,64]{4,3,2,1,0:T(2,128)(2,1)} %param.25) | copy-start | bytes 20740
  2.4 18.4 %collective-permute-start = (bf16[320,128]{1,0:T(8,128)(2,1)S(1)}, bf16[320,128]{1,0:T(8,128)(2,1)S(1)}, u32[]{:S(2)}, u32[]{:S(2)}) collective-permute-start(bf16[320,128]{1,0:T(8,128)(2,1)S(1)} %get-tuple-element.113), channel_id=1, source_target_pairs={{0,3},{1,0},{2,1},{3,2},{4,7},{5,4},{6,5},{7,6},{8,11},{9,8},{10,9... | collective-permute-start | bytes 245768 | tf_op jit(solution)/shard_map/ppermute | solution.py:195
  6.6 14.2 %collective-permute-start.1 = (bf16[320,128]{1,0:T(8,128)(2,1)S(1)}, bf16[320,128]{1,0:T(8,128)(2,1)S(1)}, u32[]{:S(2)}, u32[]{:S(2)}) collective-permute-start(bf16[320,128]{1,0:T(8,128)(2,1)S(1)} %get-tuple-element.114), channel_id=1, source_target_pairs={{0,2},{1,3},{2,0},{3,1},{4,6},{5,7},{6,4},{7,5},{8,10},{9,11},{10,... | collective-permute-start | bytes 245768 | tf_op jit(solution)/shard_map/ppermute | solution.py:195
  6.6 3.2 %copy-start.3 = (s32[1,2]{1,0:T(1,128)S(1)}, s32[1,2]{1,0:T(1,128)}, u32[]{:S(2)}) copy-start(s32[1,2]{1,0:T(1,128)} %param.27) | copy-start | bytes 28
  6.6 14.2 %collective-permute-start.2 = (bf16[320,128]{1,0:T(8,128)(2,1)S(1)}, bf16[320,128]{1,0:T(8,128)(2,1)S(1)}, u32[]{:S(2)}, u32[]{:S(2)}) collective-permute-start(bf16[320,128]{1,0:T(8,128)(2,1)S(1)} %get-tuple-element.115), channel_id=1, source_target_pairs={{0,1},{1,2},{2,3},{3,0},{4,5},{5,6},{6,7},{7,4},{8,9},{9,10},{10,1... | collective-permute-start | bytes 245768 | tf_op jit(solution)/shard_map/ppermute | solution.py:195
  17.4 3.5 %copy-start.2 = (bf16[256,1,128]{2,0,1:T(8,128)(2,1)S(1)}, bf16[256,1,128]{2,0,1:T(8,128)(2,1)}, u32[]{:S(2)}) copy-start(bf16[256,1,128]{2,0,1:T(8,128)(2,1)} %param.22) | copy-start | bytes 196612
  17.5 29.4 %collective-permute-start.5 = (f32[256,3,128]{0,2,1:T(8,128)S(1)}, f32[256,3,128]{0,2,1:T(8,128)S(1)}, u32[]{:S(2)}, u32[]{:S(2)}) collective-permute-start(f32[256,3,128]{0,2,1:T(8,128)S(1)} %get-tuple-element.100), channel_id=1, source_target_pairs={{0,1},{1,2},{2,3},{3,0},{4,5},{5,6},{6,7},{7,4},{8,9},{9,10},{10,1... | collective-permute-start | bytes 1179656 | tf_op jit(solution)/shard_map/ppermute | solution.py:19
  19.7 27.2 %collective-permute-start.6 = (f32[256,3,128]{0,2,1:T(8,128)S(1)}, f32[256,3,128]{0,2,1:T(8,128)S(1)}, u32[]{:S(2)}, u32[]{:S(2)}) collective-permute-start(f32[256,3,128]{0,2,1:T(8,128)S(1)} %get-tuple-element.101), channel_id=1, source_target_pairs={{1,0},{2,1},{3,2},{0,3},{5,4},{6,5},{7,6},{4,7},{9,8},{10,9},{11,1... | collective-permute-start | bytes 1179656 | tf_op jit(solution)/shard_map/ppermute | solution.py:21
  20.9 8.4 %collective-permute-start.3 = (bf16[256,512]{1,0:T(8,128)(2,1)S(1)}, bf16[256,512]{1,0:T(8,128)(2,1)S(1)}, u32[]{:S(2)}, u32[]{:S(2)}) collective-permute-start(bf16[256,512]{1,0:T(8,128)(2,1)S(1)} %get-tuple-element.108), channel_id=1, source_target_pairs={{0,4},{4,8},{8,12},{1,5},{5,9},{9,13},{2,6},{6,10},{10,14},{3,7},{... | collective-permute-start | bytes 786440 | tf_op jit(solution)/shard_map/ppermute | solution.py:205
  26.0 8.0 %collective-permute-start.4 = (bf16[256,512]{1,0:T(8,128)(2,1)S(1)}, bf16[256,512]{1,0:T(8,128)(2,1)S(1)}, u32[]{:S(2)}, u32[]{:S(2)}) collective-permute-start(bf16[256,512]{1,0:T(8,128)(2,1)S(1)} %get-tuple-element.108), channel_id=1, source_target_pairs={{4,0},{8,4},{12,8},{5,1},{9,5},{13,9},{6,2},{10,6},{14,10},{7,3},{... | collective-permute-start | bytes 786440 | tf_op jit(solution)/shard_map/ppermute | solution.py:206
  44.9 6.4 %collective-permute-start.10 = (f32[9,16,256]{2,1,0:T(8,128)S(1)}, f32[9,16,256]{2,1,0:T(8,128)S(1)}, u32[]{:S(2)}, u32[]{:S(2)}) collective-permute-start(f32[9,16,256]{2,1,0:T(8,128)S(1)} %get-tuple-element.104), channel_id=1, source_target_pairs={{0,8},{4,12},{8,0},{12,4},{1,9},{5,13},{9,1},{13,5},{2,10},{6,14},... | collective-permute-start | bytes 442376 | tf_op jit(solution)/shard_map/ppermute | solution.py:86
  45.0 6.7 %collective-permute-start.11 = (f32[9,16,256]{2,1,0:T(8,128)S(1)}, f32[9,16,256]{2,1,0:T(8,128)S(1)}, u32[]{:S(2)}, u32[]{:S(2)}) collective-permute-start(f32[9,16,256]{2,1,0:T(8,128)S(1)} %get-tuple-element.103), channel_id=1, source_target_pairs={{0,12},{4,8},{8,4},{12,0},{1,13},{5,9},{9,5},{13,1},{2,14},{6,10},... | collective-permute-start | bytes 442376 | tf_op jit(solution)/shard_map/ppermute | solution.py:86
  45.1 6.6 %collective-permute-start.9 = (f32[9,16,256]{2,1,0:T(8,128)S(1)}, f32[9,16,256]{2,1,0:T(8,128)S(1)}, u32[]{:S(2)}, u32[]{:S(2)}) collective-permute-start(f32[9,16,256]{2,1,0:T(8,128)S(1)} %get-tuple-element.102), channel_id=1, source_target_pairs={{0,4},{4,0},{8,12},{12,8},{1,5},{5,1},{9,13},{13,9},{2,6},{6,2},{1... | collective-permute-start | bytes 442376 | tf_op jit(solution)/shard_map/ppermute | solution.py:86
  47.0 8.7 %collective-permute-start.7 = (f32[256,1,128]{0,2,1:T(8,128)S(1)}, f32[256,1,128]{0,2,1:T(8,128)S(1)}, u32[]{:S(2)}, u32[]{:S(2)}) collective-permute-start(f32[256,1,128]{0,2,1:T(8,128)S(1)} %get-tuple-element.105), channel_id=1, source_target_pairs={{0,4},{4,8},{8,12},{1,5},{5,9},{9,13},{2,6},{6,10},{10,14},{3,7},{... | collective-permute-start | bytes 393224 | tf_op jit(solution)/shard_map/ppermute | solution.py:19
  48.9 6.8 %collective-permute-start.8 = (f32[256,1,128]{0,2,1:T(8,128)S(1)}, f32[256,1,128]{0,2,1:T(8,128)S(1)}, u32[]{:S(2)}, u32[]{:S(2)}) collective-permute-start(f32[256,1,128]{0,2,1:T(8,128)S(1)} %get-tuple-element.106), channel_id=1, source_target_pairs={{4,0},{8,4},{12,8},{5,1},{9,5},{13,9},{6,2},{10,6},{14,10},{7,3},{... | collective-permute-start | bytes 393224 | tf_op jit(solution)/shard_map/ppermute | solution.py:21
  52.8 3.7 %collective-permute-start.12 = (f32[9,16,256]{2,1,0:T(8,128)S(1)}, f32[9,16,256]{2,1,0:T(8,128)S(1)}, u32[]{:S(2)}, u32[]{:S(2)}) collective-permute-start(f32[9,16,256]{2,1,0:T(8,128)S(1)} %get-tuple-element.99), channel_id=1, source_target_pairs={{0,4},{4,0},{8,12},{12,8},{1,5},{5,1},{9,13},{13,9},{2,6},{6,2},{1... | collective-permute-start | bytes 442376 | tf_op jit(solution)/shard_map/ppermute | solution.py:93
  53.9 5.4 %collective-permute-start.13 = (f32[9,16,256]{2,1,0:T(8,128)S(1)}, f32[9,16,256]{2,1,0:T(8,128)S(1)}, u32[]{:S(2)}, u32[]{:S(2)}) collective-permute-start(f32[9,16,256]{2,1,0:T(8,128)S(1)} %get-tuple-element.99), channel_id=1, source_target_pairs={{0,8},{4,12},{8,0},{12,4},{1,9},{5,13},{9,1},{13,5},{2,10},{6,14},... | collective-permute-start | bytes 442376 | tf_op jit(solution)/shard_map/ppermute | solution.py:93
  55.4 7.3 %collective-permute-start.14 = (f32[9,16,256]{2,1,0:T(8,128)S(1)}, f32[9,16,256]{2,1,0:T(8,128)S(1)}, u32[]{:S(2)}, u32[]{:S(2)}) collective-permute-start(f32[9,16,256]{2,1,0:T(8,128)S(1)} %get-tuple-element.99), channel_id=1, source_target_pairs={{0,12},{4,8},{8,4},{12,0},{1,13},{5,9},{9,5},{13,1},{2,14},{6,10},... | collective-permute-start | bytes 442376 | tf_op jit(solution)/shard_map/ppermute | solution.py:93
  62.7 0.8 %copy-start.1 = (f32[9,64,256]{2,1,0:T(8,128)}, f32[9,64,256]{2,1,0:T(8,128)S(1)}, u32[]{:S(2)}) copy-start(f32[9,64,256]{2,1,0:T(8,128)S(1)} %constant_dynamic-update-slice_fusion) | copy-start | bytes 1769476

commit v15 on v14

--- a/solution.py
+++ b/solution.py
@@ -93,6 +93,39 @@
         recv = lax.ppermute(mine, axis, [(i, i ^ d) for i in range(count)])
         out = lax.dynamic_update_slice_in_dim(out, recv, (index ^ d) * size, axis=dim)
     return out
+
+
+def lat_allreduce_with_rims(x, axis, dim, interior):
+    count = lax.axis_size(axis)
+    index = lax.axis_index(axis)
+    size = x.shape[dim] // count
+    odd = (index & 1) == 1
+    lanes = interior.shape[2]
+    chunk_shape = lax.dynamic_slice_in_dim(x, 0, size, axis=dim).shape
+    parts = [lax.dynamic_slice_in_dim(x, index * size, size, axis=dim)]
+    rims = {}
+    for d in range(1, count):
+        send = lax.dynamic_slice_in_dim(x, (index ^ d) * size, size, axis=dim).reshape(-1, lanes)
+        rows = send.shape[0]
+        if d in (1, 3):
+            to_upper = jnp.logical_not(odd) if d == 1 else odd
+            edge = jnp.where(to_upper, interior[:, 2], interior[:, 0])
+            send = jnp.concatenate([send, edge], axis=0)
+        got = lax.ppermute(send, axis, [(i, i ^ d) for i in range(count)])
+        parts.append(got[:rows].reshape(chunk_shape))
+        if d in (1, 3):
+            rims[d] = got[rows:]
+    while len(parts) > 1:
+        parts = [parts[2 * e] + parts[2 * e + 1] for e in range(len(parts) // 2)]
+    mine = parts[0]
+    out = jnp.zeros(x.shape, x.dtype)
+    out = lax.dynamic_update_slice_in_dim(out, mine, index * size, axis=dim)
+    for d in range(1, count):
+        recv = lax.ppermute(mine, axis, [(i, i ^ d) for i in range(count)])
+        out = lax.dynamic_update_slice_in_dim(out, recv, (index ^ d) * size, axis=dim)
+    middle = (index == 1) | (index == 2)
+    result = interior[:, 1] + rims[1] + jnp.where(middle, rims[3], jnp.zeros_like(rims[3]))
+    return out, result
 
 
 def row_kernel(ext_ref, mt_ref, w_ref, up_ref, out_ref, gt_ref, acc_ref):
@@ -208,24 +241,23 @@
     ext = jnp.concatenate([rows[:, :, rows.shape[2] - HALO :], rows, rows[:, :, :HALO]], axis=2)
     out_row, grad_terms = row_products(ext, matrix, weights, up_rel)
     outputs = out_row[:, None, :]
-    weight_grad = lat_allreduce(grad_terms, "lat", 1)
-    accumulated = jnp.zeros((channels, lat_rows + 2, window_len), jnp.float32)
-    cycle_row = 0
-    accumulated = accumulated.at[:, cycle_row : cycle_row + 3].add(
-        contrib.reshape(channels, 3, window_len)
-    )
-    rim_columns = jnp.concatenate(
-        [accumulated[:, :, :HALO], accumulated[:, :, HALO + lon_cols :]], axis=2
-    )
+    terms = contrib.reshape(channels, 3, window_len)
+    rim_columns = jnp.concatenate([terms[:, :, :HALO], terms[:, :, HALO + lon_cols :]], axis=2)
     arrived = padded_2(rim_columns, (("lon", 2),), HALO, True)
-    interior = accumulated[:, :, HALO : HALO + lon_cols]
+    interior = terms[:, :, HALO : HALO + lon_cols]
     interior = interior.at[:, :, :HALO].add(arrived[:, :, :HALO])
     interior = interior.at[:, :, lon_cols - HALO :].add(arrived[:, :, 3 * HALO :])
-    edge_rows = jnp.stack([interior[:, 0], interior[:, lat_rows + 1]], axis=1)
-    arrived = padded_2(edge_rows, (("lat", 1),), 1, False)
-    result = interior[:, 1 : lat_rows + 1]
-    result = result.at[:, 0].add(arrived[:, 0])
-    result = result.at[:, lat_rows - 1].add(arrived[:, 3])
+    chunk = grad_terms.size // 4
+    if lax.axis_size("lat") == 4 and grad_terms.shape[1] % 4 == 0 and chunk % lon_cols == 0:
+        weight_grad, result = lat_allreduce_with_rims(grad_terms, "lat", 1, interior)
+        result = result[:, None, :]
+    else:
+        weight_grad = lat_allreduce(grad_terms, "lat", 1)
+        edge_rows = jnp.stack([interior[:, 0], interior[:, 2]], axis=1)
+        arrived = padded_2(edge_rows, (("lat", 1),), 1, False)
+        result = interior[:, 1:2]
+        result = result.at[:, 0].add(arrived[:, 0])
+        result = result.at[:, 0].add(arrived[:, 3])
     return (outputs, result.astype(jnp.bfloat16), weight_grad)
 
 

time: 64.1 us -> 68.8 us (1.073)
  waiting for transfers between devices: 12 us -> 17.1 us
  starting transfers between devices: 24.1 us -> 21.8 us
  local copies, waits for them, and re-layouts: 6.99 us -> 8.45 us
    ppermute x6, waiting for transfers between devices: 6.6 us -> 11.7 us  [the longest x3 6.13 us: lat_allreduce_with_rims(): recv = lax.ppermute(mine, axis, [(i, i ^ d) for i in range(count)])]
    ppermute x2 -> x1, starting transfers between devices: 3.47 us -> 1.07 us  [padded_2(): lax.ppermute(head, axis, [((i + 1) % count, i) for i in range(ends)])]
    ppermute x6, starting transfers between devices: 4.83 us -> 6.89 us  [the longest x3 4.58 us: lat_allreduce_with_rims(): recv = lax.ppermute(mine, axis, [(i, i ^ d) for i in range(count)])]
    ppermute x2 -> x1, starting transfers between devices: 4.17 us -> 2.2 us  [padded_2(): lax.ppermute(tail, axis, [(i, (i + 1) % count) for i in range(ends)])]
    slice x2 -> x3, local copies, waits for them, and re-layouts: 0.09 us -> 0.95 us  [the longest x1 0.84 us: body(): terms[:, :, HALO + lon_cols:]]
  transfers between devices with their start and end apart: 15 -> 13, of which waited for: 5 -> 5; matrix products, arithmetic and copies ran while one was open for 16% -> 16% of each run, Pallas kernels for 21% -> 19%
where the time goes in v15:
time: 68.8 us; the launch traced here: 68.2 us
  starting transfers between devices  21.8 us (32%)
  waiting for transfers between devices  17.1 us (25%)
  Pallas kernels  13.1 us (19%)
  local copies, waits for them, and re-layouts  8.45 us (12%)
  other arithmetic  4.19 us (6%)
  matrix products  1.86 us (3%)
  between operations  1.7 us (2%)
    pallas_call x1, Pallas kernels, row_products(): pl.pallas_call(row_kernel, grid=(stencil_rows,), in_specs=[pl.BlockSpec((...  8.8 us
    ppermute x3, waiting for transfers between devices, lat_allreduce_with_rims(): recv = lax.ppermute(mine, axis, [(i, i ^ d) for i in range(count)])  6.13 us
    ppermute x3, waiting for transfers between devices, lat_allreduce_with_rims(): got = lax.ppermute(send, axis, [(i, i ^ d) for i in range(count)])  5.58 us
    ppermute x1, starting transfers between devices, body(): below = lax.ppermute(row, 'lat', [(i, i + 1) for i in range(count - 1)])  5.08 us
    ppermute x1, waiting for transfers between devices, body(): above = lax.ppermute(row, 'lat', [(i + 1, i) for i in range(count - 1)])  4.69 us
    ppermute x3, starting transfers between devices, body(): lax.ppermute(jnp.concatenate([fields[:, 0], part], axis=0), 'lon', [(p, (...  4.66 us
    ppermute x3, starting transfers between devices, lat_allreduce_with_rims(): recv = lax.ppermute(mine, axis, [(i, i ^ d) for i in range(count)])  4.58 us
    pallas_call x1, Pallas kernels, toeplitz(): pl.pallas_call(toeplitz_kernel, out_shape=(jax.ShapeDtypeStruct((kernels,...  4.33 us
  transfers between devices with their start and end apart: 13, of which 5 were waited for; matrix products, arithmetic and copies ran while one was open for 16% of the time, Pallas kernels for 19%

profile of v15, /device:TPU:1, one launch (start us, length us, event | category | flops | bytes accessed | tf_op | source)
XLA Modules:
  0.0 68.2 jit_solution(11935905502863106115)
XLA Ops:
  0.7 0.8 %dynamic-slice_bitcast_fusion = (bf16[1,64,128]{2,1,0:T(8,128)(2,1)S(1)}, bf16[64,128]{1,0:T(8,128)(2,1)S(1)}, bf16[64,128]{1,0:T(8,128)(2,1)S(1)}, bf16[64,128]{1,0:T(8,128)(2,1)S(1)}) fusion(bf16[256,1,128]{2,0,1:T(8,128)(2,1)} %param.15, s32[]{:T(128)S(6)} %select_n.83, s32[]{:T(128)S(6)} %select_n.81, s32[]{:T(128)S(6)} %select_n.79, s32[]{:T(128)S(6)} %select_n.77), kind=kLoop, calls=%fused_computation.43 | loop fusion | bytes 131088 | tf_op jit(solution)/shard_map/stack | solution.py:235
  1.5 0.9 %pad_maximum_fusion.7 = (bf16[320,128]{1,0:T(8,128)(2,1)S(1)}, bf16[320,128]{1,0:T(8,128)(2,1)S(1)}, bf16[320,128]{1,0:T(8,128)(2,1)S(1)}) fusion(bf16[64,128]{1,0:T(8,128)(2,1)S(1)} %get-tuple-element.71, bf16[256,128]{1,0:T(8,128)(2,1)} %bitcast.68, bf16[64,128]{1,0:T(8,128)(2,1)S(1)} %get-tuple-element.70, bf16[64,128]{1,0:T(8,128)(2,1)S(1)} %get-tuple-element.69), kind=kLoop, calls=%fused_computation.28 | loop fusion | flops 409600 | bytes 360448 | tf_op jit(solution)/shard_map/concatenate | solution.py:229
  2.4 4.2 %collective-permute-start = (bf16[320,128]{1,0:T(8,128)(2,1)S(1)}, bf16[320,128]{1,0:T(8,128)(2,1)S(1)}, u32[]{:S(2)}, u32[]{:S(2)}) collective-permute-start(bf16[320,128]{1,0:T(8,128)(2,1)S(1)} %get-tuple-element.72), channel_id=1, source_target_pairs={{0,3},{1,0},{2,1},{3,2},{4,7},{5,4},{6,5},{7,6},{8,11},{9,8},{10,9... | collective-permute-start | bytes 245768 | tf_op jit(solution)/shard_map/ppermute | solution.py:228
  6.6 0.5 collective-permute-start.2
  7.0 1.7 %convolution_convert_fusion = bf16[128,9,256]{2,0,1:T(8,128)(2,1)S(1)} fusion(bf16[9,256,256]{2,1,0:T(8,128)(2,1)} %w_ref.1, bf16[256,1,128]{2,0,1:T(8,128)(2,1)} %param.15), kind=kOutput, calls=%fused_computation | convolution fusion | flops 151289856 | bytes 1835008 | tf_op jit(solution)/shard_map/koc,oij->cikj/dot_general | solution.py:217
  8.7 1.1 %copy.27.grad_ref = bf16[256,1152]{1,0:T(8,128)(2,1)} copy(bf16[256,1152]{0,1:T(8,128)(2,1)S(1)} %bitcast.65) | data formatting | bytes 1179648 | tf_op jit(solution)/shard_map/reshape;squeeze | solution.py:220
  10.5 0.2 fusion.3
  10.8 0.6 reshape.188.tap_ref
  11.4 4.3 %shard_map.95 = (bf16[9,128,1152]{2,1,0:T(8,128)(2,1)}, f32[256,1152]{1,0:T(8,128)}) custom-call(f32[27,384]{1,0:T(8,128)} %reshape.188.tap_ref, bf16[256,1152]{1,0:T(8,128)(2,1)} %copy.27.grad_ref), custom_call_target="tpu_custom_call" | custom-call | tf_op jit(solution)/shard_map/pallas_call | solution.py:66
  15.7 1.6 %copy.28 = f32[256,1152]{0,1:T(8,128)S(1)} copy(f32[256,1152]{1,0:T(8,128)} %get-tuple-element.49) | data formatting | bytes 2359296 | tf_op jit(solution)/shard_map/pallas_call | solution.py:66
  17.4 0.8 %fusion.21 = (f32[256,3,128]{0,2,1:T(8,128)}, f32[256,3,128]{0,2,1:T(8,128)S(1)}) fusion(f32[256,3,384]{0,2,1:T(8,128)S(1)} %bitcast.63), kind=kLoop, calls=%fused_computation.60 | loop fusion | bytes 1572864 | tf_op jit(solution)/shard_map/slice | solution.py:245
  18.2 2.2 %collective-permute-start.5 = (f32[256,3,128]{0,2,1:T(8,128)}, f32[256,3,128]{0,2,1:T(8,128)S(1)}, u32[]{:S(2)}, u32[]{:S(2)}) collective-permute-start(f32[256,3,128]{0,2,1:T(8,128)} %get-tuple-element.59), channel_id=1, source_target_pairs={{0,1},{1,2},{2,3},{3,0},{4,5},{5,6},{6,7},{7,4},{8,9},{9,10},{10,1... | collective-permute-start | bytes 1179656 | tf_op jit(solution)/shard_map/ppermute | solution.py:19
  20.4 1.1 %collective-permute-start.6 = (f32[256,3,128]{0,2,1:T(8,128)S(1)}, f32[256,3,128]{0,2,1:T(8,128)S(1)}, u32[]{:S(2)}, u32[]{:S(2)}) collective-permute-start(f32[256,3,128]{0,2,1:T(8,128)S(1)} %get-tuple-element.60), channel_id=1, source_target_pairs={{1,0},{2,1},{3,2},{0,3},{5,4},{6,5},{7,6},{4,7},{9,8},{10,9},{11,1... | collective-permute-start | bytes 1179656 | tf_op jit(solution)/shard_map/ppermute | solution.py:21
  21.6 5.1 %collective-permute-start.3 = (bf16[256,512]{1,0:T(8,128)(2,1)S(1)}, bf16[256,512]{1,0:T(8,128)(2,1)S(1)}, u32[]{:S(2)}, u32[]{:S(2)}) collective-permute-start(bf16[256,512]{1,0:T(8,128)(2,1)S(1)} %get-tuple-element.67), channel_id=1, source_target_pairs={{0,4},{4,8},{8,12},{1,5},{5,9},{9,13},{2,6},{6,10},{10,14},{3,7},{... | collective-permute-start | bytes 786440 | tf_op jit(solution)/shard_map/ppermute | solution.py:238
  26.7 1.9 %collective-permute-start.4 = (bf16[256,512]{1,0:T(8,128)(2,1)S(1)}, bf16[256,512]{1,0:T(8,128)(2,1)S(1)}, u32[]{:S(2)}, u32[]{:S(2)}) collective-permute-start(bf16[256,512]{1,0:T(8,128)(2,1)S(1)} %get-tuple-element.67), channel_id=1, source_target_pairs={{4,0},{8,4},{12,8},{5,1},{9,5},{13,9},{6,2},{10,6},{14,10},{7,3},{... | collective-permute-start | bytes 786440 | tf_op jit(solution)/shard_map/ppermute | solution.py:239
  28.6 0.6 pad_maximum_fusion.10.up_ref
  29.3 0.7 %collective-permute-done.3 = bf16[256,512]{1,0:T(8,128)(2,1)S(1)} collective-permute-done((bf16[256,512]{1,0:T(8,128)(2,1)S(1)}, bf16[256,512]{1,0:T(8,128)(2,1)S(1)}, u32[]{:S(2)}, u32[]{:S(2)}) %collective-permute-start.3) | collective-permute-done | bytes 262176 | tf_op jit(solution)/shard_map/ppermute | solution.py:238
  30.0 4.7 %collective-permute-done.4 = bf16[256,512]{1,0:T(8,128)(2,1)S(1)} collective-permute-done((bf16[256,512]{1,0:T(8,128)(2,1)S(1)}, bf16[256,512]{1,0:T(8,128)(2,1)S(1)}, u32[]{:S(2)}, u32[]{:S(2)}) %collective-permute-start.4) | collective-permute-done | bytes 262176 | tf_op jit(solution)/shard_map/ppermute | solution.py:239
  34.7 1.1 %fusion.ext_ref = bf16[3,256,768]{2,1,0:T(8,128)(2,1)} fusion(bf16[1,256,512]{2,1,0:T(8,128)(2,1)S(1)} %bitcast.67, bf16[1,256,512]{2,1,0:T(8,128)(2,1)S(1)} %get-tuple-element.66, bf16[1,256,512]{2,1,0:T(8,128)(2,1)S(1)} %bitcast.66), kind=kLoop, calls=%fused_computation.2 | loop fusion | flops 10616832 | bytes 1966080 | tf_op jit(solution)/shard_map/concatenate | solution.py:241
  35.8 8.8 %shard_map.96 = (bf16[256,128]{1,0:T(8,128)(2,1)}, f32[9,64,256]{2,1,0:T(8,128)}) custom-call(bf16[3,256,768]{2,1,0:T(8,128)(2,1)} %fusion.ext_ref, bf16[1152,1152]{1,0:T(8,128)(2,1)} %bitcast.70, bf16[9,256,256]{2,1,0:T(8,128)(2,1)} %w_ref.1, bf16[4,64,128]{2,1,0:T(8,128)(2,1)} %pad_maximum_fusion.10.up_ref), custom_call_target="tpu_custom_call" | custom-call | flops 3019898880 | bytes 5734400 | tf_op jit(solution)/shard_map/pallas_call | solution.py:187
  44.6 1.1 %constant_dynamic-slice_fusion = (f32[9,16,256]{2,1,0:T(8,128)S(1)}, f32[9,16,256]{2,1,0:T(8,128)S(1)}, f32[9,16,256]{2,1,0:T(8,128)S(1)}) fusion(f32[9,64,256]{2,1,0:T(8,128)} %get-tuple-element.50, s32[]{:T(128)S(6)} %select_n.95, s32[]{:T(128)S(6)} %select_n.89, s32[]{:T(128)S(6)} %select_n.84), kind=kLoop, calls=%fused_computation.51 | loop fusion | bytes 884748 | tf_op jit(solution)/shard_map/dynamic_slice | solution.py:108
  45.7 0.1 copy.30
  46.7 2.2 %collective-permute-start.7 = (f32[544,128]{0,1:T(8,128)S(1)}, f32[544,128]{0,1:T(8,128)S(1)}, u32[]{:S(2)}, u32[]{:S(2)}) collective-permute-start(f32[544,128]{0,1:T(8,128)S(1)} %pad_maximum_fusion.4), channel_id=1, source_target_pairs={{0,4},{4,0},{8,12},{12,8},{1,5},{5,1},{9,13},{13,9},{2,6},{6,2},{1... | collective-permute-start | bytes 835592 | tf_op jit(solution)/shard_map/ppermute | solution.py:114
  48.8 5.6 %collective-permute-done.9 = f32[288,128]{0,1:T(8,128)S(1)} collective-permute-done((f32[288,128]{0,1:T(8,128)S(1)}, f32[288,128]{0,1:T(8,128)S(1)}, u32[]{:S(2)}, u32[]{:S(2)}) %collective-permute-start.9) | collective-permute-done | bytes 147488 | tf_op jit(solution)/shard_map/ppermute | solution.py:114
  54.8 1.0 %constant_dynamic-update-slice_fusion.3 = (f32[9,64,256]{2,1,0:T(8,128)S(1)}, f32[9,16,256]{2,1,0:T(8,128)S(1)}) fusion(f32[9,64,256]{2,1,0:T(8,128)S(1)} %broadcast_in_dim.29, s32[]{:T(128)S(6)} %select_n.94, f32[9,16,256]{2,1,0:T(8,128)S(1)} %add.131, f32[9,16,256]{2,1,0:T(8,128)S(1)} %reshape.185, f32[9,64,256]{2,1,0:T(8,128)} %get-tuple-element.50), kind=kLoop, calls=%fused_computation.50 | loop fusion | flops 73728 | bytes 737284 | tf_op jit(solution)/shard_map/dynamic_update_slice | solution.py:122
  55.8 2.9 %collective-permute-start.10 = (f32[9,16,256]{2,1,0:T(8,128)S(1)}, f32[9,16,256]{2,1,0:T(8,128)S(1)}, u32[]{:S(2)}, u32[]{:S(2)}) collective-permute-start(f32[9,16,256]{2,1,0:T(8,128)S(1)} %get-tuple-element.58), channel_id=1, source_target_pairs={{0,4},{4,0},{8,12},{12,8},{1,5},{5,1},{9,13},{13,9},{2,6},{6,2},{1... | collective-permute-start | bytes 442376 | tf_op jit(solution)/shard_map/ppermute | solution.py:124
  58.7 1.7 %collective-permute-start.12 = (f32[9,16,256]{2,1,0:T(8,128)S(1)}, f32[9,16,256]{2,1,0:T(8,128)S(1)}, u32[]{:S(2)}, u32[]{:S(2)}) collective-permute-start(f32[9,16,256]{2,1,0:T(8,128)S(1)} %get-tuple-element.58), channel_id=1, source_target_pairs={{0,12},{4,8},{8,4},{12,0},{1,13},{5,9},{9,5},{13,1},{2,14},{6,10},... | collective-permute-start | bytes 442376 | tf_op jit(solution)/shard_map/ppermute | solution.py:124
  60.4 0.1 fusion.11
  60.5 0.7 %copy.34 = bf16[256,1,128]{2,0,1:T(8,128)(2,1)} copy(bf16[256,1,128]{0,2,1:T(8,128)(2,1)S(1)} %fusion.11) | data formatting | bytes 131072
  61.3 2.8 %collective-permute-done.11 = f32[9,16,256]{2,1,0:T(8,128)S(1)} collective-permute-done((f32[9,16,256]{2,1,0:T(8,128)S(1)}, f32[9,16,256]{2,1,0:T(8,128)S(1)}, u32[]{:S(2)}, u32[]{:S(2)}) %collective-permute-start.11) | collective-permute-done | bytes 147488 | tf_op jit(solution)/shard_map/ppermute | solution.py:124
  64.1 3.3 %collective-permute-done.12 = f32[9,16,256]{2,1,0:T(8,128)S(1)} collective-permute-done((f32[9,16,256]{2,1,0:T(8,128)S(1)}, f32[9,16,256]{2,1,0:T(8,128)S(1)}, u32[]{:S(2)}, u32[]{:S(2)}) %collective-permute-start.12) | collective-permute-done | bytes 147488 | tf_op jit(solution)/shard_map/ppermute | solution.py:124
  67.4 0.8 %copy-done.1 = f32[9,64,256]{2,1,0:T(8,128)} copy-done((f32[9,64,256]{2,1,0:T(8,128)}, f32[9,64,256]{2,1,0:T(8,128)S(1)}, u32[]{:S(2)}) %copy-start.1) | copy-done | bytes 589848
  (50 shorter events, 1.4 us)
Async XLA Ops:
  0.6 9.9 %copy-start = (bf16[1,9,3,2,64]{4,3,2,1,0:T(2,128)(2,1)S(1)}, bf16[1,9,3,2,64]{4,3,2,1,0:T(2,128)(2,1)}, u32[]{:S(2)}) copy-start(bf16[1,9,3,2,64]{4,3,2,1,0:T(2,128)(2,1)} %param.17) | copy-start | bytes 20740
  2.4 19.1 %collective-permute-start = (bf16[320,128]{1,0:T(8,128)(2,1)S(1)}, bf16[320,128]{1,0:T(8,128)(2,1)S(1)}, u32[]{:S(2)}, u32[]{:S(2)}) collective-permute-start(bf16[320,128]{1,0:T(8,128)(2,1)S(1)} %get-tuple-element.72), channel_id=1, source_target_pairs={{0,3},{1,0},{2,1},{3,2},{4,7},{5,4},{6,5},{7,6},{8,11},{9,8},{10,9... | collective-permute-start | bytes 245768 | tf_op jit(solution)/shard_map/ppermute | solution.py:228
  6.6 14.9 %collective-permute-start.1 = (bf16[320,128]{1,0:T(8,128)(2,1)S(1)}, bf16[320,128]{1,0:T(8,128)(2,1)S(1)}, u32[]{:S(2)}, u32[]{:S(2)}) collective-permute-start(bf16[320,128]{1,0:T(8,128)(2,1)S(1)} %get-tuple-element.73), channel_id=1, source_target_pairs={{0,2},{1,3},{2,0},{3,1},{4,6},{5,7},{6,4},{7,5},{8,10},{9,11},{10,... | collective-permute-start | bytes 245768 | tf_op jit(solution)/shard_map/ppermute | solution.py:228
  6.6 3.2 %copy-start.3 = (s32[1,2]{1,0:T(1,128)S(1)}, s32[1,2]{1,0:T(1,128)}, u32[]{:S(2)}) copy-start(s32[1,2]{1,0:T(1,128)} %param.19) | copy-start | bytes 28
  6.6 14.9 %collective-permute-start.2 = (bf16[320,128]{1,0:T(8,128)(2,1)S(1)}, bf16[320,128]{1,0:T(8,128)(2,1)S(1)}, u32[]{:S(2)}, u32[]{:S(2)}) collective-permute-start(bf16[320,128]{1,0:T(8,128)(2,1)S(1)} %get-tuple-element.74), channel_id=1, source_target_pairs={{0,1},{1,2},{2,3},{3,0},{4,5},{5,6},{6,7},{7,4},{8,9},{9,10},{10,1... | collective-permute-start | bytes 245768 | tf_op jit(solution)/shard_map/ppermute | solution.py:228
  17.4 4.2 %copy-start.2 = (bf16[256,1,128]{2,0,1:T(8,128)(2,1)S(1)}, bf16[256,1,128]{2,0,1:T(8,128)(2,1)}, u32[]{:S(2)}) copy-start(bf16[256,1,128]{2,0,1:T(8,128)(2,1)} %param.14) | copy-start | bytes 196612
  18.2 27.6 %collective-permute-start.5 = (f32[256,3,128]{0,2,1:T(8,128)}, f32[256,3,128]{0,2,1:T(8,128)S(1)}, u32[]{:S(2)}, u32[]{:S(2)}) collective-permute-start(f32[256,3,128]{0,2,1:T(8,128)} %get-tuple-element.59), channel_id=1, source_target_pairs={{0,1},{1,2},{2,3},{3,0},{4,5},{5,6},{6,7},{7,4},{8,9},{9,10},{10,1... | collective-permute-start | bytes 1179656 | tf_op jit(solution)/shard_map/ppermute | solution.py:19
  20.4 25.4 %collective-permute-start.6 = (f32[256,3,128]{0,2,1:T(8,128)S(1)}, f32[256,3,128]{0,2,1:T(8,128)S(1)}, u32[]{:S(2)}, u32[]{:S(2)}) collective-permute-start(f32[256,3,128]{0,2,1:T(8,128)S(1)} %get-tuple-element.60), channel_id=1, source_target_pairs={{1,0},{2,1},{3,2},{0,3},{5,4},{6,5},{7,6},{4,7},{9,8},{10,9},{11,1... | collective-permute-start | bytes 1179656 | tf_op jit(solution)/shard_map/ppermute | solution.py:21
  21.6 8.4 %collective-permute-start.3 = (bf16[256,512]{1,0:T(8,128)(2,1)S(1)}, bf16[256,512]{1,0:T(8,128)(2,1)S(1)}, u32[]{:S(2)}, u32[]{:S(2)}) collective-permute-start(bf16[256,512]{1,0:T(8,128)(2,1)S(1)} %get-tuple-element.67), channel_id=1, source_target_pairs={{0,4},{4,8},{8,12},{1,5},{5,9},{9,13},{2,6},{6,10},{10,14},{3,7},{... | collective-permute-start | bytes 786440 | tf_op jit(solution)/shard_map/ppermute | solution.py:238
  26.7 8.0 %collective-permute-start.4 = (bf16[256,512]{1,0:T(8,128)(2,1)S(1)}, bf16[256,512]{1,0:T(8,128)(2,1)S(1)}, u32[]{:S(2)}, u32[]{:S(2)}) collective-permute-start(bf16[256,512]{1,0:T(8,128)(2,1)S(1)} %get-tuple-element.67), channel_id=1, source_target_pairs={{4,0},{8,4},{12,8},{5,1},{9,5},{13,9},{6,2},{10,6},{14,10},{7,3},{... | collective-permute-start | bytes 786440 | tf_op jit(solution)/shard_map/ppermute | solution.py:239
  46.1 8.3 %collective-permute-start.8 = (f32[544,128]{0,1:T(8,128)S(1)}, f32[544,128]{0,1:T(8,128)S(1)}, u32[]{:S(2)}, u32[]{:S(2)}) collective-permute-start(f32[544,128]{0,1:T(8,128)S(1)} %pad_maximum_fusion.5), channel_id=1, source_target_pairs={{0,12},{4,8},{8,4},{12,0},{1,13},{5,9},{9,5},{13,1},{2,14},{6,10},... | collective-permute-start | bytes 835592 | tf_op jit(solution)/shard_map/ppermute | solution.py:114
  46.3 8.1 %collective-permute-start.9 = (f32[288,128]{0,1:T(8,128)S(1)}, f32[288,128]{0,1:T(8,128)S(1)}, u32[]{:S(2)}, u32[]{:S(2)}) collective-permute-start(f32[288,128]{0,1:T(8,128)S(1)} %copy.32), channel_id=1, source_target_pairs={{0,8},{4,12},{8,0},{12,4},{1,9},{5,13},{9,1},{13,5},{2,10},{6,14},... | collective-permute-start | bytes 442376 | tf_op jit(solution)/shard_map/ppermute | solution.py:114
  46.7 7.9 %collective-permute-start.7 = (f32[544,128]{0,1:T(8,128)S(1)}, f32[544,128]{0,1:T(8,128)S(1)}, u32[]{:S(2)}, u32[]{:S(2)}) collective-permute-start(f32[544,128]{0,1:T(8,128)S(1)} %pad_maximum_fusion.4), channel_id=1, source_target_pairs={{0,4},{4,0},{8,12},{12,8},{1,5},{5,1},{9,13},{13,9},{2,6},{6,2},{1... | collective-permute-start | bytes 835592 | tf_op jit(solution)/shard_map/ppermute | solution.py:114
  55.8 5.5 %collective-permute-start.10 = (f32[9,16,256]{2,1,0:T(8,128)S(1)}, f32[9,16,256]{2,1,0:T(8,128)S(1)}, u32[]{:S(2)}, u32[]{:S(2)}) collective-permute-start(f32[9,16,256]{2,1,0:T(8,128)S(1)} %get-tuple-element.58), channel_id=1, source_target_pairs={{0,4},{4,0},{8,12},{12,8},{1,5},{5,1},{9,13},{13,9},{2,6},{6,2},{1... | collective-permute-start | bytes 442376 | tf_op jit(solution)/shard_map/ppermute | solution.py:124
  58.6 5.4 %collective-permute-start.11 = (f32[9,16,256]{2,1,0:T(8,128)S(1)}, f32[9,16,256]{2,1,0:T(8,128)S(1)}, u32[]{:S(2)}, u32[]{:S(2)}) collective-permute-start(f32[9,16,256]{2,1,0:T(8,128)S(1)} %get-tuple-element.58), channel_id=1, source_target_pairs={{0,8},{4,12},{8,0},{12,4},{1,9},{5,13},{9,1},{13,5},{2,10},{6,14},... | collective-permute-start | bytes 442376 | tf_op jit(solution)/shard_map/ppermute | solution.py:124
  58.7 8.7 %collective-permute-start.12 = (f32[9,16,256]{2,1,0:T(8,128)S(1)}, f32[9,16,256]{2,1,0:T(8,128)S(1)}, u32[]{:S(2)}, u32[]{:S(2)}) collective-permute-start(f32[9,16,256]{2,1,0:T(8,128)S(1)} %get-tuple-element.58), channel_id=1, source_target_pairs={{0,12},{4,8},{8,4},{12,0},{1,13},{5,9},{9,5},{13,1},{2,14},{6,10},... | collective-permute-start | bytes 442376 | tf_op jit(solution)/shard_map/ppermute | solution.py:124
  67.4 0.8 %copy-start.1 = (f32[9,64,256]{2,1,0:T(8,128)}, f32[9,64,256]{2,1,0:T(8,128)S(1)}, u32[]{:S(2)}) copy-start(f32[9,64,256]{2,1,0:T(8,128)S(1)} %constant_dynamic-update-slice_fusion) | copy-start | bytes 1769476

commit v16 on v6

--- a/solution.py
+++ b/solution.py
@@ -40,15 +40,11 @@
 
 def toeplitz_kernel(tap_ref, grad_ref, out_ref, contrib_ref):
     kernels, lon_cols, width = out_ref.shape
-    window_len = tap_ref.shape[1]
-    stencil_rows = width // window_len
     acc = None
     for k in range(kernels):
-        for r in range(stencil_rows):
-            row = tap_ref[pl.ds(k * stencil_rows + r, 1), :]
-            tiled = jnp.broadcast_to(row, (lon_cols, window_len))
-            rolled = pltpu.roll(tiled, 0, 1, stride=1, stride_axis=0)
-            out_ref[k, :, pl.ds(r * window_len, window_len)] = rolled.astype(out_ref.dtype)
+        row = tap_ref[pl.ds(k, 1), :]
+        tiled = jnp.broadcast_to(row, (lon_cols, width))
+        out_ref[k] = pltpu.roll(tiled, 0, 1, stride=1, stride_axis=0)
         term = jnp.dot(
             grad_ref[:, pl.ds(k * lon_cols, lon_cols)],
             out_ref[k],
@@ -62,7 +58,7 @@
     kernels, stencil_rows, reach = tap_row.shape
     window_len = out_width + reach
     padded = jnp.pad(tap_row.astype(jnp.float32), ((0, 0), (0, 0), (0, window_len - reach)))
-    padded = padded.reshape(kernels * stencil_rows, window_len)
+    padded = padded.reshape(kernels, stencil_rows * window_len).astype(jnp.bfloat16)
     out, contrib = pl.pallas_call(
         toeplitz_kernel,
         out_shape=(

time: 63.9 us -> 63.8 us (level)
    reshape x2 -> x0, local copies, waits for them, and re-layouts: 0.67 us -> none  [toeplitz(): padded = padded.reshape(kernels * stencil_rows, window_len)]
    unnamed x9 -> x12, local copies, waits for them, and re-layouts: 1.56 us -> 2.22 us
where the time goes in v16:
time: 63.8 us; the launch traced here: 63.2 us
  starting transfers between devices  24.1 us (38%)
  Pallas kernels  12.8 us (20%)
  waiting for transfers between devices  12 us (19%)
  local copies, waits for them, and re-layouts  7 us (11%)
  other arithmetic  3.79 us (6%)
  matrix products  1.86 us (3%)
  between operations  1.63 us (3%)
    pallas_call x1, Pallas kernels, row_products(): pl.pallas_call(row_kernel, out_shape=(jax.ShapeDtypeStruct((weights.shape...  8.55 us
    ppermute x3, waiting for transfers between devices, lat_allreduce(): recv = lax.ppermute(mine, axis, [(i, i ^ d) for i in range(count)])  6.21 us
    ppermute x1, starting transfers between devices, body(): below = lax.ppermute(row, 'lat', [(i, i + 1) for i in range(count - 1)])  5.08 us
    ppermute x1, waiting for transfers between devices, body(): above = lax.ppermute(row, 'lat', [(i + 1, i) for i in range(count - 1)])  4.69 us
    ppermute x3, starting transfers between devices, body(): lax.ppermute(jnp.concatenate([fields[:, 0], part], axis=0), 'lon', [(p, (...  4.66 us
    pallas_call x1, Pallas kernels, toeplitz(): pl.pallas_call(toeplitz_kernel, out_shape=(jax.ShapeDtypeStruct((kernels,...  4.25 us
    ppermute x2, starting transfers between devices, padded_2(): lax.ppermute(tail, axis, [(i, (i + 1) % count) for i in range(ends)])  4.17 us
    ppermute x2, starting transfers between devices, padded_2(): lax.ppermute(head, axis, [((i + 1) % count, i) for i in range(ends)])  3.47 us
  transfers between devices with their start and end apart: 15, of which 5 were waited for; matrix products, arithmetic and copies ran while one was open for 16% of the time, Pallas kernels for 20%

profile of v16, /device:TPU:1, one launch (start us, length us, event | category | flops | bytes accessed | tf_op | source)
XLA Modules:
  0.0 63.2 jit_solution(14471386019339997701)
XLA Ops:
  0.7 0.8 %dynamic-slice_bitcast_fusion = (bf16[1,64,128]{2,1,0:T(8,128)(2,1)S(1)}, bf16[64,128]{1,0:T(8,128)(2,1)S(1)}, bf16[64,128]{1,0:T(8,128)(2,1)S(1)}, bf16[64,128]{1,0:T(8,128)(2,1)S(1)}) fusion(bf16[256,1,128]{2,0,1:T(8,128)(2,1)} %param.23, s32[]{:T(128)S(6)} %select_n.57, s32[]{:T(128)S(6)} %select_n.55, s32[]{:T(128)S(6)} %select_n.53, s32[]{:T(128)S(6)} %select_n.51), kind=kLoop, calls=%fused_computation.34 | loop fusion | bytes 131088 | tf_op jit(solution)/shard_map/stack | solution.py:175
  1.5 0.9 %pad_maximum_fusion.5 = (bf16[320,128]{1,0:T(8,128)(2,1)S(1)}, bf16[320,128]{1,0:T(8,128)(2,1)S(1)}, bf16[320,128]{1,0:T(8,128)(2,1)S(1)}) fusion(bf16[64,128]{1,0:T(8,128)(2,1)S(1)} %get-tuple-element.112, bf16[256,128]{1,0:T(8,128)(2,1)} %bitcast.59, bf16[64,128]{1,0:T(8,128)(2,1)S(1)} %get-tuple-element.111, bf16[64,128]{1,0:T(8,128)(2,1)S(1)} %get-tuple-element.110), kind=kLoop, calls=%fused_computation.21 | loop fusion | flops 409600 | bytes 360448 | tf_op jit(solution)/shard_map/concatenate | solution.py:169
  2.4 4.2 %collective-permute-start = (bf16[320,128]{1,0:T(8,128)(2,1)S(1)}, bf16[320,128]{1,0:T(8,128)(2,1)S(1)}, u32[]{:S(2)}, u32[]{:S(2)}) collective-permute-start(bf16[320,128]{1,0:T(8,128)(2,1)S(1)} %get-tuple-element.113), channel_id=1, source_target_pairs={{0,3},{1,0},{2,1},{3,2},{4,7},{5,4},{6,5},{7,6},{8,11},{9,8},{10,9... | collective-permute-start | bytes 245768 | tf_op jit(solution)/shard_map/ppermute | solution.py:168
  6.6 0.5 collective-permute-start.2
  7.0 1.7 %convolution_convert_fusion = bf16[128,9,256]{2,0,1:T(8,128)(2,1)S(1)} fusion(bf16[9,256,256]{2,1,0:T(8,128)(2,1)} %w_ref.1, bf16[256,1,128]{2,0,1:T(8,128)(2,1)} %param.23), kind=kOutput, calls=%fused_computation | convolution fusion | flops 151289856 | bytes 1835008 | tf_op jit(solution)/shard_map/koc,oij->cikj/dot_general | solution.py:157
  8.7 1.1 %copy.19.grad_ref = bf16[256,1152]{1,0:T(8,128)(2,1)} copy(bf16[256,1152]{0,1:T(8,128)(2,1)S(1)} %bitcast.56) | data formatting | bytes 1179648 | tf_op jit(solution)/shard_map/reshape;squeeze | solution.py:160
  10.5 0.2 fusion.3
  10.8 0.6 copy.26
  11.4 4.2 %shard_map.100 = (bf16[9,128,1152]{2,1,0:T(8,128)(2,1)}, f32[256,1152]{1,0:T(8,128)}) custom-call(bf16[9,1152]{1,0:T(8,128)(2,1)} %bitcast.62, bf16[256,1152]{1,0:T(8,128)(2,1)} %copy.19.grad_ref), custom_call_target="tpu_custom_call" | custom-call | tf_op jit(solution)/shard_map/pallas_call | solution.py:62
  15.6 1.6 %copy.20 = f32[256,1152]{0,1:T(8,128)S(1)} copy(f32[256,1152]{1,0:T(8,128)} %get-tuple-element.93) | data formatting | bytes 2359296 | tf_op jit(solution)/shard_map/pallas_call | solution.py:62
  17.4 2.3 %collective-permute-start.5 = (f32[256,3,128]{0,2,1:T(8,128)S(1)}, f32[256,3,128]{0,2,1:T(8,128)S(1)}, u32[]{:S(2)}, u32[]{:S(2)}) collective-permute-start(f32[256,3,128]{0,2,1:T(8,128)S(1)} %get-tuple-element.100), channel_id=1, source_target_pairs={{0,1},{1,2},{2,3},{3,0},{4,5},{5,6},{6,7},{7,4},{8,9},{9,10},{10,1... | collective-permute-start | bytes 1179656 | tf_op jit(solution)/shard_map/ppermute | solution.py:19
  19.6 1.1 %collective-permute-start.6 = (f32[256,3,128]{0,2,1:T(8,128)S(1)}, f32[256,3,128]{0,2,1:T(8,128)S(1)}, u32[]{:S(2)}, u32[]{:S(2)}) collective-permute-start(f32[256,3,128]{0,2,1:T(8,128)S(1)} %get-tuple-element.101), channel_id=1, source_target_pairs={{1,0},{2,1},{3,2},{0,3},{5,4},{6,5},{7,6},{4,7},{9,8},{10,9},{11,1... | collective-permute-start | bytes 1179656 | tf_op jit(solution)/shard_map/ppermute | solution.py:21
  20.8 5.1 %collective-permute-start.3 = (bf16[256,512]{1,0:T(8,128)(2,1)S(1)}, bf16[256,512]{1,0:T(8,128)(2,1)S(1)}, u32[]{:S(2)}, u32[]{:S(2)}) collective-permute-start(bf16[256,512]{1,0:T(8,128)(2,1)S(1)} %get-tuple-element.108), channel_id=1, source_target_pairs={{0,4},{4,8},{8,12},{1,5},{5,9},{9,13},{2,6},{6,10},{10,14},{3,7},{... | collective-permute-start | bytes 786440 | tf_op jit(solution)/shard_map/ppermute | solution.py:178
  25.9 1.9 %collective-permute-start.4 = (bf16[256,512]{1,0:T(8,128)(2,1)S(1)}, bf16[256,512]{1,0:T(8,128)(2,1)S(1)}, u32[]{:S(2)}, u32[]{:S(2)}) collective-permute-start(bf16[256,512]{1,0:T(8,128)(2,1)S(1)} %get-tuple-element.108), channel_id=1, source_target_pairs={{4,0},{8,4},{12,8},{5,1},{9,5},{13,9},{6,2},{10,6},{14,10},{7,3},{... | collective-permute-start | bytes 786440 | tf_op jit(solution)/shard_map/ppermute | solution.py:179
  27.9 0.6 %pad_maximum_fusion.8.up_ref = bf16[4,64,128]{2,1,0:T(8,128)(2,1)} fusion(bf16[1,64,128]{2,1,0:T(8,128)(2,1)S(1)} %slice_bitcast_fusion, bf16[1,64,128]{2,1,0:T(8,128)(2,1)S(1)} %slice_bitcast_fusion.1, bf16[1,64,128]{2,1,0:T(8,128)(2,1)S(1)} %slice_bitcast_fusion.2, bf16[1,64,128]{2,1,0:T(8,128)(2,1)S(1)} %get-tuple-element.109), kind=kLoop, calls=%fused_computation.24 | loop fusion | flops 98304 | bytes 131072 | tf_op jit(solution)/shard_map/stack | solution.py:175
  28.5 0.7 %collective-permute-done.3 = bf16[256,512]{1,0:T(8,128)(2,1)S(1)} collective-permute-done((bf16[256,512]{1,0:T(8,128)(2,1)S(1)}, bf16[256,512]{1,0:T(8,128)(2,1)S(1)}, u32[]{:S(2)}, u32[]{:S(2)}) %collective-permute-start.3) | collective-permute-done | bytes 262176 | tf_op jit(solution)/shard_map/ppermute | solution.py:178
  29.2 4.7 %collective-permute-done.4 = bf16[256,512]{1,0:T(8,128)(2,1)S(1)} collective-permute-done((bf16[256,512]{1,0:T(8,128)(2,1)S(1)}, bf16[256,512]{1,0:T(8,128)(2,1)S(1)}, u32[]{:S(2)}, u32[]{:S(2)}) %collective-permute-start.4) | collective-permute-done | bytes 262176 | tf_op jit(solution)/shard_map/ppermute | solution.py:179
  33.9 1.1 %fusion.ext_ref = bf16[3,256,768]{2,1,0:T(8,128)(2,1)} fusion(bf16[1,256,512]{2,1,0:T(8,128)(2,1)S(1)} %bitcast.58, bf16[1,256,512]{2,1,0:T(8,128)(2,1)S(1)} %get-tuple-element.107, bf16[1,256,512]{2,1,0:T(8,128)(2,1)S(1)} %bitcast.57), kind=kLoop, calls=%fused_computation.2 | loop fusion | flops 10616832 | bytes 1966080 | tf_op jit(solution)/shard_map/concatenate | solution.py:181
  35.0 8.5 %shard_map.101 = (bf16[256,128]{1,0:T(8,128)(2,1)}, f32[9,64,256]{2,1,0:T(8,128)}) custom-call(bf16[3,256,768]{2,1,0:T(8,128)(2,1)} %fusion.ext_ref, bf16[1152,1152]{1,0:T(8,128)(2,1)} %bitcast.63, bf16[9,256,256]{2,1,0:T(8,128)(2,1)} %w_ref.1, bf16[4,64,128]{2,1,0:T(8,128)(2,1)} %pad_maximum_fusion.8.up_ref), custom_call_target="tpu_custom_call" | custom-call | flops 3019898880 | bytes 5734400 | tf_op jit(solution)/shard_map/pallas_call | solution.py:140
  43.5 1.1 %constant_dynamic-slice_fusion.2 = (f32[9,16,256]{2,1,0:T(8,128)S(1)}, f32[9,16,256]{2,1,0:T(8,128)S(1)}, f32[9,16,256]{2,1,0:T(8,128)S(1)}) fusion(f32[9,64,256]{2,1,0:T(8,128)} %get-tuple-element.94, s32[]{:T(128)S(6)} %select_n.59, s32[]{:T(128)S(6)} %select_n.61, s32[]{:T(128)S(6)} %select_n.60), kind=kLoop, calls=%fused_computation.44 | loop fusion | bytes 884748 | tf_op jit(solution)/shard_map/dynamic_slice | solution.py:81
  44.8 1.8 %collective-permute-start.9 = (f32[9,16,256]{2,1,0:T(8,128)S(1)}, f32[9,16,256]{2,1,0:T(8,128)S(1)}, u32[]{:S(2)}, u32[]{:S(2)}) collective-permute-start(f32[9,16,256]{2,1,0:T(8,128)S(1)} %get-tuple-element.102), channel_id=1, source_target_pairs={{0,4},{4,0},{8,12},{12,8},{1,5},{5,1},{9,13},{13,9},{2,6},{6,2},{1... | collective-permute-start | bytes 442376 | tf_op jit(solution)/shard_map/ppermute | solution.py:82
  46.7 1.9 %collective-permute-start.7 = (f32[256,1,128]{0,2,1:T(8,128)S(1)}, f32[256,1,128]{0,2,1:T(8,128)S(1)}, u32[]{:S(2)}, u32[]{:S(2)}) collective-permute-start(f32[256,1,128]{0,2,1:T(8,128)S(1)} %get-tuple-element.105), channel_id=1, source_target_pairs={{0,4},{4,8},{8,12},{1,5},{5,9},{9,13},{2,6},{6,10},{10,14},{3,7},{... | collective-permute-start | bytes 393224 | tf_op jit(solution)/shard_map/ppermute | solution.py:19
  48.6 2.4 %collective-permute-start.8 = (f32[256,1,128]{0,2,1:T(8,128)S(1)}, f32[256,1,128]{0,2,1:T(8,128)S(1)}, u32[]{:S(2)}, u32[]{:S(2)}) collective-permute-start(f32[256,1,128]{0,2,1:T(8,128)S(1)} %get-tuple-element.106), channel_id=1, source_target_pairs={{4,0},{8,4},{12,8},{5,1},{9,5},{13,9},{6,2},{10,6},{14,10},{7,3},{... | collective-permute-start | bytes 393224 | tf_op jit(solution)/shard_map/ppermute | solution.py:21
  51.0 0.4 collective-permute-done.11
  51.5 1.0 %constant_dynamic-update-slice_fusion.3 = (f32[9,64,256]{2,1,0:T(8,128)S(1)}, f32[9,16,256]{2,1,0:T(8,128)S(1)}) fusion(f32[9,64,256]{2,1,0:T(8,128)S(1)} %broadcast_in_dim.25, s32[]{:T(128)S(6)} %select_n.58, f32[9,16,256]{2,1,0:T(8,128)S(1)} %collective-permute-done.10, f32[9,16,256]{2,1,0:T(8,128)S(1)} %collective-permute-done.11, ...), kind=kLoop, calls=%fused_computation.41 | loop fusion | flops 110592 | bytes 884740 | tf_op jit(solution)/shard_map/dynamic_update_slice | solution.py:87
  52.4 1.2 %collective-permute-start.12 = (f32[9,16,256]{2,1,0:T(8,128)S(1)}, f32[9,16,256]{2,1,0:T(8,128)S(1)}, u32[]{:S(2)}, u32[]{:S(2)}) collective-permute-start(f32[9,16,256]{2,1,0:T(8,128)S(1)} %get-tuple-element.99), channel_id=1, source_target_pairs={{0,4},{4,0},{8,12},{12,8},{1,5},{5,1},{9,13},{13,9},{2,6},{6,2},{1... | collective-permute-start | bytes 442376 | tf_op jit(solution)/shard_map/ppermute | solution.py:89
  53.6 1.5 %collective-permute-start.13 = (f32[9,16,256]{2,1,0:T(8,128)S(1)}, f32[9,16,256]{2,1,0:T(8,128)S(1)}, u32[]{:S(2)}, u32[]{:S(2)}) collective-permute-start(f32[9,16,256]{2,1,0:T(8,128)S(1)} %get-tuple-element.99), channel_id=1, source_target_pairs={{0,8},{4,12},{8,0},{12,4},{1,9},{5,13},{9,1},{13,5},{2,10},{6,14},... | collective-permute-start | bytes 442376 | tf_op jit(solution)/shard_map/ppermute | solution.py:89
  55.1 0.3 collective-permute-start.14
  55.4 0.7 %copy.21 = bf16[256,1,128]{2,0,1:T(8,128)(2,1)} copy(bf16[256,1,128]{0,2,1:T(8,128)(2,1)S(1)} %fusion.6) | data formatting | bytes 131072
  56.1 2.9 %collective-permute-done.13 = f32[9,16,256]{2,1,0:T(8,128)S(1)} collective-permute-done((f32[9,16,256]{2,1,0:T(8,128)S(1)}, f32[9,16,256]{2,1,0:T(8,128)S(1)}, u32[]{:S(2)}, u32[]{:S(2)}) %collective-permute-start.13) | collective-permute-done | bytes 147488 | tf_op jit(solution)/shard_map/ppermute | solution.py:89
  59.1 3.3 %collective-permute-done.14 = f32[9,16,256]{2,1,0:T(8,128)S(1)} collective-permute-done((f32[9,16,256]{2,1,0:T(8,128)S(1)}, f32[9,16,256]{2,1,0:T(8,128)S(1)}, u32[]{:S(2)}, u32[]{:S(2)}) %collective-permute-start.14) | collective-permute-done | bytes 147488 | tf_op jit(solution)/shard_map/ppermute | solution.py:89
  62.4 0.8 %copy-done.1 = f32[9,64,256]{2,1,0:T(8,128)} copy-done((f32[9,64,256]{2,1,0:T(8,128)}, f32[9,64,256]{2,1,0:T(8,128)S(1)}, u32[]{:S(2)}) %copy-start.1) | copy-done | bytes 589848
  (41 shorter events, 0.7 us)
Async XLA Ops:
  0.6 9.9 %copy-start = (bf16[1,9,3,2,64]{4,3,2,1,0:T(2,128)(2,1)S(1)}, bf16[1,9,3,2,64]{4,3,2,1,0:T(2,128)(2,1)}, u32[]{:S(2)}) copy-start(bf16[1,9,3,2,64]{4,3,2,1,0:T(2,128)(2,1)} %param.25) | copy-start | bytes 20740
  2.4 18.3 %collective-permute-start = (bf16[320,128]{1,0:T(8,128)(2,1)S(1)}, bf16[320,128]{1,0:T(8,128)(2,1)S(1)}, u32[]{:S(2)}, u32[]{:S(2)}) collective-permute-start(bf16[320,128]{1,0:T(8,128)(2,1)S(1)} %get-tuple-element.113), channel_id=1, source_target_pairs={{0,3},{1,0},{2,1},{3,2},{4,7},{5,4},{6,5},{7,6},{8,11},{9,8},{10,9... | collective-permute-start | bytes 245768 | tf_op jit(solution)/shard_map/ppermute | solution.py:168
  6.6 14.1 %collective-permute-start.1 = (bf16[320,128]{1,0:T(8,128)(2,1)S(1)}, bf16[320,128]{1,0:T(8,128)(2,1)S(1)}, u32[]{:S(2)}, u32[]{:S(2)}) collective-permute-start(bf16[320,128]{1,0:T(8,128)(2,1)S(1)} %get-tuple-element.114), channel_id=1, source_target_pairs={{0,2},{1,3},{2,0},{3,1},{4,6},{5,7},{6,4},{7,5},{8,10},{9,11},{10,... | collective-permute-start | bytes 245768 | tf_op jit(solution)/shard_map/ppermute | solution.py:168
  6.6 3.2 %copy-start.3 = (s32[1,2]{1,0:T(1,128)S(1)}, s32[1,2]{1,0:T(1,128)}, u32[]{:S(2)}) copy-start(s32[1,2]{1,0:T(1,128)} %param.27) | copy-start | bytes 28
  6.6 14.2 %collective-permute-start.2 = (bf16[320,128]{1,0:T(8,128)(2,1)S(1)}, bf16[320,128]{1,0:T(8,128)(2,1)S(1)}, u32[]{:S(2)}, u32[]{:S(2)}) collective-permute-start(bf16[320,128]{1,0:T(8,128)(2,1)S(1)} %get-tuple-element.115), channel_id=1, source_target_pairs={{0,1},{1,2},{2,3},{3,0},{4,5},{5,6},{6,7},{7,4},{8,9},{9,10},{10,1... | collective-permute-start | bytes 245768 | tf_op jit(solution)/shard_map/ppermute | solution.py:168
  17.3 3.5 %copy-start.2 = (bf16[256,1,128]{2,0,1:T(8,128)(2,1)S(1)}, bf16[256,1,128]{2,0,1:T(8,128)(2,1)}, u32[]{:S(2)}) copy-start(bf16[256,1,128]{2,0,1:T(8,128)(2,1)} %param.22) | copy-start | bytes 196612
  17.4 29.2 %collective-permute-start.5 = (f32[256,3,128]{0,2,1:T(8,128)S(1)}, f32[256,3,128]{0,2,1:T(8,128)S(1)}, u32[]{:S(2)}, u32[]{:S(2)}) collective-permute-start(f32[256,3,128]{0,2,1:T(8,128)S(1)} %get-tuple-element.100), channel_id=1, source_target_pairs={{0,1},{1,2},{2,3},{3,0},{4,5},{5,6},{6,7},{7,4},{8,9},{9,10},{10,1... | collective-permute-start | bytes 1179656 | tf_op jit(solution)/shard_map/ppermute | solution.py:19
  19.6 26.9 %collective-permute-start.6 = (f32[256,3,128]{0,2,1:T(8,128)S(1)}, f32[256,3,128]{0,2,1:T(8,128)S(1)}, u32[]{:S(2)}, u32[]{:S(2)}) collective-permute-start(f32[256,3,128]{0,2,1:T(8,128)S(1)} %get-tuple-element.101), channel_id=1, source_target_pairs={{1,0},{2,1},{3,2},{0,3},{5,4},{6,5},{7,6},{4,7},{9,8},{10,9},{11,1... | collective-permute-start | bytes 1179656 | tf_op jit(solution)/shard_map/ppermute | solution.py:21
  20.8 8.4 %collective-permute-start.3 = (bf16[256,512]{1,0:T(8,128)(2,1)S(1)}, bf16[256,512]{1,0:T(8,128)(2,1)S(1)}, u32[]{:S(2)}, u32[]{:S(2)}) collective-permute-start(bf16[256,512]{1,0:T(8,128)(2,1)S(1)} %get-tuple-element.108), channel_id=1, source_target_pairs={{0,4},{4,8},{8,12},{1,5},{5,9},{9,13},{2,6},{6,10},{10,14},{3,7},{... | collective-permute-start | bytes 786440 | tf_op jit(solution)/shard_map/ppermute | solution.py:178
  25.9 8.0 %collective-permute-start.4 = (bf16[256,512]{1,0:T(8,128)(2,1)S(1)}, bf16[256,512]{1,0:T(8,128)(2,1)S(1)}, u32[]{:S(2)}, u32[]{:S(2)}) collective-permute-start(bf16[256,512]{1,0:T(8,128)(2,1)S(1)} %get-tuple-element.108), channel_id=1, source_target_pairs={{4,0},{8,4},{12,8},{5,1},{9,5},{13,9},{6,2},{10,6},{14,10},{7,3},{... | collective-permute-start | bytes 786440 | tf_op jit(solution)/shard_map/ppermute | solution.py:179
  44.6 6.4 %collective-permute-start.10 = (f32[9,16,256]{2,1,0:T(8,128)S(1)}, f32[9,16,256]{2,1,0:T(8,128)S(1)}, u32[]{:S(2)}, u32[]{:S(2)}) collective-permute-start(f32[9,16,256]{2,1,0:T(8,128)S(1)} %get-tuple-element.104), channel_id=1, source_target_pairs={{0,8},{4,12},{8,0},{12,4},{1,9},{5,13},{9,1},{13,5},{2,10},{6,14},... | collective-permute-start | bytes 442376 | tf_op jit(solution)/shard_map/ppermute | solution.py:82
  44.7 6.7 %collective-permute-start.11 = (f32[9,16,256]{2,1,0:T(8,128)S(1)}, f32[9,16,256]{2,1,0:T(8,128)S(1)}, u32[]{:S(2)}, u32[]{:S(2)}) collective-permute-start(f32[9,16,256]{2,1,0:T(8,128)S(1)} %get-tuple-element.103), channel_id=1, source_target_pairs={{0,12},{4,8},{8,4},{12,0},{1,13},{5,9},{9,5},{13,1},{2,14},{6,10},... | collective-permute-start | bytes 442376 | tf_op jit(solution)/shard_map/ppermute | solution.py:82
  44.8 6.6 %collective-permute-start.9 = (f32[9,16,256]{2,1,0:T(8,128)S(1)}, f32[9,16,256]{2,1,0:T(8,128)S(1)}, u32[]{:S(2)}, u32[]{:S(2)}) collective-permute-start(f32[9,16,256]{2,1,0:T(8,128)S(1)} %get-tuple-element.102), channel_id=1, source_target_pairs={{0,4},{4,0},{8,12},{12,8},{1,5},{5,1},{9,13},{13,9},{2,6},{6,2},{1... | collective-permute-start | bytes 442376 | tf_op jit(solution)/shard_map/ppermute | solution.py:82
  46.7 8.7 %collective-permute-start.7 = (f32[256,1,128]{0,2,1:T(8,128)S(1)}, f32[256,1,128]{0,2,1:T(8,128)S(1)}, u32[]{:S(2)}, u32[]{:S(2)}) collective-permute-start(f32[256,1,128]{0,2,1:T(8,128)S(1)} %get-tuple-element.105), channel_id=1, source_target_pairs={{0,4},{4,8},{8,12},{1,5},{5,9},{9,13},{2,6},{6,10},{10,14},{3,7},{... | collective-permute-start | bytes 393224 | tf_op jit(solution)/shard_map/ppermute | solution.py:19
  48.6 6.8 %collective-permute-start.8 = (f32[256,1,128]{0,2,1:T(8,128)S(1)}, f32[256,1,128]{0,2,1:T(8,128)S(1)}, u32[]{:S(2)}, u32[]{:S(2)}) collective-permute-start(f32[256,1,128]{0,2,1:T(8,128)S(1)} %get-tuple-element.106), channel_id=1, source_target_pairs={{4,0},{8,4},{12,8},{5,1},{9,5},{13,9},{6,2},{10,6},{14,10},{7,3},{... | collective-permute-start | bytes 393224 | tf_op jit(solution)/shard_map/ppermute | solution.py:21
  52.4 3.7 %collective-permute-start.12 = (f32[9,16,256]{2,1,0:T(8,128)S(1)}, f32[9,16,256]{2,1,0:T(8,128)S(1)}, u32[]{:S(2)}, u32[]{:S(2)}) collective-permute-start(f32[9,16,256]{2,1,0:T(8,128)S(1)} %get-tuple-element.99), channel_id=1, source_target_pairs={{0,4},{4,0},{8,12},{12,8},{1,5},{5,1},{9,13},{13,9},{2,6},{6,2},{1... | collective-permute-start | bytes 442376 | tf_op jit(solution)/shard_map/ppermute | solution.py:89
  53.6 5.4 %collective-permute-start.13 = (f32[9,16,256]{2,1,0:T(8,128)S(1)}, f32[9,16,256]{2,1,0:T(8,128)S(1)}, u32[]{:S(2)}, u32[]{:S(2)}) collective-permute-start(f32[9,16,256]{2,1,0:T(8,128)S(1)} %get-tuple-element.99), channel_id=1, source_target_pairs={{0,8},{4,12},{8,0},{12,4},{1,9},{5,13},{9,1},{13,5},{2,10},{6,14},... | collective-permute-start | bytes 442376 | tf_op jit(solution)/shard_map/ppermute | solution.py:89
  55.1 7.3 %collective-permute-start.14 = (f32[9,16,256]{2,1,0:T(8,128)S(1)}, f32[9,16,256]{2,1,0:T(8,128)S(1)}, u32[]{:S(2)}, u32[]{:S(2)}) collective-permute-start(f32[9,16,256]{2,1,0:T(8,128)S(1)} %get-tuple-element.99), channel_id=1, source_target_pairs={{0,12},{4,8},{8,4},{12,0},{1,13},{5,9},{9,5},{13,1},{2,14},{6,10},... | collective-permute-start | bytes 442376 | tf_op jit(solution)/shard_map/ppermute | solution.py:89
  62.4 0.8 %copy-start.1 = (f32[9,64,256]{2,1,0:T(8,128)}, f32[9,64,256]{2,1,0:T(8,128)S(1)}, u32[]{:S(2)}) copy-start(f32[9,64,256]{2,1,0:T(8,128)S(1)} %constant_dynamic-update-slice_fusion) | copy-start | bytes 1769476

commit v17 on v16

--- a/solution.py
+++ b/solution.py
@@ -39,34 +39,47 @@
 
 
 def toeplitz_kernel(tap_ref, grad_ref, out_ref, contrib_ref):
-    kernels, lon_cols, width = out_ref.shape
-    acc = None
-    for k in range(kernels):
-        row = tap_ref[pl.ds(k, 1), :]
-        tiled = jnp.broadcast_to(row, (lon_cols, width))
-        out_ref[k] = pltpu.roll(tiled, 0, 1, stride=1, stride_axis=0)
-        term = jnp.dot(
-            grad_ref[:, pl.ds(k * lon_cols, lon_cols)],
-            out_ref[k],
-            preferred_element_type=jnp.float32,
-        )
-        acc = term if acc is None else acc + term
-    contrib_ref[...] = acc
+    _, lon_cols, width = out_ref.shape
+    k = pl.program_id(0)
+    row = tap_ref[0]
+    tiled = jnp.broadcast_to(row, (lon_cols, width))
+    out_ref[0] = pltpu.roll(tiled, 0, 1, stride=1, stride_axis=0)
+    term = jnp.dot(grad_ref[...], out_ref[0], preferred_element_type=jnp.float32)
+
+    @pl.when(k == 0)
+    def _():
+        contrib_ref[...] = term
+
+    @pl.when(k > 0)
+    def _():
+        contrib_ref[...] += term
 
 
 def toeplitz(tap_row, out_width, grad_piece):
     kernels, stencil_rows, reach = tap_row.shape
     window_len = out_width + reach
+    width = stencil_rows * window_len
     padded = jnp.pad(tap_row.astype(jnp.float32), ((0, 0), (0, 0), (0, window_len - reach)))
-    padded = padded.reshape(kernels, stencil_rows * window_len).astype(jnp.bfloat16)
+    padded = padded.reshape(kernels, 1, width).astype(jnp.bfloat16)
+    channels = grad_piece.shape[0]
     out, contrib = pl.pallas_call(
         toeplitz_kernel,
+        grid=(kernels,),
+        in_specs=[
+            pl.BlockSpec((1, 1, width), lambda k: (k, 0, 0)),
+            pl.BlockSpec((channels, out_width), lambda k: (0, k)),
+        ],
+        out_specs=[
+            pl.BlockSpec((1, out_width, width), lambda k: (k, 0, 0)),
+            pl.BlockSpec((channels, width), lambda k: (0, 0)),
+        ],
         out_shape=(
-            jax.ShapeDtypeStruct((kernels, out_width, stencil_rows * window_len), jnp.bfloat16),
-            jax.ShapeDtypeStruct((grad_piece.shape[0], stencil_rows * window_len), jnp.float32),
+            jax.ShapeDtypeStruct((kernels, out_width, width), jnp.bfloat16),
+            jax.ShapeDtypeStruct((channels, width), jnp.float32),
         ),
+        compiler_params=pltpu.CompilerParams(dimension_semantics=("arbitrary",)),
     )(padded, grad_piece)
-    return out.reshape(kernels * out_width, stencil_rows * window_len), contrib
+    return out.reshape(kernels * out_width, width), contrib
 
 
 def lat_allreduce(x, axis, dim):

time: 63.8 us -> 68.3 us (1.071)
  Pallas kernels: 12.8 us -> 16.9 us
    pallas_call x1, Pallas kernels: 4.25 us -> 8.33 us  [toeplitz(): pl.pallas_call(toeplitz_kernel, grid=(kernels,), in_specs=[pl.BlockSpec((...]
    unnamed x12 -> x10, local copies, waits for them, and re-layouts: 2.22 us -> 1.58 us
  transfers between devices with their start and end apart: 15 -> 15, of which waited for: 5 -> 5; matrix products, arithmetic and copies ran while one was open for 16% -> 15% of each run, Pallas kernels for 20% -> 25%
where the time goes in v17:
time: 68.3 us; the launch traced here: 67.3 us
  starting transfers between devices  24.1 us (35%)
  Pallas kernels  16.9 us (25%)
  waiting for transfers between devices  12 us (18%)
  local copies, waits for them, and re-layouts  7.03 us (10%)
  other arithmetic  3.79 us (6%)
  matrix products  1.86 us (3%)
  between operations  1.62 us (2%)
    pallas_call x1, Pallas kernels, row_products(): pl.pallas_call(row_kernel, out_shape=(jax.ShapeDtypeStruct((weights.shape...  8.55 us
    pallas_call x1, Pallas kernels, toeplitz(): pl.pallas_call(toeplitz_kernel, grid=(kernels,), in_specs=[pl.BlockSpec((...  8.33 us
    ppermute x3, waiting for transfers between devices, lat_allreduce(): recv = lax.ppermute(mine, axis, [(i, i ^ d) for i in range(count)])  6.21 us
    ppermute x1, starting transfers between devices, body(): below = lax.ppermute(row, 'lat', [(i, i + 1) for i in range(count - 1)])  5.09 us
    ppermute x1, waiting for transfers between devices, body(): above = lax.ppermute(row, 'lat', [(i + 1, i) for i in range(count - 1)])  4.69 us
    ppermute x3, starting transfers between devices, body(): lax.ppermute(jnp.concatenate([fields[:, 0], part], axis=0), 'lon', [(p, (...  4.66 us
    ppermute x2, starting transfers between devices, padded_2(): lax.ppermute(tail, axis, [(i, (i + 1) % count) for i in range(ends)])  4.17 us
    ppermute x2, starting transfers between devices, padded_2(): lax.ppermute(head, axis, [((i + 1) % count, i) for i in range(ends)])  3.47 us
  transfers between devices with their start and end apart: 15, of which 5 were waited for; matrix products, arithmetic and copies ran while one was open for 15% of the time, Pallas kernels for 25%

profile of v17, /device:TPU:1, one launch (start us, length us, event | category | flops | bytes accessed | tf_op | source)
XLA Modules:
  0.0 67.3 jit_solution(12221589135605985645)
XLA Ops:
  0.7 0.8 %dynamic-slice_bitcast_fusion = (bf16[1,64,128]{2,1,0:T(8,128)(2,1)S(1)}, bf16[64,128]{1,0:T(8,128)(2,1)S(1)}, bf16[64,128]{1,0:T(8,128)(2,1)S(1)}, bf16[64,128]{1,0:T(8,128)(2,1)S(1)}) fusion(bf16[256,1,128]{2,0,1:T(8,128)(2,1)} %param.23, s32[]{:T(128)S(6)} %select_n.57, s32[]{:T(128)S(6)} %select_n.55, s32[]{:T(128)S(6)} %select_n.53, s32[]{:T(128)S(6)} %select_n.51), kind=kLoop, calls=%fused_computation.34 | loop fusion | bytes 131088 | tf_op jit(solution)/shard_map/stack | solution.py:188
  1.5 0.9 %pad_maximum_fusion.5 = (bf16[320,128]{1,0:T(8,128)(2,1)S(1)}, bf16[320,128]{1,0:T(8,128)(2,1)S(1)}, bf16[320,128]{1,0:T(8,128)(2,1)S(1)}) fusion(bf16[64,128]{1,0:T(8,128)(2,1)S(1)} %get-tuple-element.112, bf16[256,128]{1,0:T(8,128)(2,1)} %bitcast.56, bf16[64,128]{1,0:T(8,128)(2,1)S(1)} %get-tuple-element.111, bf16[64,128]{1,0:T(8,128)(2,1)S(1)} %get-tuple-element.110), kind=kLoop, calls=%fused_computation.21 | loop fusion | flops 409600 | bytes 360448 | tf_op jit(solution)/shard_map/concatenate | solution.py:182
  2.4 4.2 %collective-permute-start = (bf16[320,128]{1,0:T(8,128)(2,1)S(1)}, bf16[320,128]{1,0:T(8,128)(2,1)S(1)}, u32[]{:S(2)}, u32[]{:S(2)}) collective-permute-start(bf16[320,128]{1,0:T(8,128)(2,1)S(1)} %get-tuple-element.113), channel_id=1, source_target_pairs={{0,3},{1,0},{2,1},{3,2},{4,7},{5,4},{6,5},{7,6},{8,11},{9,8},{10,9... | collective-permute-start | bytes 245768 | tf_op jit(solution)/shard_map/ppermute | solution.py:181
  6.6 0.5 collective-permute-start.2
  7.0 1.7 %convolution_convert_fusion = bf16[128,9,256]{2,0,1:T(8,128)(2,1)S(1)} fusion(bf16[9,256,256]{2,1,0:T(8,128)(2,1)} %w_ref.1, bf16[256,1,128]{2,0,1:T(8,128)(2,1)} %param.23), kind=kOutput, calls=%fused_computation | convolution fusion | flops 151289856 | bytes 1835008 | tf_op jit(solution)/shard_map/koc,oij->cikj/dot_general | solution.py:170
  8.7 1.1 %copy.20.grad_ref = bf16[256,1152]{1,0:T(8,128)(2,1)} copy(bf16[256,1152]{0,1:T(8,128)(2,1)S(1)} %bitcast.53) | data formatting | bytes 1179648 | tf_op jit(solution)/shard_map/reshape;squeeze | solution.py:173
  10.5 0.2 fusion.3
  10.8 0.7 convert_element_type.34.tap_ref
  11.4 8.3 %shard_map.100 = (bf16[9,128,1152]{2,1,0:T(8,128)(2,1)}, f32[256,1152]{1,0:T(8,128)}) custom-call(bf16[9,1,1152]{2,1,0:T(2,128)(2,1)} %convert_element_type.34.tap_ref, bf16[256,1152]{1,0:T(8,128)(2,1)} %copy.20.grad_ref), custom_call_target="tpu_custom_call" | custom-call | tf_op jit(solution)/shard_map/pallas_call | solution.py:65
  19.8 1.6 %copy.21 = f32[256,1152]{0,1:T(8,128)S(1)} copy(f32[256,1152]{1,0:T(8,128)} %get-tuple-element.93) | data formatting | bytes 2359296 | tf_op jit(solution)/shard_map/pallas_call | solution.py:65
  21.5 2.3 %collective-permute-start.5 = (f32[256,3,128]{0,2,1:T(8,128)S(1)}, f32[256,3,128]{0,2,1:T(8,128)S(1)}, u32[]{:S(2)}, u32[]{:S(2)}) collective-permute-start(f32[256,3,128]{0,2,1:T(8,128)S(1)} %get-tuple-element.100), channel_id=1, source_target_pairs={{0,1},{1,2},{2,3},{3,0},{4,5},{5,6},{6,7},{7,4},{8,9},{9,10},{10,1... | collective-permute-start | bytes 1179656 | tf_op jit(solution)/shard_map/ppermute | solution.py:19
  23.7 1.1 %collective-permute-start.6 = (f32[256,3,128]{0,2,1:T(8,128)S(1)}, f32[256,3,128]{0,2,1:T(8,128)S(1)}, u32[]{:S(2)}, u32[]{:S(2)}) collective-permute-start(f32[256,3,128]{0,2,1:T(8,128)S(1)} %get-tuple-element.101), channel_id=1, source_target_pairs={{1,0},{2,1},{3,2},{0,3},{5,4},{6,5},{7,6},{4,7},{9,8},{10,9},{11,1... | collective-permute-start | bytes 1179656 | tf_op jit(solution)/shard_map/ppermute | solution.py:21
  24.9 5.1 %collective-permute-start.3 = (bf16[256,512]{1,0:T(8,128)(2,1)S(1)}, bf16[256,512]{1,0:T(8,128)(2,1)S(1)}, u32[]{:S(2)}, u32[]{:S(2)}) collective-permute-start(bf16[256,512]{1,0:T(8,128)(2,1)S(1)} %get-tuple-element.108), channel_id=1, source_target_pairs={{0,4},{4,8},{8,12},{1,5},{5,9},{9,13},{2,6},{6,10},{10,14},{3,7},{... | collective-permute-start | bytes 786440 | tf_op jit(solution)/shard_map/ppermute | solution.py:191
  30.0 1.9 %collective-permute-start.4 = (bf16[256,512]{1,0:T(8,128)(2,1)S(1)}, bf16[256,512]{1,0:T(8,128)(2,1)S(1)}, u32[]{:S(2)}, u32[]{:S(2)}) collective-permute-start(bf16[256,512]{1,0:T(8,128)(2,1)S(1)} %get-tuple-element.108), channel_id=1, source_target_pairs={{4,0},{8,4},{12,8},{5,1},{9,5},{13,9},{6,2},{10,6},{14,10},{7,3},{... | collective-permute-start | bytes 786440 | tf_op jit(solution)/shard_map/ppermute | solution.py:192
  32.0 0.6 pad_maximum_fusion.8.up_ref
  32.6 0.7 %collective-permute-done.3 = bf16[256,512]{1,0:T(8,128)(2,1)S(1)} collective-permute-done((bf16[256,512]{1,0:T(8,128)(2,1)S(1)}, bf16[256,512]{1,0:T(8,128)(2,1)S(1)}, u32[]{:S(2)}, u32[]{:S(2)}) %collective-permute-start.3) | collective-permute-done | bytes 262176 | tf_op jit(solution)/shard_map/ppermute | solution.py:191
  33.3 4.7 %collective-permute-done.4 = bf16[256,512]{1,0:T(8,128)(2,1)S(1)} collective-permute-done((bf16[256,512]{1,0:T(8,128)(2,1)S(1)}, bf16[256,512]{1,0:T(8,128)(2,1)S(1)}, u32[]{:S(2)}, u32[]{:S(2)}) %collective-permute-start.4) | collective-permute-done | bytes 262176 | tf_op jit(solution)/shard_map/ppermute | solution.py:192
  38.0 1.1 %fusion.ext_ref = bf16[3,256,768]{2,1,0:T(8,128)(2,1)} fusion(bf16[1,256,512]{2,1,0:T(8,128)(2,1)S(1)} %bitcast.55, bf16[1,256,512]{2,1,0:T(8,128)(2,1)S(1)} %get-tuple-element.107, bf16[1,256,512]{2,1,0:T(8,128)(2,1)S(1)} %bitcast.54), kind=kLoop, calls=%fused_computation.2 | loop fusion | flops 10616832 | bytes 1966080 | tf_op jit(solution)/shard_map/concatenate | solution.py:194
  39.1 8.5 %shard_map.101 = (bf16[256,128]{1,0:T(8,128)(2,1)}, f32[9,64,256]{2,1,0:T(8,128)}) custom-call(bf16[3,256,768]{2,1,0:T(8,128)(2,1)} %fusion.ext_ref, bf16[1152,1152]{1,0:T(8,128)(2,1)} %bitcast.58, bf16[9,256,256]{2,1,0:T(8,128)(2,1)} %w_ref.1, bf16[4,64,128]{2,1,0:T(8,128)(2,1)} %pad_maximum_fusion.8.up_ref), custom_call_target="tpu_custom_call" | custom-call | flops 3019898880 | bytes 5734400 | tf_op jit(solution)/shard_map/pallas_call | solution.py:153
  47.6 1.1 %constant_dynamic-slice_fusion.2 = (f32[9,16,256]{2,1,0:T(8,128)S(1)}, f32[9,16,256]{2,1,0:T(8,128)S(1)}, f32[9,16,256]{2,1,0:T(8,128)S(1)}) fusion(f32[9,64,256]{2,1,0:T(8,128)} %get-tuple-element.94, s32[]{:T(128)S(6)} %select_n.59, s32[]{:T(128)S(6)} %select_n.61, s32[]{:T(128)S(6)} %select_n.60), kind=kLoop, calls=%fused_computation.44 | loop fusion | bytes 884748 | tf_op jit(solution)/shard_map/dynamic_slice | solution.py:94
  48.9 1.8 %collective-permute-start.9 = (f32[9,16,256]{2,1,0:T(8,128)S(1)}, f32[9,16,256]{2,1,0:T(8,128)S(1)}, u32[]{:S(2)}, u32[]{:S(2)}) collective-permute-start(f32[9,16,256]{2,1,0:T(8,128)S(1)} %get-tuple-element.102), channel_id=1, source_target_pairs={{0,4},{4,0},{8,12},{12,8},{1,5},{5,1},{9,13},{13,9},{2,6},{6,2},{1... | collective-permute-start | bytes 442376 | tf_op jit(solution)/shard_map/ppermute | solution.py:95
  50.8 1.9 %collective-permute-start.7 = (f32[256,1,128]{0,2,1:T(8,128)S(1)}, f32[256,1,128]{0,2,1:T(8,128)S(1)}, u32[]{:S(2)}, u32[]{:S(2)}) collective-permute-start(f32[256,1,128]{0,2,1:T(8,128)S(1)} %get-tuple-element.105), channel_id=1, source_target_pairs={{0,4},{4,8},{8,12},{1,5},{5,9},{9,13},{2,6},{6,10},{10,14},{3,7},{... | collective-permute-start | bytes 393224 | tf_op jit(solution)/shard_map/ppermute | solution.py:19
  52.7 2.4 %collective-permute-start.8 = (f32[256,1,128]{0,2,1:T(8,128)S(1)}, f32[256,1,128]{0,2,1:T(8,128)S(1)}, u32[]{:S(2)}, u32[]{:S(2)}) collective-permute-start(f32[256,1,128]{0,2,1:T(8,128)S(1)} %get-tuple-element.106), channel_id=1, source_target_pairs={{4,0},{8,4},{12,8},{5,1},{9,5},{13,9},{6,2},{10,6},{14,10},{7,3},{... | collective-permute-start | bytes 393224 | tf_op jit(solution)/shard_map/ppermute | solution.py:21
  55.1 0.4 collective-permute-done.11
  55.6 1.0 %constant_dynamic-update-slice_fusion.3 = (f32[9,64,256]{2,1,0:T(8,128)S(1)}, f32[9,16,256]{2,1,0:T(8,128)S(1)}) fusion(f32[9,64,256]{2,1,0:T(8,128)S(1)} %broadcast_in_dim.25, s32[]{:T(128)S(6)} %select_n.58, f32[9,16,256]{2,1,0:T(8,128)S(1)} %collective-permute-done.10, f32[9,16,256]{2,1,0:T(8,128)S(1)} %collective-permute-done.11, ...), kind=kLoop, calls=%fused_computation.41 | loop fusion | flops 110592 | bytes 884740 | tf_op jit(solution)/shard_map/dynamic_update_slice | solution.py:100
  56.5 1.2 %collective-permute-start.12 = (f32[9,16,256]{2,1,0:T(8,128)S(1)}, f32[9,16,256]{2,1,0:T(8,128)S(1)}, u32[]{:S(2)}, u32[]{:S(2)}) collective-permute-start(f32[9,16,256]{2,1,0:T(8,128)S(1)} %get-tuple-element.99), channel_id=1, source_target_pairs={{0,4},{4,0},{8,12},{12,8},{1,5},{5,1},{9,13},{13,9},{2,6},{6,2},{1... | collective-permute-start | bytes 442376 | tf_op jit(solution)/shard_map/ppermute | solution.py:102
  57.7 1.5 %collective-permute-start.13 = (f32[9,16,256]{2,1,0:T(8,128)S(1)}, f32[9,16,256]{2,1,0:T(8,128)S(1)}, u32[]{:S(2)}, u32[]{:S(2)}) collective-permute-start(f32[9,16,256]{2,1,0:T(8,128)S(1)} %get-tuple-element.99), channel_id=1, source_target_pairs={{0,8},{4,12},{8,0},{12,4},{1,9},{5,13},{9,1},{13,5},{2,10},{6,14},... | collective-permute-start | bytes 442376 | tf_op jit(solution)/shard_map/ppermute | solution.py:102
  59.2 0.3 collective-permute-start.14
  59.5 0.7 %copy.22 = bf16[256,1,128]{2,0,1:T(8,128)(2,1)} copy(bf16[256,1,128]{0,2,1:T(8,128)(2,1)S(1)} %fusion.6) | data formatting | bytes 131072
  60.3 2.9 %collective-permute-done.13 = f32[9,16,256]{2,1,0:T(8,128)S(1)} collective-permute-done((f32[9,16,256]{2,1,0:T(8,128)S(1)}, f32[9,16,256]{2,1,0:T(8,128)S(1)}, u32[]{:S(2)}, u32[]{:S(2)}) %collective-permute-start.13) | collective-permute-done | bytes 147488 | tf_op jit(solution)/shard_map/ppermute | solution.py:102
  63.2 3.3 %collective-permute-done.14 = f32[9,16,256]{2,1,0:T(8,128)S(1)} collective-permute-done((f32[9,16,256]{2,1,0:T(8,128)S(1)}, f32[9,16,256]{2,1,0:T(8,128)S(1)}, u32[]{:S(2)}, u32[]{:S(2)}) %collective-permute-start.14) | collective-permute-done | bytes 147488 | tf_op jit(solution)/shard_map/ppermute | solution.py:102
  66.5 0.8 %copy-done.1 = f32[9,64,256]{2,1,0:T(8,128)} copy-done((f32[9,64,256]{2,1,0:T(8,128)}, f32[9,64,256]{2,1,0:T(8,128)S(1)}, u32[]{:S(2)}) %copy-start.1) | copy-done | bytes 589848
  (40 shorter events, 0.7 us)
Async XLA Ops:
  0.6 9.9 %copy-start = (bf16[1,9,3,2,64]{4,3,2,1,0:T(2,128)(2,1)S(1)}, bf16[1,9,3,2,64]{4,3,2,1,0:T(2,128)(2,1)}, u32[]{:S(2)}) copy-start(bf16[1,9,3,2,64]{4,3,2,1,0:T(2,128)(2,1)} %param.25) | copy-start | bytes 20740
  2.4 22.4 %collective-permute-start = (bf16[320,128]{1,0:T(8,128)(2,1)S(1)}, bf16[320,128]{1,0:T(8,128)(2,1)S(1)}, u32[]{:S(2)}, u32[]{:S(2)}) collective-permute-start(bf16[320,128]{1,0:T(8,128)(2,1)S(1)} %get-tuple-element.113), channel_id=1, source_target_pairs={{0,3},{1,0},{2,1},{3,2},{4,7},{5,4},{6,5},{7,6},{8,11},{9,8},{10,9... | collective-permute-start | bytes 245768 | tf_op jit(solution)/shard_map/ppermute | solution.py:181
  6.6 18.3 %collective-permute-start.1 = (bf16[320,128]{1,0:T(8,128)(2,1)S(1)}, bf16[320,128]{1,0:T(8,128)(2,1)S(1)}, u32[]{:S(2)}, u32[]{:S(2)}) collective-permute-start(bf16[320,128]{1,0:T(8,128)(2,1)S(1)} %get-tuple-element.114), channel_id=1, source_target_pairs={{0,2},{1,3},{2,0},{3,1},{4,6},{5,7},{6,4},{7,5},{8,10},{9,11},{10,... | collective-permute-start | bytes 245768 | tf_op jit(solution)/shard_map/ppermute | solution.py:181
  6.6 3.2 %copy-start.3 = (s32[1,2]{1,0:T(1,128)S(1)}, s32[1,2]{1,0:T(1,128)}, u32[]{:S(2)}) copy-start(s32[1,2]{1,0:T(1,128)} %param.27) | copy-start | bytes 28
  6.6 18.3 %collective-permute-start.2 = (bf16[320,128]{1,0:T(8,128)(2,1)S(1)}, bf16[320,128]{1,0:T(8,128)(2,1)S(1)}, u32[]{:S(2)}, u32[]{:S(2)}) collective-permute-start(bf16[320,128]{1,0:T(8,128)(2,1)S(1)} %get-tuple-element.115), channel_id=1, source_target_pairs={{0,1},{1,2},{2,3},{3,0},{4,5},{5,6},{6,7},{7,4},{8,9},{9,10},{10,1... | collective-permute-start | bytes 245768 | tf_op jit(solution)/shard_map/ppermute | solution.py:181
  21.4 3.5 %copy-start.2 = (bf16[256,1,128]{2,0,1:T(8,128)(2,1)S(1)}, bf16[256,1,128]{2,0,1:T(8,128)(2,1)}, u32[]{:S(2)}) copy-start(bf16[256,1,128]{2,0,1:T(8,128)(2,1)} %param.22) | copy-start | bytes 196612
  21.5 29.2 %collective-permute-start.5 = (f32[256,3,128]{0,2,1:T(8,128)S(1)}, f32[256,3,128]{0,2,1:T(8,128)S(1)}, u32[]{:S(2)}, u32[]{:S(2)}) collective-permute-start(f32[256,3,128]{0,2,1:T(8,128)S(1)} %get-tuple-element.100), channel_id=1, source_target_pairs={{0,1},{1,2},{2,3},{3,0},{4,5},{5,6},{6,7},{7,4},{8,9},{9,10},{10,1... | collective-permute-start | bytes 1179656 | tf_op jit(solution)/shard_map/ppermute | solution.py:19
  23.7 26.9 %collective-permute-start.6 = (f32[256,3,128]{0,2,1:T(8,128)S(1)}, f32[256,3,128]{0,2,1:T(8,128)S(1)}, u32[]{:S(2)}, u32[]{:S(2)}) collective-permute-start(f32[256,3,128]{0,2,1:T(8,128)S(1)} %get-tuple-element.101), channel_id=1, source_target_pairs={{1,0},{2,1},{3,2},{0,3},{5,4},{6,5},{7,6},{4,7},{9,8},{10,9},{11,1... | collective-permute-start | bytes 1179656 | tf_op jit(solution)/shard_map/ppermute | solution.py:21
  24.9 8.4 %collective-permute-start.3 = (bf16[256,512]{1,0:T(8,128)(2,1)S(1)}, bf16[256,512]{1,0:T(8,128)(2,1)S(1)}, u32[]{:S(2)}, u32[]{:S(2)}) collective-permute-start(bf16[256,512]{1,0:T(8,128)(2,1)S(1)} %get-tuple-element.108), channel_id=1, source_target_pairs={{0,4},{4,8},{8,12},{1,5},{5,9},{9,13},{2,6},{6,10},{10,14},{3,7},{... | collective-permute-start | bytes 786440 | tf_op jit(solution)/shard_map/ppermute | solution.py:191
  30.0 8.0 %collective-permute-start.4 = (bf16[256,512]{1,0:T(8,128)(2,1)S(1)}, bf16[256,512]{1,0:T(8,128)(2,1)S(1)}, u32[]{:S(2)}, u32[]{:S(2)}) collective-permute-start(bf16[256,512]{1,0:T(8,128)(2,1)S(1)} %get-tuple-element.108), channel_id=1, source_target_pairs={{4,0},{8,4},{12,8},{5,1},{9,5},{13,9},{6,2},{10,6},{14,10},{7,3},{... | collective-permute-start | bytes 786440 | tf_op jit(solution)/shard_map/ppermute | solution.py:192
  48.7 6.4 %collective-permute-start.10 = (f32[9,16,256]{2,1,0:T(8,128)S(1)}, f32[9,16,256]{2,1,0:T(8,128)S(1)}, u32[]{:S(2)}, u32[]{:S(2)}) collective-permute-start(f32[9,16,256]{2,1,0:T(8,128)S(1)} %get-tuple-element.104), channel_id=1, source_target_pairs={{0,8},{4,12},{8,0},{12,4},{1,9},{5,13},{9,1},{13,5},{2,10},{6,14},... | collective-permute-start | bytes 442376 | tf_op jit(solution)/shard_map/ppermute | solution.py:95
  48.8 6.7 %collective-permute-start.11 = (f32[9,16,256]{2,1,0:T(8,128)S(1)}, f32[9,16,256]{2,1,0:T(8,128)S(1)}, u32[]{:S(2)}, u32[]{:S(2)}) collective-permute-start(f32[9,16,256]{2,1,0:T(8,128)S(1)} %get-tuple-element.103), channel_id=1, source_target_pairs={{0,12},{4,8},{8,4},{12,0},{1,13},{5,9},{9,5},{13,1},{2,14},{6,10},... | collective-permute-start | bytes 442376 | tf_op jit(solution)/shard_map/ppermute | solution.py:95
  48.9 6.6 %collective-permute-start.9 = (f32[9,16,256]{2,1,0:T(8,128)S(1)}, f32[9,16,256]{2,1,0:T(8,128)S(1)}, u32[]{:S(2)}, u32[]{:S(2)}) collective-permute-start(f32[9,16,256]{2,1,0:T(8,128)S(1)} %get-tuple-element.102), channel_id=1, source_target_pairs={{0,4},{4,0},{8,12},{12,8},{1,5},{5,1},{9,13},{13,9},{2,6},{6,2},{1... | collective-permute-start | bytes 442376 | tf_op jit(solution)/shard_map/ppermute | solution.py:95
  50.8 8.7 %collective-permute-start.7 = (f32[256,1,128]{0,2,1:T(8,128)S(1)}, f32[256,1,128]{0,2,1:T(8,128)S(1)}, u32[]{:S(2)}, u32[]{:S(2)}) collective-permute-start(f32[256,1,128]{0,2,1:T(8,128)S(1)} %get-tuple-element.105), channel_id=1, source_target_pairs={{0,4},{4,8},{8,12},{1,5},{5,9},{9,13},{2,6},{6,10},{10,14},{3,7},{... | collective-permute-start | bytes 393224 | tf_op jit(solution)/shard_map/ppermute | solution.py:19
  52.7 6.8 %collective-permute-start.8 = (f32[256,1,128]{0,2,1:T(8,128)S(1)}, f32[256,1,128]{0,2,1:T(8,128)S(1)}, u32[]{:S(2)}, u32[]{:S(2)}) collective-permute-start(f32[256,1,128]{0,2,1:T(8,128)S(1)} %get-tuple-element.106), channel_id=1, source_target_pairs={{4,0},{8,4},{12,8},{5,1},{9,5},{13,9},{6,2},{10,6},{14,10},{7,3},{... | collective-permute-start | bytes 393224 | tf_op jit(solution)/shard_map/ppermute | solution.py:21
  56.5 3.7 %collective-permute-start.12 = (f32[9,16,256]{2,1,0:T(8,128)S(1)}, f32[9,16,256]{2,1,0:T(8,128)S(1)}, u32[]{:S(2)}, u32[]{:S(2)}) collective-permute-start(f32[9,16,256]{2,1,0:T(8,128)S(1)} %get-tuple-element.99), channel_id=1, source_target_pairs={{0,4},{4,0},{8,12},{12,8},{1,5},{5,1},{9,13},{13,9},{2,6},{6,2},{1... | collective-permute-start | bytes 442376 | tf_op jit(solution)/shard_map/ppermute | solution.py:102
  57.7 5.4 %collective-permute-start.13 = (f32[9,16,256]{2,1,0:T(8,128)S(1)}, f32[9,16,256]{2,1,0:T(8,128)S(1)}, u32[]{:S(2)}, u32[]{:S(2)}) collective-permute-start(f32[9,16,256]{2,1,0:T(8,128)S(1)} %get-tuple-element.99), channel_id=1, source_target_pairs={{0,8},{4,12},{8,0},{12,4},{1,9},{5,13},{9,1},{13,5},{2,10},{6,14},... | collective-permute-start | bytes 442376 | tf_op jit(solution)/shard_map/ppermute | solution.py:102
  59.2 7.3 %collective-permute-start.14 = (f32[9,16,256]{2,1,0:T(8,128)S(1)}, f32[9,16,256]{2,1,0:T(8,128)S(1)}, u32[]{:S(2)}, u32[]{:S(2)}) collective-permute-start(f32[9,16,256]{2,1,0:T(8,128)S(1)} %get-tuple-element.99), channel_id=1, source_target_pairs={{0,12},{4,8},{8,4},{12,0},{1,13},{5,9},{9,5},{13,1},{2,14},{6,10},... | collective-permute-start | bytes 442376 | tf_op jit(solution)/shard_map/ppermute | solution.py:102
  66.5 0.8 %copy-start.1 = (f32[9,64,256]{2,1,0:T(8,128)}, f32[9,64,256]{2,1,0:T(8,128)S(1)}, u32[]{:S(2)}) copy-start(f32[9,64,256]{2,1,0:T(8,128)S(1)} %constant_dynamic-update-slice_fusion) | copy-start | bytes 1769476

commit v18 on v16

--- a/solution.py
+++ b/solution.py
@@ -38,23 +38,23 @@
     return jnp.einsum("ikrst,istu->ikru", filter_taps.astype(jnp.float32), onehot)
 
 
-def toeplitz_kernel(tap_ref, grad_ref, out_ref, contrib_ref):
+def toeplitz_kernel(tap_ref, w_ref, up_ref, out_ref, contrib_ref):
     kernels, lon_cols, width = out_ref.shape
+    contract_first = (((0,), (0,)), ((), ()))
     acc = None
     for k in range(kernels):
         row = tap_ref[pl.ds(k, 1), :]
         tiled = jnp.broadcast_to(row, (lon_cols, width))
         out_ref[k] = pltpu.roll(tiled, 0, 1, stride=1, stride_axis=0)
-        term = jnp.dot(
-            grad_ref[:, pl.ds(k * lon_cols, lon_cols)],
-            out_ref[k],
-            preferred_element_type=jnp.float32,
-        )
+        grad_k = lax.dot_general(
+            w_ref[k], up_ref[...], contract_first, preferred_element_type=jnp.float32
+        ).astype(jnp.bfloat16)
+        term = jnp.dot(grad_k, out_ref[k], preferred_element_type=jnp.float32)
         acc = term if acc is None else acc + term
     contrib_ref[...] = acc
 
 
-def toeplitz(tap_row, out_width, grad_piece):
+def toeplitz(tap_row, out_width, weights, up_row):
     kernels, stencil_rows, reach = tap_row.shape
     window_len = out_width + reach
     padded = jnp.pad(tap_row.astype(jnp.float32), ((0, 0), (0, 0), (0, window_len - reach)))
@@ -63,9 +63,9 @@
         toeplitz_kernel,
         out_shape=(
             jax.ShapeDtypeStruct((kernels, out_width, stencil_rows * window_len), jnp.bfloat16),
-            jax.ShapeDtypeStruct((grad_piece.shape[0], stencil_rows * window_len), jnp.float32),
+            jax.ShapeDtypeStruct((weights.shape[2], stencil_rows * window_len), jnp.float32),
         ),
-    )(padded, grad_piece)
+    )(padded, weights, up_row)
     return out.reshape(kernels * out_width, stencil_rows * window_len), contrib
 
 
@@ -154,11 +154,7 @@
     n_lon = lax.axis_size("lon")
     lon_at = lax.axis_index("lon")
     tap_table = build_taps(filter_taps, cycle_counts, cycle_blocks).astype(jnp.bfloat16)
-    response_grad = jnp.einsum(
-        "koc,oij->cikj", weights, upstream, preferred_element_type=jnp.float32
-    ).astype(jnp.bfloat16)
-    grad_piece = response_grad[:, 0].reshape(channels, kernels * lon_cols)
-    matrix, contrib = toeplitz(tap_table[0], lon_cols, grad_piece)
+    matrix, contrib = toeplitz(tap_table[0], lon_cols, weights, upstream[:, 0])
     o_block = upstream.shape[0] // n_lon
     up_row = upstream[:, 0]
     blocks = [fields[:, 0]]

time: 63.8 us -> 63 us (0.987)
  matrix products: 1.86 us -> 0.2 us
  Pallas kernels: 12.8 us -> 14 us
  local copies, waits for them, and re-layouts: 7 us -> 5.97 us
  other arithmetic: 3.79 us -> 4.46 us
    dot_general x1 -> x0, matrix products: 1.65 us -> none  [body(): jnp.einsum('koc,oij->cikj', weights, upstream, preferred_element_type=jnp...]
    pallas_call x1, Pallas kernels: 4.25 us -> 5.48 us  [toeplitz(): pl.pallas_call(toeplitz_kernel, out_shape=(jax.ShapeDtypeStruct((kernels,...]
    another operation x1 -> x0, local copies, waits for them, and re-layouts: 1.06 us -> none  [body(): grad_piece = response_grad[:, 0].reshape(channels, kernels * lon_cols)]
    add x2, other arithmetic: 0.08 us -> 0.73 us  [build_taps(): HALO + width_block * cycle_blocks[:, :, None] + offsets[None, None, :]]
    unnamed x12 -> x10, local copies, waits for them, and re-layouts: 2.22 us -> 2.22 us
  transfers between devices with their start and end apart: 15 -> 15, of which waited for: 5 -> 5; matrix products, arithmetic and copies ran while one was open for 16% -> 13% of each run, Pallas kernels for 20% -> 22%
where the time goes in v18:
time: 63 us; the launch traced here: 62.4 us
  starting transfers between devices  24.1 us (38%)
  Pallas kernels  14 us (22%)
  waiting for transfers between devices  12 us (19%)
  local copies, waits for them, and re-layouts  5.97 us (9%)
  other arithmetic  4.46 us (7%)
  between operations  1.61 us (3%)
    pallas_call x1, Pallas kernels, row_products(): pl.pallas_call(row_kernel, out_shape=(jax.ShapeDtypeStruct((weights.shape...  8.55 us
    ppermute x3, waiting for transfers between devices, lat_allreduce(): recv = lax.ppermute(mine, axis, [(i, i ^ d) for i in range(count)])  6.21 us
    pallas_call x1, Pallas kernels, toeplitz(): pl.pallas_call(toeplitz_kernel, out_shape=(jax.ShapeDtypeStruct((kernels,...  5.48 us
    ppermute x1, starting transfers between devices, body(): below = lax.ppermute(row, 'lat', [(i, i + 1) for i in range(count - 1)])  5.09 us
    ppermute x1, waiting for transfers between devices, body(): above = lax.ppermute(row, 'lat', [(i + 1, i) for i in range(count - 1)])  4.69 us
    ppermute x3, starting transfers between devices, body(): lax.ppermute(jnp.concatenate([fields[:, 0], part], axis=0), 'lon', [(p, (...  4.66 us
    ppermute x2, starting transfers between devices, padded_2(): lax.ppermute(tail, axis, [(i, (i + 1) % count) for i in range(ends)])  4.17 us
    ppermute x2, starting transfers between devices, padded_2(): lax.ppermute(head, axis, [((i + 1) % count, i) for i in range(ends)])  3.47 us
  transfers between devices with their start and end apart: 15, of which 5 were waited for; matrix products, arithmetic and copies ran while one was open for 13% of the time, Pallas kernels for 22%

profile of v18, /device:TPU:1, one launch (start us, length us, event | category | flops | bytes accessed | tf_op | source)
XLA Modules:
  0.0 62.4 jit_solution(14108354268250142980)
XLA Ops:
  0.7 0.8 %dynamic-slice_bitcast_fusion = (bf16[1,64,128]{2,1,0:T(8,128)(2,1)S(1)}, bf16[64,128]{1,0:T(8,128)(2,1)S(1)}, bf16[64,128]{1,0:T(8,128)(2,1)S(1)}, bf16[64,128]{1,0:T(8,128)(2,1)S(1)}) fusion(bf16[256,1,128]{2,0,1:T(8,128)(2,1)} %param.23, s32[]{:T(128)S(6)} %select_n.57, s32[]{:T(128)S(6)} %select_n.55, s32[]{:T(128)S(6)} %select_n.53, s32[]{:T(128)S(6)} %select_n.51), kind=kLoop, calls=%fused_computation.32 | loop fusion | bytes 131088 | tf_op jit(solution)/shard_map/stack | solution.py:171
  1.5 0.9 %pad_maximum_fusion.5 = (bf16[320,128]{1,0:T(8,128)(2,1)S(1)}, bf16[320,128]{1,0:T(8,128)(2,1)S(1)}, bf16[320,128]{1,0:T(8,128)(2,1)S(1)}) fusion(bf16[64,128]{1,0:T(8,128)(2,1)S(1)} %get-tuple-element.112, bf16[256,128]{1,0:T(8,128)(2,1)} %bitcast.49, bf16[64,128]{1,0:T(8,128)(2,1)S(1)} %get-tuple-element.111, bf16[64,128]{1,0:T(8,128)(2,1)S(1)} %get-tuple-element.110), kind=kLoop, calls=%fused_computation.20 | loop fusion | flops 409600 | bytes 360448 | tf_op jit(solution)/shard_map/concatenate | solution.py:165
  2.4 4.2 %collective-permute-start = (bf16[320,128]{1,0:T(8,128)(2,1)S(1)}, bf16[320,128]{1,0:T(8,128)(2,1)S(1)}, u32[]{:S(2)}, u32[]{:S(2)}) collective-permute-start(bf16[320,128]{1,0:T(8,128)(2,1)S(1)} %get-tuple-element.113), channel_id=1, source_target_pairs={{0,3},{1,0},{2,1},{3,2},{4,7},{5,4},{6,5},{7,6},{8,11},{9,8},{10,9... | collective-permute-start | bytes 245768 | tf_op jit(solution)/shard_map/ppermute | solution.py:164
  6.6 0.5 collective-permute-start.2
  7.0 0.7 %add_bitcast_fusion = s32[2]{0:T(128)S(1)} fusion(s32[1,2]{1,0:T(1,128)} %param.27), kind=kLoop, calls=%fused_computation.45 | loop fusion | flops 4 | bytes 16 | tf_op jit(solution)/shard_map/add | solution.py:32
  8.4 0.2 fusion.3
  8.7 0.6 copy.20
  9.3 5.5 %shard_map.100 = (bf16[9,128,1152]{2,1,0:T(8,128)(2,1)}, f32[256,1152]{1,0:T(8,128)}) custom-call(bf16[9,1152]{1,0:T(8,128)(2,1)} %bitcast.52, bf16[9,256,256]{2,1,0:T(8,128)(2,1)} %w_ref.3, bf16[256,128]{1,0:T(8,128)(2,1)} %bitcast.48), custom_call_target="tpu_custom_call" | custom-call | tf_op jit(solution)/shard_map/pallas_call | solution.py:62
  14.8 1.7 %copy.16 = f32[256,1152]{0,1:T(8,128)S(1)} copy(f32[256,1152]{1,0:T(8,128)} %get-tuple-element.93) | data formatting | bytes 2359296 | tf_op jit(solution)/shard_map/pallas_call | solution.py:62
  16.6 2.3 %collective-permute-start.5 = (f32[256,3,128]{0,2,1:T(8,128)S(1)}, f32[256,3,128]{0,2,1:T(8,128)S(1)}, u32[]{:S(2)}, u32[]{:S(2)}) collective-permute-start(f32[256,3,128]{0,2,1:T(8,128)S(1)} %get-tuple-element.100), channel_id=1, source_target_pairs={{0,1},{1,2},{2,3},{3,0},{4,5},{5,6},{6,7},{7,4},{8,9},{9,10},{10,1... | collective-permute-start | bytes 1179656 | tf_op jit(solution)/shard_map/ppermute | solution.py:19
  18.8 1.1 %collective-permute-start.6 = (f32[256,3,128]{0,2,1:T(8,128)S(1)}, f32[256,3,128]{0,2,1:T(8,128)S(1)}, u32[]{:S(2)}, u32[]{:S(2)}) collective-permute-start(f32[256,3,128]{0,2,1:T(8,128)S(1)} %get-tuple-element.101), channel_id=1, source_target_pairs={{1,0},{2,1},{3,2},{0,3},{5,4},{6,5},{7,6},{4,7},{9,8},{10,9},{11,1... | collective-permute-start | bytes 1179656 | tf_op jit(solution)/shard_map/ppermute | solution.py:21
  20.0 5.1 %collective-permute-start.3 = (bf16[256,512]{1,0:T(8,128)(2,1)S(1)}, bf16[256,512]{1,0:T(8,128)(2,1)S(1)}, u32[]{:S(2)}, u32[]{:S(2)}) collective-permute-start(bf16[256,512]{1,0:T(8,128)(2,1)S(1)} %get-tuple-element.108), channel_id=1, source_target_pairs={{0,4},{4,8},{8,12},{1,5},{5,9},{9,13},{2,6},{6,10},{10,14},{3,7},{... | collective-permute-start | bytes 786440 | tf_op jit(solution)/shard_map/ppermute | solution.py:174
  25.1 1.9 %collective-permute-start.4 = (bf16[256,512]{1,0:T(8,128)(2,1)S(1)}, bf16[256,512]{1,0:T(8,128)(2,1)S(1)}, u32[]{:S(2)}, u32[]{:S(2)}) collective-permute-start(bf16[256,512]{1,0:T(8,128)(2,1)S(1)} %get-tuple-element.108), channel_id=1, source_target_pairs={{4,0},{8,4},{12,8},{5,1},{9,5},{13,9},{6,2},{10,6},{14,10},{7,3},{... | collective-permute-start | bytes 786440 | tf_op jit(solution)/shard_map/ppermute | solution.py:175
  27.1 0.6 %pad_maximum_fusion.8.up_ref = bf16[4,64,128]{2,1,0:T(8,128)(2,1)} fusion(bf16[1,64,128]{2,1,0:T(8,128)(2,1)S(1)} %slice_bitcast_fusion, bf16[1,64,128]{2,1,0:T(8,128)(2,1)S(1)} %slice_bitcast_fusion.1, bf16[1,64,128]{2,1,0:T(8,128)(2,1)S(1)} %slice_bitcast_fusion.2, bf16[1,64,128]{2,1,0:T(8,128)(2,1)S(1)} %get-tuple-element.109), kind=kLoop, calls=%fused_computation.23 | loop fusion | flops 98304 | bytes 131072 | tf_op jit(solution)/shard_map/stack | solution.py:171
  27.7 0.7 %collective-permute-done.3 = bf16[256,512]{1,0:T(8,128)(2,1)S(1)} collective-permute-done((bf16[256,512]{1,0:T(8,128)(2,1)S(1)}, bf16[256,512]{1,0:T(8,128)(2,1)S(1)}, u32[]{:S(2)}, u32[]{:S(2)}) %collective-permute-start.3) | collective-permute-done | bytes 262176 | tf_op jit(solution)/shard_map/ppermute | solution.py:174
  28.4 4.7 %collective-permute-done.4 = bf16[256,512]{1,0:T(8,128)(2,1)S(1)} collective-permute-done((bf16[256,512]{1,0:T(8,128)(2,1)S(1)}, bf16[256,512]{1,0:T(8,128)(2,1)S(1)}, u32[]{:S(2)}, u32[]{:S(2)}) %collective-permute-start.4) | collective-permute-done | bytes 262176 | tf_op jit(solution)/shard_map/ppermute | solution.py:175
  33.1 1.1 %fusion.ext_ref = bf16[3,256,768]{2,1,0:T(8,128)(2,1)} fusion(bf16[1,256,512]{2,1,0:T(8,128)(2,1)S(1)} %bitcast.47, bf16[1,256,512]{2,1,0:T(8,128)(2,1)S(1)} %get-tuple-element.107, bf16[1,256,512]{2,1,0:T(8,128)(2,1)S(1)} %bitcast.46), kind=kLoop, calls=%fused_computation.1 | loop fusion | flops 10616832 | bytes 1966080 | tf_op jit(solution)/shard_map/concatenate | solution.py:177
  34.2 8.5 %shard_map.101 = (bf16[256,128]{1,0:T(8,128)(2,1)}, f32[9,64,256]{2,1,0:T(8,128)}) custom-call(bf16[3,256,768]{2,1,0:T(8,128)(2,1)} %fusion.ext_ref, bf16[1152,1152]{1,0:T(8,128)(2,1)} %bitcast.53, bf16[9,256,256]{2,1,0:T(8,128)(2,1)} %w_ref.3, bf16[4,64,128]{2,1,0:T(8,128)(2,1)} %pad_maximum_fusion.8.up_ref), custom_call_target="tpu_custom_call" | custom-call | flops 3019898880 | bytes 5734400 | tf_op jit(solution)/shard_map/pallas_call | solution.py:140
  42.7 1.1 %constant_dynamic-slice_fusion.2 = (f32[9,16,256]{2,1,0:T(8,128)S(1)}, f32[9,16,256]{2,1,0:T(8,128)S(1)}, f32[9,16,256]{2,1,0:T(8,128)S(1)}) fusion(f32[9,64,256]{2,1,0:T(8,128)} %get-tuple-element.94, s32[]{:T(128)S(6)} %select_n.59, s32[]{:T(128)S(6)} %select_n.61, s32[]{:T(128)S(6)} %select_n.60), kind=kLoop, calls=%fused_computation.42 | loop fusion | bytes 884748 | tf_op jit(solution)/shard_map/dynamic_slice | solution.py:81
  44.0 1.8 %collective-permute-start.9 = (f32[9,16,256]{2,1,0:T(8,128)S(1)}, f32[9,16,256]{2,1,0:T(8,128)S(1)}, u32[]{:S(2)}, u32[]{:S(2)}) collective-permute-start(f32[9,16,256]{2,1,0:T(8,128)S(1)} %get-tuple-element.102), channel_id=1, source_target_pairs={{0,4},{4,0},{8,12},{12,8},{1,5},{5,1},{9,13},{13,9},{2,6},{6,2},{1... | collective-permute-start | bytes 442376 | tf_op jit(solution)/shard_map/ppermute | solution.py:82
  45.8 0.1 fusion.4
  45.9 1.9 %collective-permute-start.7 = (f32[256,1,128]{0,2,1:T(8,128)S(1)}, f32[256,1,128]{0,2,1:T(8,128)S(1)}, u32[]{:S(2)}, u32[]{:S(2)}) collective-permute-start(f32[256,1,128]{0,2,1:T(8,128)S(1)} %get-tuple-element.105), channel_id=1, source_target_pairs={{0,4},{4,8},{8,12},{1,5},{5,9},{9,13},{2,6},{6,10},{10,14},{3,7},{... | collective-permute-start | bytes 393224 | tf_op jit(solution)/shard_map/ppermute | solution.py:19
  47.8 2.4 %collective-permute-start.8 = (f32[256,1,128]{0,2,1:T(8,128)S(1)}, f32[256,1,128]{0,2,1:T(8,128)S(1)}, u32[]{:S(2)}, u32[]{:S(2)}) collective-permute-start(f32[256,1,128]{0,2,1:T(8,128)S(1)} %get-tuple-element.106), channel_id=1, source_target_pairs={{4,0},{8,4},{12,8},{5,1},{9,5},{13,9},{6,2},{10,6},{14,10},{7,3},{... | collective-permute-start | bytes 393224 | tf_op jit(solution)/shard_map/ppermute | solution.py:21
  50.2 0.4 collective-permute-done.11
  50.7 1.0 %constant_dynamic-update-slice_fusion.3 = (f32[9,64,256]{2,1,0:T(8,128)S(1)}, f32[9,16,256]{2,1,0:T(8,128)S(1)}) fusion(f32[9,64,256]{2,1,0:T(8,128)S(1)} %broadcast_in_dim.25, s32[]{:T(128)S(6)} %select_n.58, f32[9,16,256]{2,1,0:T(8,128)S(1)} %collective-permute-done.10, f32[9,16,256]{2,1,0:T(8,128)S(1)} %collective-permute-done.11, ...), kind=kLoop, calls=%fused_computation.39 | loop fusion | flops 110592 | bytes 884740 | tf_op jit(solution)/shard_map/dynamic_update_slice | solution.py:87
  51.6 1.2 %collective-permute-start.12 = (f32[9,16,256]{2,1,0:T(8,128)S(1)}, f32[9,16,256]{2,1,0:T(8,128)S(1)}, u32[]{:S(2)}, u32[]{:S(2)}) collective-permute-start(f32[9,16,256]{2,1,0:T(8,128)S(1)} %get-tuple-element.99), channel_id=1, source_target_pairs={{0,4},{4,0},{8,12},{12,8},{1,5},{5,1},{9,13},{13,9},{2,6},{6,2},{1... | collective-permute-start | bytes 442376 | tf_op jit(solution)/shard_map/ppermute | solution.py:89
  52.8 1.5 %collective-permute-start.13 = (f32[9,16,256]{2,1,0:T(8,128)S(1)}, f32[9,16,256]{2,1,0:T(8,128)S(1)}, u32[]{:S(2)}, u32[]{:S(2)}) collective-permute-start(f32[9,16,256]{2,1,0:T(8,128)S(1)} %get-tuple-element.99), channel_id=1, source_target_pairs={{0,8},{4,12},{8,0},{12,4},{1,9},{5,13},{9,1},{13,5},{2,10},{6,14},... | collective-permute-start | bytes 442376 | tf_op jit(solution)/shard_map/ppermute | solution.py:89
  54.3 0.3 collective-permute-start.14
  54.6 0.7 %copy.17 = bf16[256,1,128]{2,0,1:T(8,128)(2,1)} copy(bf16[256,1,128]{0,2,1:T(8,128)(2,1)S(1)} %fusion.6) | data formatting | bytes 131072
  55.4 2.9 %collective-permute-done.13 = f32[9,16,256]{2,1,0:T(8,128)S(1)} collective-permute-done((f32[9,16,256]{2,1,0:T(8,128)S(1)}, f32[9,16,256]{2,1,0:T(8,128)S(1)}, u32[]{:S(2)}, u32[]{:S(2)}) %collective-permute-start.13) | collective-permute-done | bytes 147488 | tf_op jit(solution)/shard_map/ppermute | solution.py:89
  58.3 3.3 %collective-permute-done.14 = f32[9,16,256]{2,1,0:T(8,128)S(1)} collective-permute-done((f32[9,16,256]{2,1,0:T(8,128)S(1)}, f32[9,16,256]{2,1,0:T(8,128)S(1)}, u32[]{:S(2)}, u32[]{:S(2)}) %collective-permute-start.14) | collective-permute-done | bytes 147488 | tf_op jit(solution)/shard_map/ppermute | solution.py:89
  61.6 0.8 %copy-done.1 = f32[9,64,256]{2,1,0:T(8,128)} copy-done((f32[9,64,256]{2,1,0:T(8,128)}, f32[9,64,256]{2,1,0:T(8,128)S(1)}, u32[]{:S(2)}) %copy-start.1) | copy-done | bytes 589848
  (37 shorter events, 0.6 us)
Async XLA Ops:
  0.6 7.8 %copy-start = (bf16[1,9,3,2,64]{4,3,2,1,0:T(2,128)(2,1)S(1)}, bf16[1,9,3,2,64]{4,3,2,1,0:T(2,128)(2,1)}, u32[]{:S(2)}) copy-start(bf16[1,9,3,2,64]{4,3,2,1,0:T(2,128)(2,1)} %param.25) | copy-start | bytes 20740
  2.4 17.5 %collective-permute-start = (bf16[320,128]{1,0:T(8,128)(2,1)S(1)}, bf16[320,128]{1,0:T(8,128)(2,1)S(1)}, u32[]{:S(2)}, u32[]{:S(2)}) collective-permute-start(bf16[320,128]{1,0:T(8,128)(2,1)S(1)} %get-tuple-element.113), channel_id=1, source_target_pairs={{0,3},{1,0},{2,1},{3,2},{4,7},{5,4},{6,5},{7,6},{8,11},{9,8},{10,9... | collective-permute-start | bytes 245768 | tf_op jit(solution)/shard_map/ppermute | solution.py:164
  6.6 13.3 %collective-permute-start.1 = (bf16[320,128]{1,0:T(8,128)(2,1)S(1)}, bf16[320,128]{1,0:T(8,128)(2,1)S(1)}, u32[]{:S(2)}, u32[]{:S(2)}) collective-permute-start(bf16[320,128]{1,0:T(8,128)(2,1)S(1)} %get-tuple-element.114), channel_id=1, source_target_pairs={{0,2},{1,3},{2,0},{3,1},{4,6},{5,7},{6,4},{7,5},{8,10},{9,11},{10,... | collective-permute-start | bytes 245768 | tf_op jit(solution)/shard_map/ppermute | solution.py:164
  6.6 13.4 %collective-permute-start.2 = (bf16[320,128]{1,0:T(8,128)(2,1)S(1)}, bf16[320,128]{1,0:T(8,128)(2,1)S(1)}, u32[]{:S(2)}, u32[]{:S(2)}) collective-permute-start(bf16[320,128]{1,0:T(8,128)(2,1)S(1)} %get-tuple-element.115), channel_id=1, source_target_pairs={{0,1},{1,2},{2,3},{3,0},{4,5},{5,6},{6,7},{7,4},{8,9},{9,10},{10,1... | collective-permute-start | bytes 245768 | tf_op jit(solution)/shard_map/ppermute | solution.py:164
  14.8 5.1 %copy-start.2 = (bf16[256,1,128]{2,0,1:T(8,128)(2,1)S(1)}, bf16[256,1,128]{2,0,1:T(8,128)(2,1)}, u32[]{:S(2)}) copy-start(bf16[256,1,128]{2,0,1:T(8,128)(2,1)} %param.22) | copy-start | bytes 196612
  16.6 29.2 %collective-permute-start.5 = (f32[256,3,128]{0,2,1:T(8,128)S(1)}, f32[256,3,128]{0,2,1:T(8,128)S(1)}, u32[]{:S(2)}, u32[]{:S(2)}) collective-permute-start(f32[256,3,128]{0,2,1:T(8,128)S(1)} %get-tuple-element.100), channel_id=1, source_target_pairs={{0,1},{1,2},{2,3},{3,0},{4,5},{5,6},{6,7},{7,4},{8,9},{9,10},{10,1... | collective-permute-start | bytes 1179656 | tf_op jit(solution)/shard_map/ppermute | solution.py:19
  18.8 26.9 %collective-permute-start.6 = (f32[256,3,128]{0,2,1:T(8,128)S(1)}, f32[256,3,128]{0,2,1:T(8,128)S(1)}, u32[]{:S(2)}, u32[]{:S(2)}) collective-permute-start(f32[256,3,128]{0,2,1:T(8,128)S(1)} %get-tuple-element.101), channel_id=1, source_target_pairs={{1,0},{2,1},{3,2},{0,3},{5,4},{6,5},{7,6},{4,7},{9,8},{10,9},{11,1... | collective-permute-start | bytes 1179656 | tf_op jit(solution)/shard_map/ppermute | solution.py:21
  20.0 8.4 %collective-permute-start.3 = (bf16[256,512]{1,0:T(8,128)(2,1)S(1)}, bf16[256,512]{1,0:T(8,128)(2,1)S(1)}, u32[]{:S(2)}, u32[]{:S(2)}) collective-permute-start(bf16[256,512]{1,0:T(8,128)(2,1)S(1)} %get-tuple-element.108), channel_id=1, source_target_pairs={{0,4},{4,8},{8,12},{1,5},{5,9},{9,13},{2,6},{6,10},{10,14},{3,7},{... | collective-permute-start | bytes 786440 | tf_op jit(solution)/shard_map/ppermute | solution.py:174
  25.1 8.0 %collective-permute-start.4 = (bf16[256,512]{1,0:T(8,128)(2,1)S(1)}, bf16[256,512]{1,0:T(8,128)(2,1)S(1)}, u32[]{:S(2)}, u32[]{:S(2)}) collective-permute-start(bf16[256,512]{1,0:T(8,128)(2,1)S(1)} %get-tuple-element.108), channel_id=1, source_target_pairs={{4,0},{8,4},{12,8},{5,1},{9,5},{13,9},{6,2},{10,6},{14,10},{7,3},{... | collective-permute-start | bytes 786440 | tf_op jit(solution)/shard_map/ppermute | solution.py:175
  43.8 6.4 %collective-permute-start.10 = (f32[9,16,256]{2,1,0:T(8,128)S(1)}, f32[9,16,256]{2,1,0:T(8,128)S(1)}, u32[]{:S(2)}, u32[]{:S(2)}) collective-permute-start(f32[9,16,256]{2,1,0:T(8,128)S(1)} %get-tuple-element.104), channel_id=1, source_target_pairs={{0,8},{4,12},{8,0},{12,4},{1,9},{5,13},{9,1},{13,5},{2,10},{6,14},... | collective-permute-start | bytes 442376 | tf_op jit(solution)/shard_map/ppermute | solution.py:82
  43.9 6.7 %collective-permute-start.11 = (f32[9,16,256]{2,1,0:T(8,128)S(1)}, f32[9,16,256]{2,1,0:T(8,128)S(1)}, u32[]{:S(2)}, u32[]{:S(2)}) collective-permute-start(f32[9,16,256]{2,1,0:T(8,128)S(1)} %get-tuple-element.103), channel_id=1, source_target_pairs={{0,12},{4,8},{8,4},{12,0},{1,13},{5,9},{9,5},{13,1},{2,14},{6,10},... | collective-permute-start | bytes 442376 | tf_op jit(solution)/shard_map/ppermute | solution.py:82
  44.0 6.6 %collective-permute-start.9 = (f32[9,16,256]{2,1,0:T(8,128)S(1)}, f32[9,16,256]{2,1,0:T(8,128)S(1)}, u32[]{:S(2)}, u32[]{:S(2)}) collective-permute-start(f32[9,16,256]{2,1,0:T(8,128)S(1)} %get-tuple-element.102), channel_id=1, source_target_pairs={{0,4},{4,0},{8,12},{12,8},{1,5},{5,1},{9,13},{13,9},{2,6},{6,2},{1... | collective-permute-start | bytes 442376 | tf_op jit(solution)/shard_map/ppermute | solution.py:82
  45.9 8.7 %collective-permute-start.7 = (f32[256,1,128]{0,2,1:T(8,128)S(1)}, f32[256,1,128]{0,2,1:T(8,128)S(1)}, u32[]{:S(2)}, u32[]{:S(2)}) collective-permute-start(f32[256,1,128]{0,2,1:T(8,128)S(1)} %get-tuple-element.105), channel_id=1, source_target_pairs={{0,4},{4,8},{8,12},{1,5},{5,9},{9,13},{2,6},{6,10},{10,14},{3,7},{... | collective-permute-start | bytes 393224 | tf_op jit(solution)/shard_map/ppermute | solution.py:19
  47.8 6.8 %collective-permute-start.8 = (f32[256,1,128]{0,2,1:T(8,128)S(1)}, f32[256,1,128]{0,2,1:T(8,128)S(1)}, u32[]{:S(2)}, u32[]{:S(2)}) collective-permute-start(f32[256,1,128]{0,2,1:T(8,128)S(1)} %get-tuple-element.106), channel_id=1, source_target_pairs={{4,0},{8,4},{12,8},{5,1},{9,5},{13,9},{6,2},{10,6},{14,10},{7,3},{... | collective-permute-start | bytes 393224 | tf_op jit(solution)/shard_map/ppermute | solution.py:21
  51.6 3.7 %collective-permute-start.12 = (f32[9,16,256]{2,1,0:T(8,128)S(1)}, f32[9,16,256]{2,1,0:T(8,128)S(1)}, u32[]{:S(2)}, u32[]{:S(2)}) collective-permute-start(f32[9,16,256]{2,1,0:T(8,128)S(1)} %get-tuple-element.99), channel_id=1, source_target_pairs={{0,4},{4,0},{8,12},{12,8},{1,5},{5,1},{9,13},{13,9},{2,6},{6,2},{1... | collective-permute-start | bytes 442376 | tf_op jit(solution)/shard_map/ppermute | solution.py:89
  52.8 5.4 %collective-permute-start.13 = (f32[9,16,256]{2,1,0:T(8,128)S(1)}, f32[9,16,256]{2,1,0:T(8,128)S(1)}, u32[]{:S(2)}, u32[]{:S(2)}) collective-permute-start(f32[9,16,256]{2,1,0:T(8,128)S(1)} %get-tuple-element.99), channel_id=1, source_target_pairs={{0,8},{4,12},{8,0},{12,4},{1,9},{5,13},{9,1},{13,5},{2,10},{6,14},... | collective-permute-start | bytes 442376 | tf_op jit(solution)/shard_map/ppermute | solution.py:89
  54.3 7.3 %collective-permute-start.14 = (f32[9,16,256]{2,1,0:T(8,128)S(1)}, f32[9,16,256]{2,1,0:T(8,128)S(1)}, u32[]{:S(2)}, u32[]{:S(2)}) collective-permute-start(f32[9,16,256]{2,1,0:T(8,128)S(1)} %get-tuple-element.99), channel_id=1, source_target_pairs={{0,12},{4,8},{8,4},{12,0},{1,13},{5,9},{9,5},{13,1},{2,14},{6,10},... | collective-permute-start | bytes 442376 | tf_op jit(solution)/shard_map/ppermute | solution.py:89
  61.6 0.8 %copy-start.1 = (f32[9,64,256]{2,1,0:T(8,128)}, f32[9,64,256]{2,1,0:T(8,128)S(1)}, u32[]{:S(2)}) copy-start(f32[9,64,256]{2,1,0:T(8,128)S(1)} %constant_dynamic-update-slice_fusion) | copy-start | bytes 1769476

commit v19 on v18

--- a/solution.py
+++ b/solution.py
@@ -51,7 +51,9 @@
         ).astype(jnp.bfloat16)
         term = jnp.dot(grad_k, out_ref[k], preferred_element_type=jnp.float32)
         acc = term if acc is None else acc + term
-    contrib_ref[...] = acc
+    window_len = width // contrib_ref.shape[0]
+    for r in range(contrib_ref.shape[0]):
+        contrib_ref[r] = acc[:, r * window_len : (r + 1) * window_len]
 
 
 def toeplitz(tap_row, out_width, weights, up_row):
@@ -63,7 +65,7 @@
         toeplitz_kernel,
         out_shape=(
             jax.ShapeDtypeStruct((kernels, out_width, stencil_rows * window_len), jnp.bfloat16),
-            jax.ShapeDtypeStruct((weights.shape[2], stencil_rows * window_len), jnp.float32),
+            jax.ShapeDtypeStruct((stencil_rows, weights.shape[2], window_len), jnp.float32),
         ),
     )(padded, weights, up_row)
     return out.reshape(kernels * out_width, stencil_rows * window_len), contrib
@@ -181,7 +183,7 @@
     accumulated = jnp.zeros((channels, lat_rows + 2, window_len), jnp.float32)
     cycle_row = 0
     accumulated = accumulated.at[:, cycle_row : cycle_row + 3].add(
-        contrib.reshape(channels, 3, window_len)
+        contrib.transpose(1, 0, 2)
     )
     rim_columns = jnp.concatenate(
         [accumulated[:, :, :HALO], accumulated[:, :, HALO + lon_cols :]], axis=2

time: 63 us -> 62.4 us (level)
  other arithmetic: 4.46 us -> 6.04 us
  local copies, waits for them, and re-layouts: 5.97 us -> 4.67 us
    pallas_call x1 -> x0, local copies, waits for them, and re-layouts: 1.67 us -> none  [toeplitz(): pl.pallas_call(toeplitz_kernel, out_shape=(jax.ShapeDtypeStruct((kernels,...]
    slice x1, local copies, waits for them, and re-layouts: 0.08 us -> 1.17 us  [body(): accumulated[:, :, HALO + lon_cols:]]
    add x1, other arithmetic: 0.08 us -> 1.05 us  [body(): interior = interior.at[:, :, lon_cols - HALO:].add(arrived[:, :, 3 * HALO:])]
    unnamed x10 -> x9, local copies, waits for them, and re-layouts: 2.22 us -> 1.48 us
  transfers between devices with their start and end apart: 15 -> 15, of which waited for: 5 -> 5; matrix products, arithmetic and copies ran while one was open for 13% -> 14% of each run, Pallas kernels for 22% -> 23%
where the time goes in v19:
time: 62.4 us; the launch traced here: 61.8 us
  starting transfers between devices  23.5 us (38%)
  Pallas kernels  14 us (22%)
  waiting for transfers between devices  11.7 us (19%)
  other arithmetic  6.04 us (10%)
  local copies, waits for them, and re-layouts  4.67 us (7%)
  between operations  1.61 us (3%)
    pallas_call x1, Pallas kernels, row_products(): pl.pallas_call(row_kernel, out_shape=(jax.ShapeDtypeStruct((weights.shape...  8.55 us
    ppermute x3, waiting for transfers between devices, lat_allreduce(): recv = lax.ppermute(mine, axis, [(i, i ^ d) for i in range(count)])  5.83 us
    pallas_call x1, Pallas kernels, toeplitz(): pl.pallas_call(toeplitz_kernel, out_shape=(jax.ShapeDtypeStruct((kernels,...  5.49 us
    ppermute x1, starting transfers between devices, body(): below = lax.ppermute(row, 'lat', [(i, i + 1) for i in range(count - 1)])  5.08 us
    ppermute x1, waiting for transfers between devices, body(): above = lax.ppermute(row, 'lat', [(i + 1, i) for i in range(count - 1)])  4.69 us
    ppermute x3, starting transfers between devices, body(): lax.ppermute(jnp.concatenate([fields[:, 0], part], axis=0), 'lon', [(p, (...  4.66 us
    ppermute x2, starting transfers between devices, padded_2(): lax.ppermute(tail, axis, [(i, (i + 1) % count) for i in range(ends)])  4.17 us
    ppermute x2, starting transfers between devices, padded_2(): lax.ppermute(head, axis, [((i + 1) % count, i) for i in range(ends)])  3.47 us
  transfers between devices with their start and end apart: 15, of which 5 were waited for; matrix products, arithmetic and copies ran while one was open for 14% of the time, Pallas kernels for 23%

profile of v19, /device:TPU:1, one launch (start us, length us, event | category | flops | bytes accessed | tf_op | source)
XLA Modules:
  0.0 61.8 jit_solution(5224062442540668881)
XLA Ops:
  0.7 0.8 %dynamic-slice_bitcast_fusion = (bf16[1,64,128]{2,1,0:T(8,128)(2,1)S(1)}, bf16[64,128]{1,0:T(8,128)(2,1)S(1)}, bf16[64,128]{1,0:T(8,128)(2,1)S(1)}, bf16[64,128]{1,0:T(8,128)(2,1)S(1)}) fusion(bf16[256,1,128]{2,0,1:T(8,128)(2,1)} %param.23, s32[]{:T(128)S(6)} %select_n.57, s32[]{:T(128)S(6)} %select_n.55, s32[]{:T(128)S(6)} %select_n.53, s32[]{:T(128)S(6)} %select_n.51), kind=kLoop, calls=%fused_computation.32 | loop fusion | bytes 131088 | tf_op jit(solution)/shard_map/stack | solution.py:173
  1.5 0.9 %pad_maximum_fusion.5 = (bf16[320,128]{1,0:T(8,128)(2,1)S(1)}, bf16[320,128]{1,0:T(8,128)(2,1)S(1)}, bf16[320,128]{1,0:T(8,128)(2,1)S(1)}) fusion(bf16[64,128]{1,0:T(8,128)(2,1)S(1)} %get-tuple-element.109, bf16[256,128]{1,0:T(8,128)(2,1)} %bitcast.49, bf16[64,128]{1,0:T(8,128)(2,1)S(1)} %get-tuple-element.108, bf16[64,128]{1,0:T(8,128)(2,1)S(1)} %get-tuple-element.107), kind=kLoop, calls=%fused_computation.20 | loop fusion | flops 409600 | bytes 360448 | tf_op jit(solution)/shard_map/concatenate | solution.py:167
  2.4 4.2 %collective-permute-start = (bf16[320,128]{1,0:T(8,128)(2,1)S(1)}, bf16[320,128]{1,0:T(8,128)(2,1)S(1)}, u32[]{:S(2)}, u32[]{:S(2)}) collective-permute-start(bf16[320,128]{1,0:T(8,128)(2,1)S(1)} %get-tuple-element.110), channel_id=1, source_target_pairs={{0,3},{1,0},{2,1},{3,2},{4,7},{5,4},{6,5},{7,6},{8,11},{9,8},{10,9... | collective-permute-start | bytes 245768 | tf_op jit(solution)/shard_map/ppermute | solution.py:166
  6.6 0.5 collective-permute-start.2
  7.0 0.7 %add_bitcast_fusion = s32[2]{0:T(128)S(1)} fusion(s32[1,2]{1,0:T(1,128)} %param.27), kind=kLoop, calls=%fused_computation.45 | loop fusion | flops 4 | bytes 16 | tf_op jit(solution)/shard_map/add | solution.py:32
  8.4 0.2 fusion.3
  8.7 0.6 %copy.13 = bf16[2,8,3,384]{3,1,2,0:T(8,128)(2,1)} copy(bf16[2,8,3,384]{3,2,1,0:T(4,128)(2,1)S(1)} %bitcast.51) | data formatting | bytes 73728
  9.3 5.5 %shard_map.100 = (bf16[9,128,1152]{2,1,0:T(8,128)(2,1)}, f32[3,256,384]{2,1,0:T(8,128)}) custom-call(bf16[9,1152]{1,0:T(8,128)(2,1)} %bitcast.52, bf16[9,256,256]{2,1,0:T(8,128)(2,1)} %w_ref.3, bf16[256,128]{1,0:T(8,128)(2,1)} %bitcast.48), custom_call_target="tpu_custom_call" | custom-call | tf_op jit(solution)/shard_map/pallas_call | solution.py:64
  14.8 1.2 %fusion.19 = (f32[256,3,128]{2,0,1:T(8,128)S(1)}, f32[256,3,128]{2,0,1:T(8,128)S(1)}) fusion(f32[256,3,384]{2,0,1:T(8,128)} %bitcast.44), kind=kLoop, calls=%fused_computation.49 | loop fusion | bytes 1572864 | tf_op jit(solution)/shard_map/slice | solution.py:189
  16.0 2.3 %collective-permute-start.5 = (f32[256,3,128]{2,0,1:T(8,128)S(1)}, f32[256,3,128]{2,0,1:T(8,128)S(1)}, u32[]{:S(2)}, u32[]{:S(2)}) collective-permute-start(f32[256,3,128]{2,0,1:T(8,128)S(1)} %get-tuple-element.97), channel_id=1, source_target_pairs={{0,1},{1,2},{2,3},{3,0},{4,5},{5,6},{6,7},{7,4},{8,9},{9,10},{10,1... | collective-permute-start | bytes 1179656 | tf_op jit(solution)/shard_map/ppermute | solution.py:19
  18.3 1.1 %collective-permute-start.6 = (f32[256,3,128]{2,0,1:T(8,128)S(1)}, f32[256,3,128]{2,0,1:T(8,128)S(1)}, u32[]{:S(2)}, u32[]{:S(2)}) collective-permute-start(f32[256,3,128]{2,0,1:T(8,128)S(1)} %get-tuple-element.98), channel_id=1, source_target_pairs={{1,0},{2,1},{3,2},{0,3},{5,4},{6,5},{7,6},{4,7},{9,8},{10,9},{11,1... | collective-permute-start | bytes 1179656 | tf_op jit(solution)/shard_map/ppermute | solution.py:21
  19.4 5.1 %collective-permute-start.3 = (bf16[256,512]{1,0:T(8,128)(2,1)S(1)}, bf16[256,512]{1,0:T(8,128)(2,1)S(1)}, u32[]{:S(2)}, u32[]{:S(2)}) collective-permute-start(bf16[256,512]{1,0:T(8,128)(2,1)S(1)} %get-tuple-element.105), channel_id=1, source_target_pairs={{0,4},{4,8},{8,12},{1,5},{5,9},{9,13},{2,6},{6,10},{10,14},{3,7},{... | collective-permute-start | bytes 786440 | tf_op jit(solution)/shard_map/ppermute | solution.py:176
  24.5 1.9 %collective-permute-start.4 = (bf16[256,512]{1,0:T(8,128)(2,1)S(1)}, bf16[256,512]{1,0:T(8,128)(2,1)S(1)}, u32[]{:S(2)}, u32[]{:S(2)}) collective-permute-start(bf16[256,512]{1,0:T(8,128)(2,1)S(1)} %get-tuple-element.105), channel_id=1, source_target_pairs={{4,0},{8,4},{12,8},{5,1},{9,5},{13,9},{6,2},{10,6},{14,10},{7,3},{... | collective-permute-start | bytes 786440 | tf_op jit(solution)/shard_map/ppermute | solution.py:177
  26.5 0.6 %pad_maximum_fusion.8.up_ref = bf16[4,64,128]{2,1,0:T(8,128)(2,1)} fusion(bf16[1,64,128]{2,1,0:T(8,128)(2,1)S(1)} %slice_bitcast_fusion, bf16[1,64,128]{2,1,0:T(8,128)(2,1)S(1)} %slice_bitcast_fusion.1, bf16[1,64,128]{2,1,0:T(8,128)(2,1)S(1)} %slice_bitcast_fusion.2, bf16[1,64,128]{2,1,0:T(8,128)(2,1)S(1)} %get-tuple-element.106), kind=kLoop, calls=%fused_computation.23 | loop fusion | flops 98304 | bytes 131072 | tf_op jit(solution)/shard_map/stack | solution.py:173
  27.1 0.7 %collective-permute-done.3 = bf16[256,512]{1,0:T(8,128)(2,1)S(1)} collective-permute-done((bf16[256,512]{1,0:T(8,128)(2,1)S(1)}, bf16[256,512]{1,0:T(8,128)(2,1)S(1)}, u32[]{:S(2)}, u32[]{:S(2)}) %collective-permute-start.3) | collective-permute-done | bytes 262176 | tf_op jit(solution)/shard_map/ppermute | solution.py:176
  27.8 4.7 %collective-permute-done.4 = bf16[256,512]{1,0:T(8,128)(2,1)S(1)} collective-permute-done((bf16[256,512]{1,0:T(8,128)(2,1)S(1)}, bf16[256,512]{1,0:T(8,128)(2,1)S(1)}, u32[]{:S(2)}, u32[]{:S(2)}) %collective-permute-start.4) | collective-permute-done | bytes 262176 | tf_op jit(solution)/shard_map/ppermute | solution.py:177
  32.5 1.1 %fusion.ext_ref = bf16[3,256,768]{2,1,0:T(8,128)(2,1)} fusion(bf16[1,256,512]{2,1,0:T(8,128)(2,1)S(1)} %bitcast.47, bf16[1,256,512]{2,1,0:T(8,128)(2,1)S(1)} %get-tuple-element.104, bf16[1,256,512]{2,1,0:T(8,128)(2,1)S(1)} %bitcast.46), kind=kLoop, calls=%fused_computation.1 | loop fusion | flops 10616832 | bytes 1966080 | tf_op jit(solution)/shard_map/concatenate | solution.py:179
  33.6 8.5 %shard_map.101 = (bf16[256,128]{1,0:T(8,128)(2,1)}, f32[9,64,256]{2,1,0:T(8,128)}) custom-call(bf16[3,256,768]{2,1,0:T(8,128)(2,1)} %fusion.ext_ref, bf16[1152,1152]{1,0:T(8,128)(2,1)} %bitcast.53, bf16[9,256,256]{2,1,0:T(8,128)(2,1)} %w_ref.3, bf16[4,64,128]{2,1,0:T(8,128)(2,1)} %pad_maximum_fusion.8.up_ref), custom_call_target="tpu_custom_call" | custom-call | flops 3019898880 | bytes 5734400 | tf_op jit(solution)/shard_map/pallas_call | solution.py:142
  42.1 1.1 %constant_dynamic-slice_fusion.2 = (f32[9,16,256]{2,1,0:T(8,128)S(1)}, f32[9,16,256]{2,1,0:T(8,128)S(1)}, f32[9,16,256]{2,1,0:T(8,128)S(1)}) fusion(f32[9,64,256]{2,1,0:T(8,128)} %get-tuple-element.94, s32[]{:T(128)S(6)} %select_n.59, s32[]{:T(128)S(6)} %select_n.61, s32[]{:T(128)S(6)} %select_n.60), kind=kLoop, calls=%fused_computation.42 | loop fusion | bytes 884748 | tf_op jit(solution)/shard_map/dynamic_slice | solution.py:83
  43.4 1.8 %collective-permute-start.9 = (f32[9,16,256]{2,1,0:T(8,128)S(1)}, f32[9,16,256]{2,1,0:T(8,128)S(1)}, u32[]{:S(2)}, u32[]{:S(2)}) collective-permute-start(f32[9,16,256]{2,1,0:T(8,128)S(1)} %get-tuple-element.99), channel_id=1, source_target_pairs={{0,4},{4,0},{8,12},{12,8},{1,5},{5,1},{9,13},{13,9},{2,6},{6,2},{1... | collective-permute-start | bytes 442376 | tf_op jit(solution)/shard_map/ppermute | solution.py:84
  45.2 1.1 %fusion.4 = f32[256,3,128]{2,0,1:T(8,128)S(1)} fusion(f32[256,3,128]{2,0,1:T(8,128)S(1)} %collective-permute-done.6, f32[256,3,128]{2,0,1:T(8,128)S(1)} %collective-permute-done.5, f32[256,3,384]{2,0,1:T(8,128)} %bitcast.45), kind=kLoop, calls=%fused_computation.10 | loop fusion | flops 196608 | bytes 1572864 | tf_op jit(solution)/shard_map/add | solution.py:194
  46.2 1.9 %collective-permute-start.7 = (f32[256,1,128]{2,0,1:T(8,128)S(1)}, f32[256,1,128]{2,0,1:T(8,128)S(1)}, u32[]{:S(2)}, u32[]{:S(2)}) collective-permute-start(f32[256,1,128]{2,0,1:T(8,128)S(1)} %get-tuple-element.102), channel_id=1, source_target_pairs={{0,4},{4,8},{8,12},{1,5},{5,9},{9,13},{2,6},{6,10},{10,14},{3,7},{... | collective-permute-start | bytes 393224 | tf_op jit(solution)/shard_map/ppermute | solution.py:19
  48.2 2.4 %collective-permute-start.8 = (f32[256,1,128]{2,0,1:T(8,128)S(1)}, f32[256,1,128]{2,0,1:T(8,128)S(1)}, u32[]{:S(2)}, u32[]{:S(2)}) collective-permute-start(f32[256,1,128]{2,0,1:T(8,128)S(1)} %get-tuple-element.103), channel_id=1, source_target_pairs={{4,0},{8,4},{12,8},{5,1},{9,5},{13,9},{6,2},{10,6},{14,10},{7,3},{... | collective-permute-start | bytes 393224 | tf_op jit(solution)/shard_map/ppermute | solution.py:21
  50.7 1.0 %constant_dynamic-update-slice_fusion.3 = (f32[9,64,256]{2,1,0:T(8,128)S(1)}, f32[9,16,256]{2,1,0:T(8,128)S(1)}) fusion(f32[9,64,256]{2,1,0:T(8,128)S(1)} %broadcast_in_dim.25, s32[]{:T(128)S(6)} %select_n.58, f32[9,16,256]{2,1,0:T(8,128)S(1)} %collective-permute-done.10, f32[9,16,256]{2,1,0:T(8,128)S(1)} %collective-permute-done.11, ...), kind=kLoop, calls=%fused_computation.39 | loop fusion | flops 110592 | bytes 884740 | tf_op jit(solution)/shard_map/dynamic_update_slice | solution.py:89
  51.6 0.6 collective-permute-start.12
  52.2 1.5 %collective-permute-start.13 = (f32[9,16,256]{2,1,0:T(8,128)S(1)}, f32[9,16,256]{2,1,0:T(8,128)S(1)}, u32[]{:S(2)}, u32[]{:S(2)}) collective-permute-start(f32[9,16,256]{2,1,0:T(8,128)S(1)} %get-tuple-element.96), channel_id=1, source_target_pairs={{0,8},{4,12},{8,0},{12,4},{1,9},{5,13},{9,1},{13,5},{2,10},{6,14},... | collective-permute-start | bytes 442376 | tf_op jit(solution)/shard_map/ppermute | solution.py:91
  53.7 0.3 collective-permute-start.14
  54.0 0.5 collective-permute-done.8
  54.5 0.7 %fusion.6 = bf16[256,1,128]{2,0,1:T(8,128)(2,1)} fusion(f32[256,1,128]{2,0,1:T(8,128)S(1)} %collective-permute-done.8, f32[256,1,128]{2,0,1:T(8,128)S(1)} %collective-permute-done.7, f32[256,3,128]{2,0,1:T(8,128)S(1)} %fusion.4), kind=kLoop, calls=%fused_computation.15 | loop fusion | flops 98304 | bytes 458752 | tf_op jit(solution)/shard_map/convert_element_type | solution.py:200
  55.1 2.5 %collective-permute-done.13 = f32[9,16,256]{2,1,0:T(8,128)S(1)} collective-permute-done((f32[9,16,256]{2,1,0:T(8,128)S(1)}, f32[9,16,256]{2,1,0:T(8,128)S(1)}, u32[]{:S(2)}, u32[]{:S(2)}) %collective-permute-start.13) | collective-permute-done | bytes 147488 | tf_op jit(solution)/shard_map/ppermute | solution.py:91
  57.7 3.3 %collective-permute-done.14 = f32[9,16,256]{2,1,0:T(8,128)S(1)} collective-permute-done((f32[9,16,256]{2,1,0:T(8,128)S(1)}, f32[9,16,256]{2,1,0:T(8,128)S(1)}, u32[]{:S(2)}, u32[]{:S(2)}) %collective-permute-start.14) | collective-permute-done | bytes 147488 | tf_op jit(solution)/shard_map/ppermute | solution.py:91
  61.0 0.8 %copy-done.1 = f32[9,64,256]{2,1,0:T(8,128)} copy-done((f32[9,64,256]{2,1,0:T(8,128)}, f32[9,64,256]{2,1,0:T(8,128)S(1)}, u32[]{:S(2)}) %copy-start.1) | copy-done | bytes 589848
  (35 shorter events, 0.5 us)
Async XLA Ops:
  0.6 7.8 %copy-start = (bf16[1,9,3,2,64]{4,3,2,1,0:T(2,128)(2,1)S(1)}, bf16[1,9,3,2,64]{4,3,2,1,0:T(2,128)(2,1)}, u32[]{:S(2)}) copy-start(bf16[1,9,3,2,64]{4,3,2,1,0:T(2,128)(2,1)} %param.25) | copy-start | bytes 20740
  0.6 18.7 %copy-start.2 = (bf16[256,1,128]{2,0,1:T(8,128)(2,1)S(1)}, bf16[256,1,128]{2,0,1:T(8,128)(2,1)}, u32[]{:S(2)}) copy-start(bf16[256,1,128]{2,0,1:T(8,128)(2,1)} %param.22) | copy-start | bytes 196612
  2.4 16.9 %collective-permute-start = (bf16[320,128]{1,0:T(8,128)(2,1)S(1)}, bf16[320,128]{1,0:T(8,128)(2,1)S(1)}, u32[]{:S(2)}, u32[]{:S(2)}) collective-permute-start(bf16[320,128]{1,0:T(8,128)(2,1)S(1)} %get-tuple-element.110), channel_id=1, source_target_pairs={{0,3},{1,0},{2,1},{3,2},{4,7},{5,4},{6,5},{7,6},{8,11},{9,8},{10,9... | collective-permute-start | bytes 245768 | tf_op jit(solution)/shard_map/ppermute | solution.py:166
  6.6 12.8 %collective-permute-start.1 = (bf16[320,128]{1,0:T(8,128)(2,1)S(1)}, bf16[320,128]{1,0:T(8,128)(2,1)S(1)}, u32[]{:S(2)}, u32[]{:S(2)}) collective-permute-start(bf16[320,128]{1,0:T(8,128)(2,1)S(1)} %get-tuple-element.111), channel_id=1, source_target_pairs={{0,2},{1,3},{2,0},{3,1},{4,6},{5,7},{6,4},{7,5},{8,10},{9,11},{10,... | collective-permute-start | bytes 245768 | tf_op jit(solution)/shard_map/ppermute | solution.py:166
  6.6 12.8 %collective-permute-start.2 = (bf16[320,128]{1,0:T(8,128)(2,1)S(1)}, bf16[320,128]{1,0:T(8,128)(2,1)S(1)}, u32[]{:S(2)}, u32[]{:S(2)}) collective-permute-start(bf16[320,128]{1,0:T(8,128)(2,1)S(1)} %get-tuple-element.112), channel_id=1, source_target_pairs={{0,1},{1,2},{2,3},{3,0},{4,5},{5,6},{6,7},{7,4},{8,9},{9,10},{10,1... | collective-permute-start | bytes 245768 | tf_op jit(solution)/shard_map/ppermute | solution.py:166
  16.0 29.2 %collective-permute-start.5 = (f32[256,3,128]{2,0,1:T(8,128)S(1)}, f32[256,3,128]{2,0,1:T(8,128)S(1)}, u32[]{:S(2)}, u32[]{:S(2)}) collective-permute-start(f32[256,3,128]{2,0,1:T(8,128)S(1)} %get-tuple-element.97), channel_id=1, source_target_pairs={{0,1},{1,2},{2,3},{3,0},{4,5},{5,6},{6,7},{7,4},{8,9},{9,10},{10,1... | collective-permute-start | bytes 1179656 | tf_op jit(solution)/shard_map/ppermute | solution.py:19
  18.3 26.9 %collective-permute-start.6 = (f32[256,3,128]{2,0,1:T(8,128)S(1)}, f32[256,3,128]{2,0,1:T(8,128)S(1)}, u32[]{:S(2)}, u32[]{:S(2)}) collective-permute-start(f32[256,3,128]{2,0,1:T(8,128)S(1)} %get-tuple-element.98), channel_id=1, source_target_pairs={{1,0},{2,1},{3,2},{0,3},{5,4},{6,5},{7,6},{4,7},{9,8},{10,9},{11,1... | collective-permute-start | bytes 1179656 | tf_op jit(solution)/shard_map/ppermute | solution.py:21
  19.4 8.4 %collective-permute-start.3 = (bf16[256,512]{1,0:T(8,128)(2,1)S(1)}, bf16[256,512]{1,0:T(8,128)(2,1)S(1)}, u32[]{:S(2)}, u32[]{:S(2)}) collective-permute-start(bf16[256,512]{1,0:T(8,128)(2,1)S(1)} %get-tuple-element.105), channel_id=1, source_target_pairs={{0,4},{4,8},{8,12},{1,5},{5,9},{9,13},{2,6},{6,10},{10,14},{3,7},{... | collective-permute-start | bytes 786440 | tf_op jit(solution)/shard_map/ppermute | solution.py:176
  24.5 8.0 %collective-permute-start.4 = (bf16[256,512]{1,0:T(8,128)(2,1)S(1)}, bf16[256,512]{1,0:T(8,128)(2,1)S(1)}, u32[]{:S(2)}, u32[]{:S(2)}) collective-permute-start(bf16[256,512]{1,0:T(8,128)(2,1)S(1)} %get-tuple-element.105), channel_id=1, source_target_pairs={{4,0},{8,4},{12,8},{5,1},{9,5},{13,9},{6,2},{10,6},{14,10},{7,3},{... | collective-permute-start | bytes 786440 | tf_op jit(solution)/shard_map/ppermute | solution.py:177
  43.2 7.4 %collective-permute-start.10 = (f32[9,16,256]{2,1,0:T(8,128)S(1)}, f32[9,16,256]{2,1,0:T(8,128)S(1)}, u32[]{:S(2)}, u32[]{:S(2)}) collective-permute-start(f32[9,16,256]{2,1,0:T(8,128)S(1)} %get-tuple-element.101), channel_id=1, source_target_pairs={{0,8},{4,12},{8,0},{12,4},{1,9},{5,13},{9,1},{13,5},{2,10},{6,14},... | collective-permute-start | bytes 442376 | tf_op jit(solution)/shard_map/ppermute | solution.py:84
  43.3 7.3 %collective-permute-start.11 = (f32[9,16,256]{2,1,0:T(8,128)S(1)}, f32[9,16,256]{2,1,0:T(8,128)S(1)}, u32[]{:S(2)}, u32[]{:S(2)}) collective-permute-start(f32[9,16,256]{2,1,0:T(8,128)S(1)} %get-tuple-element.100), channel_id=1, source_target_pairs={{0,12},{4,8},{8,4},{12,0},{1,13},{5,9},{9,5},{13,1},{2,14},{6,10},... | collective-permute-start | bytes 442376 | tf_op jit(solution)/shard_map/ppermute | solution.py:84
  43.4 7.2 %collective-permute-start.9 = (f32[9,16,256]{2,1,0:T(8,128)S(1)}, f32[9,16,256]{2,1,0:T(8,128)S(1)}, u32[]{:S(2)}, u32[]{:S(2)}) collective-permute-start(f32[9,16,256]{2,1,0:T(8,128)S(1)} %get-tuple-element.99), channel_id=1, source_target_pairs={{0,4},{4,0},{8,12},{12,8},{1,5},{5,1},{9,13},{13,9},{2,6},{6,2},{1... | collective-permute-start | bytes 442376 | tf_op jit(solution)/shard_map/ppermute | solution.py:84
  46.2 7.7 %collective-permute-start.7 = (f32[256,1,128]{2,0,1:T(8,128)S(1)}, f32[256,1,128]{2,0,1:T(8,128)S(1)}, u32[]{:S(2)}, u32[]{:S(2)}) collective-permute-start(f32[256,1,128]{2,0,1:T(8,128)S(1)} %get-tuple-element.102), channel_id=1, source_target_pairs={{0,4},{4,8},{8,12},{1,5},{5,9},{9,13},{2,6},{6,10},{10,14},{3,7},{... | collective-permute-start | bytes 393224 | tf_op jit(solution)/shard_map/ppermute | solution.py:19
  48.2 6.3 %collective-permute-start.8 = (f32[256,1,128]{2,0,1:T(8,128)S(1)}, f32[256,1,128]{2,0,1:T(8,128)S(1)}, u32[]{:S(2)}, u32[]{:S(2)}) collective-permute-start(f32[256,1,128]{2,0,1:T(8,128)S(1)} %get-tuple-element.103), channel_id=1, source_target_pairs={{4,0},{8,4},{12,8},{5,1},{9,5},{13,9},{6,2},{10,6},{14,10},{7,3},{... | collective-permute-start | bytes 393224 | tf_op jit(solution)/shard_map/ppermute | solution.py:21
  51.6 3.5 %collective-permute-start.12 = (f32[9,16,256]{2,1,0:T(8,128)S(1)}, f32[9,16,256]{2,1,0:T(8,128)S(1)}, u32[]{:S(2)}, u32[]{:S(2)}) collective-permute-start(f32[9,16,256]{2,1,0:T(8,128)S(1)} %get-tuple-element.96), channel_id=1, source_target_pairs={{0,4},{4,0},{8,12},{12,8},{1,5},{5,1},{9,13},{13,9},{2,6},{6,2},{1... | collective-permute-start | bytes 442376 | tf_op jit(solution)/shard_map/ppermute | solution.py:91
  52.2 5.4 %collective-permute-start.13 = (f32[9,16,256]{2,1,0:T(8,128)S(1)}, f32[9,16,256]{2,1,0:T(8,128)S(1)}, u32[]{:S(2)}, u32[]{:S(2)}) collective-permute-start(f32[9,16,256]{2,1,0:T(8,128)S(1)} %get-tuple-element.96), channel_id=1, source_target_pairs={{0,8},{4,12},{8,0},{12,4},{1,9},{5,13},{9,1},{13,5},{2,10},{6,14},... | collective-permute-start | bytes 442376 | tf_op jit(solution)/shard_map/ppermute | solution.py:91
  53.7 7.3 %collective-permute-start.14 = (f32[9,16,256]{2,1,0:T(8,128)S(1)}, f32[9,16,256]{2,1,0:T(8,128)S(1)}, u32[]{:S(2)}, u32[]{:S(2)}) collective-permute-start(f32[9,16,256]{2,1,0:T(8,128)S(1)} %get-tuple-element.96), channel_id=1, source_target_pairs={{0,12},{4,8},{8,4},{12,0},{1,13},{5,9},{9,5},{13,1},{2,14},{6,10},... | collective-permute-start | bytes 442376 | tf_op jit(solution)/shard_map/ppermute | solution.py:91
  61.0 0.8 %copy-start.1 = (f32[9,64,256]{2,1,0:T(8,128)}, f32[9,64,256]{2,1,0:T(8,128)S(1)}, u32[]{:S(2)}) copy-start(f32[9,64,256]{2,1,0:T(8,128)S(1)} %constant_dynamic-update-slice_fusion) | copy-start | bytes 1769476

commit v20 on v19

--- a/solution.py
+++ b/solution.py
@@ -93,17 +93,23 @@
     return out
 
 
-def row_kernel(ext_ref, mt_ref, w_ref, up_ref, out_ref, gt_ref):
-    stencil_rows, channels, _ = ext_ref.shape
+def row_kernel(below_ref, row_ref, above_ref, mt_ref, w_ref, up_ref, out_ref, gt_ref):
+    channels, width = row_ref.shape
+    stencil_rows = 3
     n_blocks, o_block, lon_cols = up_ref.shape
     kernels = w_ref.shape[0]
     window_len = mt_ref.shape[1] // stencil_rows
     contract_last = (((1,), (1,)), ((), ()))
     gt_ref[...] = jnp.zeros(gt_ref.shape, gt_ref.dtype)
+    halo = (window_len - lon_cols) // 2
+    exts = []
+    for src_ref in (below_ref, row_ref, above_ref):
+        full = src_ref[...]
+        exts.append(jnp.concatenate([full[:, width - halo :], full, full[:, :halo]], axis=1))
     for d in range(n_blocks):
         acc = None
         for r in range(stencil_rows):
-            win = ext_ref[r, :, pl.ds(d * lon_cols, window_len)]
+            win = exts[r][:, d * lon_cols : d * lon_cols + window_len]
             part = lax.dot_general(
                 win,
                 mt_ref[:, pl.ds(r * window_len, window_len)],
@@ -130,14 +136,14 @@
             out_ref[...] = total.astype(out_ref.dtype)
 
 
-def row_products(ext, matrix, weights, up_rel):
-    stencil_rows, channels, _ = ext.shape
+def row_products(below, row, above, matrix, weights, up_rel):
+    channels = row.shape[0]
     n_blocks, o_block, lon_cols = up_rel.shape
     kernels = weights.shape[0]
     flops = 2 * n_blocks * channels * matrix.shape[0] * matrix.shape[1]
     flops += 2 * n_blocks * kernels * o_block * lon_cols * channels
     flops += 2 * kernels * weights.shape[1] * channels * lon_cols
-    nbytes = 2 * (ext.size + matrix.size + weights.size + up_rel.size)
+    nbytes = 2 * (3 * row.size + matrix.size + weights.size + up_rel.size)
     nbytes += 2 * weights.shape[1] * lon_cols + 4 * kernels * o_block * channels
     return pl.pallas_call(
         row_kernel,
@@ -146,7 +152,7 @@
             jax.ShapeDtypeStruct((kernels, o_block, channels), jnp.float32),
         ),
         cost_estimate=pl.CostEstimate(flops=flops, transcendentals=0, bytes_accessed=nbytes),
-    )(ext, matrix, weights, up_rel)
+    )(below, row, above, matrix, weights, up_rel)
 
 
 def body(fields, upstream, weights, filter_taps, cycle_counts, cycle_blocks):
@@ -175,9 +181,7 @@
     count = lax.axis_size("lat")
     below = lax.ppermute(row, "lat", [(i, i + 1) for i in range(count - 1)])
     above = lax.ppermute(row, "lat", [(i + 1, i) for i in range(count - 1)])
-    rows = jnp.stack([below, row, above], axis=0)
-    ext = jnp.concatenate([rows[:, :, rows.shape[2] - HALO :], rows, rows[:, :, :HALO]], axis=2)
-    out_row, grad_terms = row_products(ext, matrix, weights, up_rel)
+    out_row, grad_terms = row_products(below, row, above, matrix, weights, up_rel)
     outputs = out_row[:, None, :]
     weight_grad = lat_allreduce(grad_terms, "lat", 1)
     accumulated = jnp.zeros((channels, lat_rows + 2, window_len), jnp.float32)

time: 62.4 us -> 62.9 us (level)
  other arithmetic: 6.04 us -> 4.96 us
  starting transfers between devices: 23.5 us -> 24.4 us
  local copies, waits for them, and re-layouts: 4.67 us -> 5.43 us
    ppermute x2, starting transfers between devices: 4.17 us -> 2.37 us  [padded_2(): lax.ppermute(tail, axis, [(i, (i + 1) % count) for i in range(ends)])]
    ppermute x2, starting transfers between devices: 3.47 us -> 5.28 us  [padded_2(): lax.ppermute(head, axis, [((i + 1) % count, i) for i in range(ends)])]
    concatenate x1, other arithmetic: 1.08 us -> 0.04 us  [body(): row = jnp.concatenate(blocks, axis=1)]
    ppermute x3, starting transfers between devices: 4.66 us -> 5.56 us  [body(): lax.ppermute(jnp.concatenate([fields[:, 0], part], axis=0), 'lon', [(p, (...]
    unnamed x9 -> x15, local copies, waits for them, and re-layouts: 1.48 us -> 2.21 us
  transfers between devices with their start and end apart: 15 -> 15, of which waited for: 5 -> 5; matrix products, arithmetic and copies ran while one was open for 14% -> 12% of each run, Pallas kernels for 23% -> 22%
where the time goes in v20:
time: 62.9 us; the launch traced here: 62.3 us
  starting transfers between devices  24.4 us (39%)
  Pallas kernels  13.9 us (22%)
  waiting for transfers between devices  11.7 us (19%)
  local copies, waits for them, and re-layouts  5.43 us (9%)
  other arithmetic  4.96 us (8%)
  between operations  1.61 us (3%)
    pallas_call x1, Pallas kernels, row_products(): pl.pallas_call(row_kernel, out_shape=(jax.ShapeDtypeStruct((weights.shape...  8.44 us
    ppermute x3, waiting for transfers between devices, lat_allreduce(): recv = lax.ppermute(mine, axis, [(i, i ^ d) for i in range(count)])  5.83 us
    ppermute x3, starting transfers between devices, body(): lax.ppermute(jnp.concatenate([fields[:, 0], part], axis=0), 'lon', [(p, (...  5.56 us
    pallas_call x1, Pallas kernels, toeplitz(): pl.pallas_call(toeplitz_kernel, out_shape=(jax.ShapeDtypeStruct((kernels,...  5.49 us
    ppermute x2, starting transfers between devices, padded_2(): lax.ppermute(head, axis, [((i + 1) % count, i) for i in range(ends)])  5.28 us
    ppermute x1, starting transfers between devices, body(): below = lax.ppermute(row, 'lat', [(i, i + 1) for i in range(count - 1)])  5.09 us
    ppermute x1, waiting for transfers between devices, body(): above = lax.ppermute(row, 'lat', [(i + 1, i) for i in range(count - 1)])  4.69 us
    ppermute x2, starting transfers between devices, padded_2(): lax.ppermute(tail, axis, [(i, (i + 1) % count) for i in range(ends)])  2.37 us
  transfers between devices with their start and end apart: 15, of which 5 were waited for; matrix products, arithmetic and copies ran while one was open for 12% of the time, Pallas kernels for 22%

profile of v20, /device:TPU:1, one launch (start us, length us, event | category | flops | bytes accessed | tf_op | source)
XLA Modules:
  0.0 62.3 jit_solution(7064140395320566350)
XLA Ops:
  0.7 0.8 %dynamic-slice_bitcast_fusion = (bf16[1,64,128]{2,1,0:T(8,128)(2,1)S(1)}, bf16[64,128]{1,0:T(8,128)(2,1)S(1)}, bf16[64,128]{1,0:T(8,128)(2,1)S(1)}, bf16[64,128]{1,0:T(8,128)(2,1)S(1)}) fusion(bf16[256,1,128]{2,0,1:T(8,128)(2,1)} %param.23, s32[]{:T(128)S(6)} %select_n.57, s32[]{:T(128)S(6)} %select_n.55, s32[]{:T(128)S(6)} %select_n.53, s32[]{:T(128)S(6)} %select_n.51), kind=kLoop, calls=%fused_computation.26 | loop fusion | bytes 131088 | tf_op jit(solution)/shard_map/stack | solution.py:179
  1.5 0.9 %pad_maximum_fusion.1 = (bf16[320,128]{1,0:T(8,128)(2,1)S(1)}, bf16[320,128]{1,0:T(8,128)(2,1)S(1)}, bf16[320,128]{1,0:T(8,128)(2,1)S(1)}) fusion(bf16[64,128]{1,0:T(8,128)(2,1)S(1)} %get-tuple-element.107, bf16[256,128]{1,0:T(8,128)(2,1)} %bitcast.43, bf16[64,128]{1,0:T(8,128)(2,1)S(1)} %get-tuple-element.106, bf16[64,128]{1,0:T(8,128)(2,1)S(1)} %get-tuple-element.105), kind=kLoop, calls=%fused_computation.14 | loop fusion | flops 409600 | bytes 360448 | tf_op jit(solution)/shard_map/concatenate | solution.py:173
  2.4 2.2 %collective-permute-start.2 = (bf16[320,128]{1,0:T(8,128)(2,1)S(1)}, bf16[320,128]{1,0:T(8,128)(2,1)S(1)}, u32[]{:S(2)}, u32[]{:S(2)}) collective-permute-start(bf16[320,128]{1,0:T(8,128)(2,1)S(1)} %get-tuple-element.110), channel_id=1, source_target_pairs={{0,1},{1,2},{2,3},{3,0},{4,5},{5,6},{6,7},{7,4},{8,9},{9,10},{10,1... | collective-permute-start | bytes 245768 | tf_op jit(solution)/shard_map/ppermute | solution.py:172
  4.5 2.3 %collective-permute-start.1 = (bf16[320,128]{1,0:T(8,128)(2,1)S(1)}, bf16[320,128]{1,0:T(8,128)(2,1)S(1)}, u32[]{:S(2)}, u32[]{:S(2)}) collective-permute-start(bf16[320,128]{1,0:T(8,128)(2,1)S(1)} %get-tuple-element.109), channel_id=1, source_target_pairs={{0,2},{1,3},{2,0},{3,1},{4,6},{5,7},{6,4},{7,5},{8,10},{9,11},{10,... | collective-permute-start | bytes 245768 | tf_op jit(solution)/shard_map/ppermute | solution.py:172
  6.9 1.1 %collective-permute-start = (bf16[320,128]{1,0:T(8,128)(2,1)S(1)}, bf16[320,128]{1,0:T(8,128)(2,1)S(1)}, u32[]{:S(2)}, u32[]{:S(2)}) collective-permute-start(bf16[320,128]{1,0:T(8,128)(2,1)S(1)} %get-tuple-element.108), channel_id=1, source_target_pairs={{0,3},{1,0},{2,1},{3,2},{4,7},{5,4},{6,5},{7,6},{8,11},{9,8},{10,9... | collective-permute-start | bytes 245768 | tf_op jit(solution)/shard_map/ppermute | solution.py:172
  7.9 0.7 %add_bitcast_fusion = s32[2]{0:T(128)S(1)} fusion(s32[1,2]{1,0:T(1,128)} %param.27), kind=kLoop, calls=%fused_computation.39 | loop fusion | flops 4 | bytes 16 | tf_op jit(solution)/shard_map/add | solution.py:32
  9.6 0.6 %copy.13 = bf16[2,8,3,384]{3,1,2,0:T(8,128)(2,1)} copy(bf16[2,8,3,384]{3,2,1,0:T(4,128)(2,1)S(1)} %bitcast.45) | data formatting | bytes 73728
  10.2 5.5 %shard_map.100 = (bf16[9,128,1152]{2,1,0:T(8,128)(2,1)}, f32[3,256,384]{2,1,0:T(8,128)}) custom-call(bf16[9,1152]{1,0:T(8,128)(2,1)} %bitcast.46, bf16[9,256,256]{2,1,0:T(8,128)(2,1)} %w_ref.3, bf16[256,128]{1,0:T(8,128)(2,1)} %bitcast.42), custom_call_target="tpu_custom_call" | custom-call | tf_op jit(solution)/shard_map/pallas_call | solution.py:64
  15.7 1.2 %fusion.16 = (f32[256,3,128]{2,0,1:T(8,128)S(1)}, f32[256,3,128]{2,0,1:T(8,128)S(1)}) fusion(f32[256,3,384]{2,0,1:T(8,128)} %bitcast.40), kind=kLoop, calls=%fused_computation.42 | loop fusion | bytes 1572864 | tf_op jit(solution)/shard_map/slice | solution.py:193
  16.9 0.4 collective-permute-start.5
  17.4 2.9 %collective-permute-start.6 = (f32[256,3,128]{2,0,1:T(8,128)S(1)}, f32[256,3,128]{2,0,1:T(8,128)S(1)}, u32[]{:S(2)}, u32[]{:S(2)}) collective-permute-start(f32[256,3,128]{2,0,1:T(8,128)S(1)} %get-tuple-element.98), channel_id=1, source_target_pairs={{1,0},{2,1},{3,2},{0,3},{5,4},{6,5},{7,6},{4,7},{9,8},{10,9},{11,1... | collective-permute-start | bytes 1179656 | tf_op jit(solution)/shard_map/ppermute | solution.py:21
  20.4 5.1 %collective-permute-start.3 = (bf16[256,512]{1,0:T(8,128)(2,1)S(1)}, bf16[256,512]{1,0:T(8,128)(2,1)S(1)}, u32[]{:S(2)}, u32[]{:S(2)}) collective-permute-start(bf16[256,512]{1,0:T(8,128)(2,1)S(1)} %pad_maximum_fusion.row_ref), channel_id=1, source_target_pairs={{0,4},{4,8},{8,12},{1,5},{5,9},{9,13},{2,6},{6,10},{10,14},{3,7},{... | collective-permute-start | bytes 786440 | tf_op jit(solution)/shard_map/ppermute | solution.py:182
  25.5 1.9 %collective-permute-start.4 = (bf16[256,512]{1,0:T(8,128)(2,1)S(1)}, bf16[256,512]{1,0:T(8,128)(2,1)S(1)}, u32[]{:S(2)}, u32[]{:S(2)}) collective-permute-start(bf16[256,512]{1,0:T(8,128)(2,1)S(1)} %pad_maximum_fusion.row_ref), channel_id=1, source_target_pairs={{4,0},{8,4},{12,8},{5,1},{9,5},{13,9},{6,2},{10,6},{14,10},{7,3},{... | collective-permute-start | bytes 786440 | tf_op jit(solution)/shard_map/ppermute | solution.py:183
  27.4 0.6 %pad_maximum_fusion.4.up_ref = bf16[4,64,128]{2,1,0:T(8,128)(2,1)} fusion(bf16[1,64,128]{2,1,0:T(8,128)(2,1)S(1)} %slice_bitcast_fusion, bf16[1,64,128]{2,1,0:T(8,128)(2,1)S(1)} %slice_bitcast_fusion.1, bf16[1,64,128]{2,1,0:T(8,128)(2,1)S(1)} %slice_bitcast_fusion.2, bf16[1,64,128]{2,1,0:T(8,128)(2,1)S(1)} %get-tuple-element.104), kind=kLoop, calls=%fused_computation.17 | loop fusion | flops 98304 | bytes 131072 | tf_op jit(solution)/shard_map/stack | solution.py:179
  28.1 0.7 %collective-permute-done.3.below_ref = bf16[256,512]{1,0:T(8,128)(2,1)S(1)} collective-permute-done((bf16[256,512]{1,0:T(8,128)(2,1)S(1)}, bf16[256,512]{1,0:T(8,128)(2,1)S(1)}, u32[]{:S(2)}, u32[]{:S(2)}) %collective-permute-start.3) | collective-permute-done | bytes 262176 | tf_op jit(solution)/shard_map/ppermute | solution.py:182
  28.8 4.7 %collective-permute-done.4.above_ref = bf16[256,512]{1,0:T(8,128)(2,1)S(1)} collective-permute-done((bf16[256,512]{1,0:T(8,128)(2,1)S(1)}, bf16[256,512]{1,0:T(8,128)(2,1)S(1)}, u32[]{:S(2)}, u32[]{:S(2)}) %collective-permute-start.4) | collective-permute-done | bytes 262176 | tf_op jit(solution)/shard_map/ppermute | solution.py:183
  33.5 0.7 %copy-done.5 = bf16[256,512]{1,0:T(8,128)(2,1)} copy-done((bf16[256,512]{1,0:T(8,128)(2,1)}, bf16[256,512]{1,0:T(8,128)(2,1)S(1)}, u32[]{:S(2)}) %copy-start.5) | copy-done | bytes 262168
  34.2 8.4 %shard_map.101 = (bf16[256,128]{1,0:T(8,128)(2,1)}, f32[9,64,256]{2,1,0:T(8,128)}) custom-call(bf16[256,512]{1,0:T(8,128)(2,1)} %copy-done.4, bf16[256,512]{1,0:T(8,128)(2,1)} %copy-done.2, bf16[256,512]{1,0:T(8,128)(2,1)} %copy-done.5, bf16[1152,1152]{1,0:T(8,128)(2,1)} %bitcast.47, bf16[9,256,256]{2,1,0:T(8,128)(2,1)} %w_ref.3, ...), custom_call_target="tpu_custom_call" | custom-call | flops 3019898880 | bytes 5341184 | tf_op jit(solution)/shard_map/pallas_call | solution.py:148
  42.6 1.1 %constant_dynamic-slice_fusion.2 = (f32[9,16,256]{2,1,0:T(8,128)S(1)}, f32[9,16,256]{2,1,0:T(8,128)S(1)}, f32[9,16,256]{2,1,0:T(8,128)S(1)}) fusion(f32[9,64,256]{2,1,0:T(8,128)} %get-tuple-element.94, s32[]{:T(128)S(6)} %select_n.59, s32[]{:T(128)S(6)} %select_n.61, s32[]{:T(128)S(6)} %select_n.60), kind=kLoop, calls=%fused_computation.36 | loop fusion | bytes 884748 | tf_op jit(solution)/shard_map/dynamic_slice | solution.py:83
  43.9 1.8 %collective-permute-start.9 = (f32[9,16,256]{2,1,0:T(8,128)S(1)}, f32[9,16,256]{2,1,0:T(8,128)S(1)}, u32[]{:S(2)}, u32[]{:S(2)}) collective-permute-start(f32[9,16,256]{2,1,0:T(8,128)S(1)} %get-tuple-element.99), channel_id=1, source_target_pairs={{0,4},{4,0},{8,12},{12,8},{1,5},{5,1},{9,13},{13,9},{2,6},{6,2},{1... | collective-permute-start | bytes 442376 | tf_op jit(solution)/shard_map/ppermute | solution.py:84
  45.6 1.1 %fusion.2 = f32[256,3,128]{2,0,1:T(8,128)S(1)} fusion(f32[256,3,128]{2,0,1:T(8,128)S(1)} %collective-permute-done.6, f32[256,3,128]{2,0,1:T(8,128)S(1)} %collective-permute-done.5, f32[256,3,384]{2,0,1:T(8,128)} %bitcast.41), kind=kLoop, calls=%fused_computation.4 | loop fusion | flops 196608 | bytes 1572864 | tf_op jit(solution)/shard_map/add | solution.py:198
  46.7 1.9 %collective-permute-start.7 = (f32[256,1,128]{2,0,1:T(8,128)S(1)}, f32[256,1,128]{2,0,1:T(8,128)S(1)}, u32[]{:S(2)}, u32[]{:S(2)}) collective-permute-start(f32[256,1,128]{2,0,1:T(8,128)S(1)} %get-tuple-element.102), channel_id=1, source_target_pairs={{0,4},{4,8},{8,12},{1,5},{5,9},{9,13},{2,6},{6,10},{10,14},{3,7},{... | collective-permute-start | bytes 393224 | tf_op jit(solution)/shard_map/ppermute | solution.py:19
  48.7 2.4 %collective-permute-start.8 = (f32[256,1,128]{2,0,1:T(8,128)S(1)}, f32[256,1,128]{2,0,1:T(8,128)S(1)}, u32[]{:S(2)}, u32[]{:S(2)}) collective-permute-start(f32[256,1,128]{2,0,1:T(8,128)S(1)} %get-tuple-element.103), channel_id=1, source_target_pairs={{4,0},{8,4},{12,8},{5,1},{9,5},{13,9},{6,2},{10,6},{14,10},{7,3},{... | collective-permute-start | bytes 393224 | tf_op jit(solution)/shard_map/ppermute | solution.py:21
  51.2 1.0 %constant_dynamic-update-slice_fusion.3 = (f32[9,64,256]{2,1,0:T(8,128)S(1)}, f32[9,16,256]{2,1,0:T(8,128)S(1)}) fusion(f32[9,64,256]{2,1,0:T(8,128)S(1)} %broadcast_in_dim.25, s32[]{:T(128)S(6)} %select_n.58, f32[9,16,256]{2,1,0:T(8,128)S(1)} %collective-permute-done.10, f32[9,16,256]{2,1,0:T(8,128)S(1)} %collective-permute-done.11, ...), kind=kLoop, calls=%fused_computation.33 | loop fusion | flops 110592 | bytes 884740 | tf_op jit(solution)/shard_map/dynamic_update_slice | solution.py:89
  52.1 0.6 collective-permute-start.12
  52.7 1.5 %collective-permute-start.13 = (f32[9,16,256]{2,1,0:T(8,128)S(1)}, f32[9,16,256]{2,1,0:T(8,128)S(1)}, u32[]{:S(2)}, u32[]{:S(2)}) collective-permute-start(f32[9,16,256]{2,1,0:T(8,128)S(1)} %get-tuple-element.96), channel_id=1, source_target_pairs={{0,8},{4,12},{8,0},{12,4},{1,9},{5,13},{9,1},{13,5},{2,10},{6,14},... | collective-permute-start | bytes 442376 | tf_op jit(solution)/shard_map/ppermute | solution.py:91
  54.2 0.3 collective-permute-start.14
  54.4 0.5 collective-permute-done.8
  54.9 0.7 %fusion.4 = bf16[256,1,128]{2,0,1:T(8,128)(2,1)} fusion(f32[256,1,128]{2,0,1:T(8,128)S(1)} %collective-permute-done.8, f32[256,1,128]{2,0,1:T(8,128)S(1)} %collective-permute-done.7, f32[256,3,128]{2,0,1:T(8,128)S(1)} %fusion.2), kind=kLoop, calls=%fused_computation.9 | loop fusion | flops 98304 | bytes 458752 | tf_op jit(solution)/shard_map/convert_element_type | solution.py:204
  55.6 2.5 %collective-permute-done.13 = f32[9,16,256]{2,1,0:T(8,128)S(1)} collective-permute-done((f32[9,16,256]{2,1,0:T(8,128)S(1)}, f32[9,16,256]{2,1,0:T(8,128)S(1)}, u32[]{:S(2)}, u32[]{:S(2)}) %collective-permute-start.13) | collective-permute-done | bytes 147488 | tf_op jit(solution)/shard_map/ppermute | solution.py:91
  58.2 3.3 %collective-permute-done.14 = f32[9,16,256]{2,1,0:T(8,128)S(1)} collective-permute-done((f32[9,16,256]{2,1,0:T(8,128)S(1)}, f32[9,16,256]{2,1,0:T(8,128)S(1)}, u32[]{:S(2)}, u32[]{:S(2)}) %collective-permute-start.14) | collective-permute-done | bytes 147488 | tf_op jit(solution)/shard_map/ppermute | solution.py:91
  61.5 0.8 %copy-done.1 = f32[9,64,256]{2,1,0:T(8,128)} copy-done((f32[9,64,256]{2,1,0:T(8,128)}, f32[9,64,256]{2,1,0:T(8,128)S(1)}, u32[]{:S(2)}) %copy-start.1) | copy-done | bytes 589848
  (40 shorter events, 0.7 us)
Async XLA Ops:
  0.6 8.7 %copy-start = (bf16[1,9,3,2,64]{4,3,2,1,0:T(2,128)(2,1)S(1)}, bf16[1,9,3,2,64]{4,3,2,1,0:T(2,128)(2,1)}, u32[]{:S(2)}) copy-start(bf16[1,9,3,2,64]{4,3,2,1,0:T(2,128)(2,1)} %param.25) | copy-start | bytes 20740
  2.4 17.9 %collective-permute-start.2 = (bf16[320,128]{1,0:T(8,128)(2,1)S(1)}, bf16[320,128]{1,0:T(8,128)(2,1)S(1)}, u32[]{:S(2)}, u32[]{:S(2)}) collective-permute-start(bf16[320,128]{1,0:T(8,128)(2,1)S(1)} %get-tuple-element.110), channel_id=1, source_target_pairs={{0,1},{1,2},{2,3},{3,0},{4,5},{5,6},{6,7},{7,4},{8,9},{9,10},{10,1... | collective-permute-start | bytes 245768 | tf_op jit(solution)/shard_map/ppermute | solution.py:172
  4.5 15.7 %collective-permute-start.1 = (bf16[320,128]{1,0:T(8,128)(2,1)S(1)}, bf16[320,128]{1,0:T(8,128)(2,1)S(1)}, u32[]{:S(2)}, u32[]{:S(2)}) collective-permute-start(bf16[320,128]{1,0:T(8,128)(2,1)S(1)} %get-tuple-element.109), channel_id=1, source_target_pairs={{0,2},{1,3},{2,0},{3,1},{4,6},{5,7},{6,4},{7,5},{8,10},{9,11},{10,... | collective-permute-start | bytes 245768 | tf_op jit(solution)/shard_map/ppermute | solution.py:172
  6.9 13.4 %collective-permute-start = (bf16[320,128]{1,0:T(8,128)(2,1)S(1)}, bf16[320,128]{1,0:T(8,128)(2,1)S(1)}, u32[]{:S(2)}, u32[]{:S(2)}) collective-permute-start(bf16[320,128]{1,0:T(8,128)(2,1)S(1)} %get-tuple-element.108), channel_id=1, source_target_pairs={{0,3},{1,0},{2,1},{3,2},{4,7},{5,4},{6,5},{7,6},{8,11},{9,8},{10,9... | collective-permute-start | bytes 245768 | tf_op jit(solution)/shard_map/ppermute | solution.py:172
  15.7 4.6 %copy-start.3 = (bf16[256,1,128]{2,0,1:T(8,128)(2,1)S(1)}, bf16[256,1,128]{2,0,1:T(8,128)(2,1)}, u32[]{:S(2)}) copy-start(bf16[256,1,128]{2,0,1:T(8,128)(2,1)} %param.22) | copy-start | bytes 196612
  16.9 28.7 %collective-permute-start.5 = (f32[256,3,128]{2,0,1:T(8,128)S(1)}, f32[256,3,128]{2,0,1:T(8,128)S(1)}, u32[]{:S(2)}, u32[]{:S(2)}) collective-permute-start(f32[256,3,128]{2,0,1:T(8,128)S(1)} %get-tuple-element.97), channel_id=1, source_target_pairs={{0,1},{1,2},{2,3},{3,0},{4,5},{5,6},{6,7},{7,4},{8,9},{9,10},{10,1... | collective-permute-start | bytes 1179656 | tf_op jit(solution)/shard_map/ppermute | solution.py:19
  17.4 28.3 %collective-permute-start.6 = (f32[256,3,128]{2,0,1:T(8,128)S(1)}, f32[256,3,128]{2,0,1:T(8,128)S(1)}, u32[]{:S(2)}, u32[]{:S(2)}) collective-permute-start(f32[256,3,128]{2,0,1:T(8,128)S(1)} %get-tuple-element.98), channel_id=1, source_target_pairs={{1,0},{2,1},{3,2},{0,3},{5,4},{6,5},{7,6},{4,7},{9,8},{10,9},{11,1... | collective-permute-start | bytes 1179656 | tf_op jit(solution)/shard_map/ppermute | solution.py:21
  20.4 13.1 %copy-start.2 = (bf16[256,512]{1,0:T(8,128)(2,1)}, bf16[256,512]{1,0:T(8,128)(2,1)S(1)}, u32[]{:S(2)}) copy-start(bf16[256,512]{1,0:T(8,128)(2,1)S(1)} %pad_maximum_fusion.row_ref) | copy-start | bytes 786436
  20.4 8.4 %collective-permute-start.3 = (bf16[256,512]{1,0:T(8,128)(2,1)S(1)}, bf16[256,512]{1,0:T(8,128)(2,1)S(1)}, u32[]{:S(2)}, u32[]{:S(2)}) collective-permute-start(bf16[256,512]{1,0:T(8,128)(2,1)S(1)} %pad_maximum_fusion.row_ref), channel_id=1, source_target_pairs={{0,4},{4,8},{8,12},{1,5},{5,9},{9,13},{2,6},{6,10},{10,14},{3,7},{... | collective-permute-start | bytes 786440 | tf_op jit(solution)/shard_map/ppermute | solution.py:182
  25.5 8.0 %collective-permute-start.4 = (bf16[256,512]{1,0:T(8,128)(2,1)S(1)}, bf16[256,512]{1,0:T(8,128)(2,1)S(1)}, u32[]{:S(2)}, u32[]{:S(2)}) collective-permute-start(bf16[256,512]{1,0:T(8,128)(2,1)S(1)} %pad_maximum_fusion.row_ref), channel_id=1, source_target_pairs={{4,0},{8,4},{12,8},{5,1},{9,5},{13,9},{6,2},{10,6},{14,10},{7,3},{... | collective-permute-start | bytes 786440 | tf_op jit(solution)/shard_map/ppermute | solution.py:183
  28.8 4.7 %copy-start.4 = (bf16[256,512]{1,0:T(8,128)(2,1)}, bf16[256,512]{1,0:T(8,128)(2,1)S(1)}, u32[]{:S(2)}) copy-start(bf16[256,512]{1,0:T(8,128)(2,1)S(1)} %collective-permute-done.3.below_ref) | copy-start | bytes 786436
  33.5 0.7 %copy-start.5 = (bf16[256,512]{1,0:T(8,128)(2,1)}, bf16[256,512]{1,0:T(8,128)(2,1)S(1)}, u32[]{:S(2)}) copy-start(bf16[256,512]{1,0:T(8,128)(2,1)S(1)} %collective-permute-done.4.above_ref) | copy-start | bytes 786436
  43.7 7.4 %collective-permute-start.10 = (f32[9,16,256]{2,1,0:T(8,128)S(1)}, f32[9,16,256]{2,1,0:T(8,128)S(1)}, u32[]{:S(2)}, u32[]{:S(2)}) collective-permute-start(f32[9,16,256]{2,1,0:T(8,128)S(1)} %get-tuple-element.101), channel_id=1, source_target_pairs={{0,8},{4,12},{8,0},{12,4},{1,9},{5,13},{9,1},{13,5},{2,10},{6,14},... | collective-permute-start | bytes 442376 | tf_op jit(solution)/shard_map/ppermute | solution.py:84
  43.8 7.3 %collective-permute-start.11 = (f32[9,16,256]{2,1,0:T(8,128)S(1)}, f32[9,16,256]{2,1,0:T(8,128)S(1)}, u32[]{:S(2)}, u32[]{:S(2)}) collective-permute-start(f32[9,16,256]{2,1,0:T(8,128)S(1)} %get-tuple-element.100), channel_id=1, source_target_pairs={{0,12},{4,8},{8,4},{12,0},{1,13},{5,9},{9,5},{13,1},{2,14},{6,10},... | collective-permute-start | bytes 442376 | tf_op jit(solution)/shard_map/ppermute | solution.py:84
  43.9 7.2 %collective-permute-start.9 = (f32[9,16,256]{2,1,0:T(8,128)S(1)}, f32[9,16,256]{2,1,0:T(8,128)S(1)}, u32[]{:S(2)}, u32[]{:S(2)}) collective-permute-start(f32[9,16,256]{2,1,0:T(8,128)S(1)} %get-tuple-element.99), channel_id=1, source_target_pairs={{0,4},{4,0},{8,12},{12,8},{1,5},{5,1},{9,13},{13,9},{2,6},{6,2},{1... | collective-permute-start | bytes 442376 | tf_op jit(solution)/shard_map/ppermute | solution.py:84
  46.7 7.7 %collective-permute-start.7 = (f32[256,1,128]{2,0,1:T(8,128)S(1)}, f32[256,1,128]{2,0,1:T(8,128)S(1)}, u32[]{:S(2)}, u32[]{:S(2)}) collective-permute-start(f32[256,1,128]{2,0,1:T(8,128)S(1)} %get-tuple-element.102), channel_id=1, source_target_pairs={{0,4},{4,8},{8,12},{1,5},{5,9},{9,13},{2,6},{6,10},{10,14},{3,7},{... | collective-permute-start | bytes 393224 | tf_op jit(solution)/shard_map/ppermute | solution.py:19
  48.7 6.3 %collective-permute-start.8 = (f32[256,1,128]{2,0,1:T(8,128)S(1)}, f32[256,1,128]{2,0,1:T(8,128)S(1)}, u32[]{:S(2)}, u32[]{:S(2)}) collective-permute-start(f32[256,1,128]{2,0,1:T(8,128)S(1)} %get-tuple-element.103), channel_id=1, source_target_pairs={{4,0},{8,4},{12,8},{5,1},{9,5},{13,9},{6,2},{10,6},{14,10},{7,3},{... | collective-permute-start | bytes 393224 | tf_op jit(solution)/shard_map/ppermute | solution.py:21
  52.1 3.5 %collective-permute-start.12 = (f32[9,16,256]{2,1,0:T(8,128)S(1)}, f32[9,16,256]{2,1,0:T(8,128)S(1)}, u32[]{:S(2)}, u32[]{:S(2)}) collective-permute-start(f32[9,16,256]{2,1,0:T(8,128)S(1)} %get-tuple-element.96), channel_id=1, source_target_pairs={{0,4},{4,0},{8,12},{12,8},{1,5},{5,1},{9,13},{13,9},{2,6},{6,2},{1... | collective-permute-start | bytes 442376 | tf_op jit(solution)/shard_map/ppermute | solution.py:91
  52.7 5.4 %collective-permute-start.13 = (f32[9,16,256]{2,1,0:T(8,128)S(1)}, f32[9,16,256]{2,1,0:T(8,128)S(1)}, u32[]{:S(2)}, u32[]{:S(2)}) collective-permute-start(f32[9,16,256]{2,1,0:T(8,128)S(1)} %get-tuple-element.96), channel_id=1, source_target_pairs={{0,8},{4,12},{8,0},{12,4},{1,9},{5,13},{9,1},{13,5},{2,10},{6,14},... | collective-permute-start | bytes 442376 | tf_op jit(solution)/shard_map/ppermute | solution.py:91
  54.2 7.3 %collective-permute-start.14 = (f32[9,16,256]{2,1,0:T(8,128)S(1)}, f32[9,16,256]{2,1,0:T(8,128)S(1)}, u32[]{:S(2)}, u32[]{:S(2)}) collective-permute-start(f32[9,16,256]{2,1,0:T(8,128)S(1)} %get-tuple-element.96), channel_id=1, source_target_pairs={{0,12},{4,8},{8,4},{12,0},{1,13},{5,9},{9,5},{13,1},{2,14},{6,10},... | collective-permute-start | bytes 442376 | tf_op jit(solution)/shard_map/ppermute | solution.py:91
  61.5 0.8 %copy-start.1 = (f32[9,64,256]{2,1,0:T(8,128)}, f32[9,64,256]{2,1,0:T(8,128)S(1)}, u32[]{:S(2)}) copy-start(f32[9,64,256]{2,1,0:T(8,128)S(1)} %constant_dynamic-update-slice_fusion) | copy-start | bytes 1769476

commit v21 on v19

--- a/solution.py
+++ b/solution.py
@@ -159,17 +159,14 @@
     matrix, contrib = toeplitz(tap_table[0], lon_cols, weights, upstream[:, 0])
     o_block = upstream.shape[0] // n_lon
     up_row = upstream[:, 0]
-    blocks = [fields[:, 0]]
+    blocks = [fields[:, 0]] + [
+        lax.ppermute(fields[:, 0], "lon", [(p, (p - d) % n_lon) for p in range(n_lon)])
+        for d in range(1, n_lon)
+    ]
     up_parts = [lax.dynamic_slice_in_dim(up_row, lon_at * o_block, o_block, axis=0)]
     for d in range(1, n_lon):
         part = lax.dynamic_slice_in_dim(up_row, ((lon_at - d) % n_lon) * o_block, o_block, axis=0)
-        both = lax.ppermute(
-            jnp.concatenate([fields[:, 0], part], axis=0),
-            "lon",
-            [(p, (p - d) % n_lon) for p in range(n_lon)],
-        )
-        blocks.append(both[:channels])
-        up_parts.append(both[channels:])
+        up_parts.append(lax.ppermute(part, "lon", [(p, (p - d) % n_lon) for p in range(n_lon)]))
     up_rel = jnp.stack(up_parts, axis=0)
     row = jnp.concatenate(blocks, axis=1)
     count = lax.axis_size("lat")

time: 62.4 us -> 65.6 us (1.051)
  starting transfers between devices: 23.5 us -> 29.5 us
  waiting for transfers between devices: 11.7 us -> 9.06 us
    ppermute x1, waiting for transfers between devices: 4.69 us -> 0.54 us  [body(): above = lax.ppermute(row, 'lat', [(i + 1, i) for i in range(count - 1)])]
    ppermute x3 -> x6, starting transfers between devices: 4.66 us -> 8.06 us  [the longest x3 4.66 us: body(): lax.ppermute(fields[:, 0], 'lon', [(p, (p - d) % n_lon) for p in range(n_...]
    ppermute x2, waiting for transfers between devices: 0.5 us -> 3.29 us  [padded_2(): lax.ppermute(head, axis, [((i + 1) % count, i) for i in range(ends)])]
    ppermute x2, starting transfers between devices: 4.17 us -> 6.58 us  [padded_2(): lax.ppermute(tail, axis, [(i, (i + 1) % count) for i in range(ends)])]
    concatenate x1 -> x0, other arithmetic: 0.87 us -> none  [body(): jnp.concatenate([fields[:, 0], part], axis=0)]
    another operation x1, other arithmetic: 0.04 us -> 0.88 us  [body(): rows = jnp.stack([below, row, above], axis=0)]
    ppermute x1, waiting for transfers between devices: 0.69 us -> 0.01 us  [body(): below = lax.ppermute(row, 'lat', [(i, i + 1) for i in range(count - 1)])]
    unnamed x9 -> x7, local copies, waits for them, and re-layouts: 1.48 us -> 1.48 us
  transfers between devices with their start and end apart: 15 -> 18, of which waited for: 5 -> 5; matrix products, arithmetic and copies ran while one was open for 14% -> 15% of each run, Pallas kernels for 23% -> 22%
where the time goes in v21:
time: 65.6 us; the launch traced here: 64.9 us
  starting transfers between devices  29.5 us (45%)
  Pallas kernels  14 us (21%)
  waiting for transfers between devices  9.06 us (14%)
  other arithmetic  6.01 us (9%)
  local copies, waits for them, and re-layouts  4.63 us (7%)
  between operations  1.51 us (2%)
    pallas_call x1, Pallas kernels, row_products(): pl.pallas_call(row_kernel, out_shape=(jax.ShapeDtypeStruct((weights.shape...  8.55 us
    ppermute x2, starting transfers between devices, padded_2(): lax.ppermute(tail, axis, [(i, (i + 1) % count) for i in range(ends)])  6.58 us
    pallas_call x1, Pallas kernels, toeplitz(): pl.pallas_call(toeplitz_kernel, out_shape=(jax.ShapeDtypeStruct((kernels,...  5.48 us
    ppermute x3, waiting for transfers between devices, lat_allreduce(): recv = lax.ppermute(mine, axis, [(i, i ^ d) for i in range(count)])  5.19 us
    ppermute x1, starting transfers between devices, body(): below = lax.ppermute(row, 'lat', [(i, i + 1) for i in range(count - 1)])  5.07 us
    ppermute x3, starting transfers between devices, body(): lax.ppermute(fields[:, 0], 'lon', [(p, (p - d) % n_lon) for p in range(n_...  4.66 us
    ppermute x2, starting transfers between devices, padded_2(): lax.ppermute(head, axis, [((i + 1) % count, i) for i in range(ends)])  3.45 us
    ppermute x3, starting transfers between devices, body(): lax.ppermute(part, 'lon', [(p, (p - d) % n_lon) for p in range(n_lon)])  3.4 us
  transfers between devices with their start and end apart: 18, of which 5 were waited for; matrix products, arithmetic and copies ran while one was open for 15% of the time, Pallas kernels for 22%

profile of v21, /device:TPU:1, one launch (start us, length us, event | category | flops | bytes accessed | tf_op | source)
XLA Modules:
  0.0 64.9 jit_solution(1801512397287817661)
XLA Ops:
  0.6 4.2 %collective-permute-start = (bf16[256,128]{1,0:T(8,128)(2,1)}, bf16[256,128]{1,0:T(8,128)(2,1)S(1)}, u32[]{:S(2)}, u32[]{:S(2)}) collective-permute-start(bf16[256,128]{1,0:T(8,128)(2,1)} %bitcast.48), channel_id=1, source_target_pairs={{0,3},{1,0},{2,1},{3,2},{4,7},{5,4},{6,5},{7,6},{8,11},{9,8},{10,9... | collective-permute-start | bytes 196616 | tf_op jit(solution)/shard_map/ppermute | solution.py:163
  4.9 0.5 collective-permute-start.2
  5.3 0.8 %dynamic-slice_bitcast_fusion.3 = (bf16[1,64,128]{2,1,0:T(8,128)(2,1)S(1)}, bf16[64,128]{1,0:T(8,128)(2,1)S(1)}, bf16[64,128]{1,0:T(8,128)(2,1)S(1)}, bf16[64,128]{1,0:T(8,128)(2,1)S(1)}) fusion(bf16[256,1,128]{2,0,1:T(8,128)(2,1)} %param.23, s32[]{:T(128)S(6)} %select_n.51, s32[]{:T(128)S(6)} %select_n.53, s32[]{:T(128)S(6)} %select_n.57, s32[]{:T(128)S(6)} %select_n.55), kind=kLoop, calls=%fused_computation.29 | loop fusion | bytes 131088 | tf_op jit(solution)/shard_map/stack | solution.py:170
  6.1 2.8 %collective-permute-start.5 = (bf16[64,128]{1,0:T(8,128)(2,1)S(1)}, bf16[64,128]{1,0:T(8,128)(2,1)S(1)}, u32[]{:S(2)}, u32[]{:S(2)}) collective-permute-start(bf16[64,128]{1,0:T(8,128)(2,1)S(1)} %get-tuple-element.107), channel_id=1, source_target_pairs={{0,3},{1,0},{2,1},{3,2},{4,7},{5,4},{6,5},{7,6},{8,11},{9,8},{10,9... | collective-permute-start | bytes 49160 | tf_op jit(solution)/shard_map/ppermute | solution.py:169
  8.9 0.6 collective-permute-start.6
  9.5 0.7 %add_bitcast_fusion = s32[2]{0:T(128)S(1)} fusion(s32[1,2]{1,0:T(1,128)} %param.27), kind=kLoop, calls=%fused_computation.39 | loop fusion | flops 4 | bytes 16 | tf_op jit(solution)/shard_map/add | solution.py:32
  11.2 0.6 copy.13
  11.8 5.5 %shard_map.100 = (bf16[9,128,1152]{2,1,0:T(8,128)(2,1)}, f32[3,256,384]{2,1,0:T(8,128)}) custom-call(bf16[9,1152]{1,0:T(8,128)(2,1)} %bitcast.47, bf16[9,256,256]{2,1,0:T(8,128)(2,1)} %w_ref.3, bf16[256,128]{1,0:T(8,128)(2,1)} %bitcast.45), custom_call_target="tpu_custom_call" | custom-call | tf_op jit(solution)/shard_map/pallas_call | solution.py:64
  17.3 0.9 %fusion.18 = (bf16[1,256,512]{2,1,0:T(8,128)(2,1)S(1)}, bf16[256,512]{1,0:T(8,128)(2,1)S(1)}) fusion(bf16[256,128]{1,0:T(8,128)(2,1)S(1)} %collective-permute-done.2, bf16[256,128]{1,0:T(8,128)(2,1)S(1)} %collective-permute-done.1, bf16[256,128]{1,0:T(8,128)(2,1)S(1)} %collective-permute-done, bf16[256,128]{1,0:T(8,128)(2,1)} %bitcast.51), kind=kLoop, calls=%fused_computation.42 | loop fusion | flops 1048576 | bytes 786432 | tf_op jit(solution)/shard_map/stack | solution.py:175
  18.2 5.1 %collective-permute-start.3 = (bf16[256,512]{1,0:T(8,128)(2,1)S(1)}, bf16[256,512]{1,0:T(8,128)(2,1)S(1)}, u32[]{:S(2)}, u32[]{:S(2)}) collective-permute-start(bf16[256,512]{1,0:T(8,128)(2,1)S(1)} %get-tuple-element.105), channel_id=1, source_target_pairs={{0,4},{4,8},{8,12},{1,5},{5,9},{9,13},{2,6},{6,10},{10,14},{3,7},{... | collective-permute-start | bytes 786440 | tf_op jit(solution)/shard_map/ppermute | solution.py:173
  23.3 1.9 %collective-permute-start.4 = (bf16[256,512]{1,0:T(8,128)(2,1)S(1)}, bf16[256,512]{1,0:T(8,128)(2,1)S(1)}, u32[]{:S(2)}, u32[]{:S(2)}) collective-permute-start(bf16[256,512]{1,0:T(8,128)(2,1)S(1)} %get-tuple-element.105), channel_id=1, source_target_pairs={{4,0},{8,4},{12,8},{5,1},{9,5},{13,9},{6,2},{10,6},{14,10},{7,3},{... | collective-permute-start | bytes 786440 | tf_op jit(solution)/shard_map/ppermute | solution.py:174
  25.2 1.2 %fusion.19 = (f32[256,3,128]{2,0,1:T(8,128)S(1)}, f32[256,3,128]{2,0,1:T(8,128)S(1)}) fusion(f32[256,3,384]{2,0,1:T(8,128)} %bitcast.41), kind=kLoop, calls=%fused_computation.43 | loop fusion | bytes 1572864 | tf_op jit(solution)/shard_map/slice | solution.py:186
  26.4 2.1 %collective-permute-start.8 = (f32[256,3,128]{2,0,1:T(8,128)S(1)}, f32[256,3,128]{2,0,1:T(8,128)S(1)}, u32[]{:S(2)}, u32[]{:S(2)}) collective-permute-start(f32[256,3,128]{2,0,1:T(8,128)S(1)} %get-tuple-element.97), channel_id=1, source_target_pairs={{0,1},{1,2},{2,3},{3,0},{4,5},{5,6},{6,7},{7,4},{8,9},{9,10},{10,1... | collective-permute-start | bytes 1179656 | tf_op jit(solution)/shard_map/ppermute | solution.py:19
  28.5 1.5 %collective-permute-start.9 = (f32[256,3,128]{2,0,1:T(8,128)S(1)}, f32[256,3,128]{2,0,1:T(8,128)S(1)}, u32[]{:S(2)}, u32[]{:S(2)}) collective-permute-start(f32[256,3,128]{2,0,1:T(8,128)S(1)} %get-tuple-element.98), channel_id=1, source_target_pairs={{1,0},{2,1},{3,2},{0,3},{5,4},{6,5},{7,6},{4,7},{9,8},{10,9},{11,1... | collective-permute-start | bytes 1179656 | tf_op jit(solution)/shard_map/ppermute | solution.py:21
  30.1 0.6 pad_maximum_fusion.5.up_ref
  30.7 0.5 collective-permute-done.4
  31.2 1.1 %fusion.ext_ref = bf16[3,256,768]{2,1,0:T(8,128)(2,1)} fusion(bf16[1,256,512]{2,1,0:T(8,128)(2,1)S(1)} %bitcast.44, bf16[1,256,512]{2,1,0:T(8,128)(2,1)S(1)} %get-tuple-element.104, bf16[1,256,512]{2,1,0:T(8,128)(2,1)S(1)} %bitcast.43), kind=kLoop, calls=%fused_computation.1 | loop fusion | flops 10616832 | bytes 1966080 | tf_op jit(solution)/shard_map/concatenate | solution.py:176
  32.3 8.6 %shard_map.101 = (bf16[256,128]{1,0:T(8,128)(2,1)}, f32[9,64,256]{2,1,0:T(8,128)}) custom-call(bf16[3,256,768]{2,1,0:T(8,128)(2,1)} %fusion.ext_ref, bf16[1152,1152]{1,0:T(8,128)(2,1)} %bitcast.55, bf16[9,256,256]{2,1,0:T(8,128)(2,1)} %w_ref.3, bf16[4,64,128]{2,1,0:T(8,128)(2,1)} %pad_maximum_fusion.5.up_ref), custom_call_target="tpu_custom_call" | custom-call | flops 3019898880 | bytes 5734400 | tf_op jit(solution)/shard_map/pallas_call | solution.py:142
  40.9 1.1 %constant_dynamic-slice_fusion.2 = (f32[9,16,256]{2,1,0:T(8,128)S(1)}, f32[9,16,256]{2,1,0:T(8,128)S(1)}, f32[9,16,256]{2,1,0:T(8,128)S(1)}) fusion(f32[9,64,256]{2,1,0:T(8,128)} %get-tuple-element.94, s32[]{:T(128)S(6)} %select_n.59, s32[]{:T(128)S(6)} %select_n.61, s32[]{:T(128)S(6)} %select_n.60), kind=kLoop, calls=%fused_computation.36 | loop fusion | bytes 884748 | tf_op jit(solution)/shard_map/dynamic_slice | solution.py:83
  42.0 1.6 %collective-permute-start.13 = (f32[9,16,256]{2,1,0:T(8,128)S(1)}, f32[9,16,256]{2,1,0:T(8,128)S(1)}, u32[]{:S(2)}, u32[]{:S(2)}) collective-permute-start(f32[9,16,256]{2,1,0:T(8,128)S(1)} %get-tuple-element.101), channel_id=1, source_target_pairs={{0,8},{4,12},{8,0},{12,4},{1,9},{5,13},{9,1},{13,5},{2,10},{6,14},... | collective-permute-start | bytes 442376 | tf_op jit(solution)/shard_map/ppermute | solution.py:84
  43.6 0.5 collective-permute-start.14
  44.2 1.8 %collective-permute-done.9 = f32[256,3,128]{2,0,1:T(8,128)S(1)} collective-permute-done((f32[256,3,128]{2,0,1:T(8,128)S(1)}, f32[256,3,128]{2,0,1:T(8,128)S(1)}, u32[]{:S(2)}, u32[]{:S(2)}) %collective-permute-start.9) | collective-permute-done | bytes 393248 | tf_op jit(solution)/shard_map/ppermute | solution.py:21
  45.9 1.1 %fusion.4 = f32[256,3,128]{2,0,1:T(8,128)S(1)} fusion(f32[256,3,128]{2,0,1:T(8,128)S(1)} %collective-permute-done.9, f32[256,3,128]{2,0,1:T(8,128)S(1)} %collective-permute-done.8, f32[256,3,384]{2,0,1:T(8,128)} %bitcast.42), kind=kLoop, calls=%fused_computation.10 | loop fusion | flops 196608 | bytes 1572864 | tf_op jit(solution)/shard_map/add | solution.py:191
  47.0 4.5 %collective-permute-start.10 = (f32[256,1,128]{2,0,1:T(8,128)S(1)}, f32[256,1,128]{2,0,1:T(8,128)S(1)}, u32[]{:S(2)}, u32[]{:S(2)}) collective-permute-start(f32[256,1,128]{2,0,1:T(8,128)S(1)} %get-tuple-element.102), channel_id=1, source_target_pairs={{0,4},{4,8},{8,12},{1,5},{5,9},{9,13},{2,6},{6,10},{10,14},{3,7},{... | collective-permute-start | bytes 393224 | tf_op jit(solution)/shard_map/ppermute | solution.py:19
  51.5 1.9 %collective-permute-start.11 = (f32[256,1,128]{2,0,1:T(8,128)S(1)}, f32[256,1,128]{2,0,1:T(8,128)S(1)}, u32[]{:S(2)}, u32[]{:S(2)}) collective-permute-start(f32[256,1,128]{2,0,1:T(8,128)S(1)} %get-tuple-element.103), channel_id=1, source_target_pairs={{4,0},{8,4},{12,8},{5,1},{9,5},{13,9},{6,2},{10,6},{14,10},{7,3},{... | collective-permute-start | bytes 393224 | tf_op jit(solution)/shard_map/ppermute | solution.py:21
  53.5 1.0 %constant_dynamic-update-slice_fusion.3 = (f32[9,64,256]{2,1,0:T(8,128)S(1)}, f32[9,16,256]{2,1,0:T(8,128)S(1)}) fusion(f32[9,64,256]{2,1,0:T(8,128)S(1)} %broadcast_in_dim.25, s32[]{:T(128)S(6)} %select_n.58, f32[9,16,256]{2,1,0:T(8,128)S(1)} %collective-permute-done.13, f32[9,16,256]{2,1,0:T(8,128)S(1)} %collective-permute-done.14, ...), kind=kLoop, calls=%fused_computation.33 | loop fusion | flops 110592 | bytes 884740 | tf_op jit(solution)/shard_map/dynamic_update_slice | solution.py:89
  54.5 1.8 %collective-permute-start.16 = (f32[9,16,256]{2,1,0:T(8,128)S(1)}, f32[9,16,256]{2,1,0:T(8,128)S(1)}, u32[]{:S(2)}, u32[]{:S(2)}) collective-permute-start(f32[9,16,256]{2,1,0:T(8,128)S(1)} %get-tuple-element.96), channel_id=1, source_target_pairs={{0,8},{4,12},{8,0},{12,4},{1,9},{5,13},{9,1},{13,5},{2,10},{6,14},... | collective-permute-start | bytes 442376 | tf_op jit(solution)/shard_map/ppermute | solution.py:91
  56.7 1.5 %collective-permute-done.11 = f32[256,1,128]{2,0,1:T(8,128)S(1)} collective-permute-done((f32[256,1,128]{2,0,1:T(8,128)S(1)}, f32[256,1,128]{2,0,1:T(8,128)S(1)}, u32[]{:S(2)}, u32[]{:S(2)}) %collective-permute-start.11) | collective-permute-done | bytes 131104 | tf_op jit(solution)/shard_map/ppermute | solution.py:21
  58.2 0.7 %fusion.6 = bf16[256,1,128]{2,0,1:T(8,128)(2,1)} fusion(f32[256,1,128]{2,0,1:T(8,128)S(1)} %collective-permute-done.11, f32[256,1,128]{2,0,1:T(8,128)S(1)} %collective-permute-done.10, f32[256,3,128]{2,0,1:T(8,128)S(1)} %fusion.4), kind=kLoop, calls=%fused_computation.15 | loop fusion | flops 98304 | bytes 458752 | tf_op jit(solution)/shard_map/convert_element_type | solution.py:197
  58.9 1.9 %collective-permute-done.16 = f32[9,16,256]{2,1,0:T(8,128)S(1)} collective-permute-done((f32[9,16,256]{2,1,0:T(8,128)S(1)}, f32[9,16,256]{2,1,0:T(8,128)S(1)}, u32[]{:S(2)}, u32[]{:S(2)}) %collective-permute-start.16) | collective-permute-done | bytes 147488 | tf_op jit(solution)/shard_map/ppermute | solution.py:91
  60.8 3.3 %collective-permute-done.17 = f32[9,16,256]{2,1,0:T(8,128)S(1)} collective-permute-done((f32[9,16,256]{2,1,0:T(8,128)S(1)}, f32[9,16,256]{2,1,0:T(8,128)S(1)}, u32[]{:S(2)}, u32[]{:S(2)}) %collective-permute-start.17) | collective-permute-done | bytes 147488 | tf_op jit(solution)/shard_map/ppermute | solution.py:91
  64.1 0.8 %copy-done.1 = f32[9,64,256]{2,1,0:T(8,128)} copy-done((f32[9,64,256]{2,1,0:T(8,128)}, f32[9,64,256]{2,1,0:T(8,128)S(1)}, u32[]{:S(2)}) %copy-start.1) | copy-done | bytes 589848
  (32 shorter events, 0.9 us)
Async XLA Ops:
  0.6 10.2 %copy-start = (bf16[1,9,3,2,64]{4,3,2,1,0:T(2,128)(2,1)S(1)}, bf16[1,9,3,2,64]{4,3,2,1,0:T(2,128)(2,1)}, u32[]{:S(2)}) copy-start(bf16[1,9,3,2,64]{4,3,2,1,0:T(2,128)(2,1)} %param.25) | copy-start | bytes 20740
  0.6 16.6 %collective-permute-start = (bf16[256,128]{1,0:T(8,128)(2,1)}, bf16[256,128]{1,0:T(8,128)(2,1)S(1)}, u32[]{:S(2)}, u32[]{:S(2)}) collective-permute-start(bf16[256,128]{1,0:T(8,128)(2,1)} %bitcast.48), channel_id=1, source_target_pairs={{0,3},{1,0},{2,1},{3,2},{4,7},{5,4},{6,5},{7,6},{8,11},{9,8},{10,9... | collective-permute-start | bytes 196616 | tf_op jit(solution)/shard_map/ppermute | solution.py:163
  4.8 12.4 %collective-permute-start.1 = (bf16[256,128]{1,0:T(8,128)(2,1)}, bf16[256,128]{1,0:T(8,128)(2,1)S(1)}, u32[]{:S(2)}, u32[]{:S(2)}) collective-permute-start(bf16[256,128]{1,0:T(8,128)(2,1)} %bitcast.49), channel_id=1, source_target_pairs={{0,2},{1,3},{2,0},{3,1},{4,6},{5,7},{6,4},{7,5},{8,10},{9,11},{10,... | collective-permute-start | bytes 196616 | tf_op jit(solution)/shard_map/ppermute | solution.py:163
  4.9 12.4 %collective-permute-start.2 = (bf16[256,128]{1,0:T(8,128)(2,1)}, bf16[256,128]{1,0:T(8,128)(2,1)S(1)}, u32[]{:S(2)}, u32[]{:S(2)}) collective-permute-start(bf16[256,128]{1,0:T(8,128)(2,1)} %bitcast.50), channel_id=1, source_target_pairs={{0,1},{1,2},{2,3},{3,0},{4,5},{5,6},{6,7},{7,4},{8,9},{9,10},{10,1... | collective-permute-start | bytes 196616 | tf_op jit(solution)/shard_map/ppermute | solution.py:163
  6.1 20.3 %collective-permute-start.5 = (bf16[64,128]{1,0:T(8,128)(2,1)S(1)}, bf16[64,128]{1,0:T(8,128)(2,1)S(1)}, u32[]{:S(2)}, u32[]{:S(2)}) collective-permute-start(bf16[64,128]{1,0:T(8,128)(2,1)S(1)} %get-tuple-element.107), channel_id=1, source_target_pairs={{0,3},{1,0},{2,1},{3,2},{4,7},{5,4},{6,5},{7,6},{8,11},{9,8},{10,9... | collective-permute-start | bytes 49160 | tf_op jit(solution)/shard_map/ppermute | solution.py:169
  8.9 19.6 %collective-permute-start.6 = (bf16[64,128]{1,0:T(8,128)(2,1)S(1)}, bf16[64,128]{1,0:T(8,128)(2,1)S(1)}, u32[]{:S(2)}, u32[]{:S(2)}) collective-permute-start(bf16[64,128]{1,0:T(8,128)(2,1)S(1)} %get-tuple-element.109), channel_id=1, source_target_pairs={{0,2},{1,3},{2,0},{3,1},{4,6},{5,7},{6,4},{7,5},{8,10},{9,11},{10,... | collective-permute-start | bytes 49160 | tf_op jit(solution)/shard_map/ppermute | solution.py:169
  17.3 12.8 %collective-permute-start.7 = (bf16[64,128]{1,0:T(8,128)(2,1)S(1)}, bf16[64,128]{1,0:T(8,128)(2,1)S(1)}, u32[]{:S(2)}, u32[]{:S(2)}) collective-permute-start(bf16[64,128]{1,0:T(8,128)(2,1)S(1)} %get-tuple-element.108), channel_id=1, source_target_pairs={{0,1},{1,2},{2,3},{3,0},{4,5},{5,6},{6,7},{7,4},{8,9},{9,10},{10,1... | collective-permute-start | bytes 49160 | tf_op jit(solution)/shard_map/ppermute | solution.py:169
  18.2 12.5 %collective-permute-start.3 = (bf16[256,512]{1,0:T(8,128)(2,1)S(1)}, bf16[256,512]{1,0:T(8,128)(2,1)S(1)}, u32[]{:S(2)}, u32[]{:S(2)}) collective-permute-start(bf16[256,512]{1,0:T(8,128)(2,1)S(1)} %get-tuple-element.105), channel_id=1, source_target_pairs={{0,4},{4,8},{8,12},{1,5},{5,9},{9,13},{2,6},{6,10},{10,14},{3,7},{... | collective-permute-start | bytes 786440 | tf_op jit(solution)/shard_map/ppermute | solution.py:173
  23.3 8.0 %collective-permute-start.4 = (bf16[256,512]{1,0:T(8,128)(2,1)S(1)}, bf16[256,512]{1,0:T(8,128)(2,1)S(1)}, u32[]{:S(2)}, u32[]{:S(2)}) collective-permute-start(bf16[256,512]{1,0:T(8,128)(2,1)S(1)} %get-tuple-element.105), channel_id=1, source_target_pairs={{4,0},{8,4},{12,8},{5,1},{9,5},{13,9},{6,2},{10,6},{14,10},{7,3},{... | collective-permute-start | bytes 786440 | tf_op jit(solution)/shard_map/ppermute | solution.py:174
  26.4 17.8 %collective-permute-start.8 = (f32[256,3,128]{2,0,1:T(8,128)S(1)}, f32[256,3,128]{2,0,1:T(8,128)S(1)}, u32[]{:S(2)}, u32[]{:S(2)}) collective-permute-start(f32[256,3,128]{2,0,1:T(8,128)S(1)} %get-tuple-element.97), channel_id=1, source_target_pairs={{0,1},{1,2},{2,3},{3,0},{4,5},{5,6},{6,7},{7,4},{8,9},{9,10},{10,1... | collective-permute-start | bytes 1179656 | tf_op jit(solution)/shard_map/ppermute | solution.py:19
  28.5 17.4 %collective-permute-start.9 = (f32[256,3,128]{2,0,1:T(8,128)S(1)}, f32[256,3,128]{2,0,1:T(8,128)S(1)}, u32[]{:S(2)}, u32[]{:S(2)}) collective-permute-start(f32[256,3,128]{2,0,1:T(8,128)S(1)} %get-tuple-element.98), channel_id=1, source_target_pairs={{1,0},{2,1},{3,2},{0,3},{5,4},{6,5},{7,6},{4,7},{9,8},{10,9},{11,1... | collective-permute-start | bytes 1179656 | tf_op jit(solution)/shard_map/ppermute | solution.py:21
  42.0 11.4 %collective-permute-start.12 = (f32[9,16,256]{2,1,0:T(8,128)S(1)}, f32[9,16,256]{2,1,0:T(8,128)S(1)}, u32[]{:S(2)}, u32[]{:S(2)}) collective-permute-start(f32[9,16,256]{2,1,0:T(8,128)S(1)} %get-tuple-element.99), channel_id=1, source_target_pairs={{0,4},{4,0},{8,12},{12,8},{1,5},{5,1},{9,13},{13,9},{2,6},{6,2},{1... | collective-permute-start | bytes 442376 | tf_op jit(solution)/shard_map/ppermute | solution.py:84
  42.0 11.4 %collective-permute-start.13 = (f32[9,16,256]{2,1,0:T(8,128)S(1)}, f32[9,16,256]{2,1,0:T(8,128)S(1)}, u32[]{:S(2)}, u32[]{:S(2)}) collective-permute-start(f32[9,16,256]{2,1,0:T(8,128)S(1)} %get-tuple-element.101), channel_id=1, source_target_pairs={{0,8},{4,12},{8,0},{12,4},{1,9},{5,13},{9,1},{13,5},{2,10},{6,14},... | collective-permute-start | bytes 442376 | tf_op jit(solution)/shard_map/ppermute | solution.py:84
  43.6 9.8 %collective-permute-start.14 = (f32[9,16,256]{2,1,0:T(8,128)S(1)}, f32[9,16,256]{2,1,0:T(8,128)S(1)}, u32[]{:S(2)}, u32[]{:S(2)}) collective-permute-start(f32[9,16,256]{2,1,0:T(8,128)S(1)} %get-tuple-element.100), channel_id=1, source_target_pairs={{0,12},{4,8},{8,4},{12,0},{1,13},{5,9},{9,5},{13,1},{2,14},{6,10},... | collective-permute-start | bytes 442376 | tf_op jit(solution)/shard_map/ppermute | solution.py:84
  47.0 9.7 %collective-permute-start.10 = (f32[256,1,128]{2,0,1:T(8,128)S(1)}, f32[256,1,128]{2,0,1:T(8,128)S(1)}, u32[]{:S(2)}, u32[]{:S(2)}) collective-permute-start(f32[256,1,128]{2,0,1:T(8,128)S(1)} %get-tuple-element.102), channel_id=1, source_target_pairs={{0,4},{4,8},{8,12},{1,5},{5,9},{9,13},{2,6},{6,10},{10,14},{3,7},{... | collective-permute-start | bytes 393224 | tf_op jit(solution)/shard_map/ppermute | solution.py:19
  51.5 6.7 %collective-permute-start.11 = (f32[256,1,128]{2,0,1:T(8,128)S(1)}, f32[256,1,128]{2,0,1:T(8,128)S(1)}, u32[]{:S(2)}, u32[]{:S(2)}) collective-permute-start(f32[256,1,128]{2,0,1:T(8,128)S(1)} %get-tuple-element.103), channel_id=1, source_target_pairs={{4,0},{8,4},{12,8},{5,1},{9,5},{13,9},{6,2},{10,6},{14,10},{7,3},{... | collective-permute-start | bytes 393224 | tf_op jit(solution)/shard_map/ppermute | solution.py:21
  54.5 4.4 %collective-permute-start.15 = (f32[9,16,256]{2,1,0:T(8,128)S(1)}, f32[9,16,256]{2,1,0:T(8,128)S(1)}, u32[]{:S(2)}, u32[]{:S(2)}) collective-permute-start(f32[9,16,256]{2,1,0:T(8,128)S(1)} %get-tuple-element.96), channel_id=1, source_target_pairs={{0,4},{4,0},{8,12},{12,8},{1,5},{5,1},{9,13},{13,9},{2,6},{6,2},{1... | collective-permute-start | bytes 442376 | tf_op jit(solution)/shard_map/ppermute | solution.py:91
  54.5 6.2 %collective-permute-start.16 = (f32[9,16,256]{2,1,0:T(8,128)S(1)}, f32[9,16,256]{2,1,0:T(8,128)S(1)}, u32[]{:S(2)}, u32[]{:S(2)}) collective-permute-start(f32[9,16,256]{2,1,0:T(8,128)S(1)} %get-tuple-element.96), channel_id=1, source_target_pairs={{0,8},{4,12},{8,0},{12,4},{1,9},{5,13},{9,1},{13,5},{2,10},{6,14},... | collective-permute-start | bytes 442376 | tf_op jit(solution)/shard_map/ppermute | solution.py:91
  56.4 7.7 %collective-permute-start.17 = (f32[9,16,256]{2,1,0:T(8,128)S(1)}, f32[9,16,256]{2,1,0:T(8,128)S(1)}, u32[]{:S(2)}, u32[]{:S(2)}) collective-permute-start(f32[9,16,256]{2,1,0:T(8,128)S(1)} %get-tuple-element.96), channel_id=1, source_target_pairs={{0,12},{4,8},{8,4},{12,0},{1,13},{5,9},{9,5},{13,1},{2,14},{6,10},... | collective-permute-start | bytes 442376 | tf_op jit(solution)/shard_map/ppermute | solution.py:91
  64.1 0.8 %copy-start.1 = (f32[9,64,256]{2,1,0:T(8,128)}, f32[9,64,256]{2,1,0:T(8,128)S(1)}, u32[]{:S(2)}) copy-start(f32[9,64,256]{2,1,0:T(8,128)S(1)} %constant_dynamic-update-slice_fusion) | copy-start | bytes 1769476

commit v22 on v19

--- a/solution.py
+++ b/solution.py
@@ -78,10 +78,13 @@
         return lax.psum(x, axis)
     index = lax.axis_index(axis)
     size = x.shape[dim] // count
-    parts = [lax.dynamic_slice_in_dim(x, index * size, size, axis=dim)]
+    chunks = [lax.slice_in_dim(x, c * size, (c + 1) * size, axis=dim) for c in range(count)]
+    for s in range(steps):
+        flip = ((index >> s) & 1) == 1
+        chunks = [jnp.where(flip, chunks[c ^ (1 << s)], chunks[c]) for c in range(count)]
+    parts = [chunks[0]]
     for d in range(1, count):
-        send = lax.dynamic_slice_in_dim(x, (index ^ d) * size, size, axis=dim)
-        parts.append(lax.ppermute(send, axis, [(i, i ^ d) for i in range(count)]))
+        parts.append(lax.ppermute(chunks[d], axis, [(i, i ^ d) for i in range(count)]))
     for s in range(steps):
         parts = [parts[2 * e] + parts[2 * e + 1] for e in range(len(parts) // 2)]
     mine = parts[0]

time: 62.4 us -> 62.2 us (level)
  local copies, waits for them, and re-layouts: 4.67 us -> 3.59 us
  waiting for transfers between devices: 11.7 us -> 12.4 us
    ppermute x2, waiting for transfers between devices: 0.5 us -> 2.06 us  [padded_2(): lax.ppermute(head, axis, [((i + 1) % count, i) for i in range(ends)])]
    select_n x0 -> x1, other arithmetic: none -> 1.24 us  [lat_allreduce(): jnp.where(flip, chunks[c ^ 1 << s], chunks[c])]
    dynamic_slice x1 -> x0, local copies, waits for them, and re-layouts: 1.08 us -> none  [lat_allreduce(): send = lax.dynamic_slice_in_dim(x, (index ^ d) * size, size, axis=dim)]
    ppermute x3, waiting for transfers between devices: 5.83 us -> 4.93 us  [lat_allreduce(): recv = lax.ppermute(mine, axis, [(i, i ^ d) for i in range(count)])]
    dynamic_update_slice x1, other arithmetic: 0.97 us -> 0.09 us  [lat_allreduce(): out = lax.dynamic_update_slice_in_dim(out, mine, index * size, axis=dim)]
    unnamed x9 -> x11, local copies, waits for them, and re-layouts: 1.48 us -> 1.49 us
  transfers between devices with their start and end apart: 15 -> 15, of which waited for: 5 -> 5; matrix products, arithmetic and copies ran while one was open for 14% -> 12% of each run, Pallas kernels for 23% -> 23%
where the time goes in v22:
time: 62.2 us; the launch traced here: 61.8 us
  starting transfers between devices  23.5 us (38%)
  Pallas kernels  14 us (23%)
  waiting for transfers between devices  12.4 us (20%)
  other arithmetic  6.41 us (10%)
  local copies, waits for them, and re-layouts  3.59 us (6%)
  between operations  1.63 us (3%)
    pallas_call x1, Pallas kernels, row_products(): pl.pallas_call(row_kernel, out_shape=(jax.ShapeDtypeStruct((weights.shape...  8.55 us
    pallas_call x1, Pallas kernels, toeplitz(): pl.pallas_call(toeplitz_kernel, out_shape=(jax.ShapeDtypeStruct((kernels,...  5.48 us
    ppermute x1, starting transfers between devices, body(): below = lax.ppermute(row, 'lat', [(i, i + 1) for i in range(count - 1)])  5.08 us
    ppermute x3, waiting for transfers between devices, lat_allreduce(): recv = lax.ppermute(mine, axis, [(i, i ^ d) for i in range(count)])  4.93 us
    ppermute x1, waiting for transfers between devices, body(): above = lax.ppermute(row, 'lat', [(i + 1, i) for i in range(count - 1)])  4.69 us
    ppermute x3, starting transfers between devices, body(): lax.ppermute(jnp.concatenate([fields[:, 0], part], axis=0), 'lon', [(p, (...  4.66 us
    ppermute x2, starting transfers between devices, padded_2(): lax.ppermute(tail, axis, [(i, (i + 1) % count) for i in range(ends)])  4.17 us
    ppermute x2, starting transfers between devices, padded_2(): lax.ppermute(head, axis, [((i + 1) % count, i) for i in range(ends)])  3.47 us
  transfers between devices with their start and end apart: 15, of which 5 were waited for; matrix products, arithmetic and copies ran while one was open for 12% of the time, Pallas kernels for 23%

profile of v22, /device:TPU:1, one launch (start us, length us, event | category | flops | bytes accessed | tf_op | source)
XLA Modules:
  0.0 61.8 jit_solution(8915756663770778491)
XLA Ops:
  0.7 0.8 %dynamic-slice_bitcast_fusion = (bf16[1,64,128]{2,1,0:T(8,128)(2,1)S(1)}, bf16[64,128]{1,0:T(8,128)(2,1)S(1)}, bf16[64,128]{1,0:T(8,128)(2,1)S(1)}, bf16[64,128]{1,0:T(8,128)(2,1)S(1)}) fusion(bf16[256,1,128]{2,0,1:T(8,128)(2,1)} %param.23, s32[]{:T(128)S(6)} %select_n.91, s32[]{:T(128)S(6)} %select_n.89, s32[]{:T(128)S(6)} %select_n.87, s32[]{:T(128)S(6)} %select_n.85), kind=kLoop, calls=%fused_computation.39 | loop fusion | bytes 131088 | tf_op jit(solution)/shard_map/stack | solution.py:176
  1.5 0.9 %pad_maximum_fusion.5 = (bf16[320,128]{1,0:T(8,128)(2,1)S(1)}, bf16[320,128]{1,0:T(8,128)(2,1)S(1)}, bf16[320,128]{1,0:T(8,128)(2,1)S(1)}) fusion(bf16[64,128]{1,0:T(8,128)(2,1)S(1)} %get-tuple-element.109, bf16[256,128]{1,0:T(8,128)(2,1)} %bitcast.49, bf16[64,128]{1,0:T(8,128)(2,1)S(1)} %get-tuple-element.108, bf16[64,128]{1,0:T(8,128)(2,1)S(1)} %get-tuple-element.107), kind=kLoop, calls=%fused_computation.24 | loop fusion | flops 409600 | bytes 360448 | tf_op jit(solution)/shard_map/concatenate | solution.py:170
  2.4 4.2 %collective-permute-start = (bf16[320,128]{1,0:T(8,128)(2,1)S(1)}, bf16[320,128]{1,0:T(8,128)(2,1)S(1)}, u32[]{:S(2)}, u32[]{:S(2)}) collective-permute-start(bf16[320,128]{1,0:T(8,128)(2,1)S(1)} %get-tuple-element.110), channel_id=1, source_target_pairs={{0,3},{1,0},{2,1},{3,2},{4,7},{5,4},{6,5},{7,6},{8,11},{9,8},{10,9... | collective-permute-start | bytes 245768 | tf_op jit(solution)/shard_map/ppermute | solution.py:169
  6.6 0.5 collective-permute-start.2
  7.0 0.7 %add_bitcast_fusion = s32[2]{0:T(128)S(1)} fusion(s32[1,2]{1,0:T(1,128)} %param.27), kind=kLoop, calls=%fused_computation.49 | loop fusion | flops 4 | bytes 16 | tf_op jit(solution)/shard_map/add | solution.py:32
  8.4 0.2 fusion.3
  8.7 0.6 %copy.13 = bf16[2,8,3,384]{3,1,2,0:T(8,128)(2,1)} copy(bf16[2,8,3,384]{3,2,1,0:T(4,128)(2,1)S(1)} %bitcast.51) | data formatting | bytes 73728
  9.3 5.5 %shard_map.100 = (bf16[9,128,1152]{2,1,0:T(8,128)(2,1)}, f32[3,256,384]{2,1,0:T(8,128)}) custom-call(bf16[9,1152]{1,0:T(8,128)(2,1)} %bitcast.52, bf16[9,256,256]{2,1,0:T(8,128)(2,1)} %w_ref.3, bf16[256,128]{1,0:T(8,128)(2,1)} %bitcast.48), custom_call_target="tpu_custom_call" | custom-call | tf_op jit(solution)/shard_map/pallas_call | solution.py:64
  14.8 1.2 %fusion.19 = (f32[256,3,128]{2,0,1:T(8,128)S(1)}, f32[256,3,128]{2,0,1:T(8,128)S(1)}) fusion(f32[256,3,384]{2,0,1:T(8,128)} %bitcast.44), kind=kLoop, calls=%fused_computation.53 | loop fusion | bytes 1572864 | tf_op jit(solution)/shard_map/slice | solution.py:192
  16.0 2.3 %collective-permute-start.5 = (f32[256,3,128]{2,0,1:T(8,128)S(1)}, f32[256,3,128]{2,0,1:T(8,128)S(1)}, u32[]{:S(2)}, u32[]{:S(2)}) collective-permute-start(f32[256,3,128]{2,0,1:T(8,128)S(1)} %get-tuple-element.97), channel_id=1, source_target_pairs={{0,1},{1,2},{2,3},{3,0},{4,5},{5,6},{6,7},{7,4},{8,9},{9,10},{10,1... | collective-permute-start | bytes 1179656 | tf_op jit(solution)/shard_map/ppermute | solution.py:19
  18.3 1.1 %collective-permute-start.6 = (f32[256,3,128]{2,0,1:T(8,128)S(1)}, f32[256,3,128]{2,0,1:T(8,128)S(1)}, u32[]{:S(2)}, u32[]{:S(2)}) collective-permute-start(f32[256,3,128]{2,0,1:T(8,128)S(1)} %get-tuple-element.98), channel_id=1, source_target_pairs={{1,0},{2,1},{3,2},{0,3},{5,4},{6,5},{7,6},{4,7},{9,8},{10,9},{11,1... | collective-permute-start | bytes 1179656 | tf_op jit(solution)/shard_map/ppermute | solution.py:21
  19.4 5.1 %collective-permute-start.3 = (bf16[256,512]{1,0:T(8,128)(2,1)S(1)}, bf16[256,512]{1,0:T(8,128)(2,1)S(1)}, u32[]{:S(2)}, u32[]{:S(2)}) collective-permute-start(bf16[256,512]{1,0:T(8,128)(2,1)S(1)} %get-tuple-element.105), channel_id=1, source_target_pairs={{0,4},{4,8},{8,12},{1,5},{5,9},{9,13},{2,6},{6,10},{10,14},{3,7},{... | collective-permute-start | bytes 786440 | tf_op jit(solution)/shard_map/ppermute | solution.py:179
  24.5 1.9 %collective-permute-start.4 = (bf16[256,512]{1,0:T(8,128)(2,1)S(1)}, bf16[256,512]{1,0:T(8,128)(2,1)S(1)}, u32[]{:S(2)}, u32[]{:S(2)}) collective-permute-start(bf16[256,512]{1,0:T(8,128)(2,1)S(1)} %get-tuple-element.105), channel_id=1, source_target_pairs={{4,0},{8,4},{12,8},{5,1},{9,5},{13,9},{6,2},{10,6},{14,10},{7,3},{... | collective-permute-start | bytes 786440 | tf_op jit(solution)/shard_map/ppermute | solution.py:180
  26.5 0.6 %pad_maximum_fusion.8.up_ref = bf16[4,64,128]{2,1,0:T(8,128)(2,1)} fusion(bf16[1,64,128]{2,1,0:T(8,128)(2,1)S(1)} %slice_bitcast_fusion, bf16[1,64,128]{2,1,0:T(8,128)(2,1)S(1)} %slice_bitcast_fusion.1, bf16[1,64,128]{2,1,0:T(8,128)(2,1)S(1)} %slice_bitcast_fusion.2, bf16[1,64,128]{2,1,0:T(8,128)(2,1)S(1)} %get-tuple-element.106), kind=kLoop, calls=%fused_computation.30 | loop fusion | flops 98304 | bytes 131072 | tf_op jit(solution)/shard_map/stack | solution.py:176
  27.1 0.7 %collective-permute-done.3 = bf16[256,512]{1,0:T(8,128)(2,1)S(1)} collective-permute-done((bf16[256,512]{1,0:T(8,128)(2,1)S(1)}, bf16[256,512]{1,0:T(8,128)(2,1)S(1)}, u32[]{:S(2)}, u32[]{:S(2)}) %collective-permute-start.3) | collective-permute-done | bytes 262176 | tf_op jit(solution)/shard_map/ppermute | solution.py:179
  27.8 4.7 %collective-permute-done.4 = bf16[256,512]{1,0:T(8,128)(2,1)S(1)} collective-permute-done((bf16[256,512]{1,0:T(8,128)(2,1)S(1)}, bf16[256,512]{1,0:T(8,128)(2,1)S(1)}, u32[]{:S(2)}, u32[]{:S(2)}) %collective-permute-start.4) | collective-permute-done | bytes 262176 | tf_op jit(solution)/shard_map/ppermute | solution.py:180
  32.5 1.1 %fusion.ext_ref = bf16[3,256,768]{2,1,0:T(8,128)(2,1)} fusion(bf16[1,256,512]{2,1,0:T(8,128)(2,1)S(1)} %bitcast.47, bf16[1,256,512]{2,1,0:T(8,128)(2,1)S(1)} %get-tuple-element.104, bf16[1,256,512]{2,1,0:T(8,128)(2,1)S(1)} %bitcast.46), kind=kLoop, calls=%fused_computation.1 | loop fusion | flops 10616832 | bytes 1966080 | tf_op jit(solution)/shard_map/concatenate | solution.py:182
  33.6 8.5 %shard_map.101 = (bf16[256,128]{1,0:T(8,128)(2,1)}, f32[9,64,256]{2,1,0:T(8,128)}) custom-call(bf16[3,256,768]{2,1,0:T(8,128)(2,1)} %fusion.ext_ref, bf16[1152,1152]{1,0:T(8,128)(2,1)} %bitcast.53, bf16[9,256,256]{2,1,0:T(8,128)(2,1)} %w_ref.3, bf16[4,64,128]{2,1,0:T(8,128)(2,1)} %pad_maximum_fusion.8.up_ref), custom_call_target="tpu_custom_call" | custom-call | flops 3019898880 | bytes 5734400 | tf_op jit(solution)/shard_map/pallas_call | solution.py:145
  42.1 1.2 %broadcast_select_fusion.2 = (f32[9,16,256]{2,1,0:T(8,128)S(1)}, f32[9,16,256]{2,1,0:T(8,128)S(1)}, f32[9,16,256]{2,1,0:T(8,128)S(1)}) fusion(pred[]{:T(512)S(6)} %eq.29, f32[9,64,256]{2,1,0:T(8,128)} %get-tuple-element.94, pred[]{:T(512)S(6)} %eq.30), kind=kLoop, calls=%fused_computation.29 | loop fusion | flops 258048 | bytes 1032194 | tf_op jit(solution)/shard_map/jit(_where)/select_n | solution.py:84
  43.6 1.8 %collective-permute-start.9 = (f32[9,16,256]{2,1,0:T(8,128)S(1)}, f32[9,16,256]{2,1,0:T(8,128)S(1)}, u32[]{:S(2)}, u32[]{:S(2)}) collective-permute-start(f32[9,16,256]{2,1,0:T(8,128)S(1)} %get-tuple-element.99), channel_id=1, source_target_pairs={{0,4},{4,0},{8,12},{12,8},{1,5},{5,1},{9,13},{13,9},{2,6},{6,2},{1... | collective-permute-start | bytes 442376 | tf_op jit(solution)/shard_map/ppermute | solution.py:87
  45.3 1.1 %fusion.4 = f32[256,3,128]{2,0,1:T(8,128)S(1)} fusion(f32[256,3,128]{2,0,1:T(8,128)S(1)} %collective-permute-done.6, f32[256,3,128]{2,0,1:T(8,128)S(1)} %collective-permute-done.5, f32[256,3,384]{2,0,1:T(8,128)} %bitcast.45), kind=kLoop, calls=%fused_computation.10 | loop fusion | flops 196608 | bytes 1572864 | tf_op jit(solution)/shard_map/add | solution.py:197
  46.4 1.9 %collective-permute-start.7 = (f32[256,1,128]{2,0,1:T(8,128)S(1)}, f32[256,1,128]{2,0,1:T(8,128)S(1)}, u32[]{:S(2)}, u32[]{:S(2)}) collective-permute-start(f32[256,1,128]{2,0,1:T(8,128)S(1)} %get-tuple-element.102), channel_id=1, source_target_pairs={{0,4},{4,8},{8,12},{1,5},{5,9},{9,13},{2,6},{6,10},{10,14},{3,7},{... | collective-permute-start | bytes 393224 | tf_op jit(solution)/shard_map/ppermute | solution.py:19
  48.3 2.4 %collective-permute-start.8 = (f32[256,1,128]{2,0,1:T(8,128)S(1)}, f32[256,1,128]{2,0,1:T(8,128)S(1)}, u32[]{:S(2)}, u32[]{:S(2)}) collective-permute-start(f32[256,1,128]{2,0,1:T(8,128)S(1)} %get-tuple-element.103), channel_id=1, source_target_pairs={{4,0},{8,4},{12,8},{5,1},{9,5},{13,9},{6,2},{10,6},{14,10},{7,3},{... | collective-permute-start | bytes 393224 | tf_op jit(solution)/shard_map/ppermute | solution.py:21
  50.8 0.1 constant_dynamic-update-slice_fusion.3
  50.9 0.6 collective-permute-start.12
  51.5 1.5 %collective-permute-start.13 = (f32[9,16,256]{2,1,0:T(8,128)S(1)}, f32[9,16,256]{2,1,0:T(8,128)S(1)}, u32[]{:S(2)}, u32[]{:S(2)}) collective-permute-start(f32[9,16,256]{2,1,0:T(8,128)S(1)} %get-tuple-element.96), channel_id=1, source_target_pairs={{0,8},{4,12},{8,0},{12,4},{1,9},{5,13},{9,1},{13,5},{2,10},{6,14},... | collective-permute-start | bytes 442376 | tf_op jit(solution)/shard_map/ppermute | solution.py:94
  53.0 0.3 collective-permute-start.14
  53.3 2.1 %collective-permute-done.8 = f32[256,1,128]{2,0,1:T(8,128)S(1)} collective-permute-done((f32[256,1,128]{2,0,1:T(8,128)S(1)}, f32[256,1,128]{2,0,1:T(8,128)S(1)}, u32[]{:S(2)}, u32[]{:S(2)}) %collective-permute-start.8) | collective-permute-done | bytes 131104 | tf_op jit(solution)/shard_map/ppermute | solution.py:21
  55.3 0.7 %fusion.6 = bf16[256,1,128]{2,0,1:T(8,128)(2,1)} fusion(f32[256,1,128]{2,0,1:T(8,128)S(1)} %collective-permute-done.8, f32[256,1,128]{2,0,1:T(8,128)S(1)} %collective-permute-done.7, f32[256,3,128]{2,0,1:T(8,128)S(1)} %fusion.4), kind=kLoop, calls=%fused_computation.19 | loop fusion | flops 98304 | bytes 458752 | tf_op jit(solution)/shard_map/convert_element_type | solution.py:203
  56.0 1.4 %collective-permute-done.13 = f32[9,16,256]{2,1,0:T(8,128)S(1)} collective-permute-done((f32[9,16,256]{2,1,0:T(8,128)S(1)}, f32[9,16,256]{2,1,0:T(8,128)S(1)}, u32[]{:S(2)}, u32[]{:S(2)}) %collective-permute-start.13) | collective-permute-done | bytes 147488 | tf_op jit(solution)/shard_map/ppermute | solution.py:94
  57.4 3.5 %collective-permute-done.14 = f32[9,16,256]{2,1,0:T(8,128)S(1)} collective-permute-done((f32[9,16,256]{2,1,0:T(8,128)S(1)}, f32[9,16,256]{2,1,0:T(8,128)S(1)}, u32[]{:S(2)}, u32[]{:S(2)}) %collective-permute-start.14) | collective-permute-done | bytes 147488 | tf_op jit(solution)/shard_map/ppermute | solution.py:94
  61.0 0.8 %copy-done.2 = f32[9,64,256]{2,1,0:T(8,128)} copy-done((f32[9,64,256]{2,1,0:T(8,128)}, f32[9,64,256]{2,1,0:T(8,128)S(1)}, u32[]{:S(2)}) %copy-start.2) | copy-done | bytes 589848
  (37 shorter events, 0.5 us)
Async XLA Ops:
  0.6 7.8 %copy-start = (bf16[1,9,3,2,64]{4,3,2,1,0:T(2,128)(2,1)S(1)}, bf16[1,9,3,2,64]{4,3,2,1,0:T(2,128)(2,1)}, u32[]{:S(2)}) copy-start(bf16[1,9,3,2,64]{4,3,2,1,0:T(2,128)(2,1)} %param.25) | copy-start | bytes 20740
  0.6 18.7 %copy-start.3 = (bf16[256,1,128]{2,0,1:T(8,128)(2,1)S(1)}, bf16[256,1,128]{2,0,1:T(8,128)(2,1)}, u32[]{:S(2)}) copy-start(bf16[256,1,128]{2,0,1:T(8,128)(2,1)} %param.22) | copy-start | bytes 196612
  2.4 16.9 %collective-permute-start = (bf16[320,128]{1,0:T(8,128)(2,1)S(1)}, bf16[320,128]{1,0:T(8,128)(2,1)S(1)}, u32[]{:S(2)}, u32[]{:S(2)}) collective-permute-start(bf16[320,128]{1,0:T(8,128)(2,1)S(1)} %get-tuple-element.110), channel_id=1, source_target_pairs={{0,3},{1,0},{2,1},{3,2},{4,7},{5,4},{6,5},{7,6},{8,11},{9,8},{10,9... | collective-permute-start | bytes 245768 | tf_op jit(solution)/shard_map/ppermute | solution.py:169
  6.6 12.7 %collective-permute-start.1 = (bf16[320,128]{1,0:T(8,128)(2,1)S(1)}, bf16[320,128]{1,0:T(8,128)(2,1)S(1)}, u32[]{:S(2)}, u32[]{:S(2)}) collective-permute-start(bf16[320,128]{1,0:T(8,128)(2,1)S(1)} %get-tuple-element.111), channel_id=1, source_target_pairs={{0,2},{1,3},{2,0},{3,1},{4,6},{5,7},{6,4},{7,5},{8,10},{9,11},{10,... | collective-permute-start | bytes 245768 | tf_op jit(solution)/shard_map/ppermute | solution.py:169
  6.6 12.8 %collective-permute-start.2 = (bf16[320,128]{1,0:T(8,128)(2,1)S(1)}, bf16[320,128]{1,0:T(8,128)(2,1)S(1)}, u32[]{:S(2)}, u32[]{:S(2)}) collective-permute-start(bf16[320,128]{1,0:T(8,128)(2,1)S(1)} %get-tuple-element.112), channel_id=1, source_target_pairs={{0,1},{1,2},{2,3},{3,0},{4,5},{5,6},{6,7},{7,4},{8,9},{9,10},{10,1... | collective-permute-start | bytes 245768 | tf_op jit(solution)/shard_map/ppermute | solution.py:169
  16.0 29.3 %collective-permute-start.5 = (f32[256,3,128]{2,0,1:T(8,128)S(1)}, f32[256,3,128]{2,0,1:T(8,128)S(1)}, u32[]{:S(2)}, u32[]{:S(2)}) collective-permute-start(f32[256,3,128]{2,0,1:T(8,128)S(1)} %get-tuple-element.97), channel_id=1, source_target_pairs={{0,1},{1,2},{2,3},{3,0},{4,5},{5,6},{6,7},{7,4},{8,9},{9,10},{10,1... | collective-permute-start | bytes 1179656 | tf_op jit(solution)/shard_map/ppermute | solution.py:19
  18.3 27.1 %collective-permute-start.6 = (f32[256,3,128]{2,0,1:T(8,128)S(1)}, f32[256,3,128]{2,0,1:T(8,128)S(1)}, u32[]{:S(2)}, u32[]{:S(2)}) collective-permute-start(f32[256,3,128]{2,0,1:T(8,128)S(1)} %get-tuple-element.98), channel_id=1, source_target_pairs={{1,0},{2,1},{3,2},{0,3},{5,4},{6,5},{7,6},{4,7},{9,8},{10,9},{11,1... | collective-permute-start | bytes 1179656 | tf_op jit(solution)/shard_map/ppermute | solution.py:21
  19.4 8.4 %collective-permute-start.3 = (bf16[256,512]{1,0:T(8,128)(2,1)S(1)}, bf16[256,512]{1,0:T(8,128)(2,1)S(1)}, u32[]{:S(2)}, u32[]{:S(2)}) collective-permute-start(bf16[256,512]{1,0:T(8,128)(2,1)S(1)} %get-tuple-element.105), channel_id=1, source_target_pairs={{0,4},{4,8},{8,12},{1,5},{5,9},{9,13},{2,6},{6,10},{10,14},{3,7},{... | collective-permute-start | bytes 786440 | tf_op jit(solution)/shard_map/ppermute | solution.py:179
  24.5 8.0 %collective-permute-start.4 = (bf16[256,512]{1,0:T(8,128)(2,1)S(1)}, bf16[256,512]{1,0:T(8,128)(2,1)S(1)}, u32[]{:S(2)}, u32[]{:S(2)}) collective-permute-start(bf16[256,512]{1,0:T(8,128)(2,1)S(1)} %get-tuple-element.105), channel_id=1, source_target_pairs={{4,0},{8,4},{12,8},{5,1},{9,5},{13,9},{6,2},{10,6},{14,10},{7,3},{... | collective-permute-start | bytes 786440 | tf_op jit(solution)/shard_map/ppermute | solution.py:180
  42.1 8.7 %copy-start.1 = (f32[9,64,256]{2,1,0:T(8,128)S(1)}, f32[9,64,256]{2,1,0:T(8,128)}, u32[]{:S(2)}) copy-start(f32[9,64,256]{2,1,0:T(8,128)} %get-tuple-element.94) | copy-start | bytes 1769476
  43.4 7.4 %collective-permute-start.10 = (f32[9,16,256]{2,1,0:T(8,128)S(1)}, f32[9,16,256]{2,1,0:T(8,128)S(1)}, u32[]{:S(2)}, u32[]{:S(2)}) collective-permute-start(f32[9,16,256]{2,1,0:T(8,128)S(1)} %get-tuple-element.100), channel_id=1, source_target_pairs={{0,8},{4,12},{8,0},{12,4},{1,9},{5,13},{9,1},{13,5},{2,10},{6,14},... | collective-permute-start | bytes 442376 | tf_op jit(solution)/shard_map/ppermute | solution.py:87
  43.5 7.3 %collective-permute-start.11 = (f32[9,16,256]{2,1,0:T(8,128)S(1)}, f32[9,16,256]{2,1,0:T(8,128)S(1)}, u32[]{:S(2)}, u32[]{:S(2)}) collective-permute-start(f32[9,16,256]{2,1,0:T(8,128)S(1)} %get-tuple-element.101), channel_id=1, source_target_pairs={{0,12},{4,8},{8,4},{12,0},{1,13},{5,9},{9,5},{13,1},{2,14},{6,10},... | collective-permute-start | bytes 442376 | tf_op jit(solution)/shard_map/ppermute | solution.py:87
  43.6 7.2 %collective-permute-start.9 = (f32[9,16,256]{2,1,0:T(8,128)S(1)}, f32[9,16,256]{2,1,0:T(8,128)S(1)}, u32[]{:S(2)}, u32[]{:S(2)}) collective-permute-start(f32[9,16,256]{2,1,0:T(8,128)S(1)} %get-tuple-element.99), channel_id=1, source_target_pairs={{0,4},{4,0},{8,12},{12,8},{1,5},{5,1},{9,13},{13,9},{2,6},{6,2},{1... | collective-permute-start | bytes 442376 | tf_op jit(solution)/shard_map/ppermute | solution.py:87
  46.4 6.9 %collective-permute-start.7 = (f32[256,1,128]{2,0,1:T(8,128)S(1)}, f32[256,1,128]{2,0,1:T(8,128)S(1)}, u32[]{:S(2)}, u32[]{:S(2)}) collective-permute-start(f32[256,1,128]{2,0,1:T(8,128)S(1)} %get-tuple-element.102), channel_id=1, source_target_pairs={{0,4},{4,8},{8,12},{1,5},{5,9},{9,13},{2,6},{6,10},{10,14},{3,7},{... | collective-permute-start | bytes 393224 | tf_op jit(solution)/shard_map/ppermute | solution.py:19
  48.3 7.0 %collective-permute-start.8 = (f32[256,1,128]{2,0,1:T(8,128)S(1)}, f32[256,1,128]{2,0,1:T(8,128)S(1)}, u32[]{:S(2)}, u32[]{:S(2)}) collective-permute-start(f32[256,1,128]{2,0,1:T(8,128)S(1)} %get-tuple-element.103), channel_id=1, source_target_pairs={{4,0},{8,4},{12,8},{5,1},{9,5},{13,9},{6,2},{10,6},{14,10},{7,3},{... | collective-permute-start | bytes 393224 | tf_op jit(solution)/shard_map/ppermute | solution.py:21
  50.9 5.0 %collective-permute-start.12 = (f32[9,16,256]{2,1,0:T(8,128)S(1)}, f32[9,16,256]{2,1,0:T(8,128)S(1)}, u32[]{:S(2)}, u32[]{:S(2)}) collective-permute-start(f32[9,16,256]{2,1,0:T(8,128)S(1)} %get-tuple-element.96), channel_id=1, source_target_pairs={{0,4},{4,0},{8,12},{12,8},{1,5},{5,1},{9,13},{13,9},{2,6},{6,2},{1... | collective-permute-start | bytes 442376 | tf_op jit(solution)/shard_map/ppermute | solution.py:94
  51.5 5.8 %collective-permute-start.13 = (f32[9,16,256]{2,1,0:T(8,128)S(1)}, f32[9,16,256]{2,1,0:T(8,128)S(1)}, u32[]{:S(2)}, u32[]{:S(2)}) collective-permute-start(f32[9,16,256]{2,1,0:T(8,128)S(1)} %get-tuple-element.96), channel_id=1, source_target_pairs={{0,8},{4,12},{8,0},{12,4},{1,9},{5,13},{9,1},{13,5},{2,10},{6,14},... | collective-permute-start | bytes 442376 | tf_op jit(solution)/shard_map/ppermute | solution.py:94
  53.0 7.9 %collective-permute-start.14 = (f32[9,16,256]{2,1,0:T(8,128)S(1)}, f32[9,16,256]{2,1,0:T(8,128)S(1)}, u32[]{:S(2)}, u32[]{:S(2)}) collective-permute-start(f32[9,16,256]{2,1,0:T(8,128)S(1)} %get-tuple-element.96), channel_id=1, source_target_pairs={{0,12},{4,8},{8,4},{12,0},{1,13},{5,9},{9,5},{13,1},{2,14},{6,10},... | collective-permute-start | bytes 442376 | tf_op jit(solution)/shard_map/ppermute | solution.py:94
  61.0 0.8 %copy-start.2 = (f32[9,64,256]{2,1,0:T(8,128)}, f32[9,64,256]{2,1,0:T(8,128)S(1)}, u32[]{:S(2)}) copy-start(f32[9,64,256]{2,1,0:T(8,128)S(1)} %constant_dynamic-update-slice_fusion) | copy-start | bytes 1769476

commit v23 on v22

--- a/solution.py
+++ b/solution.py
@@ -88,12 +88,13 @@
     for s in range(steps):
         parts = [parts[2 * e] + parts[2 * e + 1] for e in range(len(parts) // 2)]
     mine = parts[0]
-    out = jnp.zeros(x.shape, x.dtype)
-    out = lax.dynamic_update_slice_in_dim(out, mine, index * size, axis=dim)
-    for d in range(1, count):
-        recv = lax.ppermute(mine, axis, [(i, i ^ d) for i in range(count)])
-        out = lax.dynamic_update_slice_in_dim(out, recv, (index ^ d) * size, axis=dim)
-    return out
+    gathered = [mine] + [
+        lax.ppermute(mine, axis, [(i, i ^ d) for i in range(count)]) for d in range(1, count)
+    ]
+    for s in range(steps):
+        flip = ((index >> s) & 1) == 1
+        gathered = [jnp.where(flip, gathered[c ^ (1 << s)], gathered[c]) for c in range(count)]
+    return jnp.concatenate(gathered, axis=dim)
 
 
 def row_kernel(ext_ref, mt_ref, w_ref, up_ref, out_ref, gt_ref):

time: 62.2 us -> 62.9 us (1.011)
  the two profiles are of different devices: /device:TPU:1 before, /device:TPU:0 now
where the time goes in v23:
time: 62.9 us; the launch traced here: 62.5 us
  starting transfers between devices  24.7 us (39%)
  Pallas kernels  14 us (22%)
  waiting for transfers between devices  11.9 us (19%)
  other arithmetic  7.33 us (12%)
  local copies, waits for them, and re-layouts  2.69 us (4%)
  between operations  1.57 us (2%)
    pallas_call x1, Pallas kernels, row_products(): pl.pallas_call(row_kernel, out_shape=(jax.ShapeDtypeStruct((weights.shape...  8.55 us
    ppermute x3, waiting for transfers between devices, lat_allreduce(): lax.ppermute(mine, axis, [(i, i ^ d) for i in range(count)])  7.61 us
    ppermute x3, starting transfers between devices, lat_allreduce(): lax.ppermute(chunks[d], axis, [(i, i ^ d) for i in range(count)])  6.47 us
    ppermute x3, starting transfers between devices, body(): lax.ppermute(jnp.concatenate([fields[:, 0], part], axis=0), 'lon', [(p, (...  6.11 us
    pallas_call x1, Pallas kernels, toeplitz(): pl.pallas_call(toeplitz_kernel, out_shape=(jax.ShapeDtypeStruct((kernels,...  5.49 us
    ppermute x2, starting transfers between devices, padded_2(): lax.ppermute(tail, axis, [(i, (i + 1) % count) for i in range(ends)])  4.94 us
    ppermute x1, waiting for transfers between devices, body(): above = lax.ppermute(row, 'lat', [(i + 1, i) for i in range(count - 1)])  3.16 us
    ppermute x2, starting transfers between devices, padded_2(): lax.ppermute(head, axis, [((i + 1) % count, i) for i in range(ends)])  2.65 us
  transfers between devices with their start and end apart: 15, of which 4 were waited for; matrix products, arithmetic and copies ran while one was open for 12% of the time, Pallas kernels for 22%

profile of v23, /device:TPU:0, one launch (start us, length us, event | category | flops | bytes accessed | tf_op | source)
XLA Modules:
  0.0 62.5 jit_solution(3940761447983514521)
XLA Ops:
  0.7 0.8 %dynamic-slice_bitcast_fusion = (bf16[1,64,128]{2,1,0:T(8,128)(2,1)S(1)}, bf16[64,128]{1,0:T(8,128)(2,1)S(1)}, bf16[64,128]{1,0:T(8,128)(2,1)S(1)}, bf16[64,128]{1,0:T(8,128)(2,1)S(1)}) fusion(bf16[256,1,128]{2,0,1:T(8,128)(2,1)} %param.23, s32[]{:T(128)S(6)} %select_n.111, s32[]{:T(128)S(6)} %select_n.109, s32[]{:T(128)S(6)} %select_n.107, s32[]{:T(128)S(6)} %select_n.105), kind=kLoop, calls=%fused_computation.48 | loop fusion | bytes 131088 | tf_op jit(solution)/shard_map/stack | solution.py:177
  1.5 0.9 %pad_maximum_fusion.6 = (bf16[320,128]{1,0:T(8,128)(2,1)S(1)}, bf16[320,128]{1,0:T(8,128)(2,1)S(1)}, bf16[320,128]{1,0:T(8,128)(2,1)S(1)}) fusion(bf16[64,128]{1,0:T(8,128)(2,1)S(1)} %get-tuple-element.111, bf16[256,128]{1,0:T(8,128)(2,1)} %bitcast.49, bf16[64,128]{1,0:T(8,128)(2,1)S(1)} %get-tuple-element.110, bf16[64,128]{1,0:T(8,128)(2,1)S(1)} %get-tuple-element.109), kind=kLoop, calls=%fused_computation.25 | loop fusion | flops 409600 | bytes 360448 | tf_op jit(solution)/shard_map/concatenate | solution.py:171
  2.4 5.1 %collective-permute-start = (bf16[320,128]{1,0:T(8,128)(2,1)S(1)}, bf16[320,128]{1,0:T(8,128)(2,1)S(1)}, u32[]{:S(2)}, u32[]{:S(2)}) collective-permute-start(bf16[320,128]{1,0:T(8,128)(2,1)S(1)} %get-tuple-element.112), channel_id=1, source_target_pairs={{0,3},{1,0},{2,1},{3,2},{4,7},{5,4},{6,5},{7,6},{8,11},{9,8},{10,9... | collective-permute-start | bytes 245768 | tf_op jit(solution)/shard_map/ppermute | solution.py:170
  7.5 1.0 %collective-permute-start.2 = (bf16[320,128]{1,0:T(8,128)(2,1)S(1)}, bf16[320,128]{1,0:T(8,128)(2,1)S(1)}, u32[]{:S(2)}, u32[]{:S(2)}) collective-permute-start(bf16[320,128]{1,0:T(8,128)(2,1)S(1)} %get-tuple-element.114), channel_id=1, source_target_pairs={{0,1},{1,2},{2,3},{3,0},{4,5},{5,6},{6,7},{7,4},{8,9},{9,10},{10,1... | collective-permute-start | bytes 245768 | tf_op jit(solution)/shard_map/ppermute | solution.py:170
  8.5 0.7 %add_bitcast_fusion = s32[2]{0:T(128)S(1)} fusion(s32[1,2]{1,0:T(1,128)} %param.27), kind=kLoop, calls=%fused_computation.54 | loop fusion | flops 4 | bytes 16 | tf_op jit(solution)/shard_map/add | solution.py:32
  9.9 0.2 fusion.3
  10.2 0.6 copy.13
  10.8 5.5 %shard_map.100 = (bf16[9,128,1152]{2,1,0:T(8,128)(2,1)}, f32[3,256,384]{2,1,0:T(8,128)}) custom-call(bf16[9,1152]{1,0:T(8,128)(2,1)} %bitcast.52, bf16[9,256,256]{2,1,0:T(8,128)(2,1)} %w_ref.3, bf16[256,128]{1,0:T(8,128)(2,1)} %bitcast.48), custom_call_target="tpu_custom_call" | custom-call | tf_op jit(solution)/shard_map/pallas_call | solution.py:64
  16.3 1.2 %fusion.19 = (f32[256,3,128]{2,0,1:T(8,128)S(1)}, f32[256,3,128]{2,0,1:T(8,128)S(1)}) fusion(f32[256,3,384]{2,0,1:T(8,128)} %bitcast.44), kind=kLoop, calls=%fused_computation.58 | loop fusion | bytes 1572864 | tf_op jit(solution)/shard_map/slice | solution.py:193
  17.5 2.5 %collective-permute-start.5 = (f32[256,3,128]{2,0,1:T(8,128)S(1)}, f32[256,3,128]{2,0,1:T(8,128)S(1)}, u32[]{:S(2)}, u32[]{:S(2)}) collective-permute-start(f32[256,3,128]{2,0,1:T(8,128)S(1)} %get-tuple-element.95), channel_id=1, source_target_pairs={{0,1},{1,2},{2,3},{3,0},{4,5},{5,6},{6,7},{7,4},{8,9},{9,10},{10,1... | collective-permute-start | bytes 1179656 | tf_op jit(solution)/shard_map/ppermute | solution.py:19
  20.0 1.4 %collective-permute-start.6 = (f32[256,3,128]{2,0,1:T(8,128)S(1)}, f32[256,3,128]{2,0,1:T(8,128)S(1)}, u32[]{:S(2)}, u32[]{:S(2)}) collective-permute-start(f32[256,3,128]{2,0,1:T(8,128)S(1)} %get-tuple-element.96), channel_id=1, source_target_pairs={{1,0},{2,1},{3,2},{0,3},{5,4},{6,5},{7,6},{4,7},{9,8},{10,9},{11,1... | collective-permute-start | bytes 1179656 | tf_op jit(solution)/shard_map/ppermute | solution.py:21
  21.5 1.3 %collective-permute-start.3 = (bf16[256,512]{1,0:T(8,128)(2,1)S(1)}, bf16[256,512]{1,0:T(8,128)(2,1)S(1)}, u32[]{:S(2)}, u32[]{:S(2)}) collective-permute-start(bf16[256,512]{1,0:T(8,128)(2,1)S(1)} %get-tuple-element.107), channel_id=1, source_target_pairs={{0,4},{4,8},{8,12},{1,5},{5,9},{9,13},{2,6},{6,10},{10,14},{3,7},{... | collective-permute-start | bytes 786440 | tf_op jit(solution)/shard_map/ppermute | solution.py:180
  22.8 1.3 %collective-permute-start.4 = (bf16[256,512]{1,0:T(8,128)(2,1)S(1)}, bf16[256,512]{1,0:T(8,128)(2,1)S(1)}, u32[]{:S(2)}, u32[]{:S(2)}) collective-permute-start(bf16[256,512]{1,0:T(8,128)(2,1)S(1)} %get-tuple-element.107), channel_id=1, source_target_pairs={{4,0},{8,4},{12,8},{5,1},{9,5},{13,9},{6,2},{10,6},{14,10},{7,3},{... | collective-permute-start | bytes 786440 | tf_op jit(solution)/shard_map/ppermute | solution.py:181
  24.1 0.6 %pad_maximum_fusion.9.up_ref = bf16[4,64,128]{2,1,0:T(8,128)(2,1)} fusion(bf16[1,64,128]{2,1,0:T(8,128)(2,1)S(1)} %slice_bitcast_fusion, bf16[1,64,128]{2,1,0:T(8,128)(2,1)S(1)} %slice_bitcast_fusion.1, bf16[1,64,128]{2,1,0:T(8,128)(2,1)S(1)} %slice_bitcast_fusion.2, bf16[1,64,128]{2,1,0:T(8,128)(2,1)S(1)} %get-tuple-element.108), kind=kLoop, calls=%fused_computation.39 | loop fusion | flops 98304 | bytes 131072 | tf_op jit(solution)/shard_map/stack | solution.py:177
  24.7 3.2 %collective-permute-done.4 = bf16[256,512]{1,0:T(8,128)(2,1)S(1)} collective-permute-done((bf16[256,512]{1,0:T(8,128)(2,1)S(1)}, bf16[256,512]{1,0:T(8,128)(2,1)S(1)}, u32[]{:S(2)}, u32[]{:S(2)}) %collective-permute-start.4) | collective-permute-done | bytes 262176 | tf_op jit(solution)/shard_map/ppermute | solution.py:181
  27.9 1.1 %fusion.ext_ref = bf16[3,256,768]{2,1,0:T(8,128)(2,1)} fusion(bf16[1,256,512]{2,1,0:T(8,128)(2,1)S(1)} %bitcast.47, bf16[1,256,512]{2,1,0:T(8,128)(2,1)S(1)} %get-tuple-element.106, bf16[1,256,512]{2,1,0:T(8,128)(2,1)S(1)} %bitcast.46), kind=kLoop, calls=%fused_computation.1 | loop fusion | flops 10616832 | bytes 1966080 | tf_op jit(solution)/shard_map/concatenate | solution.py:183
  29.0 8.6 %shard_map.101 = (bf16[256,128]{1,0:T(8,128)(2,1)}, f32[9,64,256]{2,1,0:T(8,128)}) custom-call(bf16[3,256,768]{2,1,0:T(8,128)(2,1)} %fusion.ext_ref, bf16[1152,1152]{1,0:T(8,128)(2,1)} %bitcast.53, bf16[9,256,256]{2,1,0:T(8,128)(2,1)} %w_ref.3, bf16[4,64,128]{2,1,0:T(8,128)(2,1)} %pad_maximum_fusion.9.up_ref), custom_call_target="tpu_custom_call" | custom-call | flops 3019898880 | bytes 5734400 | tf_op jit(solution)/shard_map/pallas_call | solution.py:146
  37.5 1.2 %broadcast_select_fusion.10 = (f32[9,16,256]{2,1,0:T(8,128)S(1)}, f32[9,16,256]{2,1,0:T(8,128)S(1)}, f32[9,16,256]{2,1,0:T(8,128)S(1)}) fusion(pred[]{:T(512)S(6)} %eq.31, f32[9,64,256]{2,1,0:T(8,128)} %get-tuple-element.94, pred[]{:T(512)S(6)} %eq.32), kind=kLoop, calls=%fused_computation.38 | loop fusion | flops 258048 | bytes 1032194 | tf_op jit(solution)/shard_map/jit(_where)/select_n | solution.py:84
  38.8 4.5 %collective-permute-start.10 = (f32[9,16,256]{2,1,0:T(8,128)S(1)}, f32[9,16,256]{2,1,0:T(8,128)S(1)}, u32[]{:S(2)}, u32[]{:S(2)}) collective-permute-start(f32[9,16,256]{2,1,0:T(8,128)S(1)} %get-tuple-element.102), channel_id=1, source_target_pairs={{0,8},{4,12},{8,0},{12,4},{1,9},{5,13},{9,1},{13,5},{2,10},{6,14},... | collective-permute-start | bytes 442376 | tf_op jit(solution)/shard_map/ppermute | solution.py:87
  43.3 1.9 %collective-permute-start.11 = (f32[9,16,256]{2,1,0:T(8,128)S(1)}, f32[9,16,256]{2,1,0:T(8,128)S(1)}, u32[]{:S(2)}, u32[]{:S(2)}) collective-permute-start(f32[9,16,256]{2,1,0:T(8,128)S(1)} %get-tuple-element.103), channel_id=1, source_target_pairs={{0,12},{4,8},{8,4},{12,0},{1,13},{5,9},{9,5},{13,1},{2,14},{6,10},... | collective-permute-start | bytes 442376 | tf_op jit(solution)/shard_map/ppermute | solution.py:87
  45.3 1.1 %fusion.4 = f32[256,3,128]{2,0,1:T(8,128)S(1)} fusion(f32[256,3,128]{2,0,1:T(8,128)S(1)} %collective-permute-done.6, f32[256,3,128]{2,0,1:T(8,128)S(1)} %collective-permute-done.5, f32[256,3,384]{2,0,1:T(8,128)} %bitcast.45), kind=kLoop, calls=%fused_computation.11 | loop fusion | flops 196608 | bytes 1572864 | tf_op jit(solution)/shard_map/add | solution.py:198
  46.4 2.4 %collective-permute-start.7 = (f32[256,1,128]{2,0,1:T(8,128)S(1)}, f32[256,1,128]{2,0,1:T(8,128)S(1)}, u32[]{:S(2)}, u32[]{:S(2)}) collective-permute-start(f32[256,1,128]{2,0,1:T(8,128)S(1)} %get-tuple-element.104), channel_id=1, source_target_pairs={{0,4},{4,8},{8,12},{1,5},{5,9},{9,13},{2,6},{6,10},{10,14},{3,7},{... | collective-permute-start | bytes 393224 | tf_op jit(solution)/shard_map/ppermute | solution.py:19
  48.8 1.3 %collective-permute-start.8 = (f32[256,1,128]{2,0,1:T(8,128)S(1)}, f32[256,1,128]{2,0,1:T(8,128)S(1)}, u32[]{:S(2)}, u32[]{:S(2)}) collective-permute-start(f32[256,1,128]{2,0,1:T(8,128)S(1)} %get-tuple-element.105), channel_id=1, source_target_pairs={{4,0},{8,4},{12,8},{5,1},{9,5},{13,9},{6,2},{10,6},{14,10},{7,3},{... | collective-permute-start | bytes 393224 | tf_op jit(solution)/shard_map/ppermute | solution.py:21
  50.1 1.2 %collective-permute-done.11 = f32[9,16,256]{2,1,0:T(8,128)S(1)} collective-permute-done((f32[9,16,256]{2,1,0:T(8,128)S(1)}, f32[9,16,256]{2,1,0:T(8,128)S(1)}, u32[]{:S(2)}, u32[]{:S(2)}) %collective-permute-start.11) | collective-permute-done | bytes 147488 | tf_op jit(solution)/shard_map/ppermute | solution.py:87
  51.2 0.1 add_add_fusion
  51.3 1.8 %collective-permute-start.12 = (f32[9,16,256]{2,1,0:T(8,128)S(1)}, f32[9,16,256]{2,1,0:T(8,128)S(1)}, u32[]{:S(2)}, u32[]{:S(2)}) collective-permute-start(f32[9,16,256]{2,1,0:T(8,128)S(1)} %add_add_fusion), channel_id=1, source_target_pairs={{0,12},{4,8},{8,4},{12,0},{1,13},{5,9},{9,5},{13,1},{2,14},{6,10},... | collective-permute-start | bytes 442376 | tf_op jit(solution)/shard_map/ppermute | solution.py:92
  53.1 0.1 collective-permute-start.13
  53.2 0.1 collective-permute-start.14
  53.3 0.7 %fusion.6 = bf16[256,1,128]{2,0,1:T(8,128)(2,1)} fusion(f32[256,1,128]{2,0,1:T(8,128)S(1)} %collective-permute-done.8, f32[256,1,128]{2,0,1:T(8,128)S(1)} %collective-permute-done.7, f32[256,3,128]{2,0,1:T(8,128)S(1)} %fusion.4), kind=kLoop, calls=%fused_computation.20 | loop fusion | flops 98304 | bytes 458752 | tf_op jit(solution)/shard_map/convert_element_type | solution.py:204
  54.0 3.5 %collective-permute-done.12 = f32[9,16,256]{2,1,0:T(8,128)S(1)} collective-permute-done((f32[9,16,256]{2,1,0:T(8,128)S(1)}, f32[9,16,256]{2,1,0:T(8,128)S(1)}, u32[]{:S(2)}, u32[]{:S(2)}) %collective-permute-start.12) | collective-permute-done | bytes 147488 | tf_op jit(solution)/shard_map/ppermute | solution.py:92
  57.5 4.1 %collective-permute-done.13 = f32[9,16,256]{2,1,0:T(8,128)S(1)} collective-permute-done((f32[9,16,256]{2,1,0:T(8,128)S(1)}, f32[9,16,256]{2,1,0:T(8,128)S(1)}, u32[]{:S(2)}, u32[]{:S(2)}) %collective-permute-start.13) | collective-permute-done | bytes 147488 | tf_op jit(solution)/shard_map/ppermute | solution.py:92
  61.7 0.9 %pad_maximum_fusion.4 = f32[9,64,256]{2,1,0:T(8,128)} fusion(f32[9,16,256]{2,1,0:T(8,128)S(1)} %get-tuple-element.100, f32[9,16,256]{2,1,0:T(8,128)S(1)} %get-tuple-element.99, f32[9,16,256]{2,1,0:T(8,128)S(1)} %get-tuple-element.98, f32[9,16,256]{2,1,0:T(8,128)S(1)} %get-tuple-element.97), kind=kLoop, calls=%fused_computation.9 | loop fusion | flops 442368 | bytes 1179648 | tf_op jit(solution)/shard_map/concatenate | solution.py:97
  (33 shorter events, 0.3 us)
Async XLA Ops:
  0.6 9.3 %copy-start = (bf16[1,9,3,2,64]{4,3,2,1,0:T(2,128)(2,1)S(1)}, bf16[1,9,3,2,64]{4,3,2,1,0:T(2,128)(2,1)}, u32[]{:S(2)}) copy-start(bf16[1,9,3,2,64]{4,3,2,1,0:T(2,128)(2,1)} %param.25) | copy-start | bytes 20740
  0.6 20.8 %copy-start.2 = (bf16[256,1,128]{2,0,1:T(8,128)(2,1)S(1)}, bf16[256,1,128]{2,0,1:T(8,128)(2,1)}, u32[]{:S(2)}) copy-start(bf16[256,1,128]{2,0,1:T(8,128)(2,1)} %param.22) | copy-start | bytes 196612
  2.4 19.0 %collective-permute-start = (bf16[320,128]{1,0:T(8,128)(2,1)S(1)}, bf16[320,128]{1,0:T(8,128)(2,1)S(1)}, u32[]{:S(2)}, u32[]{:S(2)}) collective-permute-start(bf16[320,128]{1,0:T(8,128)(2,1)S(1)} %get-tuple-element.112), channel_id=1, source_target_pairs={{0,3},{1,0},{2,1},{3,2},{4,7},{5,4},{6,5},{7,6},{8,11},{9,8},{10,9... | collective-permute-start | bytes 245768 | tf_op jit(solution)/shard_map/ppermute | solution.py:170
  7.5 13.9 %collective-permute-start.1 = (bf16[320,128]{1,0:T(8,128)(2,1)S(1)}, bf16[320,128]{1,0:T(8,128)(2,1)S(1)}, u32[]{:S(2)}, u32[]{:S(2)}) collective-permute-start(bf16[320,128]{1,0:T(8,128)(2,1)S(1)} %get-tuple-element.113), channel_id=1, source_target_pairs={{0,2},{1,3},{2,0},{3,1},{4,6},{5,7},{6,4},{7,5},{8,10},{9,11},{10,... | collective-permute-start | bytes 245768 | tf_op jit(solution)/shard_map/ppermute | solution.py:170
  7.5 13.9 %collective-permute-start.2 = (bf16[320,128]{1,0:T(8,128)(2,1)S(1)}, bf16[320,128]{1,0:T(8,128)(2,1)S(1)}, u32[]{:S(2)}, u32[]{:S(2)}) collective-permute-start(bf16[320,128]{1,0:T(8,128)(2,1)S(1)} %get-tuple-element.114), channel_id=1, source_target_pairs={{0,1},{1,2},{2,3},{3,0},{4,5},{5,6},{6,7},{7,4},{8,9},{9,10},{10,1... | collective-permute-start | bytes 245768 | tf_op jit(solution)/shard_map/ppermute | solution.py:170
  17.5 27.8 %collective-permute-start.5 = (f32[256,3,128]{2,0,1:T(8,128)S(1)}, f32[256,3,128]{2,0,1:T(8,128)S(1)}, u32[]{:S(2)}, u32[]{:S(2)}) collective-permute-start(f32[256,3,128]{2,0,1:T(8,128)S(1)} %get-tuple-element.95), channel_id=1, source_target_pairs={{0,1},{1,2},{2,3},{3,0},{4,5},{5,6},{6,7},{7,4},{8,9},{9,10},{10,1... | collective-permute-start | bytes 1179656 | tf_op jit(solution)/shard_map/ppermute | solution.py:19
  20.0 25.3 %collective-permute-start.6 = (f32[256,3,128]{2,0,1:T(8,128)S(1)}, f32[256,3,128]{2,0,1:T(8,128)S(1)}, u32[]{:S(2)}, u32[]{:S(2)}) collective-permute-start(f32[256,3,128]{2,0,1:T(8,128)S(1)} %get-tuple-element.96), channel_id=1, source_target_pairs={{1,0},{2,1},{3,2},{0,3},{5,4},{6,5},{7,6},{4,7},{9,8},{10,9},{11,1... | collective-permute-start | bytes 1179656 | tf_op jit(solution)/shard_map/ppermute | solution.py:21
  21.5 3.3 %collective-permute-start.3 = (bf16[256,512]{1,0:T(8,128)(2,1)S(1)}, bf16[256,512]{1,0:T(8,128)(2,1)S(1)}, u32[]{:S(2)}, u32[]{:S(2)}) collective-permute-start(bf16[256,512]{1,0:T(8,128)(2,1)S(1)} %get-tuple-element.107), channel_id=1, source_target_pairs={{0,4},{4,8},{8,12},{1,5},{5,9},{9,13},{2,6},{6,10},{10,14},{3,7},{... | collective-permute-start | bytes 786440 | tf_op jit(solution)/shard_map/ppermute | solution.py:180
  22.8 5.1 %collective-permute-start.4 = (bf16[256,512]{1,0:T(8,128)(2,1)S(1)}, bf16[256,512]{1,0:T(8,128)(2,1)S(1)}, u32[]{:S(2)}, u32[]{:S(2)}) collective-permute-start(bf16[256,512]{1,0:T(8,128)(2,1)S(1)} %get-tuple-element.107), channel_id=1, source_target_pairs={{4,0},{8,4},{12,8},{5,1},{9,5},{13,9},{6,2},{10,6},{14,10},{7,3},{... | collective-permute-start | bytes 786440 | tf_op jit(solution)/shard_map/ppermute | solution.py:181
  37.5 13.7 %copy-start.1 = (f32[9,64,256]{2,1,0:T(8,128)S(1)}, f32[9,64,256]{2,1,0:T(8,128)}, u32[]{:S(2)}) copy-start(f32[9,64,256]{2,1,0:T(8,128)} %get-tuple-element.94) | copy-start | bytes 1769476
  38.8 11.3 %collective-permute-start.10 = (f32[9,16,256]{2,1,0:T(8,128)S(1)}, f32[9,16,256]{2,1,0:T(8,128)S(1)}, u32[]{:S(2)}, u32[]{:S(2)}) collective-permute-start(f32[9,16,256]{2,1,0:T(8,128)S(1)} %get-tuple-element.102), channel_id=1, source_target_pairs={{0,8},{4,12},{8,0},{12,4},{1,9},{5,13},{9,1},{13,5},{2,10},{6,14},... | collective-permute-start | bytes 442376 | tf_op jit(solution)/shard_map/ppermute | solution.py:87
  43.3 7.9 %collective-permute-start.11 = (f32[9,16,256]{2,1,0:T(8,128)S(1)}, f32[9,16,256]{2,1,0:T(8,128)S(1)}, u32[]{:S(2)}, u32[]{:S(2)}) collective-permute-start(f32[9,16,256]{2,1,0:T(8,128)S(1)} %get-tuple-element.103), channel_id=1, source_target_pairs={{0,12},{4,8},{8,4},{12,0},{1,13},{5,9},{9,5},{13,1},{2,14},{6,10},... | collective-permute-start | bytes 442376 | tf_op jit(solution)/shard_map/ppermute | solution.py:87
  45.3 6.0 %collective-permute-start.9 = (f32[9,16,256]{2,1,0:T(8,128)S(1)}, f32[9,16,256]{2,1,0:T(8,128)S(1)}, u32[]{:S(2)}, u32[]{:S(2)}) collective-permute-start(f32[9,16,256]{2,1,0:T(8,128)S(1)} %get-tuple-element.101), channel_id=1, source_target_pairs={{0,4},{4,0},{8,12},{12,8},{1,5},{5,1},{9,13},{13,9},{2,6},{6,2},{1... | collective-permute-start | bytes 442376 | tf_op jit(solution)/shard_map/ppermute | solution.py:87
  46.4 7.0 %collective-permute-start.7 = (f32[256,1,128]{2,0,1:T(8,128)S(1)}, f32[256,1,128]{2,0,1:T(8,128)S(1)}, u32[]{:S(2)}, u32[]{:S(2)}) collective-permute-start(f32[256,1,128]{2,0,1:T(8,128)S(1)} %get-tuple-element.104), channel_id=1, source_target_pairs={{0,4},{4,8},{8,12},{1,5},{5,9},{9,13},{2,6},{6,10},{10,14},{3,7},{... | collective-permute-start | bytes 393224 | tf_op jit(solution)/shard_map/ppermute | solution.py:19
  48.8 4.5 %collective-permute-start.8 = (f32[256,1,128]{2,0,1:T(8,128)S(1)}, f32[256,1,128]{2,0,1:T(8,128)S(1)}, u32[]{:S(2)}, u32[]{:S(2)}) collective-permute-start(f32[256,1,128]{2,0,1:T(8,128)S(1)} %get-tuple-element.105), channel_id=1, source_target_pairs={{4,0},{8,4},{12,8},{5,1},{9,5},{13,9},{6,2},{10,6},{14,10},{7,3},{... | collective-permute-start | bytes 393224 | tf_op jit(solution)/shard_map/ppermute | solution.py:21
  51.3 6.1 %collective-permute-start.12 = (f32[9,16,256]{2,1,0:T(8,128)S(1)}, f32[9,16,256]{2,1,0:T(8,128)S(1)}, u32[]{:S(2)}, u32[]{:S(2)}) collective-permute-start(f32[9,16,256]{2,1,0:T(8,128)S(1)} %add_add_fusion), channel_id=1, source_target_pairs={{0,12},{4,8},{8,4},{12,0},{1,13},{5,9},{9,5},{13,1},{2,14},{6,10},... | collective-permute-start | bytes 442376 | tf_op jit(solution)/shard_map/ppermute | solution.py:92
  53.1 8.5 %collective-permute-start.13 = (f32[9,16,256]{2,1,0:T(8,128)S(1)}, f32[9,16,256]{2,1,0:T(8,128)S(1)}, u32[]{:S(2)}, u32[]{:S(2)}) collective-permute-start(f32[9,16,256]{2,1,0:T(8,128)S(1)} %add_add_fusion), channel_id=1, source_target_pairs={{0,8},{4,12},{8,0},{12,4},{1,9},{5,13},{9,1},{13,5},{2,10},{6,14},... | collective-permute-start | bytes 442376 | tf_op jit(solution)/shard_map/ppermute | solution.py:92
  53.2 8.3 %collective-permute-start.14 = (f32[9,16,256]{2,1,0:T(8,128)S(1)}, f32[9,16,256]{2,1,0:T(8,128)S(1)}, u32[]{:S(2)}, u32[]{:S(2)}) collective-permute-start(f32[9,16,256]{2,1,0:T(8,128)S(1)} %add_add_fusion), channel_id=1, source_target_pairs={{0,4},{4,0},{8,12},{12,8},{1,5},{5,1},{9,13},{13,9},{2,6},{6,2},{1... | collective-permute-start | bytes 442376 | tf_op jit(solution)/shard_map/ppermute | solution.py:92
